TPU v7x, 32 devices: a whole 2x2x4 slice. The times are simulated.
32 devices in a mesh: groups: 2 (over y), seq: 4 (over z), chan: 4 (over x, core).
Axes of the slice: x: 2, y: 2, z: 4, core: 2. Of those that a mesh axis runs over, the one named last changes fastest.
Arguments:
- outer_gate: bfloat16 [1024, 8192], P(('groups', 'seq'), 'chan'), parts along dimension 0, may hold values from -6 to 6
- inner_gate: bfloat16 [1024, 8192], P(('groups', 'seq'), 'chan'), parts along dimension 0, may hold values from -6 to 6
- signal: bfloat16 [1024, 8192], P(('groups', 'seq'), 'chan'), parts along dimension 0, may hold values from -6 to 6
- filter_in: float32 [33, 64], replicated, may hold values from -1 to 1
- filter_bias: float32 [64], replicated, may hold values from -3.140625 to 3.140625
- filter_out: float32 [64, 512], P(None, 'chan'), may hold values from -0.75 to 0.75
- decay: float32 [512], P('chan'), may hold values from 0.000390625 to 0.05
- skip_gain: float32 [8192], P('chan'), may hold values from -4 to 4
Outputs:
- mixed: bfloat16 [1024, 8192], P(('groups', 'seq'), 'chan'), parts along dimension 0
There are 2 independent parts, one for each index of `groups`. A program takes and returns all parts, laid end to end along the dimension named above; an argument that names none is the same for every part. Nothing has to cross between parts.
All inputs are finite; a program needn't handle non-finite values.
Results may differ from a plain program's by a relative error of at most 0.0052.
Values may be sent and summed in bfloat16 or wider, within the bound.
No kernel may reach another device: no remote copies, remote signals or barrier semaphores. Data moves between devices by JAX's collectives and lax.ppermute only.
A program may use at most 64 MiB of HBM per device.

v0:
```python
import jax
import jax.numpy as jnp
from jax import lax
from jax.sharding import PartitionSpec as P

GROUP = 16
BANDS = 16


def filter_rows(positions, total, filter_in, filter_bias, filter_out, decay):
    bands = 2.8 * 0.7 ** jnp.arange(BANDS, dtype=jnp.float32)
    angles = positions[:, None] * bands[None, :]
    feats = jnp.concatenate(
        [(positions / total)[:, None], jnp.cos(angles), jnp.sin(angles)], axis=1
    )
    hidden = jnp.sin(
        10.0 * (jnp.dot(feats, filter_in, precision=lax.Precision.HIGHEST) + filter_bias[None, :])
    )
    raw = lax.dot_general(
        filter_out, hidden, (((0,), (1,)), ((), ())), precision=lax.Precision.HIGHEST
    )
    envelope = jnp.sqrt(2.0 * decay)[:, None] * jnp.exp(-decay[:, None] * positions[None, :])
    return (raw * envelope).astype(jnp.bfloat16)


def toeplitz_part(window, out_rows, in_rows):
    filter_count = window.shape[0]
    span_len = out_rows + in_rows
    extended = jnp.concatenate([window, jnp.zeros((filter_count, 1), window.dtype)], axis=1)
    tiled = jnp.tile(extended, (1, in_rows))
    skewed = tiled[:, : in_rows * span_len].reshape(filter_count, in_rows, span_len)
    return skewed[:, :, in_rows : in_rows + out_rows]


def add_block(total, padded, out_start, piece, start, front):
    out_rows = total.shape[2]
    in_rows = piece.shape[2]
    base = out_start - start - in_rows + front
    window = lax.dynamic_slice_in_dim(padded, base, out_rows + in_rows, 1)
    matrix = toeplitz_part(window, out_rows, in_rows)
    part = jnp.einsum("gjs,gst->gjt", piece, matrix, preferred_element_type=jnp.float32)
    return total + part


def per_device(
    outer_gate, inner_gate, signal, filter_in, filter_bias, filter_out, decay, skip_gain
):
    own_rows = signal.shape[0]
    width_all = signal.shape[1]
    total_rows = own_rows * lax.axis_size("seq")
    total = float(total_rows)
    out_start = lax.axis_index("seq") * own_rows
    gated = (inner_gate.astype(jnp.float32) * signal.astype(jnp.float32)).astype(jnp.bfloat16)
    positions = (out_start + jnp.arange(own_rows, dtype=jnp.int32)).astype(jnp.float32)
    segment = filter_rows(positions, total, filter_in, filter_bias, filter_out, decay)
    filters = lax.all_gather(segment, "seq", axis=1, tiled=True)
    count = filters.shape[0]
    gated_cols = gated.T.reshape(count, GROUP, own_rows)
    padded = jnp.concatenate([jnp.zeros((count, own_rows), jnp.bfloat16), filters], axis=1)
    empty = jnp.zeros((count, GROUP, own_rows), jnp.float32)
    piece = lax.all_gather(gated_cols, "seq", axis=2, tiled=True)
    step_rows = min(piece.shape[2], own_rows)
    blocks_count = piece.shape[2] // step_rows

    def one_block(index, inner):
        sub_start = index * step_rows
        block = lax.dynamic_slice_in_dim(piece, index * step_rows, step_rows, 2)
        return lax.cond(
            sub_start < out_start + own_rows,
            lambda acc: add_block(acc, padded, out_start, block, sub_start, own_rows),
            lambda acc: acc,
            inner,
        )

    conv_cols = lax.fori_loop(0, blocks_count, one_block, empty)
    conv = conv_cols.reshape(width_all, own_rows).T
    mixed = outer_gate.astype(jnp.float32) * (conv + skip_gain[None, :] * gated.astype(jnp.float32))
    return mixed.astype(jnp.bfloat16)


def solution(mesh):
    placed = (
        P(("groups", "seq"), "chan"),
        P(("groups", "seq"), "chan"),
        P(("groups", "seq"), "chan"),
        P(),
        P(),
        P(None, "chan"),
        P("chan"),
        P("chan"),
    )
    return jax.shard_map(
        per_device,
        mesh=mesh,
        in_specs=placed,
        out_specs=P(("groups", "seq"), "chan"),
        check_vma=False,
    )
```

profile of v0, /device:TPU:27, one launch (start us, length us, event | category | flops | bytes accessed | tf_op | source)
XLA Modules:
  0.0 197.5 jit_solution(15419739358252230036)
XLA Ops:
  6.5 0.0 copy-start
  6.5 0.0 copy-start.2
  6.5 0.0 copy-start.5
  6.5 0.0 copy-start.4
  6.5 0.0 copy-start.6
  6.5 0.0 all-gather.2.cloned.1.call-start
  6.6 1.4 copy.19
  8.0 1.3 copy.20
  9.3 0.9 multiply_convert_fusion
  10.2 0.0 all-gather.2.cloned.1.call-update
  10.2 0.0 copy-done.2
  10.3 0.3 copy.18
  10.6 0.0 copy-done.5
  10.6 0.1 multiply_cosine_fusion
  10.7 0.0 copy-done.4
  10.7 0.0 copy-done.6
  10.7 0.4 fusion.5
  11.1 0.0 copy-done
  11.1 0.3 fusion.3
  11.4 11.1 %all_gather.7 = bf16[128,512]{0,1:T(8,128)(2,1)S(1)} all-gather(bf16[128,128]{0,1:T(8,128)(2,1)S(1)} %fusion.3), channel_id=1, replica_groups=mesh['groups'=2,'seq'=4,'chan'=4] {'seq'}, dimensions={1}, use_global_device_ids=true | all-gather | bytes 163840 | tf_op jit(solution)/shard_map/all_gather | solution.py:56
  22.5 33.0 %all-gather.2.cloned.1.call-done = bf16[128,16,512]{2,1,0:T(8,128)(2,1)} async-done(((bf16[128,16,128]{2,1,0:T(8,128)(2,1)}), bf16[128,16,512]{2,1,0:T(8,128)(2,1)}) %all-gather.2.cloned.1.call-update) | async-done | bytes 2097168 | tf_op jit(solution)/shard_map/all_gather | solution.py:61
  55.5 0.1 broadcast_in_dim.2
  55.5 0.0 copy-start.1
  55.6 0.0 copy-start.3
  55.6 133.7 %while.17 = (s32[]{:T(128)}, f32[128,16,128]{2,1,0:T(8,128)S(1)}, s32[]{:T(128)}, bf16[128,16,512]{2,1,0:T(8,128)(2,1)}, s32[]{:T(128)}, /*index=5*/bf16[128,640]{0,1:T(8,128)(2,1)S(1)}, s32[]{:T(128)}, s32[]{:T(128)}) while((s32[]{:T(128)}, f32[128,16,128]{2,1,0:T(8,128)S(1)}, s32[]{:T(128)}, bf16[128,16,512]{2,1,0:T(8,128)(2,1)}, s32[]{:T(128)}, ...), condition=%wide.region_3.0_spmd, body=%wide.region_0.0_spmd.sunk | while | flops 67371024 | bytes 74351376 | solution.py:75
  55.6 33.4 %conditional.2 = (f32[128,16,128]{2,1,0:T(8,128)S(1)}) conditional(s32[]{:T(128)} %convert_element_type.67, f32[128,16,128]{2,1,0:T(8,128)S(1)} %get-tuple-element.259, (s32[]{:T(128)}, bf16[128,16,512]{2,1,0:T(8,128)(2,1)}, s32[]{:T(128)}, bf16[128,640]{0,1:T(8,128)(2,1)S(1)}, f32[128,16,128]{2,1,0:T(8,128)S(1)}) %tuple.53), branch_computations={%region_1.0_spmd, %region_2.0_spmd} | conditional | flops 67371016 | bytes 74351224 | solution.py:68
  55.7 4.5 %tile.4 = bf16[128,128,257]{0,2,1:T(8,128)(2,1)} broadcast(bf16[128,257]{0,1:T(8,128)(2,1)S(1)} %concatenate.6), dimensions={0,2} | broadcast | bytes 8487168 | tf_op jit(solution)/shard_map/while/body/eval_jaxpr/cond/branch_1_fun/tile | solution.py:30
  60.1 12.9 %tile.10 = bf16[128,32896]{0,1:T(8,128)(2,1)} reshape(bf16[128,128,257]{0,2,1:T(8,128)(2,1)} %tile.4) | data formatting | bytes 16842752 | tf_op jit(solution)/shard_map/while/body/eval_jaxpr/cond/branch_1_fun/tile | solution.py:30
  73.0 0.0 slice-start
  73.0 3.4 %slice-done = bf16[128,32768]{0,1:T(8,128)(2,1)S(1)} async-done(((bf16[128,32896]{0,1:T(8,128)(2,1)}), bf16[128,32768]{0,1:T(8,128)(2,1)S(1)}, s32[]{:S(2)}) %slice-start) | async-done | bytes 8388632 | tf_op jit(solution)/shard_map/while/body/eval_jaxpr/cond/branch_1_fun/slice | solution.py:31
  76.4 2.3 %slice.11 = bf16[128,128,128]{0,2,1:T(8,128)(2,1)} slice(bf16[128,128,256]{0,2,1:T(8,128)(2,1)S(1)} %bitcast.24), slice={[0:128], [0:128], [128:256]} | slice | bytes 8388608 | tf_op jit(solution)/shard_map/while/body/eval_jaxpr/cond/branch_1_fun/slice | solution.py:32
  78.7 6.8 %copy.23 = bf16[128,128,128]{2,1,0:T(8,128)(2,1)} copy(bf16[128,128,128]{0,2,1:T(8,128)(2,1)} %slice.11) | data formatting | bytes 8388608 | tf_op jit(solution)/shard_map/while/body/eval_jaxpr/cond
  85.4 3.6 %convolution_add_fusion = f32[128,16,128]{2,1,0:T(8,128)S(1)} fusion(f32[128,16,128]{2,1,0:T(8,128)S(1)} %get-tuple-element.177, bf16[128,128,128]{2,1,0:T(8,128)(2,1)} %copy.23, bf16[128,16,512]{2,1,0:T(8,128)(2,1)} %get-tuple-element.178, s32[]{:T(128)S(6)} %select_n.14), kind=kOutput, calls=%fused_computation | convolution fusion | flops 67371008 | bytes 6815748 | tf_op jit(solution)/shard_map/while/body/eval_jaxpr/cond/branch_1_fun/gjs,gst->gjt/dot_general | solution.py:41
  89.0 33.4 %conditional.2 = (f32[128,16,128]{2,1,0:T(8,128)S(1)}) conditional(s32[]{:T(128)} %convert_element_type.67, f32[128,16,128]{2,1,0:T(8,128)S(1)} %get-tuple-element.259, (s32[]{:T(128)}, bf16[128,16,512]{2,1,0:T(8,128)(2,1)}, s32[]{:T(128)}, bf16[128,640]{0,1:T(8,128)(2,1)S(1)}, f32[128,16,128]{2,1,0:T(8,128)S(1)}) %tuple.53), branch_computations={%region_1.0_spmd, %region_2.0_spmd} | conditional | flops 67371016 | bytes 74351224 | solution.py:68
  89.1 4.5 %tile.4 = bf16[128,128,257]{0,2,1:T(8,128)(2,1)} broadcast(bf16[128,257]{0,1:T(8,128)(2,1)S(1)} %concatenate.6), dimensions={0,2} | broadcast | bytes 8487168 | tf_op jit(solution)/shard_map/while/body/eval_jaxpr/cond/branch_1_fun/tile | solution.py:30
  93.5 12.9 %tile.10 = bf16[128,32896]{0,1:T(8,128)(2,1)} reshape(bf16[128,128,257]{0,2,1:T(8,128)(2,1)} %tile.4) | data formatting | bytes 16842752 | tf_op jit(solution)/shard_map/while/body/eval_jaxpr/cond/branch_1_fun/tile | solution.py:30
  106.4 0.0 slice-start
  106.4 3.4 %slice-done = bf16[128,32768]{0,1:T(8,128)(2,1)S(1)} async-done(((bf16[128,32896]{0,1:T(8,128)(2,1)}), bf16[128,32768]{0,1:T(8,128)(2,1)S(1)}, s32[]{:S(2)}) %slice-start) | async-done | bytes 8388632 | tf_op jit(solution)/shard_map/while/body/eval_jaxpr/cond/branch_1_fun/slice | solution.py:31
  109.8 2.3 %slice.11 = bf16[128,128,128]{0,2,1:T(8,128)(2,1)} slice(bf16[128,128,256]{0,2,1:T(8,128)(2,1)S(1)} %bitcast.24), slice={[0:128], [0:128], [128:256]} | slice | bytes 8388608 | tf_op jit(solution)/shard_map/while/body/eval_jaxpr/cond/branch_1_fun/slice | solution.py:32
  112.1 6.8 %copy.23 = bf16[128,128,128]{2,1,0:T(8,128)(2,1)} copy(bf16[128,128,128]{0,2,1:T(8,128)(2,1)} %slice.11) | data formatting | bytes 8388608 | tf_op jit(solution)/shard_map/while/body/eval_jaxpr/cond
  118.9 3.6 %convolution_add_fusion = f32[128,16,128]{2,1,0:T(8,128)S(1)} fusion(f32[128,16,128]{2,1,0:T(8,128)S(1)} %get-tuple-element.177, bf16[128,128,128]{2,1,0:T(8,128)(2,1)} %copy.23, bf16[128,16,512]{2,1,0:T(8,128)(2,1)} %get-tuple-element.178, s32[]{:T(128)S(6)} %select_n.14), kind=kOutput, calls=%fused_computation | convolution fusion | flops 67371008 | bytes 6815748 | tf_op jit(solution)/shard_map/while/body/eval_jaxpr/cond/branch_1_fun/gjs,gst->gjt/dot_general | solution.py:41
  122.4 33.4 %conditional.2 = (f32[128,16,128]{2,1,0:T(8,128)S(1)}) conditional(s32[]{:T(128)} %convert_element_type.67, f32[128,16,128]{2,1,0:T(8,128)S(1)} %get-tuple-element.259, (s32[]{:T(128)}, bf16[128,16,512]{2,1,0:T(8,128)(2,1)}, s32[]{:T(128)}, bf16[128,640]{0,1:T(8,128)(2,1)S(1)}, f32[128,16,128]{2,1,0:T(8,128)S(1)}) %tuple.53), branch_computations={%region_1.0_spmd, %region_2.0_spmd} | conditional | flops 67371016 | bytes 74351224 | solution.py:68
  122.5 4.5 %tile.4 = bf16[128,128,257]{0,2,1:T(8,128)(2,1)} broadcast(bf16[128,257]{0,1:T(8,128)(2,1)S(1)} %concatenate.6), dimensions={0,2} | broadcast | bytes 8487168 | tf_op jit(solution)/shard_map/while/body/eval_jaxpr/cond/branch_1_fun/tile | solution.py:30
  127.0 12.9 %tile.10 = bf16[128,32896]{0,1:T(8,128)(2,1)} reshape(bf16[128,128,257]{0,2,1:T(8,128)(2,1)} %tile.4) | data formatting | bytes 16842752 | tf_op jit(solution)/shard_map/while/body/eval_jaxpr/cond/branch_1_fun/tile | solution.py:30
  139.9 0.0 slice-start
  139.9 3.4 %slice-done = bf16[128,32768]{0,1:T(8,128)(2,1)S(1)} async-done(((bf16[128,32896]{0,1:T(8,128)(2,1)}), bf16[128,32768]{0,1:T(8,128)(2,1)S(1)}, s32[]{:S(2)}) %slice-start) | async-done | bytes 8388632 | tf_op jit(solution)/shard_map/while/body/eval_jaxpr/cond/branch_1_fun/slice | solution.py:31
  143.2 2.3 %slice.11 = bf16[128,128,128]{0,2,1:T(8,128)(2,1)} slice(bf16[128,128,256]{0,2,1:T(8,128)(2,1)S(1)} %bitcast.24), slice={[0:128], [0:128], [128:256]} | slice | bytes 8388608 | tf_op jit(solution)/shard_map/while/body/eval_jaxpr/cond/branch_1_fun/slice | solution.py:32
  145.5 6.8 %copy.23 = bf16[128,128,128]{2,1,0:T(8,128)(2,1)} copy(bf16[128,128,128]{0,2,1:T(8,128)(2,1)} %slice.11) | data formatting | bytes 8388608 | tf_op jit(solution)/shard_map/while/body/eval_jaxpr/cond
  152.3 3.6 %convolution_add_fusion = f32[128,16,128]{2,1,0:T(8,128)S(1)} fusion(f32[128,16,128]{2,1,0:T(8,128)S(1)} %get-tuple-element.177, bf16[128,128,128]{2,1,0:T(8,128)(2,1)} %copy.23, bf16[128,16,512]{2,1,0:T(8,128)(2,1)} %get-tuple-element.178, s32[]{:T(128)S(6)} %select_n.14), kind=kOutput, calls=%fused_computation | convolution fusion | flops 67371008 | bytes 6815748 | tf_op jit(solution)/shard_map/while/body/eval_jaxpr/cond/branch_1_fun/gjs,gst->gjt/dot_general | solution.py:41
  155.9 33.4 %conditional.2 = (f32[128,16,128]{2,1,0:T(8,128)S(1)}) conditional(s32[]{:T(128)} %convert_element_type.67, f32[128,16,128]{2,1,0:T(8,128)S(1)} %get-tuple-element.259, (s32[]{:T(128)}, bf16[128,16,512]{2,1,0:T(8,128)(2,1)}, s32[]{:T(128)}, bf16[128,640]{0,1:T(8,128)(2,1)S(1)}, f32[128,16,128]{2,1,0:T(8,128)S(1)}) %tuple.53), branch_computations={%region_1.0_spmd, %region_2.0_spmd} | conditional | flops 67371016 | bytes 74351224 | solution.py:68
  155.9 4.5 %tile.4 = bf16[128,128,257]{0,2,1:T(8,128)(2,1)} broadcast(bf16[128,257]{0,1:T(8,128)(2,1)S(1)} %concatenate.6), dimensions={0,2} | broadcast | bytes 8487168 | tf_op jit(solution)/shard_map/while/body/eval_jaxpr/cond/branch_1_fun/tile | solution.py:30
  160.4 12.9 %tile.10 = bf16[128,32896]{0,1:T(8,128)(2,1)} reshape(bf16[128,128,257]{0,2,1:T(8,128)(2,1)} %tile.4) | data formatting | bytes 16842752 | tf_op jit(solution)/shard_map/while/body/eval_jaxpr/cond/branch_1_fun/tile | solution.py:30
  173.3 0.0 slice-start
  173.3 3.4 %slice-done = bf16[128,32768]{0,1:T(8,128)(2,1)S(1)} async-done(((bf16[128,32896]{0,1:T(8,128)(2,1)}), bf16[128,32768]{0,1:T(8,128)(2,1)S(1)}, s32[]{:S(2)}) %slice-start) | async-done | bytes 8388632 | tf_op jit(solution)/shard_map/while/body/eval_jaxpr/cond/branch_1_fun/slice | solution.py:31
  176.7 2.3 %slice.11 = bf16[128,128,128]{0,2,1:T(8,128)(2,1)} slice(bf16[128,128,256]{0,2,1:T(8,128)(2,1)S(1)} %bitcast.24), slice={[0:128], [0:128], [128:256]} | slice | bytes 8388608 | tf_op jit(solution)/shard_map/while/body/eval_jaxpr/cond/branch_1_fun/slice | solution.py:32
  178.9 6.8 %copy.23 = bf16[128,128,128]{2,1,0:T(8,128)(2,1)} copy(bf16[128,128,128]{0,2,1:T(8,128)(2,1)} %slice.11) | data formatting | bytes 8388608 | tf_op jit(solution)/shard_map/while/body/eval_jaxpr/cond
  185.7 3.6 %convolution_add_fusion = f32[128,16,128]{2,1,0:T(8,128)S(1)} fusion(f32[128,16,128]{2,1,0:T(8,128)S(1)} %get-tuple-element.177, bf16[128,128,128]{2,1,0:T(8,128)(2,1)} %copy.23, bf16[128,16,512]{2,1,0:T(8,128)(2,1)} %get-tuple-element.178, s32[]{:T(128)S(6)} %select_n.14), kind=kOutput, calls=%fused_computation | convolution fusion | flops 67371008 | bytes 6815748 | tf_op jit(solution)/shard_map/while/body/eval_jaxpr/cond/branch_1_fun/gjs,gst->gjt/dot_general | solution.py:41
  189.3 0.0 copy-done.1
  189.3 0.0 copy-done.3
  189.3 0.3 fusion.7
  189.6 1.0 copy.21
  (13 shorter events, 0.2 us)
Async XLA Ops:
  6.5 4.6 %copy-start = (f32[64,128]{1,0:T(8,128)S(1)}, f32[64,128]{1,0:T(8,128)}, u32[]{:S(2)}) copy-start(f32[64,128]{1,0:T(8,128)} %param.17) | copy-start | bytes 98308
  6.5 3.7 %copy-start.2 = (bf16[128,2048]{1,0:T(8,128)(2,1)S(1)}, bf16[128,2048]{1,0:T(8,128)(2,1)}, u32[]{:S(2)}) copy-start(bf16[128,2048]{1,0:T(8,128)(2,1)} %param.12) | copy-start | bytes 1572868
  6.5 4.0 %copy-start.5 = (f32[128]{0:T(128)S(1)}, f32[128]{0:T(128)}, u32[]{:S(2)}) copy-start(f32[128]{0:T(128)} %param.18) | copy-start | bytes 1540
  6.5 4.2 %copy-start.4 = (f32[33,64]{1,0:T(8,128)S(1)}, f32[33,64]{1,0:T(8,128)}, u32[]{:S(2)}) copy-start(f32[33,64]{1,0:T(8,128)} %param.15) | copy-start | bytes 25348
  6.5 4.2 %copy-start.6 = (f32[64]{0:T(128)S(1)}, f32[64]{0:T(128)}, u32[]{:S(2)}) copy-start(f32[64]{0:T(128)} %param.16) | copy-start | bytes 772
  6.5 48.9 %all-gather.2.cloned.1.call-start = ((), (), s32[]{:S(2)}) async-start(), calls=%async_computation | async-start | bytes 2621440 | tf_op jit(solution)/shard_map/all_gather | solution.py:61
  55.5 133.7 %copy-start.1 = (bf16[128,2048]{0,1:T(8,128)(2,1)S(1)}, bf16[128,2048]{0,1:T(8,128)(2,1)}, u32[]{:S(2)}) copy-start(bf16[128,2048]{0,1:T(8,128)(2,1)} %multiply_convert_fusion) | copy-start | bytes 1572868
  55.6 133.7 %copy-start.3 = (f32[2048]{0:T(1024)S(1)}, f32[2048]{0:T(1024)}, u32[]{:S(2)}) copy-start(f32[2048]{0:T(1024)} %param.19) | copy-start | bytes 24580
  73.0 3.4 %slice-start = ((bf16[128,32896]{0,1:T(8,128)(2,1)}), bf16[128,32768]{0,1:T(8,128)(2,1)S(1)}, s32[]{:S(2)}) async-start(bf16[128,32896]{0,1:T(8,128)(2,1)} %tile.10), calls=%async_computation.1 | async-start | bytes 16777216 | tf_op jit(solution)/shard_map/while/body/eval_jaxpr/cond/branch_1_fun/slice | solution.py:31
  106.4 3.4 %slice-start = ((bf16[128,32896]{0,1:T(8,128)(2,1)}), bf16[128,32768]{0,1:T(8,128)(2,1)S(1)}, s32[]{:S(2)}) async-start(bf16[128,32896]{0,1:T(8,128)(2,1)} %tile.10), calls=%async_computation.1 | async-start | bytes 16777216 | tf_op jit(solution)/shard_map/while/body/eval_jaxpr/cond/branch_1_fun/slice | solution.py:31
  139.9 3.4 %slice-start = ((bf16[128,32896]{0,1:T(8,128)(2,1)}), bf16[128,32768]{0,1:T(8,128)(2,1)S(1)}, s32[]{:S(2)}) async-start(bf16[128,32896]{0,1:T(8,128)(2,1)} %tile.10), calls=%async_computation.1 | async-start | bytes 16777216 | tf_op jit(solution)/shard_map/while/body/eval_jaxpr/cond/branch_1_fun/slice | solution.py:31
  173.3 3.4 %slice-start = ((bf16[128,32896]{0,1:T(8,128)(2,1)}), bf16[128,32768]{0,1:T(8,128)(2,1)S(1)}, s32[]{:S(2)}) async-start(bf16[128,32896]{0,1:T(8,128)(2,1)} %tile.10), calls=%async_computation.1 | async-start | bytes 16777216 | tf_op jit(solution)/shard_map/while/body/eval_jaxpr/cond/branch_1_fun/slice | solution.py:31
Sparse Core Ops, SparseCore 0:
  10.4 45.0 all-gather.1
where the time goes:
time: 200 us; the launch traced here: 197 us
  local copies, waits for them, and re-layouts  123 us (62%)
  waiting for transfers between devices  33 us (16%)
  matrix products  14.9 us (7%)
  between operations  13.6 us (7%)
  blocking collectives  11.1 us (6%)
    another operation x8, local copies, waits for them, and re-layouts, toeplitz_part(): tiled = jnp.tile(extended, (1, in_rows))  69.4 us
    all_gather x1, waiting for transfers between devices, per_device(): piece = lax.all_gather(gated_cols, 'seq', axis=2, tiled=True)  33 us
    cond x4, local copies, waits for them, and re-layouts  27 us
    dot_general x4, matrix products, add_block(): jnp.einsum('gjs,gst->gjt', piece, matrix, preferred_element_type=jnp.floa...  14.3 us
    slice x8, local copies, waits for them, and re-layouts, toeplitz_part(): tiled[:, :in_rows * span_len].reshape(filter_count, in_rows, span_len)  13.5 us
    all_gather x1, blocking collectives, per_device(): filters = lax.all_gather(segment, 'seq', axis=1, tiled=True)  11.1 us
    slice x4, local copies, waits for them, and re-layouts, toeplitz_part(): return skewed[:, :, in_rows:in_rows + out_rows]  9.1 us
  transfers between devices with their start and end apart: 1, of which 1 were waited for; matrix products, arithmetic and copies ran while one was open for 1% of the time, Pallas kernels for 0%

commit v1 on v0

v1 whole, which is shorter than its diff:
```python
import functools

import jax
import jax.numpy as jnp
from jax import lax
from jax.experimental import pallas as pl
from jax.experimental.pallas import tpu as pltpu
from jax.sharding import PartitionSpec as P

GROUP = 16
BANDS = 16
FILTERS_PER_STEP = 8


def filter_table(positions, total, filter_in, filter_bias, filter_out, decay):
    bands = 2.8 * 0.7 ** jnp.arange(BANDS, dtype=jnp.float32)
    angles = positions[:, None] * bands[None, :]
    feats = jnp.concatenate(
        [(positions / total)[:, None], jnp.cos(angles), jnp.sin(angles)], axis=1
    )
    hidden = jnp.sin(
        10.0 * (jnp.dot(feats, filter_in, precision=lax.Precision.HIGHEST) + filter_bias[None, :])
    )
    raw = jnp.dot(hidden, filter_out, precision=lax.Precision.HIGHEST)
    envelope = jnp.sqrt(2.0 * decay)[None, :] * jnp.exp(-decay[None, :] * positions[:, None])
    return (raw * envelope).astype(jnp.bfloat16)


def toeplitz_kernel(s_ref, filt_ref, x_ref, o_ref, *, block, own):
    fb = filt_ref.shape[1]
    s = s_ref[0]
    upper = (lax.broadcasted_iota(jnp.int32, (block, block), 1)
             >= lax.broadcasted_iota(jnp.int32, (block, block), 0))

    def rolled(g, k):
        w = filt_ref[k + 1, pl.ds(g, block, stride=0), :]
        return pltpu.roll(w, 0, 1, stride=1, stride_axis=0)

    for g in range(fb):
        rows = slice(g * GROUP, (g + 1) * GROUP)
        r0 = rolled(g, 0)
        if own:
            t0 = jnp.where(upper, r0, 0.0).astype(jnp.bfloat16)
            o_ref[rows, :] = jnp.dot(x_ref[0, rows, :], t0, preferred_element_type=jnp.float32)
        else:
            def body(d, carry):
                acc, prev = carry
                cur = rolled(g, d)
                t = jnp.where(upper, cur, prev).astype(jnp.bfloat16)
                acc = acc + jnp.dot(x_ref[s - d, rows, :], t, preferred_element_type=jnp.float32)
                return acc, cur

            acc0 = jnp.zeros((GROUP, block), jnp.float32)
            acc, _ = lax.fori_loop(1, s + 1, body, (acc0, r0))
            o_ref[rows, :] = acc


def toeplitz_conv(s, filt, x, own):
    nb, chans, block = x.shape
    count = filt.shape[1]
    fb = FILTERS_PER_STEP
    kernel = functools.partial(toeplitz_kernel, block=block, own=own)
    return pl.pallas_call(
        kernel,
        out_shape=jax.ShapeDtypeStruct((chans, block), jnp.float32),
        grid_spec=pltpu.PrefetchScalarGridSpec(
            num_scalar_prefetch=1,
            grid=(count // fb,),
            in_specs=[
                pl.BlockSpec((filt.shape[0], fb, block), lambda i, s_: (0, i, 0)),
                pl.BlockSpec((nb, fb * GROUP, block), lambda i, s_: (0, i, 0)),
            ],
            out_specs=pl.BlockSpec((fb * GROUP, block), lambda i, s_: (i, 0)),
        ),
    )(s, filt, x)


def per_device(
    outer_gate, inner_gate, signal, filter_in, filter_bias, filter_out, decay, skip_gain
):
    own_rows = signal.shape[0]
    nb = lax.axis_size("seq")
    total_rows = own_rows * nb
    s = lax.axis_index("seq")
    gated = (inner_gate.astype(jnp.float32) * signal.astype(jnp.float32)).astype(jnp.bfloat16)
    gated_t = gated.T
    positions = jnp.arange(total_rows, dtype=jnp.int32).astype(jnp.float32)
    filters = filter_table(positions, float(total_rows), filter_in, filter_bias, filter_out, decay)
    count = filters.shape[1]
    lagged = filters.astype(jnp.float32).reshape(nb, own_rows, count).transpose(0, 2, 1)
    filt = jnp.concatenate([jnp.zeros((1, count, own_rows), jnp.float32), lagged], axis=0)
    s_arr = jnp.reshape(s, (1,)).astype(jnp.int32)
    own = toeplitz_conv(s_arr, filt, gated_t[None], True)
    gathered = lax.all_gather(gated_t, "seq", axis=0, tiled=False)
    rest = toeplitz_conv(s_arr, filt, gathered, False)
    conv = (own + rest).T
    mixed = outer_gate.astype(jnp.float32) * (conv + skip_gain[None, :] * gated.astype(jnp.float32))
    return mixed.astype(jnp.bfloat16)


def solution(mesh):
    placed = (
        P(("groups", "seq"), "chan"),
        P(("groups", "seq"), "chan"),
        P(("groups", "seq"), "chan"),
        P(),
        P(),
        P(None, "chan"),
        P("chan"),
        P("chan"),
    )
    return jax.shard_map(
        per_device,
        mesh=mesh,
        in_specs=placed,
        out_specs=P(("groups", "seq"), "chan"),
        check_vma=False,
    )
```

time: 200 us -> 157 us (0.79)
  the two profiles are of different devices: /device:TPU:27 before, /device:TPU:25 now
where the time goes in v1:
time: 157 us; the launch traced here: 156 us
  Pallas kernels  101 us (64%)
  waiting for transfers between devices  32.3 us (21%)
  between operations  13.5 us (9%)
  local copies, waits for them, and re-layouts  4.14 us (3%)
  other arithmetic  3.77 us (2%)
    pallas_call x2, Pallas kernels, toeplitz_conv(): pl.pallas_call(kernel, out_shape=jax.ShapeDtypeStruct((chans, block), jnp...  101 us
    all_gather x1, waiting for transfers between devices, per_device(): gathered = lax.all_gather(gated_t, 'seq', axis=0, tiled=False)  32.2 us
  transfers between devices with their start and end apart: 1, of which 1 were waited for; matrix products, arithmetic and copies ran while one was open for 2% of the time, Pallas kernels for 6%

profile of v1, /device:TPU:25, one launch (start us, length us, event | category | flops | bytes accessed | tf_op | source)
XLA Modules:
  0.0 155.8 jit_solution(3863457682584095308)
XLA Ops:
  6.5 0.0 copy-start
  6.5 0.0 all-gather.3.cloned.1.call-start
  6.5 1.3 copy.20
  7.9 0.0 copy-start.6
  7.9 0.0 copy-start.3
  7.9 0.0 copy-start.5
  7.9 0.0 copy-start.2
  7.9 1.4 copy.21
  9.3 1.1 fusion.12
  10.4 0.0 all-gather.3.cloned.1.call-update
  10.5 0.0 copy-done.6
  10.5 0.2 multiply_cosine_fusion
  10.7 0.0 copy-done.3
  10.7 0.0 copy-done.5
  10.7 0.7 fusion.2
  11.5 0.0 copy-done
  11.5 0.6 fusion
  12.1 0.1 copy.19
  12.2 0.0 copy-done.2
  12.2 0.3 copy.18
  12.5 0.8 pad_convert_fusion.filt_ref
  13.3 9.9 %shard_map.82 = f32[2048,128]{1,0:T(8,128)} custom-call(s32[1]{0:T(128)} %bitcast.s_ref, f32[5,128,128]{2,1,0:T(8,128)} %pad_convert_fusion.filt_ref, bf16[1,2048,128]{2,1,0:T(8,128)(2,1)} %get-tuple-element.6.x_ref), custom_call_target="tpu_custom_call" | custom-call | tf_op jit(solution)/shard_map/pallas_call | solution.py:63
  23.2 0.0 copy-start.1
  23.2 0.0 copy-start.4
  23.2 32.2 %all-gather.3.cloned.1.call-done = bf16[8192,128]{1,0:T(8,128)(2,1)} async-done(((bf16[2048,128]{1,0:T(8,128)(2,1)}), bf16[8192,128]{1,0:T(8,128)(2,1)}) %all-gather.3.cloned.1.call-update) | async-done | bytes 2097168 | tf_op jit(solution)/shard_map/all_gather | solution.py:94
  55.5 90.8 %shard_map.83 = f32[2048,128]{1,0:T(8,128)} custom-call(s32[1]{0:T(128)} %bitcast.s_ref, f32[5,128,128]{2,1,0:T(8,128)} %pad_convert_fusion.filt_ref, bf16[4,2048,128]{2,1,0:T(8,128)(2,1)} %bitcast.18), custom_call_target="tpu_custom_call" | custom-call | tf_op jit(solution)/shard_map/pallas_call | solution.py:63
  146.3 0.0 copy-done.1
  146.3 0.0 copy-done.4
  146.3 1.7 %fusion.4 = bf16[128,2048]{0,1:T(8,128)(2,1)S(1)} fusion(f32[2048,128]{1,0:T(8,128)S(1)} %copy-done.1, f32[2048,128]{1,0:T(8,128)} %shard_map.83, bf16[128,2048]{0,1:T(8,128)(2,1)S(1)} %copy.18, f32[2048]{0:T(1024)S(1)} %copy-done.4, bf16[128,2048]{0,1:T(8,128)(2,1)S(1)} %copy.21, bf16[128,2048]{0,1:T(8,128)(2,1)S(1)} %copy.20), kind=kLoop, calls=%fused_computation.7 | loop fusion | flops 2883584 | bytes 4202496 | tf_op jit(solution)/shard_map/convert_element_type | solution.py:98
  148.0 1.0 copy.22
  (4 shorter events, 0.0 us)
Async XLA Ops:
  6.5 5.0 %copy-start = (f32[64,128]{1,0:T(8,128)S(1)}, f32[64,128]{1,0:T(8,128)}, u32[]{:S(2)}) copy-start(f32[64,128]{1,0:T(8,128)} %param.13) | copy-start | bytes 98308
  6.5 48.9 %all-gather.3.cloned.1.call-start = ((), (), s32[]{:S(2)}) async-start(), calls=%async_computation | async-start | bytes 2621440 | tf_op jit(solution)/shard_map/all_gather | solution.py:94
  7.9 2.6 %copy-start.6 = (f32[128]{0:T(128)S(1)}, f32[128]{0:T(128)}, u32[]{:S(2)}) copy-start(f32[128]{0:T(128)} %param.14) | copy-start | bytes 1540
  7.9 2.8 %copy-start.3 = (f32[33,64]{1,0:T(8,128)S(1)}, f32[33,64]{1,0:T(8,128)}, u32[]{:S(2)}) copy-start(f32[33,64]{1,0:T(8,128)} %param.11) | copy-start | bytes 25348
  7.9 2.8 %copy-start.5 = (f32[64]{0:T(128)S(1)}, f32[64]{0:T(128)}, u32[]{:S(2)}) copy-start(f32[64]{0:T(128)} %param.12) | copy-start | bytes 772
  7.9 4.3 %copy-start.2 = (bf16[128,2048]{1,0:T(8,128)(2,1)S(1)}, bf16[128,2048]{1,0:T(8,128)(2,1)}, u32[]{:S(2)}) copy-start(bf16[128,2048]{1,0:T(8,128)(2,1)} %param.8) | copy-start | bytes 1572868
  23.2 123.1 %copy-start.1 = (f32[2048,128]{1,0:T(8,128)S(1)}, f32[2048,128]{1,0:T(8,128)}, u32[]{:S(2)}) copy-start(f32[2048,128]{1,0:T(8,128)} %shard_map.82) | copy-start | bytes 3145732
  23.2 123.1 %copy-start.4 = (f32[2048]{0:T(1024)S(1)}, f32[2048]{0:T(1024)}, u32[]{:S(2)}) copy-start(f32[2048]{0:T(1024)} %param.15) | copy-start | bytes 24580
Sparse Core Ops, SparseCore 0:
  10.6 44.8 all-gather.2

commit v2 on v1

v2 whole, which is shorter than its diff:
```python
import functools

import jax
import jax.numpy as jnp
from jax import lax
from jax.experimental import pallas as pl
from jax.experimental.pallas import tpu as pltpu
from jax.sharding import PartitionSpec as P

GROUP = 16
BANDS = 16
FILTERS_PER_STEP = 8


def filter_table(positions, total, filter_in, filter_bias, filter_out, decay):
    bands = 2.8 * 0.7 ** jnp.arange(BANDS, dtype=jnp.float32)
    angles = positions[:, None] * bands[None, :]
    feats = jnp.concatenate(
        [(positions / total)[:, None], jnp.cos(angles), jnp.sin(angles)], axis=1
    )
    hidden = jnp.sin(
        10.0 * (jnp.dot(feats, filter_in, precision=lax.Precision.HIGHEST) + filter_bias[None, :])
    )
    raw = jnp.dot(hidden, filter_out, precision=lax.Precision.HIGHEST)
    envelope = jnp.sqrt(2.0 * decay)[None, :] * jnp.exp(-decay[None, :] * positions[:, None])
    return (raw * envelope).astype(jnp.bfloat16)


def toeplitz_kernel(filt_ref, x_ref, o_ref, acc_ref):
    nb = x_ref.shape[1] // GROUP
    fb = x_ref.shape[0]
    block = x_ref.shape[2]
    upper = (lax.broadcasted_iota(jnp.int32, (block, block), 1)
             >= lax.broadcasted_iota(jnp.int32, (block, block), 0))
    for g in range(fb):
        acc_ref[...] = jnp.zeros(acc_ref.shape, jnp.float32)
        prev = None
        for d in range(nb):
            w = filt_ref[d + 1, pl.ds(g, block, stride=0), :]
            cur = pltpu.roll(w, 0, 1, stride=1, stride_axis=0)
            low = 0.0 if prev is None else prev
            t = jnp.where(upper, cur, low).astype(jnp.bfloat16)
            rows = (nb - d) * GROUP
            acc_ref[d * GROUP:, :] += jnp.dot(
                x_ref[g, :rows, :], t, preferred_element_type=jnp.float32
            )
            prev = cur
        for i in range(nb):
            o_ref[i, g * GROUP:(g + 1) * GROUP, :] = acc_ref[i * GROUP:(i + 1) * GROUP, :]


def toeplitz_conv(filt, x):
    count, rows, block = x.shape
    nb = rows // GROUP
    fb = min(FILTERS_PER_STEP, count)
    return pl.pallas_call(
        toeplitz_kernel,
        out_shape=jax.ShapeDtypeStruct((nb, count * GROUP, block), jnp.float32),
        grid=(count // fb,),
        in_specs=[
            pl.BlockSpec((nb + 1, fb, block), lambda i: (0, i, 0)),
            pl.BlockSpec((fb, rows, block), lambda i: (i, 0, 0)),
        ],
        out_specs=pl.BlockSpec((nb, fb * GROUP, block), lambda i: (0, i, 0)),
        scratch_shapes=[pltpu.VMEM((rows, block), jnp.float32)],
    )(filt, x)


def per_device(
    outer_gate, inner_gate, signal, filter_in, filter_bias, filter_out, decay, skip_gain
):
    own_rows, width = signal.shape
    nb = lax.axis_size("seq")
    total_rows = own_rows * nb
    s = lax.axis_index("seq")
    count = width // GROUP
    sub = count // nb
    gated = (inner_gate.astype(jnp.float32) * signal.astype(jnp.float32)).astype(jnp.bfloat16)
    gated_t = gated.T.reshape(nb, sub, GROUP, own_rows)
    got = lax.all_to_all(gated_t, "seq", 0, 0, tiled=False)
    x = got.transpose(1, 0, 2, 3).reshape(sub, nb * GROUP, own_rows)
    positions = jnp.arange(total_rows, dtype=jnp.int32).astype(jnp.float32)
    my_out = lax.dynamic_slice_in_dim(filter_out, s * sub, sub, 1)
    my_decay = lax.dynamic_slice_in_dim(decay, s * sub, sub, 0)
    filters = filter_table(positions, float(total_rows), filter_in, filter_bias, my_out, my_decay)
    lagged = filters.astype(jnp.float32).reshape(nb, own_rows, sub).transpose(0, 2, 1)
    filt = jnp.concatenate([jnp.zeros((1, sub, own_rows), jnp.float32), lagged], axis=0)
    conv_parts = toeplitz_conv(filt, x)
    back = lax.all_to_all(conv_parts, "seq", 0, 0, tiled=False)
    conv = back.reshape(width, own_rows).T
    mixed = outer_gate.astype(jnp.float32) * (conv + skip_gain[None, :] * gated.astype(jnp.float32))
    return mixed.astype(jnp.bfloat16)


def solution(mesh):
    placed = (
        P(("groups", "seq"), "chan"),
        P(("groups", "seq"), "chan"),
        P(("groups", "seq"), "chan"),
        P(),
        P(),
        P(None, "chan"),
        P("chan"),
        P("chan"),
    )
    return jax.shard_map(
        per_device,
        mesh=mesh,
        in_specs=placed,
        out_specs=P(("groups", "seq"), "chan"),
        check_vma=False,
    )
```

time: 157 us -> 60.4 us (0.38)
  the two profiles are of different devices: /device:TPU:25 before, /device:TPU:0 now
where the time goes in v2:
time: 60.4 us; the launch traced here: 60 us
  waiting for transfers between devices  36.1 us (60%)
  starting transfers between devices  9.99 us (17%)
  local copies, waits for them, and re-layouts  5.12 us (8%)
  Pallas kernels  4.24 us (7%)
  other arithmetic  3.36 us (6%)
  matrix products  1.07 us (2%)
    all_to_all x1, waiting for transfers between devices, per_device(): back = lax.all_to_all(conv_parts, 'seq', 0, 0, tiled=False)  25 us
    all_to_all x1, waiting for transfers between devices, per_device(): got = lax.all_to_all(gated_t, 'seq', 0, 0, tiled=False)  11.1 us
    all_to_all x1, starting transfers between devices, per_device(): got = lax.all_to_all(gated_t, 'seq', 0, 0, tiled=False)  6.35 us
    pallas_call x1, Pallas kernels, toeplitz_conv(): pl.pallas_call(toeplitz_kernel, out_shape=jax.ShapeDtypeStruct((nb, count...  4.24 us
    all_to_all x1, starting transfers between devices, per_device(): back = lax.all_to_all(conv_parts, 'seq', 0, 0, tiled=False)  3.65 us
    unnamed x17, local copies, waits for them, and re-layouts  3.23 us
    convert_element_type x1, other arithmetic, per_device(): return mixed.astype(jnp.bfloat16)  1.49 us
  transfers between devices with their start and end apart: 2, of which 2 were waited for; matrix products, arithmetic and copies ran while one was open for 4% of the time, Pallas kernels for 0%

profile of v2, /device:TPU:0, one launch (start us, length us, event | category | flops | bytes accessed | tf_op | source)
XLA Modules:
  0.0 60.0 jit_solution(14756017015710686782)
XLA Ops:
  0.0 0.0 copy-start
  0.0 0.0 copy-start.1
  0.0 1.4 %copy.19 = bf16[128,2048]{0,1:T(8,128)(2,1)S(1)} copy(bf16[128,2048]{1,0:T(8,128)(2,1)} %param.9) | data formatting | bytes 1048576 | tf_op args[1]
  1.4 0.0 copy-done.1
  1.4 0.3 copy.20
  1.7 0.9 %multiply_convert_fusion = bf16[128,2048]{0,1:T(8,128)(2,1)} fusion(bf16[128,2048]{0,1:T(8,128)(2,1)S(1)} %copy.20, bf16[128,2048]{0,1:T(8,128)(2,1)S(1)} %copy.19), kind=kLoop, calls=%fused_computation.9 | loop fusion | flops 1048576 | bytes 1572864 | tf_op jit(solution)/shard_map/convert_element_type | solution.py:78
  2.6 6.3 %all-to-all-start = ((bf16[4,32,16,128]{3,2,1,0:T(8,128)(2,1)}), bf16[4,32,16,128]{3,2,1,0:T(8,128)(2,1)S(1)}, u32[]{:S(2)}, u32[]{:S(2)}) async-start(bf16[4,32,16,128]{3,2,1,0:T(8,128)(2,1)} %bitcast.2), calls=%async_computation | async-start | bytes 1048576 | tf_op jit(solution)/shard_map/all_to_all | solution.py:80
  9.0 0.0 copy-start.6
  9.0 0.6 %copy-done.6 = f32[128]{0:T(128)S(1)} copy-done((f32[128]{0:T(128)S(1)}, f32[128]{0:T(128)}, u32[]{:S(2)}) %copy-start.6) | copy-done | bytes 536
  9.6 0.1 multiply_sqrt_fusion
  9.7 0.0 copy-start.3
  9.7 0.2 multiply_cosine_fusion
  9.9 0.0 copy-start.5
  9.9 0.5 copy-done.3
  10.4 0.1 copy-done.5
  10.6 0.7 %fusion.1 = f32[512,64]{0,1:T(8,128)S(1)} fusion(f32[33,64]{1,0:T(8,128)S(1)} %copy-done.3, f32[512,16]{0,1:T(8,128)S(1)} %get-tuple-element.6, f32[512,16]{0,1:T(8,128)S(1)} %get-tuple-element.5, f32[512,1]{0,1:T(1,128)S(1)} %convert_multiply_fusion, f32[64]{0:T(128)S(1)} %copy-done.5), kind=kOutput, calls=%fused_computation.2 | convolution fusion | flops 13075456 | bytes 207360 | tf_op jit(solution)/shard_map/dot_general | solution.py:22
  11.3 0.0 copy-done
  11.3 0.3 fusion.3
  11.7 0.6 %pad_convert_fusion.filt_ref = f32[5,32,128]{2,1,0:T(8,128)} fusion(bf16[4,32,128]{2,1,0:T(8,128)(2,1)S(1)} %bitcast.25), kind=kLoop, calls=%fused_computation.17 | loop fusion | flops 20480 | bytes 114688 | tf_op jit(solution)/shard_map/concatenate | solution.py:87
  12.3 11.1 %all-to-all-done = bf16[4,32,16,128]{3,2,1,0:T(8,128)(2,1)S(1)} async-done(((bf16[4,32,16,128]{3,2,1,0:T(8,128)(2,1)}), bf16[4,32,16,128]{3,2,1,0:T(8,128)(2,1)S(1)}, u32[]{:S(2)}, u32[]{:S(2)}) %all-to-all-start) | async-done | bytes 524320 | tf_op jit(solution)/shard_map/all_to_all | solution.py:80
  23.4 0.9 %copy.21 = bf16[32,4,16,128]{3,2,1,0:T(8,128)(2,1)} copy(bf16[32,4,16,128]{3,2,0,1:T(8,128)(2,1)S(1)} %bitcast.24) | data formatting | bytes 1048576 | tf_op jit(solution)/shard_map/transpose | solution.py:81
  24.3 4.2 %shard_map.82 = f32[4,512,128]{2,1,0:T(8,128)} custom-call(f32[5,32,128]{2,1,0:T(8,128)} %pad_convert_fusion.filt_ref, bf16[32,64,128]{2,1,0:T(8,128)(2,1)} %bitcast.23), custom_call_target="tpu_custom_call" | custom-call | tf_op jit(solution)/shard_map/pallas_call | solution.py:56
  28.6 0.0 copy-start.2
  28.6 3.6 %all-to-all-start.1 = ((f32[4,512,128]{2,1,0:T(8,128)}), f32[4,512,128]{2,1,0:T(8,128)S(1)}, u32[]{:S(2)}, u32[]{:S(2)}) async-start(f32[4,512,128]{2,1,0:T(8,128)} %shard_map.82), calls=%async_computation.1 | async-start | bytes 2097152 | tf_op jit(solution)/shard_map/all_to_all | solution.py:89
  32.2 0.0 copy-done.2
  32.2 0.0 copy-start.4
  32.2 0.3 copy.17
  32.5 25.0 %all-to-all-done.1 = f32[4,512,128]{2,1,0:T(8,128)S(1)} async-done(((f32[4,512,128]{2,1,0:T(8,128)}), f32[4,512,128]{2,1,0:T(8,128)S(1)}, u32[]{:S(2)}, u32[]{:S(2)}) %all-to-all-start.1) | async-done | bytes 1048608 | tf_op jit(solution)/shard_map/all_to_all | solution.py:89
  57.5 0.0 copy-done.4
  57.5 1.5 %fusion.5 = bf16[128,2048]{0,1:T(8,128)(2,1)S(1)} fusion(f32[4,512,128]{2,1,0:T(8,128)S(1)} %all-to-all-done.1, bf16[128,2048]{0,1:T(8,128)(2,1)} %multiply_convert_fusion, bf16[128,2048]{0,1:T(8,128)(2,1)S(1)} %copy.17, f32[2048]{0:T(1024)S(1)} %copy-done.4), kind=kLoop, calls=%fused_computation.8 | loop fusion | flops 1572864 | bytes 2629632 | tf_op jit(solution)/shard_map/convert_element_type | solution.py:92
  59.0 1.0 %copy.22 = bf16[128,2048]{1,0:T(8,128)(2,1)} copy(bf16[128,2048]{0,1:T(8,128)(2,1)S(1)} %fusion.5) | data formatting | bytes 1048576 | tf_op jit(solution)/shard_map/convert_element_type | solution.py:92
  (4 shorter events, 0.0 us)
Async XLA Ops:
  0.0 11.3 %copy-start = (f32[64,128]{1,0:T(8,128)S(1)}, f32[64,128]{1,0:T(8,128)}, u32[]{:S(2)}) copy-start(f32[64,128]{1,0:T(8,128)} %param.13) | copy-start | bytes 98308
  0.0 1.4 %copy-start.1 = (bf16[128,2048]{1,0:T(8,128)(2,1)S(1)}, bf16[128,2048]{1,0:T(8,128)(2,1)}, u32[]{:S(2)}) copy-start(bf16[128,2048]{1,0:T(8,128)(2,1)} %param.10) | copy-start | bytes 1572868
  2.6 20.8 %all-to-all-start = ((bf16[4,32,16,128]{3,2,1,0:T(8,128)(2,1)}), bf16[4,32,16,128]{3,2,1,0:T(8,128)(2,1)S(1)}, u32[]{:S(2)}, u32[]{:S(2)}) async-start(bf16[4,32,16,128]{3,2,1,0:T(8,128)(2,1)} %bitcast.2), calls=%async_computation | async-start | bytes 1048576 | tf_op jit(solution)/shard_map/all_to_all | solution.py:80
  9.0 0.7 %copy-start.6 = (f32[128]{0:T(128)S(1)}, f32[128]{0:T(128)}, u32[]{:S(2)}) copy-start(f32[128]{0:T(128)} %param.14) | copy-start | bytes 1540
  9.7 0.7 %copy-start.3 = (f32[33,64]{1,0:T(8,128)S(1)}, f32[33,64]{1,0:T(8,128)}, u32[]{:S(2)}) copy-start(f32[33,64]{1,0:T(8,128)} %param.11) | copy-start | bytes 25348
  9.9 0.7 %copy-start.5 = (f32[64]{0:T(128)S(1)}, f32[64]{0:T(128)}, u32[]{:S(2)}) copy-start(f32[64]{0:T(128)} %param.12) | copy-start | bytes 772
  28.6 3.7 %copy-start.2 = (bf16[128,2048]{1,0:T(8,128)(2,1)S(1)}, bf16[128,2048]{1,0:T(8,128)(2,1)}, u32[]{:S(2)}) copy-start(bf16[128,2048]{1,0:T(8,128)(2,1)} %param.8) | copy-start | bytes 1572868
  28.6 28.9 %all-to-all-start.1 = ((f32[4,512,128]{2,1,0:T(8,128)}), f32[4,512,128]{2,1,0:T(8,128)S(1)}, u32[]{:S(2)}, u32[]{:S(2)}) async-start(f32[4,512,128]{2,1,0:T(8,128)} %shard_map.82), calls=%async_computation.1 | async-start | bytes 2097152 | tf_op jit(solution)/shard_map/all_to_all | solution.py:89
  32.2 25.2 %copy-start.4 = (f32[2048]{0:T(1024)S(1)}, f32[2048]{0:T(1024)}, u32[]{:S(2)}) copy-start(f32[2048]{0:T(1024)} %param.15) | copy-start | bytes 24580

commit v3 on v2

--- a/solution.py
+++ b/solution.py
@@ -26,7 +26,7 @@
     return (raw * envelope).astype(jnp.bfloat16)
 
 
-def toeplitz_kernel(filt_ref, x_ref, o_ref, acc_ref):
+def toeplitz_kernel(filt_ref, x_ref, outer_ref, skip_ref, o_ref, acc_ref):
     nb = x_ref.shape[1] // GROUP
     fb = x_ref.shape[0]
     block = x_ref.shape[2]
@@ -45,25 +45,31 @@
                 x_ref[g, :rows, :], t, preferred_element_type=jnp.float32
             )
             prev = cur
+        ch = slice(g * GROUP, (g + 1) * GROUP)
+        skip = skip_ref[ch, :]
         for i in range(nb):
-            o_ref[i, g * GROUP:(g + 1) * GROUP, :] = acc_ref[i * GROUP:(i + 1) * GROUP, :]
+            blk = slice(i * GROUP, (i + 1) * GROUP)
+            inner = acc_ref[blk, :] + skip * x_ref[g, blk, :].astype(jnp.float32)
+            o_ref[i, ch, :] = (outer_ref[i, ch, :].astype(jnp.float32) * inner).astype(jnp.bfloat16)
 
 
-def toeplitz_conv(filt, x):
+def toeplitz_conv(filt, x, outer, skip):
     count, rows, block = x.shape
     nb = rows // GROUP
     fb = min(FILTERS_PER_STEP, count)
     return pl.pallas_call(
         toeplitz_kernel,
-        out_shape=jax.ShapeDtypeStruct((nb, count * GROUP, block), jnp.float32),
+        out_shape=jax.ShapeDtypeStruct((nb, count * GROUP, block), jnp.bfloat16),
         grid=(count // fb,),
         in_specs=[
             pl.BlockSpec((nb + 1, fb, block), lambda i: (0, i, 0)),
             pl.BlockSpec((fb, rows, block), lambda i: (i, 0, 0)),
+            pl.BlockSpec((nb, fb * GROUP, block), lambda i: (0, i, 0)),
+            pl.BlockSpec((fb * GROUP, 1), lambda i: (i, 0)),
         ],
         out_specs=pl.BlockSpec((nb, fb * GROUP, block), lambda i: (0, i, 0)),
         scratch_shapes=[pltpu.VMEM((rows, block), jnp.float32)],
-    )(filt, x)
+    )(filt, x, outer, skip)
 
 
 def per_device(
@@ -76,20 +82,21 @@
     count = width // GROUP
     sub = count // nb
     gated = (inner_gate.astype(jnp.float32) * signal.astype(jnp.float32)).astype(jnp.bfloat16)
-    gated_t = gated.T.reshape(nb, sub, GROUP, own_rows)
-    got = lax.all_to_all(gated_t, "seq", 0, 0, tiled=False)
-    x = got.transpose(1, 0, 2, 3).reshape(sub, nb * GROUP, own_rows)
+    both = jnp.stack([outer_gate.T, gated.T]).reshape(2, nb, sub * GROUP, own_rows)
+    got = lax.all_to_all(both.transpose(1, 0, 2, 3), "seq", 0, 0, tiled=False)
+    outer_got = got[:, 0]
+    x = got[:, 1].reshape(nb, sub, GROUP, own_rows).transpose(1, 0, 2, 3).reshape(
+        sub, nb * GROUP, own_rows)
     positions = jnp.arange(total_rows, dtype=jnp.int32).astype(jnp.float32)
     my_out = lax.dynamic_slice_in_dim(filter_out, s * sub, sub, 1)
     my_decay = lax.dynamic_slice_in_dim(decay, s * sub, sub, 0)
     filters = filter_table(positions, float(total_rows), filter_in, filter_bias, my_out, my_decay)
     lagged = filters.astype(jnp.float32).reshape(nb, own_rows, sub).transpose(0, 2, 1)
     filt = jnp.concatenate([jnp.zeros((1, sub, own_rows), jnp.float32), lagged], axis=0)
-    conv_parts = toeplitz_conv(filt, x)
-    back = lax.all_to_all(conv_parts, "seq", 0, 0, tiled=False)
-    conv = back.reshape(width, own_rows).T
-    mixed = outer_gate.astype(jnp.float32) * (conv + skip_gain[None, :] * gated.astype(jnp.float32))
-    return mixed.astype(jnp.bfloat16)
+    my_skip = lax.dynamic_slice_in_dim(skip_gain, s * sub * GROUP, sub * GROUP, 0)[:, None]
+    mixed_parts = toeplitz_conv(filt, x, outer_got, my_skip)
+    back = lax.all_to_all(mixed_parts, "seq", 0, 0, tiled=False)
+    return back.reshape(width, own_rows).T
 
 
 def solution(mesh):

time: 60.4 us -> 60.8 us (level)
  blocking collectives: 0 us -> 17.5 us
  waiting for transfers between devices: 36.1 us -> 20.7 us
  starting transfers between devices: 9.99 us -> 6.35 us
  local copies, waits for them, and re-layouts: 5.12 us -> 6.97 us
    all_to_all x0 -> x1, blocking collectives: none -> 17.5 us  [per_device(): back = lax.all_to_all(mixed_parts, 'seq', 0, 0, tiled=False)]
    all_to_all x2 -> x1, waiting for transfers between devices: 36.1 us -> 20.7 us  [per_device(): got = lax.all_to_all(both.transpose(1, 0, 2, 3), 'seq', 0, 0, tiled=False)]
    all_to_all x2 -> x1, starting transfers between devices: 9.99 us -> 6.35 us  [per_device(): got = lax.all_to_all(both.transpose(1, 0, 2, 3), 'seq', 0, 0, tiled=False)]
    convert_element_type x2 -> x0, other arithmetic: 2.43 us -> none  [the longest x1 1.49 us: per_device(): return mixed.astype(jnp.bfloat16)]
    transpose x0 -> x2, other arithmetic: none -> 2.39 us  [the longest x1 1.33 us: per_device(): both = jnp.stack([outer_gate.T, gated.T]).reshape(2, nb, sub * GROUP, own...]
    unnamed x17 -> x10, local copies, waits for them, and re-layouts: 3.23 us -> 2.07 us
    convert_element_type x1 -> x0, local copies, waits for them, and re-layouts: 1.01 us -> none  [per_device(): return mixed.astype(jnp.bfloat16)]
    reshape x0 -> x1, local copies, waits for them, and re-layouts: none -> 1.01 us  [per_device(): return back.reshape(width, own_rows).T]
  transfers between devices with their start and end apart: 2 -> 1, of which waited for: 2 -> 1; matrix products, arithmetic and copies ran while one was open for 4% -> 6% of each run, Pallas kernels for 0% -> 0%
where the time goes in v3:
time: 60.8 us; the launch traced here: 60.3 us
  waiting for transfers between devices  20.7 us (34%)
  blocking collectives  17.5 us (29%)
  local copies, waits for them, and re-layouts  6.97 us (11%)
  starting transfers between devices  6.35 us (10%)
  Pallas kernels  4.33 us (7%)
  other arithmetic  3.33 us (5%)
  matrix products  1.07 us (2%)
    all_to_all x1, waiting for transfers between devices, per_device(): got = lax.all_to_all(both.transpose(1, 0, 2, 3), 'seq', 0, 0, tiled=False)  20.7 us
    all_to_all x1, blocking collectives, per_device(): back = lax.all_to_all(mixed_parts, 'seq', 0, 0, tiled=False)  17.5 us
    all_to_all x1, starting transfers between devices, per_device(): got = lax.all_to_all(both.transpose(1, 0, 2, 3), 'seq', 0, 0, tiled=False)  6.35 us
    pallas_call x1, Pallas kernels, toeplitz_conv(): pl.pallas_call(toeplitz_kernel, out_shape=jax.ShapeDtypeStruct((nb, count...  4.33 us
    unnamed x10, local copies, waits for them, and re-layouts  2.07 us
    transpose x1, other arithmetic, per_device(): both = jnp.stack([outer_gate.T, gated.T]).reshape(2, nb, sub * GROUP, own...  1.33 us
  transfers between devices with their start and end apart: 1, of which 1 were waited for; matrix products, arithmetic and copies ran while one was open for 6% of the time, Pallas kernels for 0%

profile of v3, /device:TPU:0, one launch (start us, length us, event | category | flops | bytes accessed | tf_op | source)
XLA Modules:
  0.0 60.3 jit_solution(14482414450975123844)
XLA Ops:
  0.0 0.0 copy-start
  0.0 1.3 %fusion.4 = bf16[2048,128]{0,1:T(8,128)(2,1)S(1)} fusion(bf16[128,2048]{1,0:T(8,128)(2,1)} %param.10, bf16[128,2048]{1,0:T(8,128)(2,1)} %param.9), kind=kLoop, calls=%fused_computation.8 | loop fusion | flops 1048576 | bytes 1572864 | tf_op jit(solution)/shard_map/transpose | solution.py:85
  1.3 0.0 copy-start.1
  1.4 0.3 copy.21
  1.6 0.8 %copy-done.1 = bf16[128,2048]{1,0:T(8,128)(2,1)S(1)} copy-done((bf16[128,2048]{1,0:T(8,128)(2,1)S(1)}, bf16[128,2048]{1,0:T(8,128)(2,1)}, u32[]{:S(2)}) %copy-start.1) | copy-done | bytes 524312
  2.4 0.3 copy.20
  2.7 1.1 %maximum_bitcast_fusion = bf16[4,2,512,128]{3,2,1,0:T(8,128)(2,1)} fusion(bf16[1,4,512,128]{3,2,0,1:T(8,128)(2,1)S(1)} %bitcast.31, bf16[1,4,512,128]{3,2,0,1:T(8,128)(2,1)S(1)} %bitcast.32), kind=kLoop, calls=%fused_computation.6 | loop fusion | flops 524288 | bytes 2097152 | tf_op jit(solution)/shard_map/transpose | solution.py:86
  3.7 6.3 %all-to-all-start = ((bf16[4,2,512,128]{3,2,1,0:T(8,128)(2,1)}), bf16[4,2,512,128]{3,2,1,0:T(8,128)(2,1)S(1)}, u32[]{:S(2)}, u32[]{:S(2)}) async-start(bf16[4,2,512,128]{3,2,1,0:T(8,128)(2,1)} %maximum_bitcast_fusion), calls=%async_computation | async-start | bytes 2097152 | tf_op jit(solution)/shard_map/all_to_all | solution.py:86
  10.1 0.0 copy-start.4
  10.1 0.6 %copy-done.4 = f32[128]{0:T(128)S(1)} copy-done((f32[128]{0:T(128)S(1)}, f32[128]{0:T(128)}, u32[]{:S(2)}) %copy-start.4) | copy-done | bytes 536
  10.7 0.1 multiply_sqrt_fusion
  10.8 0.0 copy-start.2
  10.8 0.2 multiply_cosine_fusion
  11.0 0.0 copy-start.3
  11.0 0.5 copy-done.2
  11.5 0.1 copy-done.3
  11.7 0.7 %fusion.1 = f32[512,64]{0,1:T(8,128)S(1)} fusion(f32[33,64]{1,0:T(8,128)S(1)} %copy-done.2, f32[512,16]{0,1:T(8,128)S(1)} %get-tuple-element.8, f32[512,16]{0,1:T(8,128)S(1)} %get-tuple-element.7, f32[512,1]{0,1:T(1,128)S(1)} %convert_multiply_fusion, f32[64]{0:T(128)S(1)} %copy-done.3), kind=kOutput, calls=%fused_computation.2 | convolution fusion | flops 13075456 | bytes 207360 | tf_op jit(solution)/shard_map/dot_general | solution.py:22
  12.4 0.0 copy-done
  12.4 0.3 fusion.3
  12.8 0.8 %dynamic_slice.11 = f32[512]{0:T(512)S(1)} dynamic-slice(f32[2048]{0:T(1024)} %param.15, s32[]{:T(128)S(6)} %select_n.8), dynamic_slice_sizes={512} | dynamic-slice | bytes 4100 | tf_op jit(solution)/shard_map/dynamic_slice | solution.py:96
  13.6 0.9 %copy.24.skip_ref = f32[512,1]{1,0:T(8,128)} copy(f32[512,1]{0,1:T(1,128)S(1)} %bitcast.35) | data formatting | bytes 4096 | tf_op jit(solution)/shard_map/broadcast_in_dim | solution.py:96
  14.4 0.6 %pad_convert_fusion.filt_ref = f32[5,32,128]{2,1,0:T(8,128)} fusion(bf16[4,32,128]{2,1,0:T(8,128)(2,1)S(1)} %bitcast.34), kind=kLoop, calls=%fused_computation.17 | loop fusion | flops 20480 | bytes 114688 | tf_op jit(solution)/shard_map/concatenate | solution.py:95
  15.1 20.7 %all-to-all-done = bf16[4,2,512,128]{3,2,1,0:T(8,128)(2,1)S(1)} async-done(((bf16[4,2,512,128]{3,2,1,0:T(8,128)(2,1)}), bf16[4,2,512,128]{3,2,1,0:T(8,128)(2,1)S(1)}, u32[]{:S(2)}, u32[]{:S(2)}) %all-to-all-start) | async-done | bytes 1048608 | tf_op jit(solution)/shard_map/all_to_all | solution.py:86
  35.8 0.9 %slice_bitcast_fusion = (bf16[4,512,128]{2,1,0:T(8,128)(2,1)}, bf16[4,1,512,128]{3,2,1,0:T(8,128)(2,1)S(1)}) fusion(bf16[4,2,512,128]{3,2,1,0:T(8,128)(2,1)S(1)} %all-to-all-done), kind=kLoop, calls=%fused_computation.9 | loop fusion | bytes 2097152 | tf_op jit(solution)/shard_map/squeeze | solution.py:87
  36.7 0.9 %copy.22 = bf16[4,32,16,128]{3,2,0,1:T(8,128)(2,1)} copy(bf16[4,32,16,128]{3,2,1,0:T(8,128)(2,1)S(1)} %bitcast.30) | data formatting | bytes 1048576 | tf_op jit(solution)/shard_map/reshape;squeeze | solution.py:88
  37.5 4.3 %shard_map.82 = bf16[4,512,128]{2,1,0:T(8,128)(2,1)} custom-call(f32[5,32,128]{2,1,0:T(8,128)} %pad_convert_fusion.filt_ref, bf16[32,64,128]{2,1,0:T(8,128)(2,1)} %bitcast.29, bf16[4,512,128]{2,1,0:T(8,128)(2,1)} %get-tuple-element.5.outer_ref, f32[512,1]{1,0:T(8,128)} %copy.24.skip_ref), custom_call_target="tpu_custom_call" | custom-call | tf_op jit(solution)/shard_map/pallas_call | solution.py:60
  41.8 17.5 %all_to_all.10 = bf16[4,512,128]{2,1,0:T(8,128)(2,1)S(1)} all-to-all(bf16[4,512,128]{2,1,0:T(8,128)(2,1)} %shard_map.82), channel_id=1, replica_groups=mesh['groups'=2,'seq'=4,'chan'=4] {'seq'}, dimensions={0} | all-to-all | bytes 1048576 | tf_op jit(solution)/shard_map/all_to_all | solution.py:98
  59.3 1.0 %copy.25 = bf16[2048,128]{0,1:T(8,128)(2,1)} copy(bf16[2048,128]{1,0:T(8,128)(2,1)S(1)} %bitcast.28) | data formatting | bytes 1048576 | tf_op jit(solution)/shard_map/reshape | solution.py:99
  (4 shorter events, 0.0 us)
Async XLA Ops:
  0.0 12.4 %copy-start = (f32[64,128]{1,0:T(8,128)S(1)}, f32[64,128]{1,0:T(8,128)}, u32[]{:S(2)}) copy-start(f32[64,128]{1,0:T(8,128)} %param.13) | copy-start | bytes 98308
  1.3 1.0 %copy-start.1 = (bf16[128,2048]{1,0:T(8,128)(2,1)S(1)}, bf16[128,2048]{1,0:T(8,128)(2,1)}, u32[]{:S(2)}) copy-start(bf16[128,2048]{1,0:T(8,128)(2,1)} %param.8) | copy-start | bytes 1572868
  3.7 32.1 %all-to-all-start = ((bf16[4,2,512,128]{3,2,1,0:T(8,128)(2,1)}), bf16[4,2,512,128]{3,2,1,0:T(8,128)(2,1)S(1)}, u32[]{:S(2)}, u32[]{:S(2)}) async-start(bf16[4,2,512,128]{3,2,1,0:T(8,128)(2,1)} %maximum_bitcast_fusion), calls=%async_computation | async-start | bytes 2097152 | tf_op jit(solution)/shard_map/all_to_all | solution.py:86
  10.1 0.7 %copy-start.4 = (f32[128]{0:T(128)S(1)}, f32[128]{0:T(128)}, u32[]{:S(2)}) copy-start(f32[128]{0:T(128)} %param.14) | copy-start | bytes 1540
  10.8 0.7 %copy-start.2 = (f32[33,64]{1,0:T(8,128)S(1)}, f32[33,64]{1,0:T(8,128)}, u32[]{:S(2)}) copy-start(f32[33,64]{1,0:T(8,128)} %param.11) | copy-start | bytes 25348
  11.0 0.7 %copy-start.3 = (f32[64]{0:T(128)S(1)}, f32[64]{0:T(128)}, u32[]{:S(2)}) copy-start(f32[64]{0:T(128)} %param.12) | copy-start | bytes 772

commit v4 on v2

--- a/solution.py
+++ b/solution.py
@@ -46,7 +46,8 @@
             )
             prev = cur
         for i in range(nb):
-            o_ref[i, g * GROUP:(g + 1) * GROUP, :] = acc_ref[i * GROUP:(i + 1) * GROUP, :]
+            o_ref[i, g * GROUP:(g + 1) * GROUP, :] = (
+                acc_ref[i * GROUP:(i + 1) * GROUP, :].astype(jnp.bfloat16))
 
 
 def toeplitz_conv(filt, x):
@@ -55,7 +56,7 @@
     fb = min(FILTERS_PER_STEP, count)
     return pl.pallas_call(
         toeplitz_kernel,
-        out_shape=jax.ShapeDtypeStruct((nb, count * GROUP, block), jnp.float32),
+        out_shape=jax.ShapeDtypeStruct((nb, count * GROUP, block), jnp.bfloat16),
         grid=(count // fb,),
         in_specs=[
             pl.BlockSpec((nb + 1, fb, block), lambda i: (0, i, 0)),
@@ -87,7 +88,7 @@
     filt = jnp.concatenate([jnp.zeros((1, sub, own_rows), jnp.float32), lagged], axis=0)
     conv_parts = toeplitz_conv(filt, x)
     back = lax.all_to_all(conv_parts, "seq", 0, 0, tiled=False)
-    conv = back.reshape(width, own_rows).T
+    conv = back.reshape(width, own_rows).T.astype(jnp.float32)
     mixed = outer_gate.astype(jnp.float32) * (conv + skip_gain[None, :] * gated.astype(jnp.float32))
     return mixed.astype(jnp.bfloat16)
 

time: 60.4 us -> 48.9 us (0.81)
  waiting for transfers between devices: 36.1 us -> 24.8 us
    all_to_all x1, waiting for transfers between devices: 25 us -> 13.7 us  [per_device(): back = lax.all_to_all(conv_parts, 'seq', 0, 0, tiled=False)]
  transfers between devices with their start and end apart: 2 -> 2, of which waited for: 2 -> 2; matrix products, arithmetic and copies ran while one was open for 4% -> 5% of each run, Pallas kernels for 0% -> 0%
where the time goes in v4:
time: 48.9 us; the launch traced here: 48.5 us
  waiting for transfers between devices  24.8 us (51%)
  starting transfers between devices  9.95 us (20%)
  local copies, waits for them, and re-layouts  5.12 us (10%)
  Pallas kernels  4.15 us (8%)
  other arithmetic  3.25 us (7%)
  matrix products  1.07 us (2%)
    all_to_all x1, waiting for transfers between devices, per_device(): back = lax.all_to_all(conv_parts, 'seq', 0, 0, tiled=False)  13.7 us
    all_to_all x1, waiting for transfers between devices, per_device(): got = lax.all_to_all(gated_t, 'seq', 0, 0, tiled=False)  11.1 us
    all_to_all x1, starting transfers between devices, per_device(): got = lax.all_to_all(gated_t, 'seq', 0, 0, tiled=False)  6.35 us
    pallas_call x1, Pallas kernels, toeplitz_conv(): pl.pallas_call(toeplitz_kernel, out_shape=jax.ShapeDtypeStruct((nb, count...  4.15 us
    all_to_all x1, starting transfers between devices, per_device(): back = lax.all_to_all(conv_parts, 'seq', 0, 0, tiled=False)  3.6 us
    unnamed x17, local copies, waits for them, and re-layouts  3.23 us
    convert_element_type x1, other arithmetic, per_device(): return mixed.astype(jnp.bfloat16)  1.38 us
    convert_element_type x1, local copies, waits for them, and re-layouts, per_device(): return mixed.astype(jnp.bfloat16)  1.01 us
  transfers between devices with their start and end apart: 2, of which 2 were waited for; matrix products, arithmetic and copies ran while one was open for 5% of the time, Pallas kernels for 0%

profile of v4, /device:TPU:0, one launch (start us, length us, event | category | flops | bytes accessed | tf_op | source)
XLA Modules:
  0.0 48.5 jit_solution(5805326946147985617)
XLA Ops:
  0.0 0.0 copy-start
  0.0 0.0 copy-start.1
  0.0 1.4 %copy.19 = bf16[128,2048]{0,1:T(8,128)(2,1)S(1)} copy(bf16[128,2048]{1,0:T(8,128)(2,1)} %param.9) | data formatting | bytes 1048576 | tf_op args[1]
  1.4 0.0 copy-done.1
  1.4 0.3 copy.20
  1.7 0.9 %multiply_convert_fusion = bf16[128,2048]{0,1:T(8,128)(2,1)} fusion(bf16[128,2048]{0,1:T(8,128)(2,1)S(1)} %copy.20, bf16[128,2048]{0,1:T(8,128)(2,1)S(1)} %copy.19), kind=kLoop, calls=%fused_computation.10 | loop fusion | flops 1048576 | bytes 1572864 | tf_op jit(solution)/shard_map/convert_element_type | solution.py:79
  2.6 6.3 %all-to-all-start = ((bf16[4,32,16,128]{3,2,1,0:T(8,128)(2,1)}), bf16[4,32,16,128]{3,2,1,0:T(8,128)(2,1)S(1)}, u32[]{:S(2)}, u32[]{:S(2)}) async-start(bf16[4,32,16,128]{3,2,1,0:T(8,128)(2,1)} %bitcast.2), calls=%async_computation | async-start | bytes 1048576 | tf_op jit(solution)/shard_map/all_to_all | solution.py:81
  9.0 0.0 copy-start.6
  9.0 0.6 %copy-done.6 = f32[128]{0:T(128)S(1)} copy-done((f32[128]{0:T(128)S(1)}, f32[128]{0:T(128)}, u32[]{:S(2)}) %copy-start.6) | copy-done | bytes 536
  9.6 0.1 multiply_sqrt_fusion
  9.7 0.0 copy-start.3
  9.7 0.2 multiply_cosine_fusion
  9.9 0.0 copy-start.5
  9.9 0.5 %copy-done.3 = f32[33,64]{1,0:T(8,128)S(1)} copy-done((f32[33,64]{1,0:T(8,128)S(1)}, f32[33,64]{1,0:T(8,128)}, u32[]{:S(2)}) %copy-start.3) | copy-done | bytes 8472
  10.4 0.1 copy-done.5
  10.6 0.7 %fusion.1 = f32[512,64]{0,1:T(8,128)S(1)} fusion(f32[33,64]{1,0:T(8,128)S(1)} %copy-done.3, f32[512,16]{0,1:T(8,128)S(1)} %get-tuple-element.6, f32[512,16]{0,1:T(8,128)S(1)} %get-tuple-element.5, f32[512,1]{0,1:T(1,128)S(1)} %convert_multiply_fusion, f32[64]{0:T(128)S(1)} %copy-done.5), kind=kOutput, calls=%fused_computation.2 | convolution fusion | flops 13075456 | bytes 207360 | tf_op jit(solution)/shard_map/dot_general | solution.py:22
  11.3 0.0 copy-done
  11.3 0.3 fusion.3
  11.7 0.6 %pad_convert_fusion.filt_ref = f32[5,32,128]{2,1,0:T(8,128)} fusion(bf16[4,32,128]{2,1,0:T(8,128)(2,1)S(1)} %bitcast.28), kind=kLoop, calls=%fused_computation.18 | loop fusion | flops 20480 | bytes 114688 | tf_op jit(solution)/shard_map/concatenate | solution.py:88
  12.3 11.1 %all-to-all-done = bf16[4,32,16,128]{3,2,1,0:T(8,128)(2,1)S(1)} async-done(((bf16[4,32,16,128]{3,2,1,0:T(8,128)(2,1)}), bf16[4,32,16,128]{3,2,1,0:T(8,128)(2,1)S(1)}, u32[]{:S(2)}, u32[]{:S(2)}) %all-to-all-start) | async-done | bytes 524320 | tf_op jit(solution)/shard_map/all_to_all | solution.py:81
  23.4 0.9 %copy.21 = bf16[32,4,16,128]{3,2,1,0:T(8,128)(2,1)} copy(bf16[32,4,16,128]{3,2,0,1:T(8,128)(2,1)S(1)} %bitcast.26) | data formatting | bytes 1048576 | tf_op jit(solution)/shard_map/transpose | solution.py:82
  24.3 4.1 %shard_map.82 = bf16[4,512,128]{2,1,0:T(8,128)(2,1)} custom-call(f32[5,32,128]{2,1,0:T(8,128)} %pad_convert_fusion.filt_ref, bf16[32,64,128]{2,1,0:T(8,128)(2,1)} %bitcast.27), custom_call_target="tpu_custom_call" | custom-call | tf_op jit(solution)/shard_map/pallas_call | solution.py:57
  28.5 0.0 copy-start.2
  28.5 3.6 %all-to-all-start.1 = ((bf16[4,512,128]{2,1,0:T(8,128)(2,1)}), bf16[4,512,128]{2,1,0:T(8,128)(2,1)S(1)}, u32[]{:S(2)}, u32[]{:S(2)}) async-start(bf16[4,512,128]{2,1,0:T(8,128)(2,1)} %shard_map.82), calls=%async_computation.1 | async-start | bytes 1048576 | tf_op jit(solution)/shard_map/all_to_all | solution.py:90
  32.1 0.0 copy-done.2
  32.1 0.0 copy-start.4
  32.1 0.3 copy.17
  32.4 13.7 %all-to-all-done.1 = bf16[4,512,128]{2,1,0:T(8,128)(2,1)S(1)} async-done(((bf16[4,512,128]{2,1,0:T(8,128)(2,1)}), bf16[4,512,128]{2,1,0:T(8,128)(2,1)S(1)}, u32[]{:S(2)}, u32[]{:S(2)}) %all-to-all-start.1) | async-done | bytes 524320 | tf_op jit(solution)/shard_map/all_to_all | solution.py:90
  46.1 0.0 copy-done.4
  46.1 1.4 %fusion.6 = bf16[128,2048]{0,1:T(8,128)(2,1)S(1)} fusion(bf16[128,2048]{0,1:T(8,128)(2,1)} %multiply_convert_fusion, bf16[128,2048]{0,1:T(8,128)(2,1)S(1)} %copy.17, bf16[4,512,128]{2,1,0:T(8,128)(2,1)S(1)} %all-to-all-done.1, f32[2048]{0:T(1024)S(1)} %copy-done.4), kind=kLoop, calls=%fused_computation.9 | loop fusion | flops 1835008 | bytes 2105344 | tf_op jit(solution)/shard_map/convert_element_type | solution.py:93
  47.5 1.0 %copy.22 = bf16[128,2048]{1,0:T(8,128)(2,1)} copy(bf16[128,2048]{0,1:T(8,128)(2,1)S(1)} %fusion.6) | data formatting | bytes 1048576 | tf_op jit(solution)/shard_map/convert_element_type | solution.py:93
  (4 shorter events, 0.0 us)
Async XLA Ops:
  0.0 11.3 %copy-start = (f32[64,128]{1,0:T(8,128)S(1)}, f32[64,128]{1,0:T(8,128)}, u32[]{:S(2)}) copy-start(f32[64,128]{1,0:T(8,128)} %param.13) | copy-start | bytes 98308
  0.0 1.4 %copy-start.1 = (bf16[128,2048]{1,0:T(8,128)(2,1)S(1)}, bf16[128,2048]{1,0:T(8,128)(2,1)}, u32[]{:S(2)}) copy-start(bf16[128,2048]{1,0:T(8,128)(2,1)} %param.10) | copy-start | bytes 1572868
  2.6 20.8 %all-to-all-start = ((bf16[4,32,16,128]{3,2,1,0:T(8,128)(2,1)}), bf16[4,32,16,128]{3,2,1,0:T(8,128)(2,1)S(1)}, u32[]{:S(2)}, u32[]{:S(2)}) async-start(bf16[4,32,16,128]{3,2,1,0:T(8,128)(2,1)} %bitcast.2), calls=%async_computation | async-start | bytes 1048576 | tf_op jit(solution)/shard_map/all_to_all | solution.py:81
  9.0 0.7 %copy-start.6 = (f32[128]{0:T(128)S(1)}, f32[128]{0:T(128)}, u32[]{:S(2)}) copy-start(f32[128]{0:T(128)} %param.14) | copy-start | bytes 1540
  9.7 0.7 %copy-start.3 = (f32[33,64]{1,0:T(8,128)S(1)}, f32[33,64]{1,0:T(8,128)}, u32[]{:S(2)}) copy-start(f32[33,64]{1,0:T(8,128)} %param.11) | copy-start | bytes 25348
  9.9 0.7 %copy-start.5 = (f32[64]{0:T(128)S(1)}, f32[64]{0:T(128)}, u32[]{:S(2)}) copy-start(f32[64]{0:T(128)} %param.12) | copy-start | bytes 772
  28.5 3.6 %copy-start.2 = (bf16[128,2048]{1,0:T(8,128)(2,1)S(1)}, bf16[128,2048]{1,0:T(8,128)(2,1)}, u32[]{:S(2)}) copy-start(bf16[128,2048]{1,0:T(8,128)(2,1)} %param.8) | copy-start | bytes 1572868
  28.5 17.6 %all-to-all-start.1 = ((bf16[4,512,128]{2,1,0:T(8,128)(2,1)}), bf16[4,512,128]{2,1,0:T(8,128)(2,1)S(1)}, u32[]{:S(2)}, u32[]{:S(2)}) async-start(bf16[4,512,128]{2,1,0:T(8,128)(2,1)} %shard_map.82), calls=%async_computation.1 | async-start | bytes 1048576 | tf_op jit(solution)/shard_map/all_to_all | solution.py:90
  32.1 14.0 %copy-start.4 = (f32[2048]{0:T(1024)S(1)}, f32[2048]{0:T(1024)}, u32[]{:S(2)}) copy-start(f32[2048]{0:T(1024)} %param.15) | copy-start | bytes 24580

commit v5 on v4

--- a/solution.py
+++ b/solution.py
@@ -67,6 +67,16 @@
     )(filt, x)
 
 
+def exchange(x, nb, s):
+    got = [x[s]]
+    for k in range(1, nb):
+        piece = lax.dynamic_index_in_dim(x, (s + k) % nb, 0, keepdims=False)
+        got.append(lax.ppermute(piece, "seq", [(i, (i + k) % nb) for i in range(nb)]))
+    z = jnp.stack(got)
+    order = (s - jnp.arange(nb, dtype=jnp.int32)) % nb
+    return jnp.take(z, order, axis=0)
+
+
 def per_device(
     outer_gate, inner_gate, signal, filter_in, filter_bias, filter_out, decay, skip_gain
 ):
@@ -78,7 +88,7 @@
     sub = count // nb
     gated = (inner_gate.astype(jnp.float32) * signal.astype(jnp.float32)).astype(jnp.bfloat16)
     gated_t = gated.T.reshape(nb, sub, GROUP, own_rows)
-    got = lax.all_to_all(gated_t, "seq", 0, 0, tiled=False)
+    got = exchange(gated_t, nb, s)
     x = got.transpose(1, 0, 2, 3).reshape(sub, nb * GROUP, own_rows)
     positions = jnp.arange(total_rows, dtype=jnp.int32).astype(jnp.float32)
     my_out = lax.dynamic_slice_in_dim(filter_out, s * sub, sub, 1)
@@ -87,7 +97,7 @@
     lagged = filters.astype(jnp.float32).reshape(nb, own_rows, sub).transpose(0, 2, 1)
     filt = jnp.concatenate([jnp.zeros((1, sub, own_rows), jnp.float32), lagged], axis=0)
     conv_parts = toeplitz_conv(filt, x)
-    back = lax.all_to_all(conv_parts, "seq", 0, 0, tiled=False)
+    back = exchange(conv_parts, nb, s)
     conv = back.reshape(width, own_rows).T.astype(jnp.float32)
     mixed = outer_gate.astype(jnp.float32) * (conv + skip_gain[None, :] * gated.astype(jnp.float32))
     return mixed.astype(jnp.bfloat16)

time: 48.9 us -> 39.6 us (0.81)
  waiting for transfers between devices: 24.8 us -> 10.8 us
  starting transfers between devices: 9.95 us -> 12.8 us
  local copies, waits for them, and re-layouts: 5.12 us -> 7.74 us
  other arithmetic: 3.25 us -> 2.11 us
    all_to_all x2 -> x0, waiting for transfers between devices: 24.8 us -> none  [the longest x1 13.7 us: per_device(): back = lax.all_to_all(conv_parts, 'seq', 0, 0, tiled=False)]
    ppermute x0 -> x6, starting transfers between devices: none -> 12.8 us  [exchange(): lax.ppermute(piece, 'seq', [(i, (i + k) % nb) for i in range(nb)])]
    ppermute x0 -> x6, waiting for transfers between devices: none -> 10.8 us  [exchange(): lax.ppermute(piece, 'seq', [(i, (i + k) % nb) for i in range(nb)])]
    all_to_all x2 -> x0, starting transfers between devices: 9.95 us -> none  [the longest x1 6.35 us: per_device(): got = lax.all_to_all(gated_t, 'seq', 0, 0, tiled=False)]
    gather x0 -> x2, local copies, waits for them, and re-layouts: none -> 1.3 us  [exchange(): return jnp.take(z, order, axis=0)]
    dynamic_slice x0 -> x2, local copies, waits for them, and re-layouts: none -> 1.23 us  [exchange(): got = [x[s]]]
    transpose x1 -> x0, local copies, waits for them, and re-layouts: 0.87 us -> none  [per_device(): x = got.transpose(1, 0, 2, 3).reshape(sub, nb * GROUP, own_rows)]
    select_n x0 -> x1, local copies, waits for them, and re-layouts: none -> 0.86 us  [exchange(): return jnp.take(z, order, axis=0)]
  transfers between devices with their start and end apart: 2 -> 6, of which waited for: 2 -> 3; matrix products, arithmetic and copies ran while one was open for 5% -> 6% of each run, Pallas kernels for 0% -> 0%
where the time goes in v5:
time: 39.6 us; the launch traced here: 38.9 us
  starting transfers between devices  12.8 us (32%)
  waiting for transfers between devices  10.8 us (27%)
  local copies, waits for them, and re-layouts  7.74 us (20%)
  Pallas kernels  4.15 us (10%)
  other arithmetic  2.11 us (5%)
  matrix products  1.07 us (3%)
    ppermute x6, starting transfers between devices, exchange(): lax.ppermute(piece, 'seq', [(i, (i + k) % nb) for i in range(nb)])  12.8 us
    ppermute x6, waiting for transfers between devices, exchange(): lax.ppermute(piece, 'seq', [(i, (i + k) % nb) for i in range(nb)])  10.8 us
    pallas_call x1, Pallas kernels, toeplitz_conv(): pl.pallas_call(toeplitz_kernel, out_shape=jax.ShapeDtypeStruct((nb, count...  4.15 us
    unnamed x19, local copies, waits for them, and re-layouts  3.34 us
    gather x2, local copies, waits for them, and re-layouts, exchange(): return jnp.take(z, order, axis=0)  1.3 us
    dynamic_slice x2, local copies, waits for them, and re-layouts, exchange(): got = [x[s]]  1.23 us
    convert_element_type x1, local copies, waits for them, and re-layouts, per_device(): return mixed.astype(jnp.bfloat16)  1.01 us
    select_n x1, local copies, waits for them, and re-layouts, exchange(): return jnp.take(z, order, axis=0)  0.86 us
  transfers between devices with their start and end apart: 6, of which 3 were waited for; matrix products, arithmetic and copies ran while one was open for 6% of the time, Pallas kernels for 0%

profile of v5, /device:TPU:0, one launch (start us, length us, event | category | flops | bytes accessed | tf_op | source)
XLA Modules:
  0.0 38.9 jit_solution(3003537141921568720)
XLA Ops:
  0.0 0.0 copy-start
  0.0 0.0 copy-start.1
  0.0 1.4 %copy.18 = bf16[128,2048]{0,1:T(8,128)(2,1)S(1)} copy(bf16[128,2048]{1,0:T(8,128)(2,1)} %param.9) | data formatting | bytes 1048576 | tf_op args[1]
  1.4 0.0 copy-done.1
  1.4 0.3 copy.19
  1.7 0.1 multiply_convert_fusion
  1.9 3.1 %collective-permute-start = (bf16[32,16,128]{2,1,0:T(8,128)(2,1)S(1)}, bf16[32,16,128]{2,1,0:T(8,128)(2,1)S(1)}, u32[]{:S(2)}, u32[]{:S(2)}) collective-permute-start(bf16[32,16,128]{2,1,0:T(8,128)(2,1)S(1)} %get-tuple-element.12), channel_id=1, source_target_pairs={{0,4},{4,8},{8,12},{12,0},{1,5},{5,9},{9,13},{13,1},{2,6},{6,10},{... | collective-permute-start | bytes 393224 | tf_op jit(solution)/shard_map/ppermute | solution.py:74
  5.0 2.6 %collective-permute-start.1 = (bf16[32,16,128]{2,1,0:T(8,128)(2,1)S(1)}, bf16[32,16,128]{2,1,0:T(8,128)(2,1)S(1)}, u32[]{:S(2)}, u32[]{:S(2)}) collective-permute-start(bf16[32,16,128]{2,1,0:T(8,128)(2,1)S(1)} %get-tuple-element.11), channel_id=1, source_target_pairs={{0,8},{4,12},{8,0},{12,4},{1,9},{5,13},{9,1},{13,5},{2,10},{6,14},... | collective-permute-start | bytes 393224 | tf_op jit(solution)/shard_map/ppermute | solution.py:74
  7.6 1.3 %collective-permute-start.2 = (bf16[32,16,128]{2,1,0:T(8,128)(2,1)S(1)}, bf16[32,16,128]{2,1,0:T(8,128)(2,1)S(1)}, u32[]{:S(2)}, u32[]{:S(2)}) collective-permute-start(bf16[32,16,128]{2,1,0:T(8,128)(2,1)S(1)} %get-tuple-element.10), channel_id=1, source_target_pairs={{0,12},{4,0},{8,4},{12,8},{1,13},{5,1},{9,5},{13,9},{2,14},{6,2},{... | collective-permute-start | bytes 393224 | tf_op jit(solution)/shard_map/ppermute | solution.py:74
  9.0 0.0 copy-start.6
  9.0 0.6 %copy-done.6 = f32[128]{0:T(128)S(1)} copy-done((f32[128]{0:T(128)S(1)}, f32[128]{0:T(128)}, u32[]{:S(2)}) %copy-start.6) | copy-done | bytes 536
  9.7 0.1 multiply_sqrt_fusion
  9.7 0.0 copy-start.3
  9.7 0.2 multiply_cosine_fusion
  9.9 0.0 copy-start.5
  9.9 0.5 %copy-done.3 = f32[33,64]{1,0:T(8,128)S(1)} copy-done((f32[33,64]{1,0:T(8,128)S(1)}, f32[33,64]{1,0:T(8,128)}, u32[]{:S(2)}) %copy-start.3) | copy-done | bytes 8472
  10.5 0.1 copy-done.5
  10.6 0.7 %fusion.1 = f32[512,64]{0,1:T(8,128)S(1)} fusion(f32[33,64]{1,0:T(8,128)S(1)} %copy-done.3, f32[512,16]{0,1:T(8,128)S(1)} %get-tuple-element.14, f32[512,16]{0,1:T(8,128)S(1)} %get-tuple-element.13, f32[512,1]{0,1:T(1,128)S(1)} %convert_multiply_fusion, f32[64]{0:T(128)S(1)} %copy-done.5), kind=kOutput, calls=%fused_computation.4 | convolution fusion | flops 13075456 | bytes 207360 | tf_op jit(solution)/shard_map/dot_general | solution.py:22
  11.3 0.0 copy-done
  11.4 0.3 fusion.3
  11.7 0.6 %pad_convert_fusion.filt_ref = f32[5,32,128]{2,1,0:T(8,128)} fusion(bf16[4,32,128]{2,1,0:T(8,128)(2,1)S(1)} %bitcast.51), kind=kLoop, calls=%fused_computation.29 | loop fusion | flops 20480 | bytes 114688 | tf_op jit(solution)/shard_map/concatenate | solution.py:98
  12.4 0.0 collective-permute-done
  12.4 3.9 %collective-permute-done.1 = bf16[32,16,128]{2,1,0:T(8,128)(2,1)S(1)} collective-permute-done((bf16[32,16,128]{2,1,0:T(8,128)(2,1)S(1)}, bf16[32,16,128]{2,1,0:T(8,128)(2,1)S(1)}, u32[]{:S(2)}, u32[]{:S(2)}) %collective-permute-start.1) | collective-permute-done | bytes 131104 | tf_op jit(solution)/shard_map/ppermute | solution.py:74
  16.2 0.0 collective-permute-done.2
  16.2 0.1 pad_maximum_fusion
  16.3 0.6 %gather_fusion = bf16[4,32,16,128]{3,2,1,0:T(8,128)(2,1)S(1)} fusion(bf16[4,32,16,128]{3,2,1,0:T(8,128)(2,1)S(1)} %pad_maximum_fusion, s32[1024]{0:T(1024)S(1)} %pad_clamp_fusion), kind=kCustom, calls=%fused_computation | custom fusion | bytes 1048592 | tf_op jit(solution)/shard_map/jit(_take)/gather | solution.py:77
  17.0 0.1 select_bitcast_fusion
  17.1 0.9 %copy.20 = bf16[32,4,16,128]{3,2,1,0:T(8,128)(2,1)} copy(bf16[32,4,16,128]{3,2,0,1:T(8,128)(2,1)S(1)} %select_bitcast_fusion) | data formatting | bytes 1048576 | tf_op jit(solution)/shard_map/jit(_take)/select_n | solution.py:77
  17.9 4.1 %shard_map.82 = bf16[4,512,128]{2,1,0:T(8,128)(2,1)} custom-call(f32[5,32,128]{2,1,0:T(8,128)} %pad_convert_fusion.filt_ref, bf16[32,64,128]{2,1,0:T(8,128)(2,1)} %bitcast.50), custom_call_target="tpu_custom_call" | custom-call | tf_op jit(solution)/shard_map/pallas_call | solution.py:57
  22.1 0.0 copy-start.2
  22.1 1.2 %constant_dynamic-slice_fusion = (bf16[1,512,128]{2,1,0:T(8,128)(2,1)S(1)}, bf16[512,128]{1,0:T(8,128)(2,1)S(1)}, bf16[512,128]{1,0:T(8,128)(2,1)S(1)}, bf16[512,128]{1,0:T(8,128)(2,1)S(1)}) fusion(bf16[4,512,128]{2,1,0:T(8,128)(2,1)} %shard_map.82, s32[]{:T(128)S(6)} %select_n.96, s32[]{:T(128)S(6)} %select_n.102, s32[]{:T(128)S(6)} %select_n.100, ...), kind=kLoop, calls=%fused_computation.36 | loop fusion | bytes 1048592 | tf_op jit(solution)/shard_map/dynamic_slice | solution.py:71
  23.3 3.3 %collective-permute-start.3 = (bf16[512,128]{1,0:T(8,128)(2,1)S(1)}, bf16[512,128]{1,0:T(8,128)(2,1)S(1)}, u32[]{:S(2)}, u32[]{:S(2)}) collective-permute-start(bf16[512,128]{1,0:T(8,128)(2,1)S(1)} %get-tuple-element.8), channel_id=1, source_target_pairs={{0,4},{4,8},{8,12},{12,0},{1,5},{5,9},{9,13},{13,1},{2,6},{6,10},{... | collective-permute-start | bytes 393224 | tf_op jit(solution)/shard_map/ppermute | solution.py:74
  26.6 1.6 %collective-permute-start.4 = (bf16[512,128]{1,0:T(8,128)(2,1)S(1)}, bf16[512,128]{1,0:T(8,128)(2,1)S(1)}, u32[]{:S(2)}, u32[]{:S(2)}) collective-permute-start(bf16[512,128]{1,0:T(8,128)(2,1)S(1)} %get-tuple-element.7), channel_id=1, source_target_pairs={{0,8},{4,12},{8,0},{12,4},{1,9},{5,13},{9,1},{13,5},{2,10},{6,14},... | collective-permute-start | bytes 393224 | tf_op jit(solution)/shard_map/ppermute | solution.py:74
  28.2 0.8 %collective-permute-start.5 = (bf16[512,128]{1,0:T(8,128)(2,1)S(1)}, bf16[512,128]{1,0:T(8,128)(2,1)S(1)}, u32[]{:S(2)}, u32[]{:S(2)}) collective-permute-start(bf16[512,128]{1,0:T(8,128)(2,1)S(1)} %get-tuple-element.6), channel_id=1, source_target_pairs={{0,12},{4,0},{8,4},{12,8},{1,13},{5,1},{9,5},{13,9},{2,14},{6,2},{... | collective-permute-start | bytes 393224 | tf_op jit(solution)/shard_map/ppermute | solution.py:74
  29.0 0.1 broadcast_bitcast_fusion
  29.1 0.0 copy-done.2
  29.1 0.3 copy.16
  29.4 2.3 %collective-permute-done.3 = bf16[512,128]{1,0:T(8,128)(2,1)S(1)} collective-permute-done((bf16[512,128]{1,0:T(8,128)(2,1)S(1)}, bf16[512,128]{1,0:T(8,128)(2,1)S(1)}, u32[]{:S(2)}, u32[]{:S(2)}) %collective-permute-start.3) | collective-permute-done | bytes 131104 | tf_op jit(solution)/shard_map/ppermute | solution.py:74
  31.7 4.6 %collective-permute-done.4 = bf16[512,128]{1,0:T(8,128)(2,1)S(1)} collective-permute-done((bf16[512,128]{1,0:T(8,128)(2,1)S(1)}, bf16[512,128]{1,0:T(8,128)(2,1)S(1)}, u32[]{:S(2)}, u32[]{:S(2)}) %collective-permute-start.4) | collective-permute-done | bytes 131104 | tf_op jit(solution)/shard_map/ppermute | solution.py:74
  36.3 0.0 collective-permute-done.5
  36.3 0.1 pad_maximum_fusion.1
  36.4 0.0 copy-start.4
  36.4 0.6 %gather_fusion.1 = bf16[4,512,128]{2,1,0:T(8,128)(2,1)S(1)} fusion(bf16[4,512,128]{2,1,0:T(8,128)(2,1)S(1)} %pad_maximum_fusion.1, s32[1024]{0:T(1024)S(1)} %pad_clamp_fusion), kind=kCustom, calls=%fused_computation.1 | custom fusion | bytes 1048592 | tf_op jit(solution)/shard_map/jit(_take)/gather | solution.py:77
  37.1 0.0 copy-done.4
  37.1 0.8 %fusion.5 = bf16[128,2048]{0,1:T(8,128)(2,1)S(1)} fusion(bf16[128,2048]{0,1:T(8,128)(2,1)S(1)} %multiply_convert_fusion, bf16[128,2048]{0,1:T(8,128)(2,1)S(1)} %copy.16, bf16[4,512,128]{2,1,0:T(8,128)(2,1)S(1)} %gather_fusion.1, f32[2048]{0:T(1024)S(1)} %copy-done.4, pred[2048]{0:T(1024)(128)(4,1)S(1)} %bitcast.58), kind=kLoop, calls=%fused_computation.10 | loop fusion | flops 2097152 | bytes 2107392 | tf_op jit(solution)/shard_map/convert_element_type | solution.py:103
  37.9 1.0 %copy.21 = bf16[128,2048]{1,0:T(8,128)(2,1)} copy(bf16[128,2048]{0,1:T(8,128)(2,1)S(1)} %fusion.5) | data formatting | bytes 1048576 | tf_op jit(solution)/shard_map/convert_element_type | solution.py:103
  (9 shorter events, 0.1 us)
Async XLA Ops:
  0.0 11.3 %copy-start = (f32[64,128]{1,0:T(8,128)S(1)}, f32[64,128]{1,0:T(8,128)}, u32[]{:S(2)}) copy-start(f32[64,128]{1,0:T(8,128)} %param.13) | copy-start | bytes 98308
  0.0 1.4 %copy-start.1 = (bf16[128,2048]{1,0:T(8,128)(2,1)S(1)}, bf16[128,2048]{1,0:T(8,128)(2,1)}, u32[]{:S(2)}) copy-start(bf16[128,2048]{1,0:T(8,128)(2,1)} %param.10) | copy-start | bytes 1572868
  1.9 10.5 %collective-permute-start = (bf16[32,16,128]{2,1,0:T(8,128)(2,1)S(1)}, bf16[32,16,128]{2,1,0:T(8,128)(2,1)S(1)}, u32[]{:S(2)}, u32[]{:S(2)}) collective-permute-start(bf16[32,16,128]{2,1,0:T(8,128)(2,1)S(1)} %get-tuple-element.12), channel_id=1, source_target_pairs={{0,4},{4,8},{8,12},{12,0},{1,5},{5,9},{9,13},{13,1},{2,6},{6,10},{... | collective-permute-start | bytes 393224 | tf_op jit(solution)/shard_map/ppermute | solution.py:74
  5.0 11.2 %collective-permute-start.1 = (bf16[32,16,128]{2,1,0:T(8,128)(2,1)S(1)}, bf16[32,16,128]{2,1,0:T(8,128)(2,1)S(1)}, u32[]{:S(2)}, u32[]{:S(2)}) collective-permute-start(bf16[32,16,128]{2,1,0:T(8,128)(2,1)S(1)} %get-tuple-element.11), channel_id=1, source_target_pairs={{0,8},{4,12},{8,0},{12,4},{1,9},{5,13},{9,1},{13,5},{2,10},{6,14},... | collective-permute-start | bytes 393224 | tf_op jit(solution)/shard_map/ppermute | solution.py:74
  7.6 8.6 %collective-permute-start.2 = (bf16[32,16,128]{2,1,0:T(8,128)(2,1)S(1)}, bf16[32,16,128]{2,1,0:T(8,128)(2,1)S(1)}, u32[]{:S(2)}, u32[]{:S(2)}) collective-permute-start(bf16[32,16,128]{2,1,0:T(8,128)(2,1)S(1)} %get-tuple-element.10), channel_id=1, source_target_pairs={{0,12},{4,0},{8,4},{12,8},{1,13},{5,1},{9,5},{13,9},{2,14},{6,2},{... | collective-permute-start | bytes 393224 | tf_op jit(solution)/shard_map/ppermute | solution.py:74
  9.0 0.7 %copy-start.6 = (f32[128]{0:T(128)S(1)}, f32[128]{0:T(128)}, u32[]{:S(2)}) copy-start(f32[128]{0:T(128)} %param.14) | copy-start | bytes 1540
  9.7 0.7 %copy-start.3 = (f32[33,64]{1,0:T(8,128)S(1)}, f32[33,64]{1,0:T(8,128)}, u32[]{:S(2)}) copy-start(f32[33,64]{1,0:T(8,128)} %param.11) | copy-start | bytes 25348
  9.9 0.7 %copy-start.5 = (f32[64]{0:T(128)S(1)}, f32[64]{0:T(128)}, u32[]{:S(2)}) copy-start(f32[64]{0:T(128)} %param.12) | copy-start | bytes 772
  22.1 7.0 %copy-start.2 = (bf16[128,2048]{1,0:T(8,128)(2,1)S(1)}, bf16[128,2048]{1,0:T(8,128)(2,1)}, u32[]{:S(2)}) copy-start(bf16[128,2048]{1,0:T(8,128)(2,1)} %param.8) | copy-start | bytes 1572868
  23.3 8.4 %collective-permute-start.3 = (bf16[512,128]{1,0:T(8,128)(2,1)S(1)}, bf16[512,128]{1,0:T(8,128)(2,1)S(1)}, u32[]{:S(2)}, u32[]{:S(2)}) collective-permute-start(bf16[512,128]{1,0:T(8,128)(2,1)S(1)} %get-tuple-element.8), channel_id=1, source_target_pairs={{0,4},{4,8},{8,12},{12,0},{1,5},{5,9},{9,13},{13,1},{2,6},{6,10},{... | collective-permute-start | bytes 393224 | tf_op jit(solution)/shard_map/ppermute | solution.py:74
  26.6 9.7 %collective-permute-start.4 = (bf16[512,128]{1,0:T(8,128)(2,1)S(1)}, bf16[512,128]{1,0:T(8,128)(2,1)S(1)}, u32[]{:S(2)}, u32[]{:S(2)}) collective-permute-start(bf16[512,128]{1,0:T(8,128)(2,1)S(1)} %get-tuple-element.7), channel_id=1, source_target_pairs={{0,8},{4,12},{8,0},{12,4},{1,9},{5,13},{9,1},{13,5},{2,10},{6,14},... | collective-permute-start | bytes 393224 | tf_op jit(solution)/shard_map/ppermute | solution.py:74
  28.2 8.1 %collective-permute-start.5 = (bf16[512,128]{1,0:T(8,128)(2,1)S(1)}, bf16[512,128]{1,0:T(8,128)(2,1)S(1)}, u32[]{:S(2)}, u32[]{:S(2)}) collective-permute-start(bf16[512,128]{1,0:T(8,128)(2,1)S(1)} %get-tuple-element.6), channel_id=1, source_target_pairs={{0,12},{4,0},{8,4},{12,8},{1,13},{5,1},{9,5},{13,9},{2,14},{6,2},{... | collective-permute-start | bytes 393224 | tf_op jit(solution)/shard_map/ppermute | solution.py:74
  36.4 0.7 %copy-start.4 = (f32[2048]{0:T(1024)S(1)}, f32[2048]{0:T(1024)}, u32[]{:S(2)}) copy-start(f32[2048]{0:T(1024)} %param.15) | copy-start | bytes 24580

commit v6 on v5

--- a/solution.py
+++ b/solution.py
@@ -10,6 +10,7 @@
 GROUP = 16
 BANDS = 16
 FILTERS_PER_STEP = 8
+CHUNKS = 2
 
 
 def filter_table(positions, total, filter_in, filter_bias, filter_out, decay):
@@ -88,16 +89,22 @@
     sub = count // nb
     gated = (inner_gate.astype(jnp.float32) * signal.astype(jnp.float32)).astype(jnp.bfloat16)
     gated_t = gated.T.reshape(nb, sub, GROUP, own_rows)
-    got = exchange(gated_t, nb, s)
-    x = got.transpose(1, 0, 2, 3).reshape(sub, nb * GROUP, own_rows)
     positions = jnp.arange(total_rows, dtype=jnp.int32).astype(jnp.float32)
     my_out = lax.dynamic_slice_in_dim(filter_out, s * sub, sub, 1)
     my_decay = lax.dynamic_slice_in_dim(decay, s * sub, sub, 0)
     filters = filter_table(positions, float(total_rows), filter_in, filter_bias, my_out, my_decay)
     lagged = filters.astype(jnp.float32).reshape(nb, own_rows, sub).transpose(0, 2, 1)
     filt = jnp.concatenate([jnp.zeros((1, sub, own_rows), jnp.float32), lagged], axis=0)
-    conv_parts = toeplitz_conv(filt, x)
-    back = exchange(conv_parts, nb, s)
+    chunks = CHUNKS if sub % CHUNKS == 0 else 1
+    part = sub // chunks
+    backs = []
+    for c in range(chunks):
+        cut = slice(c * part, (c + 1) * part)
+        got = exchange(gated_t[:, cut], nb, s)
+        x = got.transpose(1, 0, 2, 3).reshape(part, nb * GROUP, own_rows)
+        conv_parts = toeplitz_conv(filt[:, cut], x)
+        backs.append(exchange(conv_parts, nb, s).reshape(nb, 1, part * GROUP, own_rows))
+    back = jnp.concatenate(backs, axis=1)
     conv = back.reshape(width, own_rows).T.astype(jnp.float32)
     mixed = outer_gate.astype(jnp.float32) * (conv + skip_gain[None, :] * gated.astype(jnp.float32))
     return mixed.astype(jnp.bfloat16)

time: 39.6 us -> 42.7 us (1.078)
  starting transfers between devices: 12.8 us -> 19.9 us
  waiting for transfers between devices: 10.8 us -> 4.66 us
  local copies, waits for them, and re-layouts: 7.74 us -> 10.1 us
  Pallas kernels: 4.15 us -> 5.11 us
  other arithmetic: 2.11 us -> 1.29 us
    ppermute x6 -> x12, starting transfers between devices: 12.8 us -> 19.9 us  [exchange(): lax.ppermute(piece, 'seq', [(i, (i + k) % nb) for i in range(nb)])]
    ppermute x6 -> x12, waiting for transfers between devices: 10.8 us -> 4.66 us  [exchange(): lax.ppermute(piece, 'seq', [(i, (i + k) % nb) for i in range(nb)])]
    transpose x0 -> x2, local copies, waits for them, and re-layouts: none -> 1.46 us  [per_device(): x = got.transpose(1, 0, 2, 3).reshape(part, nb * GROUP, own_rows)]
    gather x2 -> x4, local copies, waits for them, and re-layouts: 1.3 us -> 2.39 us  [exchange(): return jnp.take(z, order, axis=0)]
    pallas_call x1 -> x2, Pallas kernels: 4.15 us -> 5.11 us  [toeplitz_conv(): pl.pallas_call(toeplitz_kernel, out_shape=jax.ShapeDtypeStruct((nb, count...]
    select_n x1 -> x0, local copies, waits for them, and re-layouts: 0.86 us -> none  [exchange(): return jnp.take(z, order, axis=0)]
    unnamed x19 -> x17, local copies, waits for them, and re-layouts: 3.34 us -> 2.55 us
    dynamic_slice x2 -> x4, local copies, waits for them, and re-layouts: 1.23 us -> 1.95 us  [exchange(): got = [x[s]]]
  transfers between devices with their start and end apart: 6 -> 12, of which waited for: 3 -> 4; matrix products, arithmetic and copies ran while one was open for 6% -> 12% of each run, Pallas kernels for 0% -> 6%
where the time goes in v6:
time: 42.7 us; the launch traced here: 42.4 us
  starting transfers between devices  19.9 us (47%)
  local copies, waits for them, and re-layouts  10.1 us (24%)
  Pallas kernels  5.11 us (12%)
  waiting for transfers between devices  4.66 us (11%)
  other arithmetic  1.29 us (3%)
  matrix products  1.07 us (3%)
    ppermute x12, starting transfers between devices, exchange(): lax.ppermute(piece, 'seq', [(i, (i + k) % nb) for i in range(nb)])  19.9 us
    pallas_call x2, Pallas kernels, toeplitz_conv(): pl.pallas_call(toeplitz_kernel, out_shape=jax.ShapeDtypeStruct((nb, count...  5.11 us
    ppermute x12, waiting for transfers between devices, exchange(): lax.ppermute(piece, 'seq', [(i, (i + k) % nb) for i in range(nb)])  4.66 us
    unnamed x17, local copies, waits for them, and re-layouts  2.55 us
    gather x4, local copies, waits for them, and re-layouts, exchange(): return jnp.take(z, order, axis=0)  2.39 us
    dynamic_slice x4, local copies, waits for them, and re-layouts, exchange(): got = [x[s]]  1.95 us
    transpose x2, local copies, waits for them, and re-layouts, per_device(): x = got.transpose(1, 0, 2, 3).reshape(part, nb * GROUP, own_rows)  1.46 us
    convert_element_type x1, local copies, waits for them, and re-layouts, per_device(): return mixed.astype(jnp.bfloat16)  1.01 us
  transfers between devices with their start and end apart: 12, of which 4 were waited for; matrix products, arithmetic and copies ran while one was open for 12% of the time, Pallas kernels for 6%

profile of v6, /device:TPU:0, one launch (start us, length us, event | category | flops | bytes accessed | tf_op | source)
XLA Modules:
  0.0 42.4 jit_solution(17268451814071401739)
XLA Ops:
  0.0 0.0 copy-start
  0.0 0.0 copy-start.1
  0.0 1.4 %copy.19 = bf16[128,2048]{0,1:T(8,128)(2,1)S(1)} copy(bf16[128,2048]{1,0:T(8,128)(2,1)} %param.13) | data formatting | bytes 1048576 | tf_op args[1]
  1.4 0.0 copy-done.1
  1.4 0.3 copy.20
  1.7 0.1 multiply_convert_fusion
  1.9 3.1 %collective-permute-start.6 = (bf16[16,16,128]{2,1,0:T(8,128)(2,1)S(1)}, bf16[16,16,128]{2,1,0:T(8,128)(2,1)S(1)}, u32[]{:S(2)}, u32[]{:S(2)}) collective-permute-start(bf16[16,16,128]{2,1,0:T(8,128)(2,1)S(1)} %get-tuple-element.24), channel_id=1, source_target_pairs={{0,4},{4,8},{8,12},{12,0},{1,5},{5,9},{9,13},{13,1},{2,6},{6,10},{... | collective-permute-start | bytes 196616 | tf_op jit(solution)/shard_map/ppermute | solution.py:75
  5.0 2.6 %collective-permute-start.7 = (bf16[16,16,128]{2,1,0:T(8,128)(2,1)S(1)}, bf16[16,16,128]{2,1,0:T(8,128)(2,1)S(1)}, u32[]{:S(2)}, u32[]{:S(2)}) collective-permute-start(bf16[16,16,128]{2,1,0:T(8,128)(2,1)S(1)} %get-tuple-element.23), channel_id=1, source_target_pairs={{0,8},{4,12},{8,0},{12,4},{1,9},{5,13},{9,1},{13,5},{2,10},{6,14},... | collective-permute-start | bytes 196616 | tf_op jit(solution)/shard_map/ppermute | solution.py:75
  7.6 1.3 %collective-permute-start.8 = (bf16[16,16,128]{2,1,0:T(8,128)(2,1)S(1)}, bf16[16,16,128]{2,1,0:T(8,128)(2,1)S(1)}, u32[]{:S(2)}, u32[]{:S(2)}) collective-permute-start(bf16[16,16,128]{2,1,0:T(8,128)(2,1)S(1)} %get-tuple-element.22), channel_id=1, source_target_pairs={{0,12},{4,0},{8,4},{12,8},{1,13},{5,1},{9,5},{13,9},{2,14},{6,2},{... | collective-permute-start | bytes 196616 | tf_op jit(solution)/shard_map/ppermute | solution.py:75
  9.0 0.0 copy-start.6
  9.0 0.0 copy-start.3
  9.0 0.0 copy-start.5
  9.0 0.0 copy-start.2
  9.0 0.7 %collective-permute-start = (bf16[16,16,128]{2,1,0:T(8,128)(2,1)S(1)}, bf16[16,16,128]{2,1,0:T(8,128)(2,1)S(1)}, u32[]{:S(2)}, u32[]{:S(2)}) collective-permute-start(bf16[16,16,128]{2,1,0:T(8,128)(2,1)S(1)} %get-tuple-element.16), channel_id=1, source_target_pairs={{0,4},{4,8},{8,12},{12,0},{1,5},{5,9},{9,13},{13,1},{2,6},{6,10},{... | collective-permute-start | bytes 196616 | tf_op jit(solution)/shard_map/ppermute | solution.py:75
  9.7 0.3 collective-permute-start.1
  10.1 0.0 copy-done.6
  10.1 0.1 multiply_sqrt_fusion
  10.2 0.2 multiply_cosine_fusion
  10.4 0.0 copy-done.3
  10.4 0.0 copy-done.5
  10.4 0.7 %fusion.1 = f32[512,64]{0,1:T(8,128)S(1)} fusion(f32[33,64]{1,0:T(8,128)S(1)} %copy-done.3, f32[512,16]{0,1:T(8,128)S(1)} %get-tuple-element.28, f32[512,16]{0,1:T(8,128)S(1)} %get-tuple-element.27, f32[512,1]{0,1:T(1,128)S(1)} %convert_multiply_fusion, f32[64]{0:T(128)S(1)} %copy-done.5), kind=kOutput, calls=%fused_computation.6 | convolution fusion | flops 13075456 | bytes 207360 | tf_op jit(solution)/shard_map/dot_general | solution.py:23
  11.2 0.0 copy-done
  11.2 0.3 fusion.3
  11.6 0.6 %fusion.16 = (f32[5,16,128]{2,1,0:T(8,128)}, f32[5,16,128]{2,1,0:T(8,128)}) fusion(f32[5,32,128]{2,1,0:T(8,128)S(1)} %pad_convert_fusion), kind=kLoop, calls=%fused_computation.64 | loop fusion | bytes 163840 | tf_op jit(solution)/shard_map/slice | solution.py:105
  12.2 0.0 copy-done.2
  12.2 0.3 copy.17
  12.5 0.0 collective-permute-done.6
  12.5 2.9 %collective-permute-start.2 = (bf16[16,16,128]{2,1,0:T(8,128)(2,1)S(1)}, bf16[16,16,128]{2,1,0:T(8,128)(2,1)S(1)}, u32[]{:S(2)}, u32[]{:S(2)}) collective-permute-start(bf16[16,16,128]{2,1,0:T(8,128)(2,1)S(1)} %get-tuple-element.14), channel_id=1, source_target_pairs={{0,12},{4,0},{8,4},{12,8},{1,13},{5,1},{9,5},{13,9},{2,14},{6,2},{... | collective-permute-start | bytes 196616 | tf_op jit(solution)/shard_map/ppermute | solution.py:75
  15.4 0.0 collective-permute-done.7
  15.4 0.0 collective-permute-done.8
  15.4 0.6 %gather_fusion.2 = bf16[4,16,16,128]{3,2,1,0:T(8,128)(2,1)S(1)} fusion(bf16[4,16,16,128]{3,2,1,0:T(8,128)(2,1)S(1)} %pad_maximum_fusion.2, s32[1024]{0:T(1024)S(1)} %pad_clamp_fusion), kind=kCustom, calls=%fused_computation.2.clone | custom fusion | bytes 524304 | tf_op jit(solution)/shard_map/jit(_take)/gather | solution.py:78
  16.0 0.0 collective-permute-done
  16.0 1.7 %collective-permute-done.1 = bf16[16,16,128]{2,1,0:T(8,128)(2,1)S(1)} collective-permute-done((bf16[16,16,128]{2,1,0:T(8,128)(2,1)S(1)}, bf16[16,16,128]{2,1,0:T(8,128)(2,1)S(1)}, u32[]{:S(2)}, u32[]{:S(2)}) %collective-permute-start.1) | collective-permute-done | bytes 65568 | tf_op jit(solution)/shard_map/ppermute | solution.py:75
  17.7 0.6 %collective-permute-done.2 = bf16[16,16,128]{2,1,0:T(8,128)(2,1)S(1)} collective-permute-done((bf16[16,16,128]{2,1,0:T(8,128)(2,1)S(1)}, bf16[16,16,128]{2,1,0:T(8,128)(2,1)S(1)}, u32[]{:S(2)}, u32[]{:S(2)}) %collective-permute-start.2) | collective-permute-done | bytes 65568 | tf_op jit(solution)/shard_map/ppermute | solution.py:75
  18.3 0.6 %gather_fusion = bf16[4,16,16,128]{3,2,1,0:T(8,128)(2,1)S(1)} fusion(bf16[4,16,16,128]{3,2,1,0:T(8,128)(2,1)S(1)} %pad_maximum_fusion, s32[1024]{0:T(1024)S(1)} %pad_clamp_fusion), kind=kCustom, calls=%fused_computation.clone | custom fusion | bytes 524304 | tf_op jit(solution)/shard_map/jit(_take)/gather | solution.py:78
  18.9 0.1 select_bitcast_fusion.3
  19.1 0.7 %copy.22 = bf16[16,4,16,128]{3,2,1,0:T(8,128)(2,1)} copy(bf16[16,4,16,128]{3,2,0,1:T(8,128)(2,1)S(1)} %get-tuple-element.32) | data formatting | bytes 524288 | tf_op jit(solution)/shard_map/transpose | solution.py:104
  19.8 2.6 %shard_map.83 = bf16[4,256,128]{2,1,0:T(8,128)(2,1)} custom-call(f32[5,16,128]{2,1,0:T(8,128)} %get-tuple-element.26.filt_ref, bf16[16,64,128]{2,1,0:T(8,128)(2,1)} %bitcast.69), custom_call_target="tpu_custom_call" | custom-call | tf_op jit(solution)/shard_map/pallas_call | solution.py:58
  22.4 1.0 %constant_dynamic-slice_fusion = (bf16[1,256,128]{2,1,0:T(8,128)(2,1)S(1)}, bf16[256,128]{1,0:T(8,128)(2,1)S(1)}, bf16[256,128]{1,0:T(8,128)(2,1)S(1)}, bf16[256,128]{1,0:T(8,128)(2,1)S(1)}) fusion(bf16[4,256,128]{2,1,0:T(8,128)(2,1)} %shard_map.83, s32[]{:T(128)S(6)} %select_n.89, s32[]{:T(128)S(6)} %select_n.95, s32[]{:T(128)S(6)} %select_n.93, ...), kind=kLoop, calls=%fused_computation.45 | loop fusion | bytes 524304 | tf_op jit(solution)/shard_map/dynamic_slice | solution.py:72
  23.3 2.0 %collective-permute-start.9 = (bf16[256,128]{1,0:T(8,128)(2,1)S(1)}, bf16[256,128]{1,0:T(8,128)(2,1)S(1)}, u32[]{:S(2)}, u32[]{:S(2)}) collective-permute-start(bf16[256,128]{1,0:T(8,128)(2,1)S(1)} %get-tuple-element.20), channel_id=1, source_target_pairs={{0,4},{4,8},{8,12},{12,0},{1,5},{5,9},{9,13},{13,1},{2,6},{6,10},{... | collective-permute-start | bytes 196616 | tf_op jit(solution)/shard_map/ppermute | solution.py:75
  25.3 1.8 %collective-permute-start.10 = (bf16[256,128]{1,0:T(8,128)(2,1)S(1)}, bf16[256,128]{1,0:T(8,128)(2,1)S(1)}, u32[]{:S(2)}, u32[]{:S(2)}) collective-permute-start(bf16[256,128]{1,0:T(8,128)(2,1)S(1)} %get-tuple-element.19), channel_id=1, source_target_pairs={{0,8},{4,12},{8,0},{12,4},{1,9},{5,13},{9,1},{13,5},{2,10},{6,14},... | collective-permute-start | bytes 196616 | tf_op jit(solution)/shard_map/ppermute | solution.py:75
  27.1 0.6 %collective-permute-start.11 = (bf16[256,128]{1,0:T(8,128)(2,1)S(1)}, bf16[256,128]{1,0:T(8,128)(2,1)S(1)}, u32[]{:S(2)}, u32[]{:S(2)}) collective-permute-start(bf16[256,128]{1,0:T(8,128)(2,1)S(1)} %get-tuple-element.18), channel_id=1, source_target_pairs={{0,12},{4,0},{8,4},{12,8},{1,13},{5,1},{9,5},{13,9},{2,14},{6,2},{... | collective-permute-start | bytes 196616 | tf_op jit(solution)/shard_map/ppermute | solution.py:75
  27.7 0.7 %copy.21 = bf16[16,4,16,128]{3,2,1,0:T(8,128)(2,1)} copy(bf16[16,4,16,128]{3,2,0,1:T(8,128)(2,1)S(1)} %get-tuple-element.31) | data formatting | bytes 524288 | tf_op jit(solution)/shard_map/transpose | solution.py:104
  28.4 2.6 %shard_map.82 = bf16[4,256,128]{2,1,0:T(8,128)(2,1)} custom-call(f32[5,16,128]{2,1,0:T(8,128)} %get-tuple-element.25.filt_ref, bf16[16,64,128]{2,1,0:T(8,128)(2,1)} %bitcast.68), custom_call_target="tpu_custom_call" | custom-call | tf_op jit(solution)/shard_map/pallas_call | solution.py:58
  31.0 1.0 %constant_dynamic-slice_fusion.2 = (bf16[1,256,128]{2,1,0:T(8,128)(2,1)S(1)}, bf16[256,128]{1,0:T(8,128)(2,1)S(1)}, bf16[256,128]{1,0:T(8,128)(2,1)S(1)}, bf16[256,128]{1,0:T(8,128)(2,1)S(1)}) fusion(bf16[4,256,128]{2,1,0:T(8,128)(2,1)} %shard_map.82, s32[]{:T(128)S(6)} %select_n.89, s32[]{:T(128)S(6)} %select_n.95, s32[]{:T(128)S(6)} %select_n.93, ...), kind=kLoop, calls=%fused_computation.47 | loop fusion | bytes 524304 | tf_op jit(solution)/shard_map/dynamic_slice | solution.py:72
  31.9 1.4 %collective-permute-start.3 = (bf16[256,128]{1,0:T(8,128)(2,1)S(1)}, bf16[256,128]{1,0:T(8,128)(2,1)S(1)}, u32[]{:S(2)}, u32[]{:S(2)}) collective-permute-start(bf16[256,128]{1,0:T(8,128)(2,1)S(1)} %get-tuple-element.12), channel_id=1, source_target_pairs={{0,4},{4,8},{8,12},{12,0},{1,5},{5,9},{9,13},{13,1},{2,6},{6,10},{... | collective-permute-start | bytes 196616 | tf_op jit(solution)/shard_map/ppermute | solution.py:75
  33.4 1.1 %collective-permute-start.4 = (bf16[256,128]{1,0:T(8,128)(2,1)S(1)}, bf16[256,128]{1,0:T(8,128)(2,1)S(1)}, u32[]{:S(2)}, u32[]{:S(2)}) collective-permute-start(bf16[256,128]{1,0:T(8,128)(2,1)S(1)} %get-tuple-element.11), channel_id=1, source_target_pairs={{0,8},{4,12},{8,0},{12,4},{1,9},{5,13},{9,1},{13,5},{2,10},{6,14},... | collective-permute-start | bytes 196616 | tf_op jit(solution)/shard_map/ppermute | solution.py:75
  34.5 0.0 collective-permute-done.9
  34.5 1.9 %collective-permute-start.5 = (bf16[256,128]{1,0:T(8,128)(2,1)S(1)}, bf16[256,128]{1,0:T(8,128)(2,1)S(1)}, u32[]{:S(2)}, u32[]{:S(2)}) collective-permute-start(bf16[256,128]{1,0:T(8,128)(2,1)S(1)} %get-tuple-element.10), channel_id=1, source_target_pairs={{0,12},{4,0},{8,4},{12,8},{1,13},{5,1},{9,5},{13,9},{2,14},{6,2},{... | collective-permute-start | bytes 196616 | tf_op jit(solution)/shard_map/ppermute | solution.py:75
  36.4 0.0 collective-permute-done.10
  36.4 0.0 collective-permute-done.11
  36.5 0.6 %gather_fusion.3 = bf16[4,256,128]{2,1,0:T(8,128)(2,1)S(1)} fusion(bf16[4,256,128]{2,1,0:T(8,128)(2,1)S(1)} %pad_maximum_fusion.3, s32[1024]{0:T(1024)S(1)} %pad_clamp_fusion), kind=kCustom, calls=%fused_computation.3.clone | custom fusion | bytes 524304 | tf_op jit(solution)/shard_map/jit(_take)/gather | solution.py:78
  37.1 1.0 %collective-permute-done.3 = bf16[256,128]{1,0:T(8,128)(2,1)S(1)} collective-permute-done((bf16[256,128]{1,0:T(8,128)(2,1)S(1)}, bf16[256,128]{1,0:T(8,128)(2,1)S(1)}, u32[]{:S(2)}, u32[]{:S(2)}) %collective-permute-start.3) | collective-permute-done | bytes 65568 | tf_op jit(solution)/shard_map/ppermute | solution.py:75
  38.1 1.4 %collective-permute-done.4 = bf16[256,128]{1,0:T(8,128)(2,1)S(1)} collective-permute-done((bf16[256,128]{1,0:T(8,128)(2,1)S(1)}, bf16[256,128]{1,0:T(8,128)(2,1)S(1)}, u32[]{:S(2)}, u32[]{:S(2)}) %collective-permute-start.4) | collective-permute-done | bytes 65568 | tf_op jit(solution)/shard_map/ppermute | solution.py:75
  39.5 0.0 collective-permute-done.5
  39.5 0.6 %gather_fusion.1 = bf16[4,256,128]{2,1,0:T(8,128)(2,1)S(1)} fusion(bf16[4,256,128]{2,1,0:T(8,128)(2,1)S(1)} %pad_maximum_fusion.1, s32[1024]{0:T(1024)S(1)} %pad_clamp_fusion), kind=kCustom, calls=%fused_computation.1.clone | custom fusion | bytes 524304 | tf_op jit(solution)/shard_map/jit(_take)/gather | solution.py:78
  40.1 0.1 select_bitcast_fusion.2
  40.2 0.1 maximum_convert_fusion
  40.3 0.0 copy-start.4
  40.3 0.1 copy.23
  40.4 0.6 %copy-done.4 = f32[2048]{0:T(1024)S(1)} copy-done((f32[2048]{0:T(1024)S(1)}, f32[2048]{0:T(1024)}, u32[]{:S(2)}) %copy-start.4) | copy-done | bytes 8216
  41.0 0.4 fusion.5
  41.4 1.0 %copy.24 = bf16[128,2048]{1,0:T(8,128)(2,1)} copy(bf16[128,2048]{0,1:T(8,128)(2,1)S(1)} %fusion.5) | data formatting | bytes 1048576 | tf_op jit(solution)/shard_map/convert_element_type | solution.py:110
  (15 shorter events, 0.3 us)
Async XLA Ops:
  0.0 11.2 %copy-start = (f32[64,128]{1,0:T(8,128)S(1)}, f32[64,128]{1,0:T(8,128)}, u32[]{:S(2)}) copy-start(f32[64,128]{1,0:T(8,128)} %param.17) | copy-start | bytes 98308
  0.0 1.4 %copy-start.1 = (bf16[128,2048]{1,0:T(8,128)(2,1)S(1)}, bf16[128,2048]{1,0:T(8,128)(2,1)}, u32[]{:S(2)}) copy-start(bf16[128,2048]{1,0:T(8,128)(2,1)} %param.14) | copy-start | bytes 1572868
  1.9 10.6 %collective-permute-start.6 = (bf16[16,16,128]{2,1,0:T(8,128)(2,1)S(1)}, bf16[16,16,128]{2,1,0:T(8,128)(2,1)S(1)}, u32[]{:S(2)}, u32[]{:S(2)}) collective-permute-start(bf16[16,16,128]{2,1,0:T(8,128)(2,1)S(1)} %get-tuple-element.24), channel_id=1, source_target_pairs={{0,4},{4,8},{8,12},{12,0},{1,5},{5,9},{9,13},{13,1},{2,6},{6,10},{... | collective-permute-start | bytes 196616 | tf_op jit(solution)/shard_map/ppermute | solution.py:75
  5.0 10.4 %collective-permute-start.7 = (bf16[16,16,128]{2,1,0:T(8,128)(2,1)S(1)}, bf16[16,16,128]{2,1,0:T(8,128)(2,1)S(1)}, u32[]{:S(2)}, u32[]{:S(2)}) collective-permute-start(bf16[16,16,128]{2,1,0:T(8,128)(2,1)S(1)} %get-tuple-element.23), channel_id=1, source_target_pairs={{0,8},{4,12},{8,0},{12,4},{1,9},{5,13},{9,1},{13,5},{2,10},{6,14},... | collective-permute-start | bytes 196616 | tf_op jit(solution)/shard_map/ppermute | solution.py:75
  7.6 7.8 %collective-permute-start.8 = (bf16[16,16,128]{2,1,0:T(8,128)(2,1)S(1)}, bf16[16,16,128]{2,1,0:T(8,128)(2,1)S(1)}, u32[]{:S(2)}, u32[]{:S(2)}) collective-permute-start(bf16[16,16,128]{2,1,0:T(8,128)(2,1)S(1)} %get-tuple-element.22), channel_id=1, source_target_pairs={{0,12},{4,0},{8,4},{12,8},{1,13},{5,1},{9,5},{13,9},{2,14},{6,2},{... | collective-permute-start | bytes 196616 | tf_op jit(solution)/shard_map/ppermute | solution.py:75
  9.0 1.2 %copy-start.6 = (f32[128]{0:T(128)S(1)}, f32[128]{0:T(128)}, u32[]{:S(2)}) copy-start(f32[128]{0:T(128)} %param.18) | copy-start | bytes 1540
  9.0 1.5 %copy-start.3 = (f32[33,64]{1,0:T(8,128)S(1)}, f32[33,64]{1,0:T(8,128)}, u32[]{:S(2)}) copy-start(f32[33,64]{1,0:T(8,128)} %param.15) | copy-start | bytes 25348
  9.0 1.5 %copy-start.5 = (f32[64]{0:T(128)S(1)}, f32[64]{0:T(128)}, u32[]{:S(2)}) copy-start(f32[64]{0:T(128)} %param.16) | copy-start | bytes 772
  9.0 3.2 %copy-start.2 = (bf16[128,2048]{1,0:T(8,128)(2,1)S(1)}, bf16[128,2048]{1,0:T(8,128)(2,1)}, u32[]{:S(2)}) copy-start(bf16[128,2048]{1,0:T(8,128)(2,1)} %param.12) | copy-start | bytes 1572868
  9.0 7.0 %collective-permute-start = (bf16[16,16,128]{2,1,0:T(8,128)(2,1)S(1)}, bf16[16,16,128]{2,1,0:T(8,128)(2,1)S(1)}, u32[]{:S(2)}, u32[]{:S(2)}) collective-permute-start(bf16[16,16,128]{2,1,0:T(8,128)(2,1)S(1)} %get-tuple-element.16), channel_id=1, source_target_pairs={{0,4},{4,8},{8,12},{12,0},{1,5},{5,9},{9,13},{13,1},{2,6},{6,10},{... | collective-permute-start | bytes 196616 | tf_op jit(solution)/shard_map/ppermute | solution.py:75
  9.7 8.0 %collective-permute-start.1 = (bf16[16,16,128]{2,1,0:T(8,128)(2,1)S(1)}, bf16[16,16,128]{2,1,0:T(8,128)(2,1)S(1)}, u32[]{:S(2)}, u32[]{:S(2)}) collective-permute-start(bf16[16,16,128]{2,1,0:T(8,128)(2,1)S(1)} %get-tuple-element.15), channel_id=1, source_target_pairs={{0,8},{4,12},{8,0},{12,4},{1,9},{5,13},{9,1},{13,5},{2,10},{6,14},... | collective-permute-start | bytes 196616 | tf_op jit(solution)/shard_map/ppermute | solution.py:75
  12.5 5.8 %collective-permute-start.2 = (bf16[16,16,128]{2,1,0:T(8,128)(2,1)S(1)}, bf16[16,16,128]{2,1,0:T(8,128)(2,1)S(1)}, u32[]{:S(2)}, u32[]{:S(2)}) collective-permute-start(bf16[16,16,128]{2,1,0:T(8,128)(2,1)S(1)} %get-tuple-element.14), channel_id=1, source_target_pairs={{0,12},{4,0},{8,4},{12,8},{1,13},{5,1},{9,5},{13,9},{2,14},{6,2},{... | collective-permute-start | bytes 196616 | tf_op jit(solution)/shard_map/ppermute | solution.py:75
  23.3 11.2 %collective-permute-start.9 = (bf16[256,128]{1,0:T(8,128)(2,1)S(1)}, bf16[256,128]{1,0:T(8,128)(2,1)S(1)}, u32[]{:S(2)}, u32[]{:S(2)}) collective-permute-start(bf16[256,128]{1,0:T(8,128)(2,1)S(1)} %get-tuple-element.20), channel_id=1, source_target_pairs={{0,4},{4,8},{8,12},{12,0},{1,5},{5,9},{9,13},{13,1},{2,6},{6,10},{... | collective-permute-start | bytes 196616 | tf_op jit(solution)/shard_map/ppermute | solution.py:75
  25.3 11.2 %collective-permute-start.10 = (bf16[256,128]{1,0:T(8,128)(2,1)S(1)}, bf16[256,128]{1,0:T(8,128)(2,1)S(1)}, u32[]{:S(2)}, u32[]{:S(2)}) collective-permute-start(bf16[256,128]{1,0:T(8,128)(2,1)S(1)} %get-tuple-element.19), channel_id=1, source_target_pairs={{0,8},{4,12},{8,0},{12,4},{1,9},{5,13},{9,1},{13,5},{2,10},{6,14},... | collective-permute-start | bytes 196616 | tf_op jit(solution)/shard_map/ppermute | solution.py:75
  27.1 9.4 %collective-permute-start.11 = (bf16[256,128]{1,0:T(8,128)(2,1)S(1)}, bf16[256,128]{1,0:T(8,128)(2,1)S(1)}, u32[]{:S(2)}, u32[]{:S(2)}) collective-permute-start(bf16[256,128]{1,0:T(8,128)(2,1)S(1)} %get-tuple-element.18), channel_id=1, source_target_pairs={{0,12},{4,0},{8,4},{12,8},{1,13},{5,1},{9,5},{13,9},{2,14},{6,2},{... | collective-permute-start | bytes 196616 | tf_op jit(solution)/shard_map/ppermute | solution.py:75
  31.9 6.1 %collective-permute-start.3 = (bf16[256,128]{1,0:T(8,128)(2,1)S(1)}, bf16[256,128]{1,0:T(8,128)(2,1)S(1)}, u32[]{:S(2)}, u32[]{:S(2)}) collective-permute-start(bf16[256,128]{1,0:T(8,128)(2,1)S(1)} %get-tuple-element.12), channel_id=1, source_target_pairs={{0,4},{4,8},{8,12},{12,0},{1,5},{5,9},{9,13},{13,1},{2,6},{6,10},{... | collective-permute-start | bytes 196616 | tf_op jit(solution)/shard_map/ppermute | solution.py:75
  33.4 6.1 %collective-permute-start.4 = (bf16[256,128]{1,0:T(8,128)(2,1)S(1)}, bf16[256,128]{1,0:T(8,128)(2,1)S(1)}, u32[]{:S(2)}, u32[]{:S(2)}) collective-permute-start(bf16[256,128]{1,0:T(8,128)(2,1)S(1)} %get-tuple-element.11), channel_id=1, source_target_pairs={{0,8},{4,12},{8,0},{12,4},{1,9},{5,13},{9,1},{13,5},{2,10},{6,14},... | collective-permute-start | bytes 196616 | tf_op jit(solution)/shard_map/ppermute | solution.py:75
  34.5 5.0 %collective-permute-start.5 = (bf16[256,128]{1,0:T(8,128)(2,1)S(1)}, bf16[256,128]{1,0:T(8,128)(2,1)S(1)}, u32[]{:S(2)}, u32[]{:S(2)}) collective-permute-start(bf16[256,128]{1,0:T(8,128)(2,1)S(1)} %get-tuple-element.10), channel_id=1, source_target_pairs={{0,12},{4,0},{8,4},{12,8},{1,13},{5,1},{9,5},{13,9},{2,14},{6,2},{... | collective-permute-start | bytes 196616 | tf_op jit(solution)/shard_map/ppermute | solution.py:75
  40.3 0.7 %copy-start.4 = (f32[2048]{0:T(1024)S(1)}, f32[2048]{0:T(1024)}, u32[]{:S(2)}) copy-start(f32[2048]{0:T(1024)} %param.19) | copy-start | bytes 24580

commit v7 on v4

--- a/solution.py
+++ b/solution.py
@@ -26,13 +26,17 @@
     return (raw * envelope).astype(jnp.bfloat16)
 
 
-def toeplitz_kernel(filt_ref, x_ref, o_ref, acc_ref):
-    nb = x_ref.shape[1] // GROUP
-    fb = x_ref.shape[0]
-    block = x_ref.shape[2]
+def toeplitz_kernel(s_ref, filt_ref, z_ref, o_ref, x_ref, acc_ref):
+    nb = z_ref.shape[0]
+    fb = filt_ref.shape[1]
+    block = z_ref.shape[2]
+    s = s_ref[0]
     upper = (lax.broadcasted_iota(jnp.int32, (block, block), 1)
              >= lax.broadcasted_iota(jnp.int32, (block, block), 0))
     for g in range(fb):
+        ch = slice(g * GROUP, (g + 1) * GROUP)
+        for j in range(nb):
+            x_ref[j * GROUP:(j + 1) * GROUP, :] = z_ref[(s - j + nb) % nb, ch, :]
         acc_ref[...] = jnp.zeros(acc_ref.shape, jnp.float32)
         prev = None
         for d in range(nb):
@@ -42,29 +46,44 @@
             t = jnp.where(upper, cur, low).astype(jnp.bfloat16)
             rows = (nb - d) * GROUP
             acc_ref[d * GROUP:, :] += jnp.dot(
-                x_ref[g, :rows, :], t, preferred_element_type=jnp.float32
+                x_ref[:rows, :], t, preferred_element_type=jnp.float32
             )
             prev = cur
         for i in range(nb):
-            o_ref[i, g * GROUP:(g + 1) * GROUP, :] = (
+            o_ref[(i - s + nb) % nb, ch, :] = (
                 acc_ref[i * GROUP:(i + 1) * GROUP, :].astype(jnp.bfloat16))
 
 
-def toeplitz_conv(filt, x):
-    count, rows, block = x.shape
-    nb = rows // GROUP
+def toeplitz_conv(s, filt, z):
+    nb, chans, block = z.shape
+    count = chans // GROUP
     fb = min(FILTERS_PER_STEP, count)
     return pl.pallas_call(
         toeplitz_kernel,
-        out_shape=jax.ShapeDtypeStruct((nb, count * GROUP, block), jnp.bfloat16),
-        grid=(count // fb,),
-        in_specs=[
-            pl.BlockSpec((nb + 1, fb, block), lambda i: (0, i, 0)),
-            pl.BlockSpec((fb, rows, block), lambda i: (i, 0, 0)),
-        ],
-        out_specs=pl.BlockSpec((nb, fb * GROUP, block), lambda i: (0, i, 0)),
-        scratch_shapes=[pltpu.VMEM((rows, block), jnp.float32)],
-    )(filt, x)
+        out_shape=jax.ShapeDtypeStruct((nb, chans, block), jnp.bfloat16),
+        grid_spec=pltpu.PrefetchScalarGridSpec(
+            num_scalar_prefetch=1,
+            grid=(count // fb,),
+            in_specs=[
+                pl.BlockSpec((nb + 1, fb, block), lambda i, s_: (0, i, 0)),
+                pl.BlockSpec((nb, fb * GROUP, block), lambda i, s_: (0, i, 0)),
+            ],
+            out_specs=pl.BlockSpec((nb, fb * GROUP, block), lambda i, s_: (0, i, 0)),
+            scratch_shapes=[pltpu.VMEM((nb * GROUP, block), jnp.bfloat16),
+                            pltpu.VMEM((nb * GROUP, block), jnp.float32)],
+        ),
+    )(s, filt, z)
+
+
+def exchange(x, nb, s, ordered):
+    got = [x[0] if ordered else lax.dynamic_index_in_dim(x, s, 0, keepdims=False)]
+    for k in range(1, nb):
+        if ordered:
+            piece = x[k]
+        else:
+            piece = lax.dynamic_index_in_dim(x, (s + k) % nb, 0, keepdims=False)
+        got.append(lax.ppermute(piece, "seq", [(i, (i + k) % nb) for i in range(nb)]))
+    return jnp.stack(got)
 
 
 def per_device(
@@ -77,17 +96,19 @@
     count = width // GROUP
     sub = count // nb
     gated = (inner_gate.astype(jnp.float32) * signal.astype(jnp.float32)).astype(jnp.bfloat16)
-    gated_t = gated.T.reshape(nb, sub, GROUP, own_rows)
-    got = lax.all_to_all(gated_t, "seq", 0, 0, tiled=False)
-    x = got.transpose(1, 0, 2, 3).reshape(sub, nb * GROUP, own_rows)
+    gated_t = gated.T.reshape(nb, sub * GROUP, own_rows)
+    got = exchange(gated_t, nb, s, False)
     positions = jnp.arange(total_rows, dtype=jnp.int32).astype(jnp.float32)
     my_out = lax.dynamic_slice_in_dim(filter_out, s * sub, sub, 1)
     my_decay = lax.dynamic_slice_in_dim(decay, s * sub, sub, 0)
     filters = filter_table(positions, float(total_rows), filter_in, filter_bias, my_out, my_decay)
     lagged = filters.astype(jnp.float32).reshape(nb, own_rows, sub).transpose(0, 2, 1)
     filt = jnp.concatenate([jnp.zeros((1, sub, own_rows), jnp.float32), lagged], axis=0)
-    conv_parts = toeplitz_conv(filt, x)
-    back = lax.all_to_all(conv_parts, "seq", 0, 0, tiled=False)
+    s_arr = jnp.reshape(s, (1,)).astype(jnp.int32)
+    conv_parts = toeplitz_conv(s_arr, filt, got)
+    back = exchange(conv_parts, nb, s, True)
+    order = (s - jnp.arange(nb, dtype=jnp.int32) + nb) % nb
+    back = jnp.take(back, order, axis=0)
     conv = back.reshape(width, own_rows).T.astype(jnp.float32)
     mixed = outer_gate.astype(jnp.float32) * (conv + skip_gain[None, :] * gated.astype(jnp.float32))
     return mixed.astype(jnp.bfloat16)

time: 48.9 us -> 39.1 us (0.80)
  waiting for transfers between devices: 24.8 us -> 11.1 us
  starting transfers between devices: 9.95 us -> 12.8 us
  other arithmetic: 3.25 us -> 4.4 us
    all_to_all x2 -> x0, waiting for transfers between devices: 24.8 us -> none  [the longest x1 13.7 us: per_device(): back = lax.all_to_all(conv_parts, 'seq', 0, 0, tiled=False)]
    ppermute x0 -> x6, starting transfers between devices: none -> 12.8 us  [exchange(): lax.ppermute(piece, 'seq', [(i, (i + k) % nb) for i in range(nb)])]
    ppermute x0 -> x6, waiting for transfers between devices: none -> 11.1 us  [exchange(): lax.ppermute(piece, 'seq', [(i, (i + k) % nb) for i in range(nb)])]
    all_to_all x2 -> x0, starting transfers between devices: 9.95 us -> none  [the longest x1 6.35 us: per_device(): got = lax.all_to_all(gated_t, 'seq', 0, 0, tiled=False)]
    transpose x0 -> x1, other arithmetic: none -> 1.33 us  [per_device(): gated_t = gated.T.reshape(nb, sub * GROUP, own_rows)]
    slice x0 -> x1, local copies, waits for them, and re-layouts: none -> 1.13 us  [exchange(): x[0]]
    convert_element_type x1 -> x0, local copies, waits for them, and re-layouts: 1.01 us -> none  [per_device(): return mixed.astype(jnp.bfloat16)]
    convert_element_type x1 -> x0, other arithmetic: 0.94 us -> none  [per_device(): (inner_gate.astype(jnp.float32) * signal.astype(jnp.float32)).astype(jnp....]
  transfers between devices with their start and end apart: 2 -> 6, of which waited for: 2 -> 3; matrix products, arithmetic and copies ran while one was open for 5% -> 6% of each run, Pallas kernels for 0% -> 0%
where the time goes in v7:
time: 39.1 us; the launch traced here: 38.4 us
  starting transfers between devices  12.8 us (33%)
  waiting for transfers between devices  11.1 us (28%)
  local copies, waits for them, and re-layouts  4.72 us (12%)
  other arithmetic  4.4 us (11%)
  Pallas kernels  4.16 us (11%)
  matrix products  1.07 us (3%)
    ppermute x6, starting transfers between devices, exchange(): lax.ppermute(piece, 'seq', [(i, (i + k) % nb) for i in range(nb)])  12.8 us
    ppermute x6, waiting for transfers between devices, exchange(): lax.ppermute(piece, 'seq', [(i, (i + k) % nb) for i in range(nb)])  11.1 us
    pallas_call x1, Pallas kernels, toeplitz_conv(): pl.pallas_call(toeplitz_kernel, out_shape=jax.ShapeDtypeStruct((nb, chans...  4.16 us
    unnamed x18, local copies, waits for them, and re-layouts  2.41 us
    transpose x1, other arithmetic, per_device(): gated_t = gated.T.reshape(nb, sub * GROUP, own_rows)  1.33 us
    convert_element_type x1, other arithmetic, per_device(): return mixed.astype(jnp.bfloat16)  1.16 us
    slice x1, local copies, waits for them, and re-layouts, exchange(): x[0]  1.13 us
    another operation x2, other arithmetic, exchange(): return jnp.stack(got)  0.93 us
  transfers between devices with their start and end apart: 6, of which 3 were waited for; matrix products, arithmetic and copies ran while one was open for 6% of the time, Pallas kernels for 0%

profile of v7, /device:TPU:0, one launch (start us, length us, event | category | flops | bytes accessed | tf_op | source)
XLA Modules:
  0.0 38.4 jit_solution(17057629194056329752)
XLA Ops:
  0.0 0.0 copy-start
  0.0 1.3 %fusion.6 = bf16[2048,128]{0,1:T(8,128)(2,1)S(1)} fusion(bf16[128,2048]{1,0:T(8,128)(2,1)} %param.10, bf16[128,2048]{1,0:T(8,128)(2,1)} %param.9), kind=kLoop, calls=%fused_computation.13 | loop fusion | flops 1048576 | bytes 1572864 | tf_op jit(solution)/shard_map/transpose | solution.py:99
  1.3 0.3 copy.15
  1.7 3.1 %collective-permute-start = (bf16[512,128]{1,0:T(8,128)(2,1)S(1)}, bf16[512,128]{1,0:T(8,128)(2,1)S(1)}, u32[]{:S(2)}, u32[]{:S(2)}) collective-permute-start(bf16[512,128]{1,0:T(8,128)(2,1)S(1)} %get-tuple-element.12), channel_id=1, source_target_pairs={{0,4},{4,8},{8,12},{12,0},{1,5},{5,9},{9,13},{13,1},{2,6},{6,10},{... | collective-permute-start | bytes 393224 | tf_op jit(solution)/shard_map/ppermute | solution.py:85
  4.8 2.6 %collective-permute-start.1 = (bf16[512,128]{1,0:T(8,128)(2,1)S(1)}, bf16[512,128]{1,0:T(8,128)(2,1)S(1)}, u32[]{:S(2)}, u32[]{:S(2)}) collective-permute-start(bf16[512,128]{1,0:T(8,128)(2,1)S(1)} %get-tuple-element.11), channel_id=1, source_target_pairs={{0,8},{4,12},{8,0},{12,4},{1,9},{5,13},{9,1},{13,5},{2,10},{6,14},... | collective-permute-start | bytes 393224 | tf_op jit(solution)/shard_map/ppermute | solution.py:85
  7.4 1.3 %collective-permute-start.2 = (bf16[512,128]{1,0:T(8,128)(2,1)S(1)}, bf16[512,128]{1,0:T(8,128)(2,1)S(1)}, u32[]{:S(2)}, u32[]{:S(2)}) collective-permute-start(bf16[512,128]{1,0:T(8,128)(2,1)S(1)} %get-tuple-element.10), channel_id=1, source_target_pairs={{0,12},{4,0},{8,4},{12,8},{1,13},{5,1},{9,5},{13,9},{2,14},{6,2},{... | collective-permute-start | bytes 393224 | tf_op jit(solution)/shard_map/ppermute | solution.py:85
  8.8 0.1 broadcast_bitcast_fusion
  8.8 0.0 copy-start.7
  8.9 0.7 %copy-done.7 = f32[128]{0:T(128)S(1)} copy-done((f32[128]{0:T(128)S(1)}, f32[128]{0:T(128)}, u32[]{:S(2)}) %copy-start.7) | copy-done | bytes 536
  9.5 0.1 multiply_sqrt_fusion
  9.6 0.0 copy-start.4
  9.6 0.2 multiply_cosine_fusion
  9.8 0.0 copy-start.6
  9.8 0.5 %copy-done.4 = f32[33,64]{1,0:T(8,128)S(1)} copy-done((f32[33,64]{1,0:T(8,128)S(1)}, f32[33,64]{1,0:T(8,128)}, u32[]{:S(2)}) %copy-start.4) | copy-done | bytes 8472
  10.3 0.1 copy-done.6
  10.4 0.7 %fusion.1 = f32[512,64]{0,1:T(8,128)S(1)} fusion(f32[33,64]{1,0:T(8,128)S(1)} %copy-done.4, f32[512,16]{0,1:T(8,128)S(1)} %get-tuple-element.14, f32[512,16]{0,1:T(8,128)S(1)} %get-tuple-element.13, f32[512,1]{0,1:T(1,128)S(1)} %convert_multiply_fusion, f32[64]{0:T(128)S(1)} %copy-done.6), kind=kOutput, calls=%fused_computation.3 | convolution fusion | flops 13075456 | bytes 207360 | tf_op jit(solution)/shard_map/dot_general | solution.py:22
  11.2 0.0 copy-done
  11.2 0.3 fusion.3
  11.6 0.6 %pad_convert_fusion.filt_ref = f32[5,32,128]{2,1,0:T(8,128)} fusion(bf16[4,32,128]{2,1,0:T(8,128)(2,1)S(1)} %bitcast.46), kind=kLoop, calls=%fused_computation.27 | loop fusion | flops 20480 | bytes 114688 | tf_op jit(solution)/shard_map/concatenate | solution.py:106
  12.2 0.0 collective-permute-done
  12.2 3.8 %collective-permute-done.1 = bf16[512,128]{1,0:T(8,128)(2,1)S(1)} collective-permute-done((bf16[512,128]{1,0:T(8,128)(2,1)S(1)}, bf16[512,128]{1,0:T(8,128)(2,1)S(1)}, u32[]{:S(2)}, u32[]{:S(2)}) %collective-permute-start.1) | collective-permute-done | bytes 131104 | tf_op jit(solution)/shard_map/ppermute | solution.py:85
  16.0 0.0 collective-permute-done.2
  16.0 0.9 %pad_maximum_fusion.z_ref = bf16[4,512,128]{2,1,0:T(8,128)(2,1)} fusion(bf16[1,512,128]{2,1,0:T(8,128)(2,1)S(1)} %bitcast.49, bf16[1,512,128]{2,1,0:T(8,128)(2,1)S(1)} %bitcast.48, bf16[1,512,128]{2,1,0:T(8,128)(2,1)S(1)} %bitcast.47, bf16[1,512,128]{2,1,0:T(8,128)(2,1)S(1)} %get-tuple-element.9), kind=kLoop, calls=%fused_computation.11 | loop fusion | flops 786432 | bytes 1048576 | tf_op jit(solution)/shard_map/stack | solution.py:86
  16.9 4.2 %shard_map.82 = bf16[4,512,128]{2,1,0:T(8,128)(2,1)} custom-call(s32[1]{0:T(128)} %bitcast.s_ref, f32[5,32,128]{2,1,0:T(8,128)} %pad_convert_fusion.filt_ref, bf16[4,512,128]{2,1,0:T(8,128)(2,1)} %pad_maximum_fusion.z_ref), custom_call_target="tpu_custom_call" | custom-call | tf_op jit(solution)/shard_map/pallas_call | solution.py:61
  21.0 1.1 %fusion.18 = (bf16[1,512,128]{2,1,0:T(8,128)(2,1)S(1)}, bf16[512,128]{1,0:T(8,128)(2,1)S(1)}, bf16[512,128]{1,0:T(8,128)(2,1)S(1)}, bf16[512,128]{1,0:T(8,128)(2,1)S(1)}) fusion(bf16[4,512,128]{2,1,0:T(8,128)(2,1)} %shard_map.82), kind=kLoop, calls=%fused_computation.52 | loop fusion | bytes 1048576 | tf_op jit(solution)/shard_map/slice | solution.py:79
  22.2 3.3 %collective-permute-start.3 = (bf16[512,128]{1,0:T(8,128)(2,1)S(1)}, bf16[512,128]{1,0:T(8,128)(2,1)S(1)}, u32[]{:S(2)}, u32[]{:S(2)}) collective-permute-start(bf16[512,128]{1,0:T(8,128)(2,1)S(1)} %get-tuple-element.8), channel_id=1, source_target_pairs={{0,4},{4,8},{8,12},{12,0},{1,5},{5,9},{9,13},{13,1},{2,6},{6,10},{... | collective-permute-start | bytes 393224 | tf_op jit(solution)/shard_map/ppermute | solution.py:85
  25.5 1.6 %collective-permute-start.4 = (bf16[512,128]{1,0:T(8,128)(2,1)S(1)}, bf16[512,128]{1,0:T(8,128)(2,1)S(1)}, u32[]{:S(2)}, u32[]{:S(2)}) collective-permute-start(bf16[512,128]{1,0:T(8,128)(2,1)S(1)} %get-tuple-element.7), channel_id=1, source_target_pairs={{0,8},{4,12},{8,0},{12,4},{1,9},{5,13},{9,1},{13,5},{2,10},{6,14},... | collective-permute-start | bytes 393224 | tf_op jit(solution)/shard_map/ppermute | solution.py:85
  27.1 0.8 %collective-permute-start.5 = (bf16[512,128]{1,0:T(8,128)(2,1)S(1)}, bf16[512,128]{1,0:T(8,128)(2,1)S(1)}, u32[]{:S(2)}, u32[]{:S(2)}) collective-permute-start(bf16[512,128]{1,0:T(8,128)(2,1)S(1)} %get-tuple-element.6), channel_id=1, source_target_pairs={{0,12},{4,0},{8,4},{12,8},{1,13},{5,1},{9,5},{13,9},{2,14},{6,2},{... | collective-permute-start | bytes 393224 | tf_op jit(solution)/shard_map/ppermute | solution.py:85
  28.0 2.6 %collective-permute-done.3 = bf16[512,128]{1,0:T(8,128)(2,1)S(1)} collective-permute-done((bf16[512,128]{1,0:T(8,128)(2,1)S(1)}, bf16[512,128]{1,0:T(8,128)(2,1)S(1)}, u32[]{:S(2)}, u32[]{:S(2)}) %collective-permute-start.3) | collective-permute-done | bytes 131104 | tf_op jit(solution)/shard_map/ppermute | solution.py:85
  30.6 4.6 %collective-permute-done.4 = bf16[512,128]{1,0:T(8,128)(2,1)S(1)} collective-permute-done((bf16[512,128]{1,0:T(8,128)(2,1)S(1)}, bf16[512,128]{1,0:T(8,128)(2,1)S(1)}, u32[]{:S(2)}, u32[]{:S(2)}) %collective-permute-start.4) | collective-permute-done | bytes 131104 | tf_op jit(solution)/shard_map/ppermute | solution.py:85
  35.2 0.0 collective-permute-done.5
  35.2 0.1 pad_maximum_fusion.1
  35.3 0.0 copy-start.3
  35.3 0.0 copy-start.5
  35.3 0.6 %gather_fusion = bf16[4,512,128]{2,1,0:T(8,128)(2,1)S(1)} fusion(bf16[4,512,128]{2,1,0:T(8,128)(2,1)S(1)} %pad_maximum_fusion.1, s32[1024]{0:T(1024)S(1)} %pad_clamp_fusion), kind=kCustom, calls=%fused_computation | custom fusion | bytes 1048592 | tf_op jit(solution)/shard_map/jit(_take)/gather | solution.py:111
  36.0 0.0 copy-start.1
  36.0 0.0 copy-start.2
  36.0 0.2 copy.16
  36.2 0.1 copy-done.3
  36.4 0.0 copy-done.5
  36.4 0.7 %copy-done.1 = bf16[128,2048]{1,0:T(8,128)(2,1)S(1)} copy-done((bf16[128,2048]{1,0:T(8,128)(2,1)S(1)}, bf16[128,2048]{1,0:T(8,128)(2,1)}, u32[]{:S(2)}) %copy-start.1) | copy-done | bytes 524312
  37.1 0.2 copy-done.2
  37.2 1.2 %fusion.5 = bf16[128,2048]{1,0:T(8,128)(2,1)} fusion(bf16[128,2048]{1,0:T(8,128)(2,1)S(1)} %copy-done.3, f32[2048]{0:T(1024)S(1)} %copy-done.5, bf16[2048,128]{0,1:T(8,128)(2,1)S(1)} %copy.16, pred[2048]{0:T(1024)(128)(4,1)S(1)} %bitcast.53, bf16[128,2048]{1,0:T(8,128)(2,1)S(1)} %copy-done.1, bf16[128,2048]{1,0:T(8,128)(2,1)S(1)} %copy-done.2), kind=kLoop, calls=%fused_computation.9 | loop fusion | flops 3145728 | bytes 2631680 | tf_op jit(solution)/shard_map/convert_element_type | solution.py:114
  (9 shorter events, 0.1 us)
Async XLA Ops:
  0.0 11.2 %copy-start = (f32[64,128]{1,0:T(8,128)S(1)}, f32[64,128]{1,0:T(8,128)}, u32[]{:S(2)}) copy-start(f32[64,128]{1,0:T(8,128)} %param.13) | copy-start | bytes 98308
  1.7 10.5 %collective-permute-start = (bf16[512,128]{1,0:T(8,128)(2,1)S(1)}, bf16[512,128]{1,0:T(8,128)(2,1)S(1)}, u32[]{:S(2)}, u32[]{:S(2)}) collective-permute-start(bf16[512,128]{1,0:T(8,128)(2,1)S(1)} %get-tuple-element.12), channel_id=1, source_target_pairs={{0,4},{4,8},{8,12},{12,0},{1,5},{5,9},{9,13},{13,1},{2,6},{6,10},{... | collective-permute-start | bytes 393224 | tf_op jit(solution)/shard_map/ppermute | solution.py:85
  4.8 11.2 %collective-permute-start.1 = (bf16[512,128]{1,0:T(8,128)(2,1)S(1)}, bf16[512,128]{1,0:T(8,128)(2,1)S(1)}, u32[]{:S(2)}, u32[]{:S(2)}) collective-permute-start(bf16[512,128]{1,0:T(8,128)(2,1)S(1)} %get-tuple-element.11), channel_id=1, source_target_pairs={{0,8},{4,12},{8,0},{12,4},{1,9},{5,13},{9,1},{13,5},{2,10},{6,14},... | collective-permute-start | bytes 393224 | tf_op jit(solution)/shard_map/ppermute | solution.py:85
  7.4 8.6 %collective-permute-start.2 = (bf16[512,128]{1,0:T(8,128)(2,1)S(1)}, bf16[512,128]{1,0:T(8,128)(2,1)S(1)}, u32[]{:S(2)}, u32[]{:S(2)}) collective-permute-start(bf16[512,128]{1,0:T(8,128)(2,1)S(1)} %get-tuple-element.10), channel_id=1, source_target_pairs={{0,12},{4,0},{8,4},{12,8},{1,13},{5,1},{9,5},{13,9},{2,14},{6,2},{... | collective-permute-start | bytes 393224 | tf_op jit(solution)/shard_map/ppermute | solution.py:85
  8.8 0.7 %copy-start.7 = (f32[128]{0:T(128)S(1)}, f32[128]{0:T(128)}, u32[]{:S(2)}) copy-start(f32[128]{0:T(128)} %param.14) | copy-start | bytes 1540
  9.6 0.7 %copy-start.4 = (f32[33,64]{1,0:T(8,128)S(1)}, f32[33,64]{1,0:T(8,128)}, u32[]{:S(2)}) copy-start(f32[33,64]{1,0:T(8,128)} %param.11) | copy-start | bytes 25348
  9.8 0.7 %copy-start.6 = (f32[64]{0:T(128)S(1)}, f32[64]{0:T(128)}, u32[]{:S(2)}) copy-start(f32[64]{0:T(128)} %param.12) | copy-start | bytes 772
  22.2 8.4 %collective-permute-start.3 = (bf16[512,128]{1,0:T(8,128)(2,1)S(1)}, bf16[512,128]{1,0:T(8,128)(2,1)S(1)}, u32[]{:S(2)}, u32[]{:S(2)}) collective-permute-start(bf16[512,128]{1,0:T(8,128)(2,1)S(1)} %get-tuple-element.8), channel_id=1, source_target_pairs={{0,4},{4,8},{8,12},{12,0},{1,5},{5,9},{9,13},{13,1},{2,6},{6,10},{... | collective-permute-start | bytes 393224 | tf_op jit(solution)/shard_map/ppermute | solution.py:85
  25.5 9.7 %collective-permute-start.4 = (bf16[512,128]{1,0:T(8,128)(2,1)S(1)}, bf16[512,128]{1,0:T(8,128)(2,1)S(1)}, u32[]{:S(2)}, u32[]{:S(2)}) collective-permute-start(bf16[512,128]{1,0:T(8,128)(2,1)S(1)} %get-tuple-element.7), channel_id=1, source_target_pairs={{0,8},{4,12},{8,0},{12,4},{1,9},{5,13},{9,1},{13,5},{2,10},{6,14},... | collective-permute-start | bytes 393224 | tf_op jit(solution)/shard_map/ppermute | solution.py:85
  27.1 8.1 %collective-permute-start.5 = (bf16[512,128]{1,0:T(8,128)(2,1)S(1)}, bf16[512,128]{1,0:T(8,128)(2,1)S(1)}, u32[]{:S(2)}, u32[]{:S(2)}) collective-permute-start(bf16[512,128]{1,0:T(8,128)(2,1)S(1)} %get-tuple-element.6), channel_id=1, source_target_pairs={{0,12},{4,0},{8,4},{12,8},{1,13},{5,1},{9,5},{13,9},{2,14},{6,2},{... | collective-permute-start | bytes 393224 | tf_op jit(solution)/shard_map/ppermute | solution.py:85
  35.3 1.0 %copy-start.3 = (bf16[128,2048]{1,0:T(8,128)(2,1)S(1)}, bf16[128,2048]{1,0:T(8,128)(2,1)}, u32[]{:S(2)}) copy-start(bf16[128,2048]{1,0:T(8,128)(2,1)} %param.8) | copy-start | bytes 1572868
  35.3 1.0 %copy-start.5 = (f32[2048]{0:T(1024)S(1)}, f32[2048]{0:T(1024)}, u32[]{:S(2)}) copy-start(f32[2048]{0:T(1024)} %param.15) | copy-start | bytes 24580
  36.0 1.1 %copy-start.1 = (bf16[128,2048]{1,0:T(8,128)(2,1)S(1)}, bf16[128,2048]{1,0:T(8,128)(2,1)}, u32[]{:S(2)}) copy-start(bf16[128,2048]{1,0:T(8,128)(2,1)} %param.10) | copy-start | bytes 1572868
  36.0 1.2 %copy-start.2 = (bf16[128,2048]{1,0:T(8,128)(2,1)S(1)}, bf16[128,2048]{1,0:T(8,128)(2,1)}, u32[]{:S(2)}) copy-start(bf16[128,2048]{1,0:T(8,128)(2,1)} %param.9) | copy-start | bytes 1572868

commit v8 on v7

--- a/solution.py
+++ b/solution.py
@@ -95,7 +95,9 @@
     s = lax.axis_index("seq")
     count = width // GROUP
     sub = count // nb
-    gated = (inner_gate.astype(jnp.float32) * signal.astype(jnp.float32)).astype(jnp.bfloat16)
+    gated_f = lax.reduce_precision(
+        inner_gate.astype(jnp.float32) * signal.astype(jnp.float32), exponent_bits=8, mantissa_bits=7)
+    gated = gated_f.astype(jnp.bfloat16)
     gated_t = gated.T.reshape(nb, sub * GROUP, own_rows)
     got = exchange(gated_t, nb, s, False)
     positions = jnp.arange(total_rows, dtype=jnp.int32).astype(jnp.float32)
@@ -110,7 +112,7 @@
     order = (s - jnp.arange(nb, dtype=jnp.int32) + nb) % nb
     back = jnp.take(back, order, axis=0)
     conv = back.reshape(width, own_rows).T.astype(jnp.float32)
-    mixed = outer_gate.astype(jnp.float32) * (conv + skip_gain[None, :] * gated.astype(jnp.float32))
+    mixed = outer_gate.astype(jnp.float32) * (conv + skip_gain[None, :] * gated_f)
     return mixed.astype(jnp.bfloat16)
 
 

time: 39.1 us -> 39.1 us (level)
  no operation moved by 1% of the time
where the time goes in v8:
time: 39.1 us; the launch traced here: 38.4 us
  starting transfers between devices  12.8 us (33%)
  waiting for transfers between devices  11.1 us (28%)
  local copies, waits for them, and re-layouts  4.72 us (12%)
  other arithmetic  4.42 us (11%)
  Pallas kernels  4.16 us (11%)
  matrix products  1.07 us (3%)
    ppermute x6, starting transfers between devices, exchange(): lax.ppermute(piece, 'seq', [(i, (i + k) % nb) for i in range(nb)])  12.8 us
    ppermute x6, waiting for transfers between devices, exchange(): lax.ppermute(piece, 'seq', [(i, (i + k) % nb) for i in range(nb)])  11.1 us
    pallas_call x1, Pallas kernels, toeplitz_conv(): pl.pallas_call(toeplitz_kernel, out_shape=jax.ShapeDtypeStruct((nb, chans...  4.16 us
    unnamed x18, local copies, waits for them, and re-layouts  2.41 us
    transpose x1, other arithmetic, per_device(): gated_t = gated.T.reshape(nb, sub * GROUP, own_rows)  1.33 us
    convert_element_type x1, other arithmetic, per_device(): return mixed.astype(jnp.bfloat16)  1.18 us
    slice x1, local copies, waits for them, and re-layouts, exchange(): x[0]  1.13 us
    another operation x2, other arithmetic, exchange(): return jnp.stack(got)  0.93 us
  transfers between devices with their start and end apart: 6, of which 3 were waited for; matrix products, arithmetic and copies ran while one was open for 6% of the time, Pallas kernels for 0%

profile of v8, /device:TPU:0, one launch (start us, length us, event | category | flops | bytes accessed | tf_op | source)
XLA Modules:
  0.0 38.4 jit_solution(17367960898923518194)
XLA Ops:
  0.0 0.0 copy-start
  0.0 1.3 %fusion.7 = bf16[2048,128]{0,1:T(8,128)(2,1)S(1)} fusion(bf16[128,2048]{1,0:T(8,128)(2,1)} %param.10, bf16[128,2048]{1,0:T(8,128)(2,1)} %param.9), kind=kLoop, calls=%fused_computation.12 | loop fusion | flops 1310720 | bytes 1572864 | tf_op jit(solution)/shard_map/transpose | solution.py:101
  1.3 0.3 copy.15
  1.7 3.1 %collective-permute-start = (bf16[512,128]{1,0:T(8,128)(2,1)S(1)}, bf16[512,128]{1,0:T(8,128)(2,1)S(1)}, u32[]{:S(2)}, u32[]{:S(2)}) collective-permute-start(bf16[512,128]{1,0:T(8,128)(2,1)S(1)} %get-tuple-element.12), channel_id=1, source_target_pairs={{0,4},{4,8},{8,12},{12,0},{1,5},{5,9},{9,13},{13,1},{2,6},{6,10},{... | collective-permute-start | bytes 393224 | tf_op jit(solution)/shard_map/ppermute | solution.py:85
  4.8 2.6 %collective-permute-start.1 = (bf16[512,128]{1,0:T(8,128)(2,1)S(1)}, bf16[512,128]{1,0:T(8,128)(2,1)S(1)}, u32[]{:S(2)}, u32[]{:S(2)}) collective-permute-start(bf16[512,128]{1,0:T(8,128)(2,1)S(1)} %get-tuple-element.11), channel_id=1, source_target_pairs={{0,8},{4,12},{8,0},{12,4},{1,9},{5,13},{9,1},{13,5},{2,10},{6,14},... | collective-permute-start | bytes 393224 | tf_op jit(solution)/shard_map/ppermute | solution.py:85
  7.4 1.3 %collective-permute-start.2 = (bf16[512,128]{1,0:T(8,128)(2,1)S(1)}, bf16[512,128]{1,0:T(8,128)(2,1)S(1)}, u32[]{:S(2)}, u32[]{:S(2)}) collective-permute-start(bf16[512,128]{1,0:T(8,128)(2,1)S(1)} %get-tuple-element.10), channel_id=1, source_target_pairs={{0,12},{4,0},{8,4},{12,8},{1,13},{5,1},{9,5},{13,9},{2,14},{6,2},{... | collective-permute-start | bytes 393224 | tf_op jit(solution)/shard_map/ppermute | solution.py:85
  8.8 0.1 broadcast_bitcast_fusion
  8.8 0.0 copy-start.7
  8.9 0.7 %copy-done.7 = f32[128]{0:T(128)S(1)} copy-done((f32[128]{0:T(128)S(1)}, f32[128]{0:T(128)}, u32[]{:S(2)}) %copy-start.7) | copy-done | bytes 536
  9.5 0.1 multiply_sqrt_fusion
  9.6 0.0 copy-start.4
  9.6 0.2 multiply_cosine_fusion
  9.8 0.0 copy-start.6
  9.8 0.5 %copy-done.4 = f32[33,64]{1,0:T(8,128)S(1)} copy-done((f32[33,64]{1,0:T(8,128)S(1)}, f32[33,64]{1,0:T(8,128)}, u32[]{:S(2)}) %copy-start.4) | copy-done | bytes 8472
  10.3 0.1 copy-done.6
  10.4 0.7 %fusion.1 = f32[512,64]{0,1:T(8,128)S(1)} fusion(f32[33,64]{1,0:T(8,128)S(1)} %copy-done.4, f32[512,16]{0,1:T(8,128)S(1)} %get-tuple-element.14, f32[512,16]{0,1:T(8,128)S(1)} %get-tuple-element.13, f32[512,1]{0,1:T(1,128)S(1)} %convert_multiply_fusion, f32[64]{0:T(128)S(1)} %copy-done.6), kind=kOutput, calls=%fused_computation.3 | convolution fusion | flops 13075456 | bytes 207360 | tf_op jit(solution)/shard_map/dot_general | solution.py:22
  11.2 0.0 copy-done
  11.2 0.3 fusion.3
  11.6 0.6 %pad_convert_fusion.filt_ref = f32[5,32,128]{2,1,0:T(8,128)} fusion(bf16[4,32,128]{2,1,0:T(8,128)(2,1)S(1)} %bitcast.46), kind=kLoop, calls=%fused_computation.28 | loop fusion | flops 20480 | bytes 114688 | tf_op jit(solution)/shard_map/concatenate | solution.py:108
  12.2 0.0 collective-permute-done
  12.2 3.8 %collective-permute-done.1 = bf16[512,128]{1,0:T(8,128)(2,1)S(1)} collective-permute-done((bf16[512,128]{1,0:T(8,128)(2,1)S(1)}, bf16[512,128]{1,0:T(8,128)(2,1)S(1)}, u32[]{:S(2)}, u32[]{:S(2)}) %collective-permute-start.1) | collective-permute-done | bytes 131104 | tf_op jit(solution)/shard_map/ppermute | solution.py:85
  16.0 0.0 collective-permute-done.2
  16.0 0.9 %pad_maximum_fusion.z_ref = bf16[4,512,128]{2,1,0:T(8,128)(2,1)} fusion(bf16[1,512,128]{2,1,0:T(8,128)(2,1)S(1)} %bitcast.49, bf16[1,512,128]{2,1,0:T(8,128)(2,1)S(1)} %bitcast.48, bf16[1,512,128]{2,1,0:T(8,128)(2,1)S(1)} %bitcast.47, bf16[1,512,128]{2,1,0:T(8,128)(2,1)S(1)} %get-tuple-element.9), kind=kLoop, calls=%fused_computation.13 | loop fusion | flops 786432 | bytes 1048576 | tf_op jit(solution)/shard_map/stack | solution.py:86
  16.9 4.2 %shard_map.82 = bf16[4,512,128]{2,1,0:T(8,128)(2,1)} custom-call(s32[1]{0:T(128)} %bitcast.s_ref, f32[5,32,128]{2,1,0:T(8,128)} %pad_convert_fusion.filt_ref, bf16[4,512,128]{2,1,0:T(8,128)(2,1)} %pad_maximum_fusion.z_ref), custom_call_target="tpu_custom_call" | custom-call | tf_op jit(solution)/shard_map/pallas_call | solution.py:61
  21.0 1.1 %fusion.19 = (bf16[1,512,128]{2,1,0:T(8,128)(2,1)S(1)}, bf16[512,128]{1,0:T(8,128)(2,1)S(1)}, bf16[512,128]{1,0:T(8,128)(2,1)S(1)}, bf16[512,128]{1,0:T(8,128)(2,1)S(1)}) fusion(bf16[4,512,128]{2,1,0:T(8,128)(2,1)} %shard_map.82), kind=kLoop, calls=%fused_computation.53 | loop fusion | bytes 1048576 | tf_op jit(solution)/shard_map/slice | solution.py:79
  22.2 3.3 %collective-permute-start.3 = (bf16[512,128]{1,0:T(8,128)(2,1)S(1)}, bf16[512,128]{1,0:T(8,128)(2,1)S(1)}, u32[]{:S(2)}, u32[]{:S(2)}) collective-permute-start(bf16[512,128]{1,0:T(8,128)(2,1)S(1)} %get-tuple-element.8), channel_id=1, source_target_pairs={{0,4},{4,8},{8,12},{12,0},{1,5},{5,9},{9,13},{13,1},{2,6},{6,10},{... | collective-permute-start | bytes 393224 | tf_op jit(solution)/shard_map/ppermute | solution.py:85
  25.5 1.6 %collective-permute-start.4 = (bf16[512,128]{1,0:T(8,128)(2,1)S(1)}, bf16[512,128]{1,0:T(8,128)(2,1)S(1)}, u32[]{:S(2)}, u32[]{:S(2)}) collective-permute-start(bf16[512,128]{1,0:T(8,128)(2,1)S(1)} %get-tuple-element.7), channel_id=1, source_target_pairs={{0,8},{4,12},{8,0},{12,4},{1,9},{5,13},{9,1},{13,5},{2,10},{6,14},... | collective-permute-start | bytes 393224 | tf_op jit(solution)/shard_map/ppermute | solution.py:85
  27.1 0.8 %collective-permute-start.5 = (bf16[512,128]{1,0:T(8,128)(2,1)S(1)}, bf16[512,128]{1,0:T(8,128)(2,1)S(1)}, u32[]{:S(2)}, u32[]{:S(2)}) collective-permute-start(bf16[512,128]{1,0:T(8,128)(2,1)S(1)} %get-tuple-element.6), channel_id=1, source_target_pairs={{0,12},{4,0},{8,4},{12,8},{1,13},{5,1},{9,5},{13,9},{2,14},{6,2},{... | collective-permute-start | bytes 393224 | tf_op jit(solution)/shard_map/ppermute | solution.py:85
  28.0 2.6 %collective-permute-done.3 = bf16[512,128]{1,0:T(8,128)(2,1)S(1)} collective-permute-done((bf16[512,128]{1,0:T(8,128)(2,1)S(1)}, bf16[512,128]{1,0:T(8,128)(2,1)S(1)}, u32[]{:S(2)}, u32[]{:S(2)}) %collective-permute-start.3) | collective-permute-done | bytes 131104 | tf_op jit(solution)/shard_map/ppermute | solution.py:85
  30.6 4.6 %collective-permute-done.4 = bf16[512,128]{1,0:T(8,128)(2,1)S(1)} collective-permute-done((bf16[512,128]{1,0:T(8,128)(2,1)S(1)}, bf16[512,128]{1,0:T(8,128)(2,1)S(1)}, u32[]{:S(2)}, u32[]{:S(2)}) %collective-permute-start.4) | collective-permute-done | bytes 131104 | tf_op jit(solution)/shard_map/ppermute | solution.py:85
  35.2 0.0 collective-permute-done.5
  35.2 0.1 pad_maximum_fusion.1
  35.3 0.0 copy-start.3
  35.3 0.0 copy-start.5
  35.3 0.6 %gather_fusion = bf16[4,512,128]{2,1,0:T(8,128)(2,1)S(1)} fusion(bf16[4,512,128]{2,1,0:T(8,128)(2,1)S(1)} %pad_maximum_fusion.1, s32[1024]{0:T(1024)S(1)} %pad_clamp_fusion), kind=kCustom, calls=%fused_computation | custom fusion | bytes 1048592 | tf_op jit(solution)/shard_map/jit(_take)/gather | solution.py:113
  36.0 0.0 copy-start.1
  36.0 0.0 copy-start.2
  36.0 0.2 copy.16
  36.2 0.1 copy-done.3
  36.4 0.0 copy-done.5
  36.4 0.7 %copy-done.1 = bf16[128,2048]{1,0:T(8,128)(2,1)S(1)} copy-done((bf16[128,2048]{1,0:T(8,128)(2,1)S(1)}, bf16[128,2048]{1,0:T(8,128)(2,1)}, u32[]{:S(2)}) %copy-start.1) | copy-done | bytes 524312
  37.1 0.2 copy-done.2
  37.2 1.2 %fusion.5 = bf16[128,2048]{1,0:T(8,128)(2,1)} fusion(bf16[128,2048]{1,0:T(8,128)(2,1)S(1)} %copy-done.3, bf16[128,2048]{1,0:T(8,128)(2,1)S(1)} %copy-done.1, bf16[128,2048]{1,0:T(8,128)(2,1)S(1)} %copy-done.2, f32[2048]{0:T(1024)S(1)} %copy-done.5, bf16[2048,128]{0,1:T(8,128)(2,1)S(1)} %copy.16, pred[2048]{0:T(1024)(128)(4,1)S(1)} %bitcast.53), kind=kLoop, calls=%fused_computation.9 | loop fusion | flops 2883584 | bytes 2631680 | tf_op jit(solution)/shard_map/convert_element_type | solution.py:116
  (9 shorter events, 0.1 us)
Async XLA Ops:
  0.0 11.2 %copy-start = (f32[64,128]{1,0:T(8,128)S(1)}, f32[64,128]{1,0:T(8,128)}, u32[]{:S(2)}) copy-start(f32[64,128]{1,0:T(8,128)} %param.13) | copy-start | bytes 98308
  1.7 10.5 %collective-permute-start = (bf16[512,128]{1,0:T(8,128)(2,1)S(1)}, bf16[512,128]{1,0:T(8,128)(2,1)S(1)}, u32[]{:S(2)}, u32[]{:S(2)}) collective-permute-start(bf16[512,128]{1,0:T(8,128)(2,1)S(1)} %get-tuple-element.12), channel_id=1, source_target_pairs={{0,4},{4,8},{8,12},{12,0},{1,5},{5,9},{9,13},{13,1},{2,6},{6,10},{... | collective-permute-start | bytes 393224 | tf_op jit(solution)/shard_map/ppermute | solution.py:85
  4.8 11.2 %collective-permute-start.1 = (bf16[512,128]{1,0:T(8,128)(2,1)S(1)}, bf16[512,128]{1,0:T(8,128)(2,1)S(1)}, u32[]{:S(2)}, u32[]{:S(2)}) collective-permute-start(bf16[512,128]{1,0:T(8,128)(2,1)S(1)} %get-tuple-element.11), channel_id=1, source_target_pairs={{0,8},{4,12},{8,0},{12,4},{1,9},{5,13},{9,1},{13,5},{2,10},{6,14},... | collective-permute-start | bytes 393224 | tf_op jit(solution)/shard_map/ppermute | solution.py:85
  7.4 8.6 %collective-permute-start.2 = (bf16[512,128]{1,0:T(8,128)(2,1)S(1)}, bf16[512,128]{1,0:T(8,128)(2,1)S(1)}, u32[]{:S(2)}, u32[]{:S(2)}) collective-permute-start(bf16[512,128]{1,0:T(8,128)(2,1)S(1)} %get-tuple-element.10), channel_id=1, source_target_pairs={{0,12},{4,0},{8,4},{12,8},{1,13},{5,1},{9,5},{13,9},{2,14},{6,2},{... | collective-permute-start | bytes 393224 | tf_op jit(solution)/shard_map/ppermute | solution.py:85
  8.8 0.7 %copy-start.7 = (f32[128]{0:T(128)S(1)}, f32[128]{0:T(128)}, u32[]{:S(2)}) copy-start(f32[128]{0:T(128)} %param.14) | copy-start | bytes 1540
  9.6 0.7 %copy-start.4 = (f32[33,64]{1,0:T(8,128)S(1)}, f32[33,64]{1,0:T(8,128)}, u32[]{:S(2)}) copy-start(f32[33,64]{1,0:T(8,128)} %param.11) | copy-start | bytes 25348
  9.8 0.7 %copy-start.6 = (f32[64]{0:T(128)S(1)}, f32[64]{0:T(128)}, u32[]{:S(2)}) copy-start(f32[64]{0:T(128)} %param.12) | copy-start | bytes 772
  22.2 8.4 %collective-permute-start.3 = (bf16[512,128]{1,0:T(8,128)(2,1)S(1)}, bf16[512,128]{1,0:T(8,128)(2,1)S(1)}, u32[]{:S(2)}, u32[]{:S(2)}) collective-permute-start(bf16[512,128]{1,0:T(8,128)(2,1)S(1)} %get-tuple-element.8), channel_id=1, source_target_pairs={{0,4},{4,8},{8,12},{12,0},{1,5},{5,9},{9,13},{13,1},{2,6},{6,10},{... | collective-permute-start | bytes 393224 | tf_op jit(solution)/shard_map/ppermute | solution.py:85
  25.5 9.7 %collective-permute-start.4 = (bf16[512,128]{1,0:T(8,128)(2,1)S(1)}, bf16[512,128]{1,0:T(8,128)(2,1)S(1)}, u32[]{:S(2)}, u32[]{:S(2)}) collective-permute-start(bf16[512,128]{1,0:T(8,128)(2,1)S(1)} %get-tuple-element.7), channel_id=1, source_target_pairs={{0,8},{4,12},{8,0},{12,4},{1,9},{5,13},{9,1},{13,5},{2,10},{6,14},... | collective-permute-start | bytes 393224 | tf_op jit(solution)/shard_map/ppermute | solution.py:85
  27.1 8.1 %collective-permute-start.5 = (bf16[512,128]{1,0:T(8,128)(2,1)S(1)}, bf16[512,128]{1,0:T(8,128)(2,1)S(1)}, u32[]{:S(2)}, u32[]{:S(2)}) collective-permute-start(bf16[512,128]{1,0:T(8,128)(2,1)S(1)} %get-tuple-element.6), channel_id=1, source_target_pairs={{0,12},{4,0},{8,4},{12,8},{1,13},{5,1},{9,5},{13,9},{2,14},{6,2},{... | collective-permute-start | bytes 393224 | tf_op jit(solution)/shard_map/ppermute | solution.py:85
  35.3 1.0 %copy-start.3 = (bf16[128,2048]{1,0:T(8,128)(2,1)S(1)}, bf16[128,2048]{1,0:T(8,128)(2,1)}, u32[]{:S(2)}) copy-start(bf16[128,2048]{1,0:T(8,128)(2,1)} %param.8) | copy-start | bytes 1572868
  35.3 1.0 %copy-start.5 = (f32[2048]{0:T(1024)S(1)}, f32[2048]{0:T(1024)}, u32[]{:S(2)}) copy-start(f32[2048]{0:T(1024)} %param.15) | copy-start | bytes 24580
  36.0 1.1 %copy-start.1 = (bf16[128,2048]{1,0:T(8,128)(2,1)S(1)}, bf16[128,2048]{1,0:T(8,128)(2,1)}, u32[]{:S(2)}) copy-start(bf16[128,2048]{1,0:T(8,128)(2,1)} %param.10) | copy-start | bytes 1572868
  36.0 1.2 %copy-start.2 = (bf16[128,2048]{1,0:T(8,128)(2,1)S(1)}, bf16[128,2048]{1,0:T(8,128)(2,1)}, u32[]{:S(2)}) copy-start(bf16[128,2048]{1,0:T(8,128)(2,1)} %param.9) | copy-start | bytes 1572868

commit v9 on v8

--- a/solution.py
+++ b/solution.py
@@ -26,17 +26,20 @@
     return (raw * envelope).astype(jnp.bfloat16)
 
 
-def toeplitz_kernel(s_ref, filt_ref, z_ref, o_ref, x_ref, acc_ref):
-    nb = z_ref.shape[0]
+def toeplitz_kernel(s_ref, filt_ref, *refs):
+    nb = filt_ref.shape[0] - 1
+    z_refs, o_refs = refs[:nb], refs[nb:2 * nb]
+    x_ref, acc_ref = refs[2 * nb:]
     fb = filt_ref.shape[1]
-    block = z_ref.shape[2]
+    block = filt_ref.shape[2]
     s = s_ref[0]
     upper = (lax.broadcasted_iota(jnp.int32, (block, block), 1)
              >= lax.broadcasted_iota(jnp.int32, (block, block), 0))
     for g in range(fb):
         ch = slice(g * GROUP, (g + 1) * GROUP)
-        for j in range(nb):
-            x_ref[j * GROUP:(j + 1) * GROUP, :] = z_ref[(s - j + nb) % nb, ch, :]
+        for k in range(nb):
+            j = (s - k + nb) % nb
+            x_ref[pl.ds(pl.multiple_of(j * GROUP, GROUP), GROUP), :] = z_refs[k][ch, :]
         acc_ref[...] = jnp.zeros(acc_ref.shape, jnp.float32)
         prev = None
         for d in range(nb):
@@ -49,41 +52,38 @@
                 x_ref[:rows, :], t, preferred_element_type=jnp.float32
             )
             prev = cur
-        for i in range(nb):
-            o_ref[(i - s + nb) % nb, ch, :] = (
-                acc_ref[i * GROUP:(i + 1) * GROUP, :].astype(jnp.bfloat16))
+        for k in range(nb):
+            i = (s + k) % nb
+            o_refs[k][ch, :] = acc_ref[pl.ds(pl.multiple_of(i * GROUP, GROUP), GROUP), :].astype(
+                jnp.bfloat16)
 
 
-def toeplitz_conv(s, filt, z):
-    nb, chans, block = z.shape
+def toeplitz_conv(s, filt, pieces):
+    nb = len(pieces)
+    chans, block = pieces[0].shape
     count = chans // GROUP
     fb = min(FILTERS_PER_STEP, count)
+    piece_spec = pl.BlockSpec((fb * GROUP, block), lambda i, s_: (i, 0))
     return pl.pallas_call(
         toeplitz_kernel,
-        out_shape=jax.ShapeDtypeStruct((nb, chans, block), jnp.bfloat16),
+        out_shape=[jax.ShapeDtypeStruct((chans, block), jnp.bfloat16) for _ in range(nb)],
         grid_spec=pltpu.PrefetchScalarGridSpec(
             num_scalar_prefetch=1,
             grid=(count // fb,),
-            in_specs=[
-                pl.BlockSpec((nb + 1, fb, block), lambda i, s_: (0, i, 0)),
-                pl.BlockSpec((nb, fb * GROUP, block), lambda i, s_: (0, i, 0)),
-            ],
-            out_specs=pl.BlockSpec((nb, fb * GROUP, block), lambda i, s_: (0, i, 0)),
+            in_specs=[pl.BlockSpec((nb + 1, fb, block), lambda i, s_: (0, i, 0))]
+            + [piece_spec] * nb,
+            out_specs=[piece_spec] * nb,
             scratch_shapes=[pltpu.VMEM((nb * GROUP, block), jnp.bfloat16),
                             pltpu.VMEM((nb * GROUP, block), jnp.float32)],
         ),
-    )(s, filt, z)
+    )(s, filt, *pieces)
 
 
-def exchange(x, nb, s, ordered):
-    got = [x[0] if ordered else lax.dynamic_index_in_dim(x, s, 0, keepdims=False)]
+def exchange(pieces, nb):
+    got = [pieces[0]]
     for k in range(1, nb):
-        if ordered:
-            piece = x[k]
-        else:
-            piece = lax.dynamic_index_in_dim(x, (s + k) % nb, 0, keepdims=False)
-        got.append(lax.ppermute(piece, "seq", [(i, (i + k) % nb) for i in range(nb)]))
-    return jnp.stack(got)
+        got.append(lax.ppermute(pieces[k], "seq", [(i, (i + k) % nb) for i in range(nb)]))
+    return got
 
 
 def per_device(
@@ -99,7 +99,8 @@
         inner_gate.astype(jnp.float32) * signal.astype(jnp.float32), exponent_bits=8, mantissa_bits=7)
     gated = gated_f.astype(jnp.bfloat16)
     gated_t = gated.T.reshape(nb, sub * GROUP, own_rows)
-    got = exchange(gated_t, nb, s, False)
+    got = exchange(
+        [lax.dynamic_index_in_dim(gated_t, (s + k) % nb, 0, keepdims=False) for k in range(nb)], nb)
     positions = jnp.arange(total_rows, dtype=jnp.int32).astype(jnp.float32)
     my_out = lax.dynamic_slice_in_dim(filter_out, s * sub, sub, 1)
     my_decay = lax.dynamic_slice_in_dim(decay, s * sub, sub, 0)
@@ -108,7 +109,7 @@
     filt = jnp.concatenate([jnp.zeros((1, sub, own_rows), jnp.float32), lagged], axis=0)
     s_arr = jnp.reshape(s, (1,)).astype(jnp.int32)
     conv_parts = toeplitz_conv(s_arr, filt, got)
-    back = exchange(conv_parts, nb, s, True)
+    back = jnp.stack(exchange(conv_parts, nb))
     order = (s - jnp.arange(nb, dtype=jnp.int32) + nb) % nb
     back = jnp.take(back, order, axis=0)
     conv = back.reshape(width, own_rows).T.astype(jnp.float32)

time: 39.1 us -> 42.6 us (1.090)
  waiting for transfers between devices: 11.1 us -> 15.5 us
  starting transfers between devices: 12.8 us -> 12 us
    ppermute x6, waiting for transfers between devices: 11.1 us -> 15.5 us  [exchange(): lax.ppermute(pieces[k], 'seq', [(i, (i + k) % nb) for i in range(nb)])]
    slice x1 -> x0, local copies, waits for them, and re-layouts: 1.13 us -> none  [exchange(): x[0]]
    ppermute x6, starting transfers between devices: 12.8 us -> 12 us  [exchange(): lax.ppermute(pieces[k], 'seq', [(i, (i + k) % nb) for i in range(nb)])]
    unnamed x18 -> x24, local copies, waits for them, and re-layouts: 2.41 us -> 3.11 us
    squeeze x0 -> x1, local copies, waits for them, and re-layouts: none -> 0.7 us  [per_device(): lax.dynamic_index_in_dim(gated_t, (s + k) % nb, 0, keepdims=False)]
    another operation x2 -> x1, other arithmetic: 0.93 us -> 0.97 us  [per_device(): back = jnp.stack(exchange(conv_parts, nb))]
  transfers between devices with their start and end apart: 6 -> 6, of which waited for: 3 -> 4; matrix products, arithmetic and copies ran while one was open for 6% -> 5% of each run, Pallas kernels for 0% -> 0%
where the time goes in v9:
time: 42.6 us; the launch traced here: 42.1 us
  waiting for transfers between devices  15.5 us (36%)
  starting transfers between devices  12 us (28%)
  local copies, waits for them, and re-layouts  4.95 us (12%)
  other arithmetic  4.46 us (10%)
  Pallas kernels  4 us (9%)
  matrix products  1.07 us (3%)
    ppermute x6, waiting for transfers between devices, exchange(): lax.ppermute(pieces[k], 'seq', [(i, (i + k) % nb) for i in range(nb)])  15.5 us
    ppermute x6, starting transfers between devices, exchange(): lax.ppermute(pieces[k], 'seq', [(i, (i + k) % nb) for i in range(nb)])  12 us
    pallas_call x1, Pallas kernels, toeplitz_conv(): pl.pallas_call(toeplitz_kernel, out_shape=[jax.ShapeDtypeStruct((chans, b...  4 us
    unnamed x24, local copies, waits for them, and re-layouts  3.11 us
    transpose x1, other arithmetic, per_device(): gated_t = gated.T.reshape(nb, sub * GROUP, own_rows)  1.33 us
    convert_element_type x1, other arithmetic, per_device(): return mixed.astype(jnp.bfloat16)  1.18 us
    another operation x1, other arithmetic, per_device(): back = jnp.stack(exchange(conv_parts, nb))  0.97 us
    gather x2, local copies, waits for them, and re-layouts, per_device(): back = jnp.take(back, order, axis=0)  0.86 us
  transfers between devices with their start and end apart: 6, of which 4 were waited for; matrix products, arithmetic and copies ran while one was open for 5% of the time, Pallas kernels for 0%

profile of v9, /device:TPU:0, one launch (start us, length us, event | category | flops | bytes accessed | tf_op | source)
XLA Modules:
  0.0 42.1 jit_solution(3441776918777761295)
XLA Ops:
  0.0 0.0 copy-start
  0.0 1.3 %fusion.7 = bf16[2048,128]{0,1:T(8,128)(2,1)S(1)} fusion(bf16[128,2048]{1,0:T(8,128)(2,1)} %param.10, bf16[128,2048]{1,0:T(8,128)(2,1)} %param.9), kind=kLoop, calls=%fused_computation.12 | loop fusion | flops 1310720 | bytes 1572864 | tf_op jit(solution)/shard_map/transpose | solution.py:101
  1.3 0.3 copy.26
  1.6 0.7 %dynamic-slice_bitcast_fusion = (bf16[512,128]{1,0:T(8,128)(2,1)S(1)}, bf16[512,128]{1,0:T(8,128)(2,1)S(1)}, bf16[512,128]{1,0:T(8,128)(2,1)S(1)}, bf16[512,128]{1,0:T(8,128)(2,1)}) fusion(bf16[4,512,128]{2,1,0:T(8,128)(2,1)S(1)} %bitcast.38, s32[]{:T(128)S(6)} %select_n.84, s32[]{:T(128)S(6)} %select_n.82, s32[]{:T(128)S(6)} %select_n.80, s32[]{:T(128)S(6)} %select_n.78), kind=kLoop, calls=%fused_computation.14 | loop fusion | bytes 1048592 | tf_op jit(solution)/shard_map/jit(dynamic_index_in_dim)/squeeze | solution.py:103
  2.3 3.1 %collective-permute-start = (bf16[512,128]{1,0:T(8,128)(2,1)S(1)}, bf16[512,128]{1,0:T(8,128)(2,1)S(1)}, u32[]{:S(2)}, u32[]{:S(2)}) collective-permute-start(bf16[512,128]{1,0:T(8,128)(2,1)S(1)} %get-tuple-element.15), channel_id=1, source_target_pairs={{0,4},{4,8},{8,12},{12,0},{1,5},{5,9},{9,13},{13,1},{2,6},{6,10},{... | collective-permute-start | bytes 393224 | tf_op jit(solution)/shard_map/ppermute | solution.py:85
  5.4 2.6 %collective-permute-start.1 = (bf16[512,128]{1,0:T(8,128)(2,1)S(1)}, bf16[512,128]{1,0:T(8,128)(2,1)S(1)}, u32[]{:S(2)}, u32[]{:S(2)}) collective-permute-start(bf16[512,128]{1,0:T(8,128)(2,1)S(1)} %get-tuple-element.14), channel_id=1, source_target_pairs={{0,8},{4,12},{8,0},{12,4},{1,9},{5,13},{9,1},{13,5},{2,10},{6,14},... | collective-permute-start | bytes 393224 | tf_op jit(solution)/shard_map/ppermute | solution.py:85
  8.0 1.3 %collective-permute-start.2 = (bf16[512,128]{1,0:T(8,128)(2,1)S(1)}, bf16[512,128]{1,0:T(8,128)(2,1)S(1)}, u32[]{:S(2)}, u32[]{:S(2)}) collective-permute-start(bf16[512,128]{1,0:T(8,128)(2,1)S(1)} %get-tuple-element.13), channel_id=1, source_target_pairs={{0,12},{4,0},{8,4},{12,8},{1,13},{5,1},{9,5},{13,9},{2,14},{6,2},{... | collective-permute-start | bytes 393224 | tf_op jit(solution)/shard_map/ppermute | solution.py:85
  9.4 0.1 broadcast_bitcast_fusion
  9.4 0.0 copy-start.10
  9.4 0.7 %copy-done.10 = f32[128]{0:T(128)S(1)} copy-done((f32[128]{0:T(128)S(1)}, f32[128]{0:T(128)}, u32[]{:S(2)}) %copy-start.10) | copy-done | bytes 536
  10.1 0.1 multiply_sqrt_fusion
  10.2 0.0 copy-start.7
  10.2 0.2 multiply_cosine_fusion
  10.4 0.0 copy-start.9
  10.4 0.5 %copy-done.7 = f32[33,64]{1,0:T(8,128)S(1)} copy-done((f32[33,64]{1,0:T(8,128)S(1)}, f32[33,64]{1,0:T(8,128)}, u32[]{:S(2)}) %copy-start.7) | copy-done | bytes 8472
  10.9 0.1 copy-done.9
  11.0 0.7 %fusion.1 = f32[512,64]{0,1:T(8,128)S(1)} fusion(f32[33,64]{1,0:T(8,128)S(1)} %copy-done.7, f32[512,16]{0,1:T(8,128)S(1)} %get-tuple-element.18, f32[512,16]{0,1:T(8,128)S(1)} %get-tuple-element.17, f32[512,1]{0,1:T(1,128)S(1)} %convert_multiply_fusion, f32[64]{0:T(128)S(1)} %copy-done.9), kind=kOutput, calls=%fused_computation.3 | convolution fusion | flops 13075456 | bytes 207360 | tf_op jit(solution)/shard_map/dot_general | solution.py:22
  11.8 0.0 copy-done
  11.8 0.3 fusion.3
  12.2 0.6 %pad_convert_fusion.filt_ref = f32[5,32,128]{2,1,0:T(8,128)} fusion(bf16[4,32,128]{2,1,0:T(8,128)(2,1)S(1)} %bitcast.40), kind=kLoop, calls=%fused_computation.25 | loop fusion | flops 20480 | bytes 114688 | tf_op jit(solution)/shard_map/concatenate | solution.py:109
  12.8 0.0 collective-permute-done.refs_1_
  12.8 0.0 copy-start.4
  12.8 3.8 %collective-permute-done.1.refs_2_ = bf16[512,128]{1,0:T(8,128)(2,1)S(1)} collective-permute-done((bf16[512,128]{1,0:T(8,128)(2,1)S(1)}, bf16[512,128]{1,0:T(8,128)(2,1)S(1)}, u32[]{:S(2)}, u32[]{:S(2)}) %collective-permute-start.1) | collective-permute-done | bytes 131104 | tf_op jit(solution)/shard_map/ppermute | solution.py:85
  16.6 0.0 copy-start.5
  16.6 0.0 collective-permute-done.2.refs_3_
  16.6 0.0 copy-start.6
  16.6 0.0 copy-done.4
  16.6 0.6 %copy-done.5 = bf16[512,128]{1,0:T(8,128)(2,1)} copy-done((bf16[512,128]{1,0:T(8,128)(2,1)}, bf16[512,128]{1,0:T(8,128)(2,1)S(1)}, u32[]{:S(2)}) %copy-start.5) | copy-done | bytes 131096
  17.3 0.1 copy-done.6
  17.3 4.0 %shard_map.82 = (bf16[512,128]{1,0:T(8,128)(2,1)}, bf16[512,128]{1,0:T(8,128)(2,1)}, bf16[512,128]{1,0:T(8,128)(2,1)}, bf16[512,128]{1,0:T(8,128)(2,1)}) custom-call(s32[1]{0:T(128)} %bitcast.s_ref, f32[5,32,128]{2,1,0:T(8,128)} %pad_convert_fusion.filt_ref, bf16[512,128]{1,0:T(8,128)(2,1)} %get-tuple-element.16.refs_0_, bf16[512,128]{1,0:T(8,128)(2,1)} %copy-done.4, ...), custom_call_target="tpu_custom_call" | custom-call | tf_op jit(solution)/shard_map/pallas_call | solution.py:67
  21.3 4.4 %collective-permute-start.5 = (bf16[512,128]{1,0:T(8,128)(2,1)}, bf16[512,128]{1,0:T(8,128)(2,1)S(1)}, u32[]{:S(2)}, u32[]{:S(2)}) collective-permute-start(bf16[512,128]{1,0:T(8,128)(2,1)} %get-tuple-element.12), channel_id=1, source_target_pairs={{0,12},{4,0},{8,4},{12,8},{1,13},{5,1},{9,5},{13,9},{2,14},{6,2},{... | collective-permute-start | bytes 393224 | tf_op jit(solution)/shard_map/ppermute | solution.py:85
  25.7 0.0 collective-permute-start.3
  25.7 0.6 %collective-permute-start.4 = (bf16[512,128]{1,0:T(8,128)(2,1)}, bf16[512,128]{1,0:T(8,128)(2,1)S(1)}, u32[]{:S(2)}, u32[]{:S(2)}) collective-permute-start(bf16[512,128]{1,0:T(8,128)(2,1)} %get-tuple-element.11), channel_id=1, source_target_pairs={{0,8},{4,12},{8,0},{12,4},{1,9},{5,13},{9,1},{13,5},{2,10},{6,14},... | collective-permute-start | bytes 393224 | tf_op jit(solution)/shard_map/ppermute | solution.py:85
  26.4 3.6 %collective-permute-done.5 = bf16[512,128]{1,0:T(8,128)(2,1)S(1)} collective-permute-done((bf16[512,128]{1,0:T(8,128)(2,1)}, bf16[512,128]{1,0:T(8,128)(2,1)S(1)}, u32[]{:S(2)}, u32[]{:S(2)}) %collective-permute-start.5) | collective-permute-done | bytes 131104 | tf_op jit(solution)/shard_map/ppermute | solution.py:85
  30.0 3.4 %collective-permute-done.3 = bf16[512,128]{1,0:T(8,128)(2,1)S(1)} collective-permute-done((bf16[512,128]{1,0:T(8,128)(2,1)}, bf16[512,128]{1,0:T(8,128)(2,1)S(1)}, u32[]{:S(2)}, u32[]{:S(2)}) %collective-permute-start.3) | collective-permute-done | bytes 131104 | tf_op jit(solution)/shard_map/ppermute | solution.py:85
  33.3 4.7 %collective-permute-done.4 = bf16[512,128]{1,0:T(8,128)(2,1)S(1)} collective-permute-done((bf16[512,128]{1,0:T(8,128)(2,1)}, bf16[512,128]{1,0:T(8,128)(2,1)S(1)}, u32[]{:S(2)}, u32[]{:S(2)}) %collective-permute-start.4) | collective-permute-done | bytes 131104 | tf_op jit(solution)/shard_map/ppermute | solution.py:85
  38.1 1.0 %pad_maximum_fusion = bf16[4,512,128]{2,1,0:T(8,128)(2,1)S(1)} fusion(bf16[1,512,128]{2,1,0:T(8,128)(2,1)S(1)} %bitcast.42, bf16[1,512,128]{2,1,0:T(8,128)(2,1)S(1)} %bitcast.44, bf16[1,512,128]{2,1,0:T(8,128)(2,1)S(1)} %bitcast.43, bf16[1,512,128]{2,1,0:T(8,128)(2,1)} %bitcast.41), kind=kLoop, calls=%fused_computation.13 | loop fusion | flops 786432 | bytes 1048576 | tf_op jit(solution)/shard_map/stack | solution.py:112
  39.0 0.0 copy-start.3
  39.0 0.0 copy-start.8
  39.1 0.6 %gather_fusion = bf16[4,512,128]{2,1,0:T(8,128)(2,1)S(1)} fusion(bf16[4,512,128]{2,1,0:T(8,128)(2,1)S(1)} %pad_maximum_fusion, s32[1024]{0:T(1024)S(1)} %pad_clamp_fusion), kind=kCustom, calls=%fused_computation | custom fusion | bytes 1048592 | tf_op jit(solution)/shard_map/jit(_take)/gather | solution.py:114
  39.7 0.0 copy-start.1
  39.7 0.0 copy-start.2
  39.7 0.2 copy.25
  40.0 0.1 copy-done.3
  40.1 0.0 copy-done.8
  40.1 0.7 %copy-done.1 = bf16[128,2048]{1,0:T(8,128)(2,1)S(1)} copy-done((bf16[128,2048]{1,0:T(8,128)(2,1)S(1)}, bf16[128,2048]{1,0:T(8,128)(2,1)}, u32[]{:S(2)}) %copy-start.1) | copy-done | bytes 524312
  40.8 0.2 copy-done.2
  41.0 1.2 %fusion.5 = bf16[128,2048]{1,0:T(8,128)(2,1)} fusion(bf16[128,2048]{1,0:T(8,128)(2,1)S(1)} %copy-done.3, bf16[128,2048]{1,0:T(8,128)(2,1)S(1)} %copy-done.1, bf16[128,2048]{1,0:T(8,128)(2,1)S(1)} %copy-done.2, f32[2048]{0:T(1024)S(1)} %copy-done.8, bf16[2048,128]{0,1:T(8,128)(2,1)S(1)} %copy.25, pred[2048]{0:T(1024)(128)(4,1)S(1)} %bitcast.45), kind=kLoop, calls=%fused_computation.9 | loop fusion | flops 2883584 | bytes 2631680 | tf_op jit(solution)/shard_map/convert_element_type | solution.py:117
  (8 shorter events, 0.1 us)
Async XLA Ops:
  0.0 11.8 %copy-start = (f32[64,128]{1,0:T(8,128)S(1)}, f32[64,128]{1,0:T(8,128)}, u32[]{:S(2)}) copy-start(f32[64,128]{1,0:T(8,128)} %param.13) | copy-start | bytes 98308
  2.3 10.5 %collective-permute-start = (bf16[512,128]{1,0:T(8,128)(2,1)S(1)}, bf16[512,128]{1,0:T(8,128)(2,1)S(1)}, u32[]{:S(2)}, u32[]{:S(2)}) collective-permute-start(bf16[512,128]{1,0:T(8,128)(2,1)S(1)} %get-tuple-element.15), channel_id=1, source_target_pairs={{0,4},{4,8},{8,12},{12,0},{1,5},{5,9},{9,13},{13,1},{2,6},{6,10},{... | collective-permute-start | bytes 393224 | tf_op jit(solution)/shard_map/ppermute | solution.py:85
  5.4 11.2 %collective-permute-start.1 = (bf16[512,128]{1,0:T(8,128)(2,1)S(1)}, bf16[512,128]{1,0:T(8,128)(2,1)S(1)}, u32[]{:S(2)}, u32[]{:S(2)}) collective-permute-start(bf16[512,128]{1,0:T(8,128)(2,1)S(1)} %get-tuple-element.14), channel_id=1, source_target_pairs={{0,8},{4,12},{8,0},{12,4},{1,9},{5,13},{9,1},{13,5},{2,10},{6,14},... | collective-permute-start | bytes 393224 | tf_op jit(solution)/shard_map/ppermute | solution.py:85
  8.0 8.6 %collective-permute-start.2 = (bf16[512,128]{1,0:T(8,128)(2,1)S(1)}, bf16[512,128]{1,0:T(8,128)(2,1)S(1)}, u32[]{:S(2)}, u32[]{:S(2)}) collective-permute-start(bf16[512,128]{1,0:T(8,128)(2,1)S(1)} %get-tuple-element.13), channel_id=1, source_target_pairs={{0,12},{4,0},{8,4},{12,8},{1,13},{5,1},{9,5},{13,9},{2,14},{6,2},{... | collective-permute-start | bytes 393224 | tf_op jit(solution)/shard_map/ppermute | solution.py:85
  9.4 0.7 %copy-start.10 = (f32[128]{0:T(128)S(1)}, f32[128]{0:T(128)}, u32[]{:S(2)}) copy-start(f32[128]{0:T(128)} %param.14) | copy-start | bytes 1540
  10.2 0.7 %copy-start.7 = (f32[33,64]{1,0:T(8,128)S(1)}, f32[33,64]{1,0:T(8,128)}, u32[]{:S(2)}) copy-start(f32[33,64]{1,0:T(8,128)} %param.11) | copy-start | bytes 25348
  10.4 0.7 %copy-start.9 = (f32[64]{0:T(128)S(1)}, f32[64]{0:T(128)}, u32[]{:S(2)}) copy-start(f32[64]{0:T(128)} %param.12) | copy-start | bytes 772
  12.8 3.8 %copy-start.4 = (bf16[512,128]{1,0:T(8,128)(2,1)}, bf16[512,128]{1,0:T(8,128)(2,1)S(1)}, u32[]{:S(2)}) copy-start(bf16[512,128]{1,0:T(8,128)(2,1)S(1)} %collective-permute-done.refs_1_) | copy-start | bytes 393220
  16.6 0.7 %copy-start.5 = (bf16[512,128]{1,0:T(8,128)(2,1)}, bf16[512,128]{1,0:T(8,128)(2,1)S(1)}, u32[]{:S(2)}) copy-start(bf16[512,128]{1,0:T(8,128)(2,1)S(1)} %collective-permute-done.1.refs_2_) | copy-start | bytes 393220
  16.6 0.7 %copy-start.6 = (bf16[512,128]{1,0:T(8,128)(2,1)}, bf16[512,128]{1,0:T(8,128)(2,1)S(1)}, u32[]{:S(2)}) copy-start(bf16[512,128]{1,0:T(8,128)(2,1)S(1)} %collective-permute-done.2.refs_3_) | copy-start | bytes 393220
  21.3 8.6 %collective-permute-start.5 = (bf16[512,128]{1,0:T(8,128)(2,1)}, bf16[512,128]{1,0:T(8,128)(2,1)S(1)}, u32[]{:S(2)}, u32[]{:S(2)}) collective-permute-start(bf16[512,128]{1,0:T(8,128)(2,1)} %get-tuple-element.12), channel_id=1, source_target_pairs={{0,12},{4,0},{8,4},{12,8},{1,13},{5,1},{9,5},{13,9},{2,14},{6,2},{... | collective-permute-start | bytes 393224 | tf_op jit(solution)/shard_map/ppermute | solution.py:85
  25.7 7.6 %collective-permute-start.3 = (bf16[512,128]{1,0:T(8,128)(2,1)}, bf16[512,128]{1,0:T(8,128)(2,1)S(1)}, u32[]{:S(2)}, u32[]{:S(2)}) collective-permute-start(bf16[512,128]{1,0:T(8,128)(2,1)} %get-tuple-element.10), channel_id=1, source_target_pairs={{0,4},{4,8},{8,12},{12,0},{1,5},{5,9},{9,13},{13,1},{2,6},{6,10},{... | collective-permute-start | bytes 393224 | tf_op jit(solution)/shard_map/ppermute | solution.py:85
  25.7 12.3 %collective-permute-start.4 = (bf16[512,128]{1,0:T(8,128)(2,1)}, bf16[512,128]{1,0:T(8,128)(2,1)S(1)}, u32[]{:S(2)}, u32[]{:S(2)}) collective-permute-start(bf16[512,128]{1,0:T(8,128)(2,1)} %get-tuple-element.11), channel_id=1, source_target_pairs={{0,8},{4,12},{8,0},{12,4},{1,9},{5,13},{9,1},{13,5},{2,10},{6,14},... | collective-permute-start | bytes 393224 | tf_op jit(solution)/shard_map/ppermute | solution.py:85
  39.0 1.0 %copy-start.3 = (bf16[128,2048]{1,0:T(8,128)(2,1)S(1)}, bf16[128,2048]{1,0:T(8,128)(2,1)}, u32[]{:S(2)}) copy-start(bf16[128,2048]{1,0:T(8,128)(2,1)} %param.8) | copy-start | bytes 1572868
  39.0 1.0 %copy-start.8 = (f32[2048]{0:T(1024)S(1)}, f32[2048]{0:T(1024)}, u32[]{:S(2)}) copy-start(f32[2048]{0:T(1024)} %param.15) | copy-start | bytes 24580
  39.7 1.1 %copy-start.1 = (bf16[128,2048]{1,0:T(8,128)(2,1)S(1)}, bf16[128,2048]{1,0:T(8,128)(2,1)}, u32[]{:S(2)}) copy-start(bf16[128,2048]{1,0:T(8,128)(2,1)} %param.10) | copy-start | bytes 1572868
  39.7 1.2 %copy-start.2 = (bf16[128,2048]{1,0:T(8,128)(2,1)S(1)}, bf16[128,2048]{1,0:T(8,128)(2,1)}, u32[]{:S(2)}) copy-start(bf16[128,2048]{1,0:T(8,128)(2,1)} %param.9) | copy-start | bytes 1572868

commit v10 on v8

--- a/solution.py
+++ b/solution.py
@@ -9,7 +9,7 @@
 
 GROUP = 16
 BANDS = 16
-FILTERS_PER_STEP = 8
+FILTERS_PER_STEP = 16
 
 
 def filter_table(positions, total, filter_in, filter_bias, filter_out, decay):

time: 39.1 us -> 38.2 us (0.977)
  Pallas kernels: 4.16 us -> 3.27 us
    pallas_call x1, Pallas kernels: 4.16 us -> 3.27 us  [toeplitz_conv(): pl.pallas_call(toeplitz_kernel, out_shape=jax.ShapeDtypeStruct((nb, chans...]
where the time goes in v10:
time: 38.2 us; the launch traced here: 37.5 us
  starting transfers between devices  12.8 us (34%)
  waiting for transfers between devices  11.1 us (29%)
  local copies, waits for them, and re-layouts  4.72 us (12%)
  other arithmetic  4.42 us (12%)
  Pallas kernels  3.27 us (9%)
  matrix products  1.07 us (3%)
    ppermute x6, starting transfers between devices, exchange(): lax.ppermute(piece, 'seq', [(i, (i + k) % nb) for i in range(nb)])  12.8 us
    ppermute x6, waiting for transfers between devices, exchange(): lax.ppermute(piece, 'seq', [(i, (i + k) % nb) for i in range(nb)])  11.1 us
    pallas_call x1, Pallas kernels, toeplitz_conv(): pl.pallas_call(toeplitz_kernel, out_shape=jax.ShapeDtypeStruct((nb, chans...  3.27 us
    unnamed x18, local copies, waits for them, and re-layouts  2.41 us
    transpose x1, other arithmetic, per_device(): gated_t = gated.T.reshape(nb, sub * GROUP, own_rows)  1.33 us
    convert_element_type x1, other arithmetic, per_device(): return mixed.astype(jnp.bfloat16)  1.18 us
    slice x1, local copies, waits for them, and re-layouts, exchange(): x[0]  1.13 us
    another operation x2, other arithmetic, exchange(): return jnp.stack(got)  0.93 us
  transfers between devices with their start and end apart: 6, of which 3 were waited for; matrix products, arithmetic and copies ran while one was open for 6% of the time, Pallas kernels for 0%

profile of v10, /device:TPU:0, one launch (start us, length us, event | category | flops | bytes accessed | tf_op | source)
XLA Modules:
  0.0 37.5 jit_solution(4176439410170732759)
XLA Ops:
  0.0 0.0 copy-start
  0.0 1.3 %fusion.7 = bf16[2048,128]{0,1:T(8,128)(2,1)S(1)} fusion(bf16[128,2048]{1,0:T(8,128)(2,1)} %param.10, bf16[128,2048]{1,0:T(8,128)(2,1)} %param.9), kind=kLoop, calls=%fused_computation.12 | loop fusion | flops 1310720 | bytes 1572864 | tf_op jit(solution)/shard_map/transpose | solution.py:101
  1.3 0.3 copy.15
  1.7 3.1 %collective-permute-start = (bf16[512,128]{1,0:T(8,128)(2,1)S(1)}, bf16[512,128]{1,0:T(8,128)(2,1)S(1)}, u32[]{:S(2)}, u32[]{:S(2)}) collective-permute-start(bf16[512,128]{1,0:T(8,128)(2,1)S(1)} %get-tuple-element.12), channel_id=1, source_target_pairs={{0,4},{4,8},{8,12},{12,0},{1,5},{5,9},{9,13},{13,1},{2,6},{6,10},{... | collective-permute-start | bytes 393224 | tf_op jit(solution)/shard_map/ppermute | solution.py:85
  4.8 2.6 %collective-permute-start.1 = (bf16[512,128]{1,0:T(8,128)(2,1)S(1)}, bf16[512,128]{1,0:T(8,128)(2,1)S(1)}, u32[]{:S(2)}, u32[]{:S(2)}) collective-permute-start(bf16[512,128]{1,0:T(8,128)(2,1)S(1)} %get-tuple-element.11), channel_id=1, source_target_pairs={{0,8},{4,12},{8,0},{12,4},{1,9},{5,13},{9,1},{13,5},{2,10},{6,14},... | collective-permute-start | bytes 393224 | tf_op jit(solution)/shard_map/ppermute | solution.py:85
  7.4 1.3 %collective-permute-start.2 = (bf16[512,128]{1,0:T(8,128)(2,1)S(1)}, bf16[512,128]{1,0:T(8,128)(2,1)S(1)}, u32[]{:S(2)}, u32[]{:S(2)}) collective-permute-start(bf16[512,128]{1,0:T(8,128)(2,1)S(1)} %get-tuple-element.10), channel_id=1, source_target_pairs={{0,12},{4,0},{8,4},{12,8},{1,13},{5,1},{9,5},{13,9},{2,14},{6,2},{... | collective-permute-start | bytes 393224 | tf_op jit(solution)/shard_map/ppermute | solution.py:85
  8.8 0.1 broadcast_bitcast_fusion
  8.8 0.0 copy-start.7
  8.9 0.7 %copy-done.7 = f32[128]{0:T(128)S(1)} copy-done((f32[128]{0:T(128)S(1)}, f32[128]{0:T(128)}, u32[]{:S(2)}) %copy-start.7) | copy-done | bytes 536
  9.5 0.1 multiply_sqrt_fusion
  9.6 0.0 copy-start.4
  9.6 0.2 multiply_cosine_fusion
  9.8 0.0 copy-start.6
  9.8 0.5 %copy-done.4 = f32[33,64]{1,0:T(8,128)S(1)} copy-done((f32[33,64]{1,0:T(8,128)S(1)}, f32[33,64]{1,0:T(8,128)}, u32[]{:S(2)}) %copy-start.4) | copy-done | bytes 8472
  10.3 0.1 copy-done.6
  10.4 0.7 %fusion.1 = f32[512,64]{0,1:T(8,128)S(1)} fusion(f32[33,64]{1,0:T(8,128)S(1)} %copy-done.4, f32[512,16]{0,1:T(8,128)S(1)} %get-tuple-element.14, f32[512,16]{0,1:T(8,128)S(1)} %get-tuple-element.13, f32[512,1]{0,1:T(1,128)S(1)} %convert_multiply_fusion, f32[64]{0:T(128)S(1)} %copy-done.6), kind=kOutput, calls=%fused_computation.3 | convolution fusion | flops 13075456 | bytes 207360 | tf_op jit(solution)/shard_map/dot_general | solution.py:22
  11.2 0.0 copy-done
  11.2 0.3 fusion.3
  11.6 0.6 %pad_convert_fusion.filt_ref = f32[5,32,128]{2,1,0:T(8,128)} fusion(bf16[4,32,128]{2,1,0:T(8,128)(2,1)S(1)} %bitcast.46), kind=kLoop, calls=%fused_computation.28 | loop fusion | flops 20480 | bytes 114688 | tf_op jit(solution)/shard_map/concatenate | solution.py:108
  12.2 0.0 collective-permute-done
  12.2 3.8 %collective-permute-done.1 = bf16[512,128]{1,0:T(8,128)(2,1)S(1)} collective-permute-done((bf16[512,128]{1,0:T(8,128)(2,1)S(1)}, bf16[512,128]{1,0:T(8,128)(2,1)S(1)}, u32[]{:S(2)}, u32[]{:S(2)}) %collective-permute-start.1) | collective-permute-done | bytes 131104 | tf_op jit(solution)/shard_map/ppermute | solution.py:85
  16.0 0.0 collective-permute-done.2
  16.0 0.9 %pad_maximum_fusion.z_ref = bf16[4,512,128]{2,1,0:T(8,128)(2,1)} fusion(bf16[1,512,128]{2,1,0:T(8,128)(2,1)S(1)} %bitcast.49, bf16[1,512,128]{2,1,0:T(8,128)(2,1)S(1)} %bitcast.48, bf16[1,512,128]{2,1,0:T(8,128)(2,1)S(1)} %bitcast.47, bf16[1,512,128]{2,1,0:T(8,128)(2,1)S(1)} %get-tuple-element.9), kind=kLoop, calls=%fused_computation.13 | loop fusion | flops 786432 | bytes 1048576 | tf_op jit(solution)/shard_map/stack | solution.py:86
  16.9 3.3 %shard_map.82 = bf16[4,512,128]{2,1,0:T(8,128)(2,1)} custom-call(s32[1]{0:T(128)} %bitcast.s_ref, f32[5,32,128]{2,1,0:T(8,128)} %pad_convert_fusion.filt_ref, bf16[4,512,128]{2,1,0:T(8,128)(2,1)} %pad_maximum_fusion.z_ref), custom_call_target="tpu_custom_call" | custom-call | tf_op jit(solution)/shard_map/pallas_call | solution.py:61
  20.2 1.1 %fusion.19 = (bf16[1,512,128]{2,1,0:T(8,128)(2,1)S(1)}, bf16[512,128]{1,0:T(8,128)(2,1)S(1)}, bf16[512,128]{1,0:T(8,128)(2,1)S(1)}, bf16[512,128]{1,0:T(8,128)(2,1)S(1)}) fusion(bf16[4,512,128]{2,1,0:T(8,128)(2,1)} %shard_map.82), kind=kLoop, calls=%fused_computation.53 | loop fusion | bytes 1048576 | tf_op jit(solution)/shard_map/slice | solution.py:79
  21.3 3.3 %collective-permute-start.3 = (bf16[512,128]{1,0:T(8,128)(2,1)S(1)}, bf16[512,128]{1,0:T(8,128)(2,1)S(1)}, u32[]{:S(2)}, u32[]{:S(2)}) collective-permute-start(bf16[512,128]{1,0:T(8,128)(2,1)S(1)} %get-tuple-element.8), channel_id=1, source_target_pairs={{0,4},{4,8},{8,12},{12,0},{1,5},{5,9},{9,13},{13,1},{2,6},{6,10},{... | collective-permute-start | bytes 393224 | tf_op jit(solution)/shard_map/ppermute | solution.py:85
  24.6 1.6 %collective-permute-start.4 = (bf16[512,128]{1,0:T(8,128)(2,1)S(1)}, bf16[512,128]{1,0:T(8,128)(2,1)S(1)}, u32[]{:S(2)}, u32[]{:S(2)}) collective-permute-start(bf16[512,128]{1,0:T(8,128)(2,1)S(1)} %get-tuple-element.7), channel_id=1, source_target_pairs={{0,8},{4,12},{8,0},{12,4},{1,9},{5,13},{9,1},{13,5},{2,10},{6,14},... | collective-permute-start | bytes 393224 | tf_op jit(solution)/shard_map/ppermute | solution.py:85
  26.3 0.8 %collective-permute-start.5 = (bf16[512,128]{1,0:T(8,128)(2,1)S(1)}, bf16[512,128]{1,0:T(8,128)(2,1)S(1)}, u32[]{:S(2)}, u32[]{:S(2)}) collective-permute-start(bf16[512,128]{1,0:T(8,128)(2,1)S(1)} %get-tuple-element.6), channel_id=1, source_target_pairs={{0,12},{4,0},{8,4},{12,8},{1,13},{5,1},{9,5},{13,9},{2,14},{6,2},{... | collective-permute-start | bytes 393224 | tf_op jit(solution)/shard_map/ppermute | solution.py:85
  27.1 2.6 %collective-permute-done.3 = bf16[512,128]{1,0:T(8,128)(2,1)S(1)} collective-permute-done((bf16[512,128]{1,0:T(8,128)(2,1)S(1)}, bf16[512,128]{1,0:T(8,128)(2,1)S(1)}, u32[]{:S(2)}, u32[]{:S(2)}) %collective-permute-start.3) | collective-permute-done | bytes 131104 | tf_op jit(solution)/shard_map/ppermute | solution.py:85
  29.7 4.6 %collective-permute-done.4 = bf16[512,128]{1,0:T(8,128)(2,1)S(1)} collective-permute-done((bf16[512,128]{1,0:T(8,128)(2,1)S(1)}, bf16[512,128]{1,0:T(8,128)(2,1)S(1)}, u32[]{:S(2)}, u32[]{:S(2)}) %collective-permute-start.4) | collective-permute-done | bytes 131104 | tf_op jit(solution)/shard_map/ppermute | solution.py:85
  34.4 0.0 collective-permute-done.5
  34.4 0.1 pad_maximum_fusion.1
  34.4 0.0 copy-start.3
  34.4 0.0 copy-start.5
  34.5 0.6 %gather_fusion = bf16[4,512,128]{2,1,0:T(8,128)(2,1)S(1)} fusion(bf16[4,512,128]{2,1,0:T(8,128)(2,1)S(1)} %pad_maximum_fusion.1, s32[1024]{0:T(1024)S(1)} %pad_clamp_fusion), kind=kCustom, calls=%fused_computation | custom fusion | bytes 1048592 | tf_op jit(solution)/shard_map/jit(_take)/gather | solution.py:113
  35.1 0.0 copy-start.1
  35.1 0.0 copy-start.2
  35.1 0.2 copy.16
  35.4 0.1 copy-done.3
  35.5 0.0 copy-done.5
  35.5 0.7 %copy-done.1 = bf16[128,2048]{1,0:T(8,128)(2,1)S(1)} copy-done((bf16[128,2048]{1,0:T(8,128)(2,1)S(1)}, bf16[128,2048]{1,0:T(8,128)(2,1)}, u32[]{:S(2)}) %copy-start.1) | copy-done | bytes 524312
  36.2 0.2 copy-done.2
  36.4 1.2 %fusion.5 = bf16[128,2048]{1,0:T(8,128)(2,1)} fusion(bf16[128,2048]{1,0:T(8,128)(2,1)S(1)} %copy-done.3, bf16[128,2048]{1,0:T(8,128)(2,1)S(1)} %copy-done.1, bf16[128,2048]{1,0:T(8,128)(2,1)S(1)} %copy-done.2, f32[2048]{0:T(1024)S(1)} %copy-done.5, bf16[2048,128]{0,1:T(8,128)(2,1)S(1)} %copy.16, pred[2048]{0:T(1024)(128)(4,1)S(1)} %bitcast.53), kind=kLoop, calls=%fused_computation.9 | loop fusion | flops 2883584 | bytes 2631680 | tf_op jit(solution)/shard_map/convert_element_type | solution.py:116
  (9 shorter events, 0.1 us)
Async XLA Ops:
  0.0 11.2 %copy-start = (f32[64,128]{1,0:T(8,128)S(1)}, f32[64,128]{1,0:T(8,128)}, u32[]{:S(2)}) copy-start(f32[64,128]{1,0:T(8,128)} %param.13) | copy-start | bytes 98308
  1.7 10.5 %collective-permute-start = (bf16[512,128]{1,0:T(8,128)(2,1)S(1)}, bf16[512,128]{1,0:T(8,128)(2,1)S(1)}, u32[]{:S(2)}, u32[]{:S(2)}) collective-permute-start(bf16[512,128]{1,0:T(8,128)(2,1)S(1)} %get-tuple-element.12), channel_id=1, source_target_pairs={{0,4},{4,8},{8,12},{12,0},{1,5},{5,9},{9,13},{13,1},{2,6},{6,10},{... | collective-permute-start | bytes 393224 | tf_op jit(solution)/shard_map/ppermute | solution.py:85
  4.8 11.2 %collective-permute-start.1 = (bf16[512,128]{1,0:T(8,128)(2,1)S(1)}, bf16[512,128]{1,0:T(8,128)(2,1)S(1)}, u32[]{:S(2)}, u32[]{:S(2)}) collective-permute-start(bf16[512,128]{1,0:T(8,128)(2,1)S(1)} %get-tuple-element.11), channel_id=1, source_target_pairs={{0,8},{4,12},{8,0},{12,4},{1,9},{5,13},{9,1},{13,5},{2,10},{6,14},... | collective-permute-start | bytes 393224 | tf_op jit(solution)/shard_map/ppermute | solution.py:85
  7.4 8.6 %collective-permute-start.2 = (bf16[512,128]{1,0:T(8,128)(2,1)S(1)}, bf16[512,128]{1,0:T(8,128)(2,1)S(1)}, u32[]{:S(2)}, u32[]{:S(2)}) collective-permute-start(bf16[512,128]{1,0:T(8,128)(2,1)S(1)} %get-tuple-element.10), channel_id=1, source_target_pairs={{0,12},{4,0},{8,4},{12,8},{1,13},{5,1},{9,5},{13,9},{2,14},{6,2},{... | collective-permute-start | bytes 393224 | tf_op jit(solution)/shard_map/ppermute | solution.py:85
  8.8 0.7 %copy-start.7 = (f32[128]{0:T(128)S(1)}, f32[128]{0:T(128)}, u32[]{:S(2)}) copy-start(f32[128]{0:T(128)} %param.14) | copy-start | bytes 1540
  9.6 0.7 %copy-start.4 = (f32[33,64]{1,0:T(8,128)S(1)}, f32[33,64]{1,0:T(8,128)}, u32[]{:S(2)}) copy-start(f32[33,64]{1,0:T(8,128)} %param.11) | copy-start | bytes 25348
  9.8 0.7 %copy-start.6 = (f32[64]{0:T(128)S(1)}, f32[64]{0:T(128)}, u32[]{:S(2)}) copy-start(f32[64]{0:T(128)} %param.12) | copy-start | bytes 772
  21.3 8.4 %collective-permute-start.3 = (bf16[512,128]{1,0:T(8,128)(2,1)S(1)}, bf16[512,128]{1,0:T(8,128)(2,1)S(1)}, u32[]{:S(2)}, u32[]{:S(2)}) collective-permute-start(bf16[512,128]{1,0:T(8,128)(2,1)S(1)} %get-tuple-element.8), channel_id=1, source_target_pairs={{0,4},{4,8},{8,12},{12,0},{1,5},{5,9},{9,13},{13,1},{2,6},{6,10},{... | collective-permute-start | bytes 393224 | tf_op jit(solution)/shard_map/ppermute | solution.py:85
  24.6 9.7 %collective-permute-start.4 = (bf16[512,128]{1,0:T(8,128)(2,1)S(1)}, bf16[512,128]{1,0:T(8,128)(2,1)S(1)}, u32[]{:S(2)}, u32[]{:S(2)}) collective-permute-start(bf16[512,128]{1,0:T(8,128)(2,1)S(1)} %get-tuple-element.7), channel_id=1, source_target_pairs={{0,8},{4,12},{8,0},{12,4},{1,9},{5,13},{9,1},{13,5},{2,10},{6,14},... | collective-permute-start | bytes 393224 | tf_op jit(solution)/shard_map/ppermute | solution.py:85
  26.3 8.1 %collective-permute-start.5 = (bf16[512,128]{1,0:T(8,128)(2,1)S(1)}, bf16[512,128]{1,0:T(8,128)(2,1)S(1)}, u32[]{:S(2)}, u32[]{:S(2)}) collective-permute-start(bf16[512,128]{1,0:T(8,128)(2,1)S(1)} %get-tuple-element.6), channel_id=1, source_target_pairs={{0,12},{4,0},{8,4},{12,8},{1,13},{5,1},{9,5},{13,9},{2,14},{6,2},{... | collective-permute-start | bytes 393224 | tf_op jit(solution)/shard_map/ppermute | solution.py:85
  34.4 1.0 %copy-start.3 = (bf16[128,2048]{1,0:T(8,128)(2,1)S(1)}, bf16[128,2048]{1,0:T(8,128)(2,1)}, u32[]{:S(2)}) copy-start(bf16[128,2048]{1,0:T(8,128)(2,1)} %param.8) | copy-start | bytes 1572868
  34.4 1.0 %copy-start.5 = (f32[2048]{0:T(1024)S(1)}, f32[2048]{0:T(1024)}, u32[]{:S(2)}) copy-start(f32[2048]{0:T(1024)} %param.15) | copy-start | bytes 24580
  35.1 1.1 %copy-start.1 = (bf16[128,2048]{1,0:T(8,128)(2,1)S(1)}, bf16[128,2048]{1,0:T(8,128)(2,1)}, u32[]{:S(2)}) copy-start(bf16[128,2048]{1,0:T(8,128)(2,1)} %param.10) | copy-start | bytes 1572868
  35.1 1.2 %copy-start.2 = (bf16[128,2048]{1,0:T(8,128)(2,1)S(1)}, bf16[128,2048]{1,0:T(8,128)(2,1)}, u32[]{:S(2)}) copy-start(bf16[128,2048]{1,0:T(8,128)(2,1)} %param.9) | copy-start | bytes 1572868

commit v11 on v10

--- a/solution.py
+++ b/solution.py
@@ -9,7 +9,7 @@
 
 GROUP = 16
 BANDS = 16
-FILTERS_PER_STEP = 16
+FILTERS_PER_STEP = 32
 
 
 def filter_table(positions, total, filter_in, filter_bias, filter_out, decay):

time: 38.2 us -> 38.2 us (level)
  no operation moved by 1% of the time
where the time goes in v11:
time: 38.2 us; the launch traced here: 37.5 us
  starting transfers between devices  12.8 us (34%)
  waiting for transfers between devices  11 us (29%)
  local copies, waits for them, and re-layouts  4.72 us (12%)
  other arithmetic  4.42 us (12%)
  Pallas kernels  3.27 us (9%)
  matrix products  1.07 us (3%)
    ppermute x6, starting transfers between devices, exchange(): lax.ppermute(piece, 'seq', [(i, (i + k) % nb) for i in range(nb)])  12.8 us
    ppermute x6, waiting for transfers between devices, exchange(): lax.ppermute(piece, 'seq', [(i, (i + k) % nb) for i in range(nb)])  11 us
    pallas_call x1, Pallas kernels, toeplitz_conv(): pl.pallas_call(toeplitz_kernel, out_shape=jax.ShapeDtypeStruct((nb, chans...  3.27 us
    unnamed x18, local copies, waits for them, and re-layouts  2.41 us
    transpose x1, other arithmetic, per_device(): gated_t = gated.T.reshape(nb, sub * GROUP, own_rows)  1.33 us
    convert_element_type x1, other arithmetic, per_device(): return mixed.astype(jnp.bfloat16)  1.18 us
    slice x1, local copies, waits for them, and re-layouts, exchange(): x[0]  1.13 us
    another operation x2, other arithmetic, exchange(): return jnp.stack(got)  0.93 us
  transfers between devices with their start and end apart: 6, of which 3 were waited for; matrix products, arithmetic and copies ran while one was open for 6% of the time, Pallas kernels for 0%

profile of v11, /device:TPU:0, one launch (start us, length us, event | category | flops | bytes accessed | tf_op | source)
XLA Modules:
  0.0 37.5 jit_solution(13060737740316959081)
XLA Ops:
  0.0 0.0 copy-start
  0.0 1.3 %fusion.7 = bf16[2048,128]{0,1:T(8,128)(2,1)S(1)} fusion(bf16[128,2048]{1,0:T(8,128)(2,1)} %param.10, bf16[128,2048]{1,0:T(8,128)(2,1)} %param.9), kind=kLoop, calls=%fused_computation.12 | loop fusion | flops 1310720 | bytes 1572864 | tf_op jit(solution)/shard_map/transpose | solution.py:101
  1.3 0.3 copy.15
  1.7 3.1 %collective-permute-start = (bf16[512,128]{1,0:T(8,128)(2,1)S(1)}, bf16[512,128]{1,0:T(8,128)(2,1)S(1)}, u32[]{:S(2)}, u32[]{:S(2)}) collective-permute-start(bf16[512,128]{1,0:T(8,128)(2,1)S(1)} %get-tuple-element.12), channel_id=1, source_target_pairs={{0,4},{4,8},{8,12},{12,0},{1,5},{5,9},{9,13},{13,1},{2,6},{6,10},{... | collective-permute-start | bytes 393224 | tf_op jit(solution)/shard_map/ppermute | solution.py:85
  4.8 2.6 %collective-permute-start.1 = (bf16[512,128]{1,0:T(8,128)(2,1)S(1)}, bf16[512,128]{1,0:T(8,128)(2,1)S(1)}, u32[]{:S(2)}, u32[]{:S(2)}) collective-permute-start(bf16[512,128]{1,0:T(8,128)(2,1)S(1)} %get-tuple-element.11), channel_id=1, source_target_pairs={{0,8},{4,12},{8,0},{12,4},{1,9},{5,13},{9,1},{13,5},{2,10},{6,14},... | collective-permute-start | bytes 393224 | tf_op jit(solution)/shard_map/ppermute | solution.py:85
  7.4 1.3 %collective-permute-start.2 = (bf16[512,128]{1,0:T(8,128)(2,1)S(1)}, bf16[512,128]{1,0:T(8,128)(2,1)S(1)}, u32[]{:S(2)}, u32[]{:S(2)}) collective-permute-start(bf16[512,128]{1,0:T(8,128)(2,1)S(1)} %get-tuple-element.10), channel_id=1, source_target_pairs={{0,12},{4,0},{8,4},{12,8},{1,13},{5,1},{9,5},{13,9},{2,14},{6,2},{... | collective-permute-start | bytes 393224 | tf_op jit(solution)/shard_map/ppermute | solution.py:85
  8.8 0.1 broadcast_bitcast_fusion
  8.8 0.0 copy-start.7
  8.9 0.7 %copy-done.7 = f32[128]{0:T(128)S(1)} copy-done((f32[128]{0:T(128)S(1)}, f32[128]{0:T(128)}, u32[]{:S(2)}) %copy-start.7) | copy-done | bytes 536
  9.5 0.1 multiply_sqrt_fusion
  9.6 0.0 copy-start.4
  9.6 0.2 multiply_cosine_fusion
  9.8 0.0 copy-start.6
  9.8 0.5 %copy-done.4 = f32[33,64]{1,0:T(8,128)S(1)} copy-done((f32[33,64]{1,0:T(8,128)S(1)}, f32[33,64]{1,0:T(8,128)}, u32[]{:S(2)}) %copy-start.4) | copy-done | bytes 8472
  10.3 0.1 copy-done.6
  10.4 0.7 %fusion.1 = f32[512,64]{0,1:T(8,128)S(1)} fusion(f32[33,64]{1,0:T(8,128)S(1)} %copy-done.4, f32[512,16]{0,1:T(8,128)S(1)} %get-tuple-element.14, f32[512,16]{0,1:T(8,128)S(1)} %get-tuple-element.13, f32[512,1]{0,1:T(1,128)S(1)} %convert_multiply_fusion, f32[64]{0:T(128)S(1)} %copy-done.6), kind=kOutput, calls=%fused_computation.3 | convolution fusion | flops 13075456 | bytes 207360 | tf_op jit(solution)/shard_map/dot_general | solution.py:22
  11.2 0.0 copy-done
  11.2 0.3 fusion.3
  11.6 0.6 %pad_convert_fusion.filt_ref = f32[5,32,128]{2,1,0:T(8,128)} fusion(bf16[4,32,128]{2,1,0:T(8,128)(2,1)S(1)} %bitcast.46), kind=kLoop, calls=%fused_computation.28 | loop fusion | flops 20480 | bytes 114688 | tf_op jit(solution)/shard_map/concatenate | solution.py:108
  12.2 0.0 collective-permute-done
  12.2 3.8 %collective-permute-done.1 = bf16[512,128]{1,0:T(8,128)(2,1)S(1)} collective-permute-done((bf16[512,128]{1,0:T(8,128)(2,1)S(1)}, bf16[512,128]{1,0:T(8,128)(2,1)S(1)}, u32[]{:S(2)}, u32[]{:S(2)}) %collective-permute-start.1) | collective-permute-done | bytes 131104 | tf_op jit(solution)/shard_map/ppermute | solution.py:85
  16.0 0.0 collective-permute-done.2
  16.0 0.9 %pad_maximum_fusion.z_ref = bf16[4,512,128]{2,1,0:T(8,128)(2,1)} fusion(bf16[1,512,128]{2,1,0:T(8,128)(2,1)S(1)} %bitcast.49, bf16[1,512,128]{2,1,0:T(8,128)(2,1)S(1)} %bitcast.48, bf16[1,512,128]{2,1,0:T(8,128)(2,1)S(1)} %bitcast.47, bf16[1,512,128]{2,1,0:T(8,128)(2,1)S(1)} %get-tuple-element.9), kind=kLoop, calls=%fused_computation.13 | loop fusion | flops 786432 | bytes 1048576 | tf_op jit(solution)/shard_map/stack | solution.py:86
  16.9 3.3 %shard_map.82 = bf16[4,512,128]{2,1,0:T(8,128)(2,1)} custom-call(s32[1]{0:T(128)} %bitcast.s_ref, f32[5,32,128]{2,1,0:T(8,128)} %pad_convert_fusion.filt_ref, bf16[4,512,128]{2,1,0:T(8,128)(2,1)} %pad_maximum_fusion.z_ref), custom_call_target="tpu_custom_call" | custom-call | tf_op jit(solution)/shard_map/pallas_call | solution.py:61
  20.2 1.1 %fusion.19 = (bf16[1,512,128]{2,1,0:T(8,128)(2,1)S(1)}, bf16[512,128]{1,0:T(8,128)(2,1)S(1)}, bf16[512,128]{1,0:T(8,128)(2,1)S(1)}, bf16[512,128]{1,0:T(8,128)(2,1)S(1)}) fusion(bf16[4,512,128]{2,1,0:T(8,128)(2,1)} %shard_map.82), kind=kLoop, calls=%fused_computation.53 | loop fusion | bytes 1048576 | tf_op jit(solution)/shard_map/slice | solution.py:79
  21.3 3.3 %collective-permute-start.3 = (bf16[512,128]{1,0:T(8,128)(2,1)S(1)}, bf16[512,128]{1,0:T(8,128)(2,1)S(1)}, u32[]{:S(2)}, u32[]{:S(2)}) collective-permute-start(bf16[512,128]{1,0:T(8,128)(2,1)S(1)} %get-tuple-element.8), channel_id=1, source_target_pairs={{0,4},{4,8},{8,12},{12,0},{1,5},{5,9},{9,13},{13,1},{2,6},{6,10},{... | collective-permute-start | bytes 393224 | tf_op jit(solution)/shard_map/ppermute | solution.py:85
  24.6 1.6 %collective-permute-start.4 = (bf16[512,128]{1,0:T(8,128)(2,1)S(1)}, bf16[512,128]{1,0:T(8,128)(2,1)S(1)}, u32[]{:S(2)}, u32[]{:S(2)}) collective-permute-start(bf16[512,128]{1,0:T(8,128)(2,1)S(1)} %get-tuple-element.7), channel_id=1, source_target_pairs={{0,8},{4,12},{8,0},{12,4},{1,9},{5,13},{9,1},{13,5},{2,10},{6,14},... | collective-permute-start | bytes 393224 | tf_op jit(solution)/shard_map/ppermute | solution.py:85
  26.2 0.8 %collective-permute-start.5 = (bf16[512,128]{1,0:T(8,128)(2,1)S(1)}, bf16[512,128]{1,0:T(8,128)(2,1)S(1)}, u32[]{:S(2)}, u32[]{:S(2)}) collective-permute-start(bf16[512,128]{1,0:T(8,128)(2,1)S(1)} %get-tuple-element.6), channel_id=1, source_target_pairs={{0,12},{4,0},{8,4},{12,8},{1,13},{5,1},{9,5},{13,9},{2,14},{6,2},{... | collective-permute-start | bytes 393224 | tf_op jit(solution)/shard_map/ppermute | solution.py:85
  27.1 2.6 %collective-permute-done.3 = bf16[512,128]{1,0:T(8,128)(2,1)S(1)} collective-permute-done((bf16[512,128]{1,0:T(8,128)(2,1)S(1)}, bf16[512,128]{1,0:T(8,128)(2,1)S(1)}, u32[]{:S(2)}, u32[]{:S(2)}) %collective-permute-start.3) | collective-permute-done | bytes 131104 | tf_op jit(solution)/shard_map/ppermute | solution.py:85
  29.7 4.6 %collective-permute-done.4 = bf16[512,128]{1,0:T(8,128)(2,1)S(1)} collective-permute-done((bf16[512,128]{1,0:T(8,128)(2,1)S(1)}, bf16[512,128]{1,0:T(8,128)(2,1)S(1)}, u32[]{:S(2)}, u32[]{:S(2)}) %collective-permute-start.4) | collective-permute-done | bytes 131104 | tf_op jit(solution)/shard_map/ppermute | solution.py:85
  34.3 0.0 collective-permute-done.5
  34.3 0.1 pad_maximum_fusion.1
  34.4 0.0 copy-start.3
  34.4 0.0 copy-start.5
  34.4 0.6 %gather_fusion = bf16[4,512,128]{2,1,0:T(8,128)(2,1)S(1)} fusion(bf16[4,512,128]{2,1,0:T(8,128)(2,1)S(1)} %pad_maximum_fusion.1, s32[1024]{0:T(1024)S(1)} %pad_clamp_fusion), kind=kCustom, calls=%fused_computation | custom fusion | bytes 1048592 | tf_op jit(solution)/shard_map/jit(_take)/gather | solution.py:113
  35.1 0.0 copy-start.1
  35.1 0.0 copy-start.2
  35.1 0.2 copy.16
  35.3 0.1 copy-done.3
  35.5 0.0 copy-done.5
  35.5 0.7 %copy-done.1 = bf16[128,2048]{1,0:T(8,128)(2,1)S(1)} copy-done((bf16[128,2048]{1,0:T(8,128)(2,1)S(1)}, bf16[128,2048]{1,0:T(8,128)(2,1)}, u32[]{:S(2)}) %copy-start.1) | copy-done | bytes 524312
  36.2 0.2 copy-done.2
  36.3 1.2 %fusion.5 = bf16[128,2048]{1,0:T(8,128)(2,1)} fusion(bf16[128,2048]{1,0:T(8,128)(2,1)S(1)} %copy-done.3, bf16[128,2048]{1,0:T(8,128)(2,1)S(1)} %copy-done.1, bf16[128,2048]{1,0:T(8,128)(2,1)S(1)} %copy-done.2, f32[2048]{0:T(1024)S(1)} %copy-done.5, bf16[2048,128]{0,1:T(8,128)(2,1)S(1)} %copy.16, pred[2048]{0:T(1024)(128)(4,1)S(1)} %bitcast.53), kind=kLoop, calls=%fused_computation.9 | loop fusion | flops 2883584 | bytes 2631680 | tf_op jit(solution)/shard_map/convert_element_type | solution.py:116
  (9 shorter events, 0.1 us)
Async XLA Ops:
  0.0 11.2 %copy-start = (f32[64,128]{1,0:T(8,128)S(1)}, f32[64,128]{1,0:T(8,128)}, u32[]{:S(2)}) copy-start(f32[64,128]{1,0:T(8,128)} %param.13) | copy-start | bytes 98308
  1.7 10.5 %collective-permute-start = (bf16[512,128]{1,0:T(8,128)(2,1)S(1)}, bf16[512,128]{1,0:T(8,128)(2,1)S(1)}, u32[]{:S(2)}, u32[]{:S(2)}) collective-permute-start(bf16[512,128]{1,0:T(8,128)(2,1)S(1)} %get-tuple-element.12), channel_id=1, source_target_pairs={{0,4},{4,8},{8,12},{12,0},{1,5},{5,9},{9,13},{13,1},{2,6},{6,10},{... | collective-permute-start | bytes 393224 | tf_op jit(solution)/shard_map/ppermute | solution.py:85
  4.8 11.2 %collective-permute-start.1 = (bf16[512,128]{1,0:T(8,128)(2,1)S(1)}, bf16[512,128]{1,0:T(8,128)(2,1)S(1)}, u32[]{:S(2)}, u32[]{:S(2)}) collective-permute-start(bf16[512,128]{1,0:T(8,128)(2,1)S(1)} %get-tuple-element.11), channel_id=1, source_target_pairs={{0,8},{4,12},{8,0},{12,4},{1,9},{5,13},{9,1},{13,5},{2,10},{6,14},... | collective-permute-start | bytes 393224 | tf_op jit(solution)/shard_map/ppermute | solution.py:85
  7.4 8.6 %collective-permute-start.2 = (bf16[512,128]{1,0:T(8,128)(2,1)S(1)}, bf16[512,128]{1,0:T(8,128)(2,1)S(1)}, u32[]{:S(2)}, u32[]{:S(2)}) collective-permute-start(bf16[512,128]{1,0:T(8,128)(2,1)S(1)} %get-tuple-element.10), channel_id=1, source_target_pairs={{0,12},{4,0},{8,4},{12,8},{1,13},{5,1},{9,5},{13,9},{2,14},{6,2},{... | collective-permute-start | bytes 393224 | tf_op jit(solution)/shard_map/ppermute | solution.py:85
  8.8 0.7 %copy-start.7 = (f32[128]{0:T(128)S(1)}, f32[128]{0:T(128)}, u32[]{:S(2)}) copy-start(f32[128]{0:T(128)} %param.14) | copy-start | bytes 1540
  9.6 0.7 %copy-start.4 = (f32[33,64]{1,0:T(8,128)S(1)}, f32[33,64]{1,0:T(8,128)}, u32[]{:S(2)}) copy-start(f32[33,64]{1,0:T(8,128)} %param.11) | copy-start | bytes 25348
  9.8 0.7 %copy-start.6 = (f32[64]{0:T(128)S(1)}, f32[64]{0:T(128)}, u32[]{:S(2)}) copy-start(f32[64]{0:T(128)} %param.12) | copy-start | bytes 772
  21.3 8.4 %collective-permute-start.3 = (bf16[512,128]{1,0:T(8,128)(2,1)S(1)}, bf16[512,128]{1,0:T(8,128)(2,1)S(1)}, u32[]{:S(2)}, u32[]{:S(2)}) collective-permute-start(bf16[512,128]{1,0:T(8,128)(2,1)S(1)} %get-tuple-element.8), channel_id=1, source_target_pairs={{0,4},{4,8},{8,12},{12,0},{1,5},{5,9},{9,13},{13,1},{2,6},{6,10},{... | collective-permute-start | bytes 393224 | tf_op jit(solution)/shard_map/ppermute | solution.py:85
  24.6 9.7 %collective-permute-start.4 = (bf16[512,128]{1,0:T(8,128)(2,1)S(1)}, bf16[512,128]{1,0:T(8,128)(2,1)S(1)}, u32[]{:S(2)}, u32[]{:S(2)}) collective-permute-start(bf16[512,128]{1,0:T(8,128)(2,1)S(1)} %get-tuple-element.7), channel_id=1, source_target_pairs={{0,8},{4,12},{8,0},{12,4},{1,9},{5,13},{9,1},{13,5},{2,10},{6,14},... | collective-permute-start | bytes 393224 | tf_op jit(solution)/shard_map/ppermute | solution.py:85
  26.2 8.1 %collective-permute-start.5 = (bf16[512,128]{1,0:T(8,128)(2,1)S(1)}, bf16[512,128]{1,0:T(8,128)(2,1)S(1)}, u32[]{:S(2)}, u32[]{:S(2)}) collective-permute-start(bf16[512,128]{1,0:T(8,128)(2,1)S(1)} %get-tuple-element.6), channel_id=1, source_target_pairs={{0,12},{4,0},{8,4},{12,8},{1,13},{5,1},{9,5},{13,9},{2,14},{6,2},{... | collective-permute-start | bytes 393224 | tf_op jit(solution)/shard_map/ppermute | solution.py:85
  34.4 1.0 %copy-start.3 = (bf16[128,2048]{1,0:T(8,128)(2,1)S(1)}, bf16[128,2048]{1,0:T(8,128)(2,1)}, u32[]{:S(2)}) copy-start(bf16[128,2048]{1,0:T(8,128)(2,1)} %param.8) | copy-start | bytes 1572868
  34.4 1.0 %copy-start.5 = (f32[2048]{0:T(1024)S(1)}, f32[2048]{0:T(1024)}, u32[]{:S(2)}) copy-start(f32[2048]{0:T(1024)} %param.15) | copy-start | bytes 24580
  35.1 1.1 %copy-start.1 = (bf16[128,2048]{1,0:T(8,128)(2,1)S(1)}, bf16[128,2048]{1,0:T(8,128)(2,1)}, u32[]{:S(2)}) copy-start(bf16[128,2048]{1,0:T(8,128)(2,1)} %param.10) | copy-start | bytes 1572868
  35.1 1.2 %copy-start.2 = (bf16[128,2048]{1,0:T(8,128)(2,1)S(1)}, bf16[128,2048]{1,0:T(8,128)(2,1)}, u32[]{:S(2)}) copy-start(bf16[128,2048]{1,0:T(8,128)(2,1)} %param.9) | copy-start | bytes 1572868

commit v12 on v10

--- a/solution.py
+++ b/solution.py
@@ -86,6 +86,37 @@
     return jnp.stack(got)
 
 
+def mix_kernel(s_ref, z_ref, outer_ref, inner_ref, signal_ref, skip_ref, o_ref):
+    conv = z_ref[0].astype(jnp.float32).T
+    gated = (inner_ref[...].astype(jnp.float32) * signal_ref[...].astype(jnp.float32)).astype(
+        jnp.bfloat16).astype(jnp.float32)
+    o_ref[...] = (outer_ref[...].astype(jnp.float32) * (conv + skip_ref[...] * gated)).astype(
+        jnp.bfloat16)
+
+
+def mix(s, back, outer_gate, inner_gate, signal, skip_gain):
+    nb, chunk, block = back.shape
+
+    def cols(k, s_):
+        return (0, (s_[0] - k + nb) % nb)
+
+    row_spec = pl.BlockSpec((block, chunk), cols)
+    return pl.pallas_call(
+        mix_kernel,
+        out_shape=jax.ShapeDtypeStruct(outer_gate.shape, jnp.bfloat16),
+        grid_spec=pltpu.PrefetchScalarGridSpec(
+            num_scalar_prefetch=1,
+            grid=(nb,),
+            in_specs=[
+                pl.BlockSpec((1, chunk, block), lambda k, s_: (k, 0, 0)),
+                row_spec, row_spec, row_spec,
+                pl.BlockSpec((1, chunk), cols),
+            ],
+            out_specs=row_spec,
+        ),
+    )(s, back, outer_gate, inner_gate, signal, skip_gain[None, :])
+
+
 def per_device(
     outer_gate, inner_gate, signal, filter_in, filter_bias, filter_out, decay, skip_gain
 ):
@@ -109,6 +140,8 @@
     s_arr = jnp.reshape(s, (1,)).astype(jnp.int32)
     conv_parts = toeplitz_conv(s_arr, filt, got)
     back = exchange(conv_parts, nb, s, True)
+    if (sub * GROUP) % 128 == 0:
+        return mix(s_arr, back, outer_gate, inner_gate, signal, skip_gain)
     order = (s - jnp.arange(nb, dtype=jnp.int32) + nb) % nb
     back = jnp.take(back, order, axis=0)
     conv = back.reshape(width, own_rows).T.astype(jnp.float32)

time: 38.2 us -> 39.6 us (1.037)
  Pallas kernels: 3.27 us -> 6.98 us
  local copies, waits for them, and re-layouts: 4.72 us -> 2.76 us
  other arithmetic: 4.42 us -> 3.98 us
    pallas_call x0 -> x1, Pallas kernels: none -> 3.7 us  [mix(): pl.pallas_call(mix_kernel, out_shape=jax.ShapeDtypeStruct(outer_gate.shap...]
    convert_element_type x1 -> x0, other arithmetic: 1.18 us -> none  [per_device(): return mixed.astype(jnp.bfloat16)]
    unnamed x18 -> x8, local copies, waits for them, and re-layouts: 2.41 us -> 1.31 us
    gather x2 -> x0, local copies, waits for them, and re-layouts: 0.86 us -> none  [per_device(): back = jnp.take(back, order, axis=0)]
    another operation x2, other arithmetic: 0.93 us -> 1.73 us  [exchange(): return jnp.stack(got)]
  transfers between devices with their start and end apart: 6 -> 6, of which waited for: 3 -> 3; matrix products, arithmetic and copies ran while one was open for 6% -> 5% of each run, Pallas kernels for 0% -> 0%
where the time goes in v12:
time: 39.6 us; the launch traced here: 38.9 us
  starting transfers between devices  12.8 us (32%)
  waiting for transfers between devices  11.2 us (28%)
  Pallas kernels  6.98 us (18%)
  other arithmetic  3.98 us (10%)
  local copies, waits for them, and re-layouts  2.76 us (7%)
  matrix products  1.07 us (3%)
    ppermute x6, starting transfers between devices, exchange(): lax.ppermute(piece, 'seq', [(i, (i + k) % nb) for i in range(nb)])  12.8 us
    ppermute x6, waiting for transfers between devices, exchange(): lax.ppermute(piece, 'seq', [(i, (i + k) % nb) for i in range(nb)])  11.2 us
    pallas_call x1, Pallas kernels, mix(): pl.pallas_call(mix_kernel, out_shape=jax.ShapeDtypeStruct(outer_gate.shap...  3.7 us
    pallas_call x1, Pallas kernels, toeplitz_conv(): pl.pallas_call(toeplitz_kernel, out_shape=jax.ShapeDtypeStruct((nb, chans...  3.28 us
    another operation x2, other arithmetic, exchange(): return jnp.stack(got)  1.73 us
    transpose x1, other arithmetic, per_device(): gated_t = gated.T.reshape(nb, sub * GROUP, own_rows)  1.33 us
    unnamed x8, local copies, waits for them, and re-layouts  1.31 us
    slice x1, local copies, waits for them, and re-layouts, exchange(): x[0]  1.13 us
  transfers between devices with their start and end apart: 6, of which 3 were waited for; matrix products, arithmetic and copies ran while one was open for 5% of the time, Pallas kernels for 0%

profile of v12, /device:TPU:0, one launch (start us, length us, event | category | flops | bytes accessed | tf_op | source)
XLA Modules:
  0.0 38.9 jit_solution(88872785982744807)
XLA Ops:
  0.0 0.0 copy-start
  0.0 1.3 %fusion.4 = bf16[2048,128]{0,1:T(8,128)(2,1)S(1)} fusion(bf16[128,2048]{1,0:T(8,128)(2,1)} %signal_ref.1, bf16[128,2048]{1,0:T(8,128)(2,1)} %inner_ref.1), kind=kLoop, calls=%fused_computation.7 | loop fusion | flops 1310720 | bytes 1572864 | tf_op jit(solution)/shard_map/transpose | solution.py:132
  1.3 0.3 copy.13
  1.7 3.1 %collective-permute-start = (bf16[512,128]{1,0:T(8,128)(2,1)S(1)}, bf16[512,128]{1,0:T(8,128)(2,1)S(1)}, u32[]{:S(2)}, u32[]{:S(2)}) collective-permute-start(bf16[512,128]{1,0:T(8,128)(2,1)S(1)} %get-tuple-element.12), channel_id=1, source_target_pairs={{0,4},{4,8},{8,12},{12,0},{1,5},{5,9},{9,13},{13,1},{2,6},{6,10},{... | collective-permute-start | bytes 393224 | tf_op jit(solution)/shard_map/ppermute | solution.py:85
  4.8 2.6 %collective-permute-start.1 = (bf16[512,128]{1,0:T(8,128)(2,1)S(1)}, bf16[512,128]{1,0:T(8,128)(2,1)S(1)}, u32[]{:S(2)}, u32[]{:S(2)}) collective-permute-start(bf16[512,128]{1,0:T(8,128)(2,1)S(1)} %get-tuple-element.11), channel_id=1, source_target_pairs={{0,8},{4,12},{8,0},{12,4},{1,9},{5,13},{9,1},{13,5},{2,10},{6,14},... | collective-permute-start | bytes 393224 | tf_op jit(solution)/shard_map/ppermute | solution.py:85
  7.4 1.3 %collective-permute-start.2 = (bf16[512,128]{1,0:T(8,128)(2,1)S(1)}, bf16[512,128]{1,0:T(8,128)(2,1)S(1)}, u32[]{:S(2)}, u32[]{:S(2)}) collective-permute-start(bf16[512,128]{1,0:T(8,128)(2,1)S(1)} %get-tuple-element.10), channel_id=1, source_target_pairs={{0,12},{4,0},{8,4},{12,8},{1,13},{5,1},{9,5},{13,9},{2,14},{6,2},{... | collective-permute-start | bytes 393224 | tf_op jit(solution)/shard_map/ppermute | solution.py:85
  8.8 0.0 copy-start.3
  8.8 0.6 %copy-done.3 = f32[128]{0:T(128)S(1)} copy-done((f32[128]{0:T(128)S(1)}, f32[128]{0:T(128)}, u32[]{:S(2)}) %copy-start.3) | copy-done | bytes 536
  9.4 0.1 multiply_sqrt_fusion
  9.5 0.0 copy-start.1
  9.5 0.2 multiply_cosine_fusion
  9.7 0.0 copy-start.2
  9.7 0.5 %copy-done.1 = f32[33,64]{1,0:T(8,128)S(1)} copy-done((f32[33,64]{1,0:T(8,128)S(1)}, f32[33,64]{1,0:T(8,128)}, u32[]{:S(2)}) %copy-start.1) | copy-done | bytes 8472
  10.2 0.1 copy-done.2
  10.4 0.7 %fusion.1 = f32[512,64]{0,1:T(8,128)S(1)} fusion(f32[33,64]{1,0:T(8,128)S(1)} %copy-done.1, f32[512,16]{0,1:T(8,128)S(1)} %get-tuple-element.14, f32[512,16]{0,1:T(8,128)S(1)} %get-tuple-element.13, f32[512,1]{0,1:T(1,128)S(1)} %convert_multiply_fusion, f32[64]{0:T(128)S(1)} %copy-done.2), kind=kOutput, calls=%fused_computation.2 | convolution fusion | flops 13075456 | bytes 207360 | tf_op jit(solution)/shard_map/dot_general | solution.py:22
  11.1 0.0 copy-done
  11.1 0.3 fusion.3
  11.5 0.6 %pad_convert_fusion.filt_ref = f32[5,32,128]{2,1,0:T(8,128)} fusion(bf16[4,32,128]{2,1,0:T(8,128)(2,1)S(1)} %bitcast.34), kind=kLoop, calls=%fused_computation.23 | loop fusion | flops 20480 | bytes 114688 | tf_op jit(solution)/shard_map/concatenate | solution.py:139
  12.1 0.0 collective-permute-done
  12.1 3.9 %collective-permute-done.1 = bf16[512,128]{1,0:T(8,128)(2,1)S(1)} collective-permute-done((bf16[512,128]{1,0:T(8,128)(2,1)S(1)}, bf16[512,128]{1,0:T(8,128)(2,1)S(1)}, u32[]{:S(2)}, u32[]{:S(2)}) %collective-permute-start.1) | collective-permute-done | bytes 131104 | tf_op jit(solution)/shard_map/ppermute | solution.py:85
  16.0 0.0 collective-permute-done.2
  16.0 0.9 %pad_maximum_fusion.z_ref = bf16[4,512,128]{2,1,0:T(8,128)(2,1)} fusion(bf16[1,512,128]{2,1,0:T(8,128)(2,1)S(1)} %bitcast.37, bf16[1,512,128]{2,1,0:T(8,128)(2,1)S(1)} %bitcast.36, bf16[1,512,128]{2,1,0:T(8,128)(2,1)S(1)} %bitcast.35, bf16[1,512,128]{2,1,0:T(8,128)(2,1)S(1)} %get-tuple-element.9), kind=kLoop, calls=%fused_computation.8 | loop fusion | flops 786432 | bytes 1048576 | tf_op jit(solution)/shard_map/stack | solution.py:86
  16.9 3.3 %shard_map.82 = bf16[4,512,128]{2,1,0:T(8,128)(2,1)} custom-call(s32[1]{0:T(128)} %bitcast.s_ref, f32[5,32,128]{2,1,0:T(8,128)} %pad_convert_fusion.filt_ref, bf16[4,512,128]{2,1,0:T(8,128)(2,1)} %pad_maximum_fusion.z_ref), custom_call_target="tpu_custom_call" | custom-call | tf_op jit(solution)/shard_map/pallas_call | solution.py:61
  20.2 1.1 %fusion.13 = (bf16[1,512,128]{2,1,0:T(8,128)(2,1)S(1)}, bf16[512,128]{1,0:T(8,128)(2,1)S(1)}, bf16[512,128]{1,0:T(8,128)(2,1)S(1)}, bf16[512,128]{1,0:T(8,128)(2,1)S(1)}) fusion(bf16[4,512,128]{2,1,0:T(8,128)(2,1)} %shard_map.82), kind=kLoop, calls=%fused_computation.34 | loop fusion | bytes 1048576 | tf_op jit(solution)/shard_map/slice | solution.py:79
  21.3 3.3 %collective-permute-start.3 = (bf16[512,128]{1,0:T(8,128)(2,1)S(1)}, bf16[512,128]{1,0:T(8,128)(2,1)S(1)}, u32[]{:S(2)}, u32[]{:S(2)}) collective-permute-start(bf16[512,128]{1,0:T(8,128)(2,1)S(1)} %get-tuple-element.8), channel_id=1, source_target_pairs={{0,4},{4,8},{8,12},{12,0},{1,5},{5,9},{9,13},{13,1},{2,6},{6,10},{... | collective-permute-start | bytes 393224 | tf_op jit(solution)/shard_map/ppermute | solution.py:85
  24.6 1.6 %collective-permute-start.4 = (bf16[512,128]{1,0:T(8,128)(2,1)S(1)}, bf16[512,128]{1,0:T(8,128)(2,1)S(1)}, u32[]{:S(2)}, u32[]{:S(2)}) collective-permute-start(bf16[512,128]{1,0:T(8,128)(2,1)S(1)} %get-tuple-element.7), channel_id=1, source_target_pairs={{0,8},{4,12},{8,0},{12,4},{1,9},{5,13},{9,1},{13,5},{2,10},{6,14},... | collective-permute-start | bytes 393224 | tf_op jit(solution)/shard_map/ppermute | solution.py:85
  26.3 0.8 %collective-permute-start.5 = (bf16[512,128]{1,0:T(8,128)(2,1)S(1)}, bf16[512,128]{1,0:T(8,128)(2,1)S(1)}, u32[]{:S(2)}, u32[]{:S(2)}) collective-permute-start(bf16[512,128]{1,0:T(8,128)(2,1)S(1)} %get-tuple-element.6), channel_id=1, source_target_pairs={{0,12},{4,0},{8,4},{12,8},{1,13},{5,1},{9,5},{13,9},{2,14},{6,2},{... | collective-permute-start | bytes 393224 | tf_op jit(solution)/shard_map/ppermute | solution.py:85
  27.1 2.7 %collective-permute-done.3 = bf16[512,128]{1,0:T(8,128)(2,1)S(1)} collective-permute-done((bf16[512,128]{1,0:T(8,128)(2,1)S(1)}, bf16[512,128]{1,0:T(8,128)(2,1)S(1)}, u32[]{:S(2)}, u32[]{:S(2)}) %collective-permute-start.3) | collective-permute-done | bytes 131104 | tf_op jit(solution)/shard_map/ppermute | solution.py:85
  29.7 4.6 %collective-permute-done.4 = bf16[512,128]{1,0:T(8,128)(2,1)S(1)} collective-permute-done((bf16[512,128]{1,0:T(8,128)(2,1)S(1)}, bf16[512,128]{1,0:T(8,128)(2,1)S(1)}, u32[]{:S(2)}, u32[]{:S(2)}) %collective-permute-start.4) | collective-permute-done | bytes 131104 | tf_op jit(solution)/shard_map/ppermute | solution.py:85
  34.4 0.0 collective-permute-done.5
  34.4 0.9 %pad_maximum_fusion.1.z_ref = bf16[4,512,128]{2,1,0:T(8,128)(2,1)} fusion(bf16[1,512,128]{2,1,0:T(8,128)(2,1)S(1)} %bitcast.40, bf16[1,512,128]{2,1,0:T(8,128)(2,1)S(1)} %bitcast.39, bf16[1,512,128]{2,1,0:T(8,128)(2,1)S(1)} %bitcast.38, bf16[1,512,128]{2,1,0:T(8,128)(2,1)S(1)} %get-tuple-element.5), kind=kLoop, calls=%fused_computation.9 | loop fusion | flops 786432 | bytes 1048576 | tf_op jit(solution)/shard_map/stack | solution.py:86
  35.2 3.7 %shard_map.83 = bf16[128,2048]{1,0:T(8,128)(2,1)} custom-call(s32[1]{0:T(128)} %bitcast.s_ref, bf16[4,512,128]{2,1,0:T(8,128)(2,1)} %pad_maximum_fusion.1.z_ref, bf16[128,2048]{1,0:T(8,128)(2,1)} %outer_ref.1, bf16[128,2048]{1,0:T(8,128)(2,1)} %inner_ref.1, bf16[128,2048]{1,0:T(8,128)(2,1)} %signal_ref.1, f32[1,2048]{1,0:T(1,128)} %bitcast.41), custom_call_target="tpu_custom_call" | custom-call | tf_op jit(solution)/shard_map/pallas_call | solution.py:104
  (5 shorter events, 0.1 us)
Async XLA Ops:
  0.0 11.1 %copy-start = (f32[64,128]{1,0:T(8,128)S(1)}, f32[64,128]{1,0:T(8,128)}, u32[]{:S(2)}) copy-start(f32[64,128]{1,0:T(8,128)} %param.13) | copy-start | bytes 98308
  1.7 10.4 %collective-permute-start = (bf16[512,128]{1,0:T(8,128)(2,1)S(1)}, bf16[512,128]{1,0:T(8,128)(2,1)S(1)}, u32[]{:S(2)}, u32[]{:S(2)}) collective-permute-start(bf16[512,128]{1,0:T(8,128)(2,1)S(1)} %get-tuple-element.12), channel_id=1, source_target_pairs={{0,4},{4,8},{8,12},{12,0},{1,5},{5,9},{9,13},{13,1},{2,6},{6,10},{... | collective-permute-start | bytes 393224 | tf_op jit(solution)/shard_map/ppermute | solution.py:85
  4.8 11.2 %collective-permute-start.1 = (bf16[512,128]{1,0:T(8,128)(2,1)S(1)}, bf16[512,128]{1,0:T(8,128)(2,1)S(1)}, u32[]{:S(2)}, u32[]{:S(2)}) collective-permute-start(bf16[512,128]{1,0:T(8,128)(2,1)S(1)} %get-tuple-element.11), channel_id=1, source_target_pairs={{0,8},{4,12},{8,0},{12,4},{1,9},{5,13},{9,1},{13,5},{2,10},{6,14},... | collective-permute-start | bytes 393224 | tf_op jit(solution)/shard_map/ppermute | solution.py:85
  7.4 8.6 %collective-permute-start.2 = (bf16[512,128]{1,0:T(8,128)(2,1)S(1)}, bf16[512,128]{1,0:T(8,128)(2,1)S(1)}, u32[]{:S(2)}, u32[]{:S(2)}) collective-permute-start(bf16[512,128]{1,0:T(8,128)(2,1)S(1)} %get-tuple-element.10), channel_id=1, source_target_pairs={{0,12},{4,0},{8,4},{12,8},{1,13},{5,1},{9,5},{13,9},{2,14},{6,2},{... | collective-permute-start | bytes 393224 | tf_op jit(solution)/shard_map/ppermute | solution.py:85
  8.8 0.7 %copy-start.3 = (f32[128]{0:T(128)S(1)}, f32[128]{0:T(128)}, u32[]{:S(2)}) copy-start(f32[128]{0:T(128)} %param.14) | copy-start | bytes 1540
  9.5 0.7 %copy-start.1 = (f32[33,64]{1,0:T(8,128)S(1)}, f32[33,64]{1,0:T(8,128)}, u32[]{:S(2)}) copy-start(f32[33,64]{1,0:T(8,128)} %param.11) | copy-start | bytes 25348
  9.7 0.7 %copy-start.2 = (f32[64]{0:T(128)S(1)}, f32[64]{0:T(128)}, u32[]{:S(2)}) copy-start(f32[64]{0:T(128)} %param.12) | copy-start | bytes 772
  21.3 8.4 %collective-permute-start.3 = (bf16[512,128]{1,0:T(8,128)(2,1)S(1)}, bf16[512,128]{1,0:T(8,128)(2,1)S(1)}, u32[]{:S(2)}, u32[]{:S(2)}) collective-permute-start(bf16[512,128]{1,0:T(8,128)(2,1)S(1)} %get-tuple-element.8), channel_id=1, source_target_pairs={{0,4},{4,8},{8,12},{12,0},{1,5},{5,9},{9,13},{13,1},{2,6},{6,10},{... | collective-permute-start | bytes 393224 | tf_op jit(solution)/shard_map/ppermute | solution.py:85
  24.6 9.7 %collective-permute-start.4 = (bf16[512,128]{1,0:T(8,128)(2,1)S(1)}, bf16[512,128]{1,0:T(8,128)(2,1)S(1)}, u32[]{:S(2)}, u32[]{:S(2)}) collective-permute-start(bf16[512,128]{1,0:T(8,128)(2,1)S(1)} %get-tuple-element.7), channel_id=1, source_target_pairs={{0,8},{4,12},{8,0},{12,4},{1,9},{5,13},{9,1},{13,5},{2,10},{6,14},... | collective-permute-start | bytes 393224 | tf_op jit(solution)/shard_map/ppermute | solution.py:85
  26.3 8.1 %collective-permute-start.5 = (bf16[512,128]{1,0:T(8,128)(2,1)S(1)}, bf16[512,128]{1,0:T(8,128)(2,1)S(1)}, u32[]{:S(2)}, u32[]{:S(2)}) collective-permute-start(bf16[512,128]{1,0:T(8,128)(2,1)S(1)} %get-tuple-element.6), channel_id=1, source_target_pairs={{0,12},{4,0},{8,4},{12,8},{1,13},{5,1},{9,5},{13,9},{2,14},{6,2},{... | collective-permute-start | bytes 393224 | tf_op jit(solution)/shard_map/ppermute | solution.py:85

commit v13 on v10

--- a/solution.py
+++ b/solution.py
@@ -36,7 +36,7 @@
     for g in range(fb):
         ch = slice(g * GROUP, (g + 1) * GROUP)
         for j in range(nb):
-            x_ref[j * GROUP:(j + 1) * GROUP, :] = z_ref[(s - j + nb) % nb, ch, :]
+            x_ref[j * GROUP:(j + 1) * GROUP, :] = z_ref[source(s, j, nb), ch, :]
         acc_ref[...] = jnp.zeros(acc_ref.shape, jnp.float32)
         prev = None
         for d in range(nb):
@@ -50,7 +50,7 @@
             )
             prev = cur
         for i in range(nb):
-            o_ref[(i - s + nb) % nb, ch, :] = (
+            o_ref[source(i, s, nb), ch, :] = (
                 acc_ref[i * GROUP:(i + 1) * GROUP, :].astype(jnp.bfloat16))
 
 
@@ -75,14 +75,26 @@
     )(s, filt, z)
 
 
+def partner(s, k, nb):
+    if nb & (nb - 1) == 0:
+        return s ^ k
+    return (s + k) % nb
+
+
+def source(s, k, nb):
+    if nb & (nb - 1) == 0:
+        return s ^ k
+    return (s - k + nb) % nb
+
+
 def exchange(x, nb, s, ordered):
     got = [x[0] if ordered else lax.dynamic_index_in_dim(x, s, 0, keepdims=False)]
     for k in range(1, nb):
         if ordered:
             piece = x[k]
         else:
-            piece = lax.dynamic_index_in_dim(x, (s + k) % nb, 0, keepdims=False)
-        got.append(lax.ppermute(piece, "seq", [(i, (i + k) % nb) for i in range(nb)]))
+            piece = lax.dynamic_index_in_dim(x, partner(s, k, nb), 0, keepdims=False)
+        got.append(lax.ppermute(piece, "seq", [(i, partner(i, k, nb)) for i in range(nb)]))
     return jnp.stack(got)
 
 
@@ -109,7 +121,7 @@
     s_arr = jnp.reshape(s, (1,)).astype(jnp.int32)
     conv_parts = toeplitz_conv(s_arr, filt, got)
     back = exchange(conv_parts, nb, s, True)
-    order = (s - jnp.arange(nb, dtype=jnp.int32) + nb) % nb
+    order = source(s, jnp.arange(nb, dtype=jnp.int32), nb)
     back = jnp.take(back, order, axis=0)
     conv = back.reshape(width, own_rows).T.astype(jnp.float32)
     mixed = outer_gate.astype(jnp.float32) * (conv + skip_gain[None, :] * gated_f)

time: 38.2 us -> 40.3 us (1.055)
  waiting for transfers between devices: 11.1 us -> 16.2 us
  starting transfers between devices: 12.8 us -> 10.2 us
    ppermute x6, waiting for transfers between devices: 11.1 us -> 16.2 us  [exchange(): lax.ppermute(piece, 'seq', [(i, partner(i, k, nb)) for i in range(nb)])]
    ppermute x6, starting transfers between devices: 12.8 us -> 10.2 us  [exchange(): lax.ppermute(piece, 'seq', [(i, partner(i, k, nb)) for i in range(nb)])]
  transfers between devices with their start and end apart: 6 -> 6, of which waited for: 3 -> 3; matrix products, arithmetic and copies ran while one was open for 6% -> 5% of each run, Pallas kernels for 0% -> 0%
where the time goes in v13:
time: 40.3 us; the launch traced here: 40 us
  waiting for transfers between devices  16.2 us (40%)
  starting transfers between devices  10.2 us (25%)
  local copies, waits for them, and re-layouts  4.72 us (12%)
  other arithmetic  4.4 us (11%)
  Pallas kernels  3.27 us (8%)
  matrix products  1.07 us (3%)
    ppermute x6, waiting for transfers between devices, exchange(): lax.ppermute(piece, 'seq', [(i, partner(i, k, nb)) for i in range(nb)])  16.2 us
    ppermute x6, starting transfers between devices, exchange(): lax.ppermute(piece, 'seq', [(i, partner(i, k, nb)) for i in range(nb)])  10.2 us
    pallas_call x1, Pallas kernels, toeplitz_conv(): pl.pallas_call(toeplitz_kernel, out_shape=jax.ShapeDtypeStruct((nb, chans...  3.27 us
    unnamed x18, local copies, waits for them, and re-layouts  2.41 us
    transpose x1, other arithmetic, per_device(): gated_t = gated.T.reshape(nb, sub * GROUP, own_rows)  1.33 us
    convert_element_type x1, other arithmetic, per_device(): return mixed.astype(jnp.bfloat16)  1.18 us
    slice x1, local copies, waits for them, and re-layouts, exchange(): x[0]  1.13 us
    another operation x2, other arithmetic, exchange(): return jnp.stack(got)  0.93 us
  transfers between devices with their start and end apart: 6, of which 3 were waited for; matrix products, arithmetic and copies ran while one was open for 5% of the time, Pallas kernels for 0%

profile of v13, /device:TPU:0, one launch (start us, length us, event | category | flops | bytes accessed | tf_op | source)
XLA Modules:
  0.0 40.0 jit_solution(1783922149500793603)
XLA Ops:
  0.0 0.0 copy-start
  0.0 1.3 %fusion.7 = bf16[2048,128]{0,1:T(8,128)(2,1)S(1)} fusion(bf16[128,2048]{1,0:T(8,128)(2,1)} %param.10, bf16[128,2048]{1,0:T(8,128)(2,1)} %param.9), kind=kLoop, calls=%fused_computation.12 | loop fusion | flops 1310720 | bytes 1572864 | tf_op jit(solution)/shard_map/transpose | solution.py:113
  1.3 0.3 copy.15
  1.7 3.1 %collective-permute-start = (bf16[512,128]{1,0:T(8,128)(2,1)S(1)}, bf16[512,128]{1,0:T(8,128)(2,1)S(1)}, u32[]{:S(2)}, u32[]{:S(2)}) collective-permute-start(bf16[512,128]{1,0:T(8,128)(2,1)S(1)} %get-tuple-element.12), channel_id=1, source_target_pairs={{0,4},{4,0},{8,12},{12,8},{1,5},{5,1},{9,13},{13,9},{2,6},{6,2},{1... | collective-permute-start | bytes 393224 | tf_op jit(solution)/shard_map/ppermute | solution.py:97
  4.8 2.6 %collective-permute-start.1 = (bf16[512,128]{1,0:T(8,128)(2,1)S(1)}, bf16[512,128]{1,0:T(8,128)(2,1)S(1)}, u32[]{:S(2)}, u32[]{:S(2)}) collective-permute-start(bf16[512,128]{1,0:T(8,128)(2,1)S(1)} %get-tuple-element.11), channel_id=1, source_target_pairs={{0,8},{4,12},{8,0},{12,4},{1,9},{5,13},{9,1},{13,5},{2,10},{6,14},... | collective-permute-start | bytes 393224 | tf_op jit(solution)/shard_map/ppermute | solution.py:97
  7.4 0.0 collective-permute-start.2
  7.4 0.1 broadcast_bitcast_fusion
  7.5 0.0 copy-start.7
  7.5 0.7 %copy-done.7 = f32[128]{0:T(128)S(1)} copy-done((f32[128]{0:T(128)S(1)}, f32[128]{0:T(128)}, u32[]{:S(2)}) %copy-start.7) | copy-done | bytes 536
  8.2 0.1 multiply_sqrt_fusion
  8.2 0.0 copy-start.4
  8.2 0.2 multiply_cosine_fusion
  8.5 0.0 copy-start.6
  8.5 0.5 %copy-done.4 = f32[33,64]{1,0:T(8,128)S(1)} copy-done((f32[33,64]{1,0:T(8,128)S(1)}, f32[33,64]{1,0:T(8,128)}, u32[]{:S(2)}) %copy-start.4) | copy-done | bytes 8472
  9.0 0.1 copy-done.6
  9.1 0.7 %fusion.1 = f32[512,64]{0,1:T(8,128)S(1)} fusion(f32[33,64]{1,0:T(8,128)S(1)} %copy-done.4, f32[512,16]{0,1:T(8,128)S(1)} %get-tuple-element.14, f32[512,16]{0,1:T(8,128)S(1)} %get-tuple-element.13, f32[512,1]{0,1:T(1,128)S(1)} %convert_multiply_fusion, f32[64]{0:T(128)S(1)} %copy-done.6), kind=kOutput, calls=%fused_computation.3 | convolution fusion | flops 13075456 | bytes 207360 | tf_op jit(solution)/shard_map/dot_general | solution.py:22
  9.9 0.0 copy-done
  9.9 0.3 fusion.3
  10.2 0.6 %pad_convert_fusion.filt_ref = f32[5,32,128]{2,1,0:T(8,128)} fusion(bf16[4,32,128]{2,1,0:T(8,128)(2,1)S(1)} %bitcast.46), kind=kLoop, calls=%fused_computation.28 | loop fusion | flops 20480 | bytes 114688 | tf_op jit(solution)/shard_map/concatenate | solution.py:120
  10.9 0.0 collective-permute-done
  10.9 6.8 %collective-permute-done.1 = bf16[512,128]{1,0:T(8,128)(2,1)S(1)} collective-permute-done((bf16[512,128]{1,0:T(8,128)(2,1)S(1)}, bf16[512,128]{1,0:T(8,128)(2,1)S(1)}, u32[]{:S(2)}, u32[]{:S(2)}) %collective-permute-start.1) | collective-permute-done | bytes 131104 | tf_op jit(solution)/shard_map/ppermute | solution.py:97
  17.7 0.0 collective-permute-done.2
  17.7 0.9 %pad_maximum_fusion.z_ref = bf16[4,512,128]{2,1,0:T(8,128)(2,1)} fusion(bf16[1,512,128]{2,1,0:T(8,128)(2,1)S(1)} %bitcast.49, bf16[1,512,128]{2,1,0:T(8,128)(2,1)S(1)} %bitcast.48, bf16[1,512,128]{2,1,0:T(8,128)(2,1)S(1)} %bitcast.47, bf16[1,512,128]{2,1,0:T(8,128)(2,1)S(1)} %get-tuple-element.9), kind=kLoop, calls=%fused_computation.13 | loop fusion | flops 786432 | bytes 1048576 | tf_op jit(solution)/shard_map/stack | solution.py:98
  18.6 3.3 %shard_map.82 = bf16[4,512,128]{2,1,0:T(8,128)(2,1)} custom-call(s32[1]{0:T(128)} %bitcast.s_ref, f32[5,32,128]{2,1,0:T(8,128)} %pad_convert_fusion.filt_ref, bf16[4,512,128]{2,1,0:T(8,128)(2,1)} %pad_maximum_fusion.z_ref), custom_call_target="tpu_custom_call" | custom-call | tf_op jit(solution)/shard_map/pallas_call | solution.py:61
  21.8 1.1 %fusion.17 = (bf16[1,512,128]{2,1,0:T(8,128)(2,1)S(1)}, bf16[512,128]{1,0:T(8,128)(2,1)S(1)}, bf16[512,128]{1,0:T(8,128)(2,1)S(1)}, bf16[512,128]{1,0:T(8,128)(2,1)S(1)}) fusion(bf16[4,512,128]{2,1,0:T(8,128)(2,1)} %shard_map.82), kind=kLoop, calls=%fused_computation.45 | loop fusion | bytes 1048576 | tf_op jit(solution)/shard_map/slice | solution.py:91
  23.0 2.1 %collective-permute-start.3 = (bf16[512,128]{1,0:T(8,128)(2,1)S(1)}, bf16[512,128]{1,0:T(8,128)(2,1)S(1)}, u32[]{:S(2)}, u32[]{:S(2)}) collective-permute-start(bf16[512,128]{1,0:T(8,128)(2,1)S(1)} %get-tuple-element.8), channel_id=1, source_target_pairs={{0,4},{4,0},{8,12},{12,8},{1,5},{5,1},{9,13},{13,9},{2,6},{6,2},{1... | collective-permute-start | bytes 393224 | tf_op jit(solution)/shard_map/ppermute | solution.py:97
  25.0 1.1 %collective-permute-start.4 = (bf16[512,128]{1,0:T(8,128)(2,1)S(1)}, bf16[512,128]{1,0:T(8,128)(2,1)S(1)}, u32[]{:S(2)}, u32[]{:S(2)}) collective-permute-start(bf16[512,128]{1,0:T(8,128)(2,1)S(1)} %get-tuple-element.7), channel_id=1, source_target_pairs={{0,8},{4,12},{8,0},{12,4},{1,9},{5,13},{9,1},{13,5},{2,10},{6,14},... | collective-permute-start | bytes 393224 | tf_op jit(solution)/shard_map/ppermute | solution.py:97
  26.1 1.4 %collective-permute-start.5 = (bf16[512,128]{1,0:T(8,128)(2,1)S(1)}, bf16[512,128]{1,0:T(8,128)(2,1)S(1)}, u32[]{:S(2)}, u32[]{:S(2)}) collective-permute-start(bf16[512,128]{1,0:T(8,128)(2,1)S(1)} %get-tuple-element.6), channel_id=1, source_target_pairs={{0,12},{4,8},{8,4},{12,0},{1,13},{5,9},{9,5},{13,1},{2,14},{6,10},... | collective-permute-start | bytes 393224 | tf_op jit(solution)/shard_map/ppermute | solution.py:97
  27.5 1.9 %collective-permute-done.3 = bf16[512,128]{1,0:T(8,128)(2,1)S(1)} collective-permute-done((bf16[512,128]{1,0:T(8,128)(2,1)S(1)}, bf16[512,128]{1,0:T(8,128)(2,1)S(1)}, u32[]{:S(2)}, u32[]{:S(2)}) %collective-permute-start.3) | collective-permute-done | bytes 131104 | tf_op jit(solution)/shard_map/ppermute | solution.py:97
  29.4 7.4 %collective-permute-done.4 = bf16[512,128]{1,0:T(8,128)(2,1)S(1)} collective-permute-done((bf16[512,128]{1,0:T(8,128)(2,1)S(1)}, bf16[512,128]{1,0:T(8,128)(2,1)S(1)}, u32[]{:S(2)}, u32[]{:S(2)}) %collective-permute-start.4) | collective-permute-done | bytes 131104 | tf_op jit(solution)/shard_map/ppermute | solution.py:97
  36.8 0.0 collective-permute-done.5
  36.9 0.1 pad_maximum_fusion.1
  36.9 0.0 copy-start.3
  36.9 0.0 copy-start.5
  36.9 0.6 %gather_fusion = bf16[4,512,128]{2,1,0:T(8,128)(2,1)S(1)} fusion(bf16[4,512,128]{2,1,0:T(8,128)(2,1)S(1)} %pad_maximum_fusion.1, s32[1024]{0:T(1024)S(1)} %pad_clamp_fusion), kind=kCustom, calls=%fused_computation | custom fusion | bytes 1048592 | tf_op jit(solution)/shard_map/jit(_take)/gather | solution.py:125
  37.6 0.0 copy-start.1
  37.6 0.0 copy-start.2
  37.6 0.2 copy.16
  37.8 0.1 copy-done.3
  38.0 0.0 copy-done.5
  38.0 0.7 %copy-done.1 = bf16[128,2048]{1,0:T(8,128)(2,1)S(1)} copy-done((bf16[128,2048]{1,0:T(8,128)(2,1)S(1)}, bf16[128,2048]{1,0:T(8,128)(2,1)}, u32[]{:S(2)}) %copy-start.1) | copy-done | bytes 524312
  38.7 0.2 copy-done.2
  38.8 1.2 %fusion.5 = bf16[128,2048]{1,0:T(8,128)(2,1)} fusion(bf16[128,2048]{1,0:T(8,128)(2,1)S(1)} %copy-done.3, bf16[128,2048]{1,0:T(8,128)(2,1)S(1)} %copy-done.1, bf16[128,2048]{1,0:T(8,128)(2,1)S(1)} %copy-done.2, f32[2048]{0:T(1024)S(1)} %copy-done.5, bf16[2048,128]{0,1:T(8,128)(2,1)S(1)} %copy.16, pred[2048]{0:T(1024)(128)(4,1)S(1)} %bitcast.53), kind=kLoop, calls=%fused_computation.9 | loop fusion | flops 2883584 | bytes 2631680 | tf_op jit(solution)/shard_map/convert_element_type | solution.py:128
  (9 shorter events, 0.1 us)
Async XLA Ops:
  0.0 9.9 %copy-start = (f32[64,128]{1,0:T(8,128)S(1)}, f32[64,128]{1,0:T(8,128)}, u32[]{:S(2)}) copy-start(f32[64,128]{1,0:T(8,128)} %param.13) | copy-start | bytes 98308
  1.7 9.2 %collective-permute-start = (bf16[512,128]{1,0:T(8,128)(2,1)S(1)}, bf16[512,128]{1,0:T(8,128)(2,1)S(1)}, u32[]{:S(2)}, u32[]{:S(2)}) collective-permute-start(bf16[512,128]{1,0:T(8,128)(2,1)S(1)} %get-tuple-element.12), channel_id=1, source_target_pairs={{0,4},{4,0},{8,12},{12,8},{1,5},{5,1},{9,13},{13,9},{2,6},{6,2},{1... | collective-permute-start | bytes 393224 | tf_op jit(solution)/shard_map/ppermute | solution.py:97
  4.8 12.9 %collective-permute-start.1 = (bf16[512,128]{1,0:T(8,128)(2,1)S(1)}, bf16[512,128]{1,0:T(8,128)(2,1)S(1)}, u32[]{:S(2)}, u32[]{:S(2)}) collective-permute-start(bf16[512,128]{1,0:T(8,128)(2,1)S(1)} %get-tuple-element.11), channel_id=1, source_target_pairs={{0,8},{4,12},{8,0},{12,4},{1,9},{5,13},{9,1},{13,5},{2,10},{6,14},... | collective-permute-start | bytes 393224 | tf_op jit(solution)/shard_map/ppermute | solution.py:97
  7.4 10.3 %collective-permute-start.2 = (bf16[512,128]{1,0:T(8,128)(2,1)S(1)}, bf16[512,128]{1,0:T(8,128)(2,1)S(1)}, u32[]{:S(2)}, u32[]{:S(2)}) collective-permute-start(bf16[512,128]{1,0:T(8,128)(2,1)S(1)} %get-tuple-element.10), channel_id=1, source_target_pairs={{0,12},{4,8},{8,4},{12,0},{1,13},{5,9},{9,5},{13,1},{2,14},{6,10},... | collective-permute-start | bytes 393224 | tf_op jit(solution)/shard_map/ppermute | solution.py:97
  7.5 0.7 %copy-start.7 = (f32[128]{0:T(128)S(1)}, f32[128]{0:T(128)}, u32[]{:S(2)}) copy-start(f32[128]{0:T(128)} %param.14) | copy-start | bytes 1540
  8.2 0.7 %copy-start.4 = (f32[33,64]{1,0:T(8,128)S(1)}, f32[33,64]{1,0:T(8,128)}, u32[]{:S(2)}) copy-start(f32[33,64]{1,0:T(8,128)} %param.11) | copy-start | bytes 25348
  8.5 0.7 %copy-start.6 = (f32[64]{0:T(128)S(1)}, f32[64]{0:T(128)}, u32[]{:S(2)}) copy-start(f32[64]{0:T(128)} %param.12) | copy-start | bytes 772
  23.0 6.4 %collective-permute-start.3 = (bf16[512,128]{1,0:T(8,128)(2,1)S(1)}, bf16[512,128]{1,0:T(8,128)(2,1)S(1)}, u32[]{:S(2)}, u32[]{:S(2)}) collective-permute-start(bf16[512,128]{1,0:T(8,128)(2,1)S(1)} %get-tuple-element.8), channel_id=1, source_target_pairs={{0,4},{4,0},{8,12},{12,8},{1,5},{5,1},{9,13},{13,9},{2,6},{6,2},{1... | collective-permute-start | bytes 393224 | tf_op jit(solution)/shard_map/ppermute | solution.py:97
  25.0 11.8 %collective-permute-start.4 = (bf16[512,128]{1,0:T(8,128)(2,1)S(1)}, bf16[512,128]{1,0:T(8,128)(2,1)S(1)}, u32[]{:S(2)}, u32[]{:S(2)}) collective-permute-start(bf16[512,128]{1,0:T(8,128)(2,1)S(1)} %get-tuple-element.7), channel_id=1, source_target_pairs={{0,8},{4,12},{8,0},{12,4},{1,9},{5,13},{9,1},{13,5},{2,10},{6,14},... | collective-permute-start | bytes 393224 | tf_op jit(solution)/shard_map/ppermute | solution.py:97
  26.1 10.7 %collective-permute-start.5 = (bf16[512,128]{1,0:T(8,128)(2,1)S(1)}, bf16[512,128]{1,0:T(8,128)(2,1)S(1)}, u32[]{:S(2)}, u32[]{:S(2)}) collective-permute-start(bf16[512,128]{1,0:T(8,128)(2,1)S(1)} %get-tuple-element.6), channel_id=1, source_target_pairs={{0,12},{4,8},{8,4},{12,0},{1,13},{5,9},{9,5},{13,1},{2,14},{6,10},... | collective-permute-start | bytes 393224 | tf_op jit(solution)/shard_map/ppermute | solution.py:97
  36.9 1.0 %copy-start.3 = (bf16[128,2048]{1,0:T(8,128)(2,1)S(1)}, bf16[128,2048]{1,0:T(8,128)(2,1)}, u32[]{:S(2)}) copy-start(bf16[128,2048]{1,0:T(8,128)(2,1)} %param.8) | copy-start | bytes 1572868
  36.9 1.0 %copy-start.5 = (f32[2048]{0:T(1024)S(1)}, f32[2048]{0:T(1024)}, u32[]{:S(2)}) copy-start(f32[2048]{0:T(1024)} %param.15) | copy-start | bytes 24580
  37.6 1.1 %copy-start.1 = (bf16[128,2048]{1,0:T(8,128)(2,1)S(1)}, bf16[128,2048]{1,0:T(8,128)(2,1)}, u32[]{:S(2)}) copy-start(bf16[128,2048]{1,0:T(8,128)(2,1)} %param.10) | copy-start | bytes 1572868
  37.6 1.2 %copy-start.2 = (bf16[128,2048]{1,0:T(8,128)(2,1)S(1)}, bf16[128,2048]{1,0:T(8,128)(2,1)}, u32[]{:S(2)}) copy-start(bf16[128,2048]{1,0:T(8,128)(2,1)} %param.9) | copy-start | bytes 1572868

commit v14 on v10

--- a/solution.py
+++ b/solution.py
@@ -108,11 +108,14 @@
     filt = jnp.concatenate([jnp.zeros((1, sub, own_rows), jnp.float32), lagged], axis=0)
     s_arr = jnp.reshape(s, (1,)).astype(jnp.int32)
     conv_parts = toeplitz_conv(s_arr, filt, got)
+    base = skip_gain[None, :] * gated_f
     back = exchange(conv_parts, nb, s, True)
-    order = (s - jnp.arange(nb, dtype=jnp.int32) + nb) % nb
-    back = jnp.take(back, order, axis=0)
-    conv = back.reshape(width, own_rows).T.astype(jnp.float32)
-    mixed = outer_gate.astype(jnp.float32) * (conv + skip_gain[None, :] * gated_f)
+    chunk = sub * GROUP
+    conv_t = jnp.zeros((width, own_rows), jnp.bfloat16)
+    for k in range(nb):
+        conv_t = lax.dynamic_update_slice_in_dim(conv_t, back[k], ((s - k + nb) % nb) * chunk, 0)
+    conv = conv_t.T.astype(jnp.float32)
+    mixed = outer_gate.astype(jnp.float32) * (conv + base)
     return mixed.astype(jnp.bfloat16)
 
 

time: 38.2 us -> 40.1 us (1.050); the launches traced: 37.5 us -> 39.9 us
  waiting for transfers between devices: 11.1 us -> 16.8 us
  starting transfers between devices: 12.8 us -> 10.9 us
  local copies, waits for them, and re-layouts: 4.72 us -> 3.35 us
    ppermute x6, waiting for transfers between devices: 11.1 us -> 16.8 us  [exchange(): lax.ppermute(piece, 'seq', [(i, (i + k) % nb) for i in range(nb)])]
    ppermute x6, starting transfers between devices: 12.8 us -> 10.9 us  [exchange(): lax.ppermute(piece, 'seq', [(i, (i + k) % nb) for i in range(nb)])]
    slice x1 -> x0, local copies, waits for them, and re-layouts: 1.13 us -> none  [exchange(): x[0]]
    squeeze x0 -> x1, local copies, waits for them, and re-layouts: none -> 1.13 us  [exchange(): piece = x[k]]
    unnamed x18 -> x16, local copies, waits for them, and re-layouts: 2.41 us -> 1.33 us
    gather x2 -> x0, local copies, waits for them, and re-layouts: 0.86 us -> none  [per_device(): back = jnp.take(back, order, axis=0)]
    another operation x2 -> x1, other arithmetic: 0.93 us -> 0.86 us  [exchange(): return jnp.stack(got)]
where the time goes in v14:
time: 40.1 us; the launch traced here: 39.9 us
  waiting for transfers between devices  16.8 us (42%)
  starting transfers between devices  10.9 us (27%)
  other arithmetic  4.29 us (11%)
  local copies, waits for them, and re-layouts  3.35 us (8%)
  Pallas kernels  3.28 us (8%)
  matrix products  1.07 us (3%)
    ppermute x6, waiting for transfers between devices, exchange(): lax.ppermute(piece, 'seq', [(i, (i + k) % nb) for i in range(nb)])  16.8 us
    ppermute x6, starting transfers between devices, exchange(): lax.ppermute(piece, 'seq', [(i, (i + k) % nb) for i in range(nb)])  10.9 us
    pallas_call x1, Pallas kernels, toeplitz_conv(): pl.pallas_call(toeplitz_kernel, out_shape=jax.ShapeDtypeStruct((nb, chans...  3.28 us
    unnamed x16, local copies, waits for them, and re-layouts  1.33 us
    transpose x1, other arithmetic, per_device(): gated_t = gated.T.reshape(nb, sub * GROUP, own_rows)  1.33 us
    convert_element_type x1, other arithmetic, per_device(): return mixed.astype(jnp.bfloat16)  1.16 us
    squeeze x1, local copies, waits for them, and re-layouts, exchange(): piece = x[k]  1.13 us
    another operation x1, other arithmetic, exchange(): return jnp.stack(got)  0.86 us
  transfers between devices with their start and end apart: 6, of which 3 were waited for; matrix products, arithmetic and copies ran while one was open for 6% of the time, Pallas kernels for 0%

profile of v14, /device:TPU:0, one launch (start us, length us, event | category | flops | bytes accessed | tf_op | source)
XLA Modules:
  0.0 39.9 jit_solution(390587937476193690)
XLA Ops:
  0.0 0.0 copy-start
  0.0 1.3 %fusion.7 = bf16[2048,128]{0,1:T(8,128)(2,1)S(1)} fusion(bf16[128,2048]{1,0:T(8,128)(2,1)} %param.10, bf16[128,2048]{1,0:T(8,128)(2,1)} %param.9), kind=kLoop, calls=%fused_computation.11 | loop fusion | flops 1310720 | bytes 1572864 | tf_op jit(solution)/shard_map/transpose | solution.py:101
  1.3 0.3 copy.21
  1.7 5.1 %collective-permute-start.2 = (bf16[512,128]{1,0:T(8,128)(2,1)S(1)}, bf16[512,128]{1,0:T(8,128)(2,1)S(1)}, u32[]{:S(2)}, u32[]{:S(2)}) collective-permute-start(bf16[512,128]{1,0:T(8,128)(2,1)S(1)} %get-tuple-element.10), channel_id=1, source_target_pairs={{0,12},{4,0},{8,4},{12,8},{1,13},{5,1},{9,5},{13,9},{2,14},{6,2},{... | collective-permute-start | bytes 393224 | tf_op jit(solution)/shard_map/ppermute | solution.py:85
  6.8 0.0 collective-permute-start.1
  6.8 1.0 %collective-permute-start = (bf16[512,128]{1,0:T(8,128)(2,1)S(1)}, bf16[512,128]{1,0:T(8,128)(2,1)S(1)}, u32[]{:S(2)}, u32[]{:S(2)}) collective-permute-start(bf16[512,128]{1,0:T(8,128)(2,1)S(1)} %get-tuple-element.12), channel_id=1, source_target_pairs={{0,4},{4,8},{8,12},{12,0},{1,5},{5,9},{9,13},{13,1},{2,6},{6,10},{... | collective-permute-start | bytes 393224 | tf_op jit(solution)/shard_map/ppermute | solution.py:85
  7.9 0.0 copy-start.7
  7.9 0.6 %copy-done.7 = f32[128]{0:T(128)S(1)} copy-done((f32[128]{0:T(128)S(1)}, f32[128]{0:T(128)}, u32[]{:S(2)}) %copy-start.7) | copy-done | bytes 536
  8.5 0.1 multiply_sqrt_fusion
  8.6 0.0 copy-start.4
  8.6 0.2 multiply_cosine_fusion
  8.8 0.0 copy-start.6
  8.8 0.5 %copy-done.4 = f32[33,64]{1,0:T(8,128)S(1)} copy-done((f32[33,64]{1,0:T(8,128)S(1)}, f32[33,64]{1,0:T(8,128)}, u32[]{:S(2)}) %copy-start.4) | copy-done | bytes 8472
  9.3 0.1 copy-done.6
  9.5 0.7 %fusion.1 = f32[512,64]{0,1:T(8,128)S(1)} fusion(f32[33,64]{1,0:T(8,128)S(1)} %copy-done.4, f32[512,16]{0,1:T(8,128)S(1)} %get-tuple-element.14, f32[512,16]{0,1:T(8,128)S(1)} %get-tuple-element.13, f32[512,1]{0,1:T(1,128)S(1)} %convert_multiply_fusion, f32[64]{0:T(128)S(1)} %copy-done.6), kind=kOutput, calls=%fused_computation.2 | convolution fusion | flops 13075456 | bytes 207360 | tf_op jit(solution)/shard_map/dot_general | solution.py:22
  10.2 0.0 copy-done
  10.2 0.3 fusion.3
  10.6 0.6 %pad_convert_fusion.filt_ref = f32[5,32,128]{2,1,0:T(8,128)} fusion(bf16[4,32,128]{2,1,0:T(8,128)(2,1)S(1)} %bitcast.38), kind=kLoop, calls=%fused_computation.27 | loop fusion | flops 20480 | bytes 114688 | tf_op jit(solution)/shard_map/concatenate | solution.py:108
  11.2 0.0 collective-permute-done.2
  11.2 6.8 %collective-permute-done.1 = bf16[512,128]{1,0:T(8,128)(2,1)S(1)} collective-permute-done((bf16[512,128]{1,0:T(8,128)(2,1)S(1)}, bf16[512,128]{1,0:T(8,128)(2,1)S(1)}, u32[]{:S(2)}, u32[]{:S(2)}) %collective-permute-start.1) | collective-permute-done | bytes 131104 | tf_op jit(solution)/shard_map/ppermute | solution.py:85
  18.0 0.0 collective-permute-done
  18.0 0.9 %pad_maximum_fusion.z_ref = bf16[4,512,128]{2,1,0:T(8,128)(2,1)} fusion(bf16[1,512,128]{2,1,0:T(8,128)(2,1)S(1)} %bitcast.39, bf16[1,512,128]{2,1,0:T(8,128)(2,1)S(1)} %bitcast.40, bf16[1,512,128]{2,1,0:T(8,128)(2,1)S(1)} %bitcast.41, bf16[1,512,128]{2,1,0:T(8,128)(2,1)S(1)} %get-tuple-element.9), kind=kLoop, calls=%fused_computation.12 | loop fusion | flops 786432 | bytes 1048576 | tf_op jit(solution)/shard_map/stack | solution.py:86
  18.9 3.3 %shard_map.82 = bf16[4,512,128]{2,1,0:T(8,128)(2,1)} custom-call(s32[1]{0:T(128)} %bitcast.s_ref, f32[5,32,128]{2,1,0:T(8,128)} %pad_convert_fusion.filt_ref, bf16[4,512,128]{2,1,0:T(8,128)(2,1)} %pad_maximum_fusion.z_ref), custom_call_target="tpu_custom_call" | custom-call | tf_op jit(solution)/shard_map/pallas_call | solution.py:61
  22.2 1.1 %slice_bitcast_fusion = (bf16[512,128]{1,0:T(8,128)(2,1)S(1)}, bf16[512,128]{1,0:T(8,128)(2,1)S(1)}, bf16[512,128]{1,0:T(8,128)(2,1)S(1)}, bf16[512,128]{1,0:T(8,128)(2,1)S(1)}) fusion(bf16[4,512,128]{2,1,0:T(8,128)(2,1)} %shard_map.82), kind=kLoop, calls=%fused_computation.13 | loop fusion | bytes 1048576 | tf_op jit(solution)/shard_map/squeeze | solution.py:82
  23.3 0.8 %collective-permute-start.3 = (bf16[512,128]{1,0:T(8,128)(2,1)S(1)}, bf16[512,128]{1,0:T(8,128)(2,1)S(1)}, u32[]{:S(2)}, u32[]{:S(2)}) collective-permute-start(bf16[512,128]{1,0:T(8,128)(2,1)S(1)} %get-tuple-element.7), channel_id=1, source_target_pairs={{0,4},{4,8},{8,12},{12,0},{1,5},{5,9},{9,13},{13,1},{2,6},{6,10},{... | collective-permute-start | bytes 393224 | tf_op jit(solution)/shard_map/ppermute | solution.py:85
  24.1 0.1 copy.22
  24.2 3.2 %collective-permute-start.5 = (bf16[512,128]{1,0:T(8,128)(2,1)S(1)}, bf16[512,128]{1,0:T(8,128)(2,1)S(1)}, u32[]{:S(2)}, u32[]{:S(2)}) collective-permute-start(bf16[512,128]{1,0:T(8,128)(2,1)S(1)} %get-tuple-element.5), channel_id=1, source_target_pairs={{0,12},{4,0},{8,4},{12,8},{1,13},{5,1},{9,5},{13,9},{2,14},{6,2},{... | collective-permute-start | bytes 393224 | tf_op jit(solution)/shard_map/ppermute | solution.py:85
  27.4 0.8 %collective-permute-start.4 = (bf16[512,128]{1,0:T(8,128)(2,1)S(1)}, bf16[512,128]{1,0:T(8,128)(2,1)S(1)}, u32[]{:S(2)}, u32[]{:S(2)}) collective-permute-start(bf16[512,128]{1,0:T(8,128)(2,1)S(1)} %get-tuple-element.6), channel_id=1, source_target_pairs={{0,8},{4,12},{8,0},{12,4},{1,9},{5,13},{9,1},{13,5},{2,10},{6,14},... | collective-permute-start | bytes 393224 | tf_op jit(solution)/shard_map/ppermute | solution.py:85
  28.2 0.0 copy-start.5
  28.3 3.3 %collective-permute-done.3 = bf16[512,128]{1,0:T(8,128)(2,1)S(1)} collective-permute-done((bf16[512,128]{1,0:T(8,128)(2,1)S(1)}, bf16[512,128]{1,0:T(8,128)(2,1)S(1)}, u32[]{:S(2)}, u32[]{:S(2)}) %collective-permute-start.3) | collective-permute-done | bytes 131104 | tf_op jit(solution)/shard_map/ppermute | solution.py:85
  31.5 0.0 copy-start.3
  31.5 0.1 copy.23
  31.7 0.0 copy-start.1
  31.7 0.0 copy-start.2
  31.7 6.7 %collective-permute-done.4 = bf16[512,128]{1,0:T(8,128)(2,1)S(1)} collective-permute-done((bf16[512,128]{1,0:T(8,128)(2,1)S(1)}, bf16[512,128]{1,0:T(8,128)(2,1)S(1)}, u32[]{:S(2)}, u32[]{:S(2)}) %collective-permute-start.4) | collective-permute-done | bytes 131104 | tf_op jit(solution)/shard_map/ppermute | solution.py:85
  38.4 0.1 copy.24
  38.5 0.0 collective-permute-done.5
  38.6 0.1 copy.25
  38.7 0.0 copy-done.5
  38.7 0.0 copy-done.3
  38.7 0.0 copy-done.1
  38.7 0.0 copy-done.2
  38.7 1.2 %fusion.5 = bf16[128,2048]{1,0:T(8,128)(2,1)} fusion(bf16[2048,128]{0,1:T(8,128)(2,1)S(1)} %constant_dynamic-update-slice_fusion, bf16[128,2048]{1,0:T(8,128)(2,1)S(1)} %copy-done.3, bf16[128,2048]{1,0:T(8,128)(2,1)S(1)} %copy-done.1, bf16[128,2048]{1,0:T(8,128)(2,1)S(1)} %copy-done.2, f32[2048]{0:T(1024)S(1)} %copy-done.5), kind=kLoop, calls=%fused_computation.8 | loop fusion | flops 2621440 | bytes 2629632 | tf_op jit(solution)/shard_map/convert_element_type | solution.py:119
  (10 shorter events, 0.2 us)
Async XLA Ops:
  0.0 10.2 %copy-start = (f32[64,128]{1,0:T(8,128)S(1)}, f32[64,128]{1,0:T(8,128)}, u32[]{:S(2)}) copy-start(f32[64,128]{1,0:T(8,128)} %param.13) | copy-start | bytes 98308
  1.7 9.5 %collective-permute-start.2 = (bf16[512,128]{1,0:T(8,128)(2,1)S(1)}, bf16[512,128]{1,0:T(8,128)(2,1)S(1)}, u32[]{:S(2)}, u32[]{:S(2)}) collective-permute-start(bf16[512,128]{1,0:T(8,128)(2,1)S(1)} %get-tuple-element.10), channel_id=1, source_target_pairs={{0,12},{4,0},{8,4},{12,8},{1,13},{5,1},{9,5},{13,9},{2,14},{6,2},{... | collective-permute-start | bytes 393224 | tf_op jit(solution)/shard_map/ppermute | solution.py:85
  6.8 11.2 %collective-permute-start.1 = (bf16[512,128]{1,0:T(8,128)(2,1)S(1)}, bf16[512,128]{1,0:T(8,128)(2,1)S(1)}, u32[]{:S(2)}, u32[]{:S(2)}) collective-permute-start(bf16[512,128]{1,0:T(8,128)(2,1)S(1)} %get-tuple-element.11), channel_id=1, source_target_pairs={{0,8},{4,12},{8,0},{12,4},{1,9},{5,13},{9,1},{13,5},{2,10},{6,14},... | collective-permute-start | bytes 393224 | tf_op jit(solution)/shard_map/ppermute | solution.py:85
  6.8 11.2 %collective-permute-start = (bf16[512,128]{1,0:T(8,128)(2,1)S(1)}, bf16[512,128]{1,0:T(8,128)(2,1)S(1)}, u32[]{:S(2)}, u32[]{:S(2)}) collective-permute-start(bf16[512,128]{1,0:T(8,128)(2,1)S(1)} %get-tuple-element.12), channel_id=1, source_target_pairs={{0,4},{4,8},{8,12},{12,0},{1,5},{5,9},{9,13},{13,1},{2,6},{6,10},{... | collective-permute-start | bytes 393224 | tf_op jit(solution)/shard_map/ppermute | solution.py:85
  7.9 0.7 %copy-start.7 = (f32[128]{0:T(128)S(1)}, f32[128]{0:T(128)}, u32[]{:S(2)}) copy-start(f32[128]{0:T(128)} %param.14) | copy-start | bytes 1540
  8.6 0.7 %copy-start.4 = (f32[33,64]{1,0:T(8,128)S(1)}, f32[33,64]{1,0:T(8,128)}, u32[]{:S(2)}) copy-start(f32[33,64]{1,0:T(8,128)} %param.11) | copy-start | bytes 25348
  8.8 0.7 %copy-start.6 = (f32[64]{0:T(128)S(1)}, f32[64]{0:T(128)}, u32[]{:S(2)}) copy-start(f32[64]{0:T(128)} %param.12) | copy-start | bytes 772
  23.3 8.2 %collective-permute-start.3 = (bf16[512,128]{1,0:T(8,128)(2,1)S(1)}, bf16[512,128]{1,0:T(8,128)(2,1)S(1)}, u32[]{:S(2)}, u32[]{:S(2)}) collective-permute-start(bf16[512,128]{1,0:T(8,128)(2,1)S(1)} %get-tuple-element.7), channel_id=1, source_target_pairs={{0,4},{4,8},{8,12},{12,0},{1,5},{5,9},{9,13},{13,1},{2,6},{6,10},{... | collective-permute-start | bytes 393224 | tf_op jit(solution)/shard_map/ppermute | solution.py:85
  24.2 14.4 %collective-permute-start.5 = (bf16[512,128]{1,0:T(8,128)(2,1)S(1)}, bf16[512,128]{1,0:T(8,128)(2,1)S(1)}, u32[]{:S(2)}, u32[]{:S(2)}) collective-permute-start(bf16[512,128]{1,0:T(8,128)(2,1)S(1)} %get-tuple-element.5), channel_id=1, source_target_pairs={{0,12},{4,0},{8,4},{12,8},{1,13},{5,1},{9,5},{13,9},{2,14},{6,2},{... | collective-permute-start | bytes 393224 | tf_op jit(solution)/shard_map/ppermute | solution.py:85
  27.4 11.0 %collective-permute-start.4 = (bf16[512,128]{1,0:T(8,128)(2,1)S(1)}, bf16[512,128]{1,0:T(8,128)(2,1)S(1)}, u32[]{:S(2)}, u32[]{:S(2)}) collective-permute-start(bf16[512,128]{1,0:T(8,128)(2,1)S(1)} %get-tuple-element.6), channel_id=1, source_target_pairs={{0,8},{4,12},{8,0},{12,4},{1,9},{5,13},{9,1},{13,5},{2,10},{6,14},... | collective-permute-start | bytes 393224 | tf_op jit(solution)/shard_map/ppermute | solution.py:85
  28.2 10.5 %copy-start.5 = (f32[2048]{0:T(1024)S(1)}, f32[2048]{0:T(1024)}, u32[]{:S(2)}) copy-start(f32[2048]{0:T(1024)} %param.15) | copy-start | bytes 24580
  31.5 7.2 %copy-start.3 = (bf16[128,2048]{1,0:T(8,128)(2,1)S(1)}, bf16[128,2048]{1,0:T(8,128)(2,1)}, u32[]{:S(2)}) copy-start(bf16[128,2048]{1,0:T(8,128)(2,1)} %param.8) | copy-start | bytes 1572868
  31.7 7.0 %copy-start.1 = (bf16[128,2048]{1,0:T(8,128)(2,1)S(1)}, bf16[128,2048]{1,0:T(8,128)(2,1)}, u32[]{:S(2)}) copy-start(bf16[128,2048]{1,0:T(8,128)(2,1)} %param.10) | copy-start | bytes 1572868
  31.7 7.0 %copy-start.2 = (bf16[128,2048]{1,0:T(8,128)(2,1)S(1)}, bf16[128,2048]{1,0:T(8,128)(2,1)}, u32[]{:S(2)}) copy-start(bf16[128,2048]{1,0:T(8,128)(2,1)} %param.9) | copy-start | bytes 1572868

commit v15 on v10

--- a/solution.py
+++ b/solution.py
@@ -1,11 +1,10 @@
-import functools
-
 import jax
 import jax.numpy as jnp
 from jax import lax
 from jax.experimental import pallas as pl
 from jax.experimental.pallas import tpu as pltpu
 from jax.sharding import PartitionSpec as P
+
 
 GROUP = 16
 BANDS = 16
@@ -75,18 +74,23 @@
     )(s, filt, z)
 
 
+def shift_order(nb):
+    return sorted(range(1, nb), key=lambda k: (abs(2 * k - nb), k))
+
+
 def exchange(x, nb, s, ordered):
-    got = [x[0] if ordered else lax.dynamic_index_in_dim(x, s, 0, keepdims=False)]
-    for k in range(1, nb):
+    got = [None] * nb
+    got[0] = x[0] if ordered else lax.dynamic_index_in_dim(x, s, 0, keepdims=False)
+    for k in shift_order(nb):
         if ordered:
             piece = x[k]
         else:
             piece = lax.dynamic_index_in_dim(x, (s + k) % nb, 0, keepdims=False)
-        got.append(lax.ppermute(piece, "seq", [(i, (i + k) % nb) for i in range(nb)]))
+        got[k] = lax.ppermute(piece, "seq", [(i, (i + k) % nb) for i in range(nb)])
     return jnp.stack(got)
 
 
-def per_device(
+def mixer(
     outer_gate, inner_gate, signal, filter_in, filter_bias, filter_out, decay, skip_gain
 ):
     own_rows, width = signal.shape
@@ -128,7 +132,7 @@
         P("chan"),
     )
     return jax.shard_map(
-        per_device,
+        mixer,
         mesh=mesh,
         in_specs=placed,
         out_specs=P(("groups", "seq"), "chan"),

time: 38.2 us -> 38.2 us (level)
  no operation moved by 1% of the time
where the time goes in v15:
time: 38.2 us; the launch traced here: 37.5 us
  starting transfers between devices  12.8 us (34%)
  waiting for transfers between devices  11.1 us (29%)
  local copies, waits for them, and re-layouts  4.72 us (12%)
  other arithmetic  4.42 us (12%)
  Pallas kernels  3.27 us (9%)
  matrix products  1.07 us (3%)
    ppermute x6, starting transfers between devices, exchange(): got[k] = lax.ppermute(piece, 'seq', [(i, (i + k) % nb) for i in range(nb)])  12.8 us
    ppermute x6, waiting for transfers between devices, exchange(): got[k] = lax.ppermute(piece, 'seq', [(i, (i + k) % nb) for i in range(nb)])  11.1 us
    pallas_call x1, Pallas kernels, toeplitz_conv(): pl.pallas_call(toeplitz_kernel, out_shape=jax.ShapeDtypeStruct((nb, chans...  3.27 us
    unnamed x18, local copies, waits for them, and re-layouts  2.41 us
    transpose x1, other arithmetic, mixer(): gated_t = gated.T.reshape(nb, sub * GROUP, own_rows)  1.33 us
    convert_element_type x1, other arithmetic, mixer(): return mixed.astype(jnp.bfloat16)  1.18 us
    slice x1, local copies, waits for them, and re-layouts, exchange(): x[0]  1.13 us
    another operation x2, other arithmetic, exchange(): return jnp.stack(got)  0.93 us
  transfers between devices with their start and end apart: 6, of which 3 were waited for; matrix products, arithmetic and copies ran while one was open for 6% of the time, Pallas kernels for 0%

profile of v15, /device:TPU:0, one launch (start us, length us, event | category | flops | bytes accessed | tf_op | source)
XLA Modules:
  0.0 37.5 jit_solution(4176439410170732759)
XLA Ops:
  0.0 0.0 copy-start
  0.0 1.3 %fusion.7 = bf16[2048,128]{0,1:T(8,128)(2,1)S(1)} fusion(bf16[128,2048]{1,0:T(8,128)(2,1)} %param.10, bf16[128,2048]{1,0:T(8,128)(2,1)} %param.9), kind=kLoop, calls=%fused_computation.12 | loop fusion | flops 1310720 | bytes 1572864 | tf_op jit(solution)/shard_map/transpose | solution.py:105
  1.3 0.3 copy.15
  1.7 3.1 %collective-permute-start = (bf16[512,128]{1,0:T(8,128)(2,1)S(1)}, bf16[512,128]{1,0:T(8,128)(2,1)S(1)}, u32[]{:S(2)}, u32[]{:S(2)}) collective-permute-start(bf16[512,128]{1,0:T(8,128)(2,1)S(1)} %get-tuple-element.12), channel_id=1, source_target_pairs={{0,4},{4,8},{8,12},{12,0},{1,5},{5,9},{9,13},{13,1},{2,6},{6,10},{... | collective-permute-start | bytes 393224 | tf_op jit(solution)/shard_map/ppermute | solution.py:89
  4.8 2.6 %collective-permute-start.1 = (bf16[512,128]{1,0:T(8,128)(2,1)S(1)}, bf16[512,128]{1,0:T(8,128)(2,1)S(1)}, u32[]{:S(2)}, u32[]{:S(2)}) collective-permute-start(bf16[512,128]{1,0:T(8,128)(2,1)S(1)} %get-tuple-element.11), channel_id=1, source_target_pairs={{0,8},{4,12},{8,0},{12,4},{1,9},{5,13},{9,1},{13,5},{2,10},{6,14},... | collective-permute-start | bytes 393224 | tf_op jit(solution)/shard_map/ppermute | solution.py:89
  7.4 1.3 %collective-permute-start.2 = (bf16[512,128]{1,0:T(8,128)(2,1)S(1)}, bf16[512,128]{1,0:T(8,128)(2,1)S(1)}, u32[]{:S(2)}, u32[]{:S(2)}) collective-permute-start(bf16[512,128]{1,0:T(8,128)(2,1)S(1)} %get-tuple-element.10), channel_id=1, source_target_pairs={{0,12},{4,0},{8,4},{12,8},{1,13},{5,1},{9,5},{13,9},{2,14},{6,2},{... | collective-permute-start | bytes 393224 | tf_op jit(solution)/shard_map/ppermute | solution.py:89
  8.8 0.1 broadcast_bitcast_fusion
  8.8 0.0 copy-start.7
  8.9 0.7 %copy-done.7 = f32[128]{0:T(128)S(1)} copy-done((f32[128]{0:T(128)S(1)}, f32[128]{0:T(128)}, u32[]{:S(2)}) %copy-start.7) | copy-done | bytes 536
  9.5 0.1 multiply_sqrt_fusion
  9.6 0.0 copy-start.4
  9.6 0.2 multiply_cosine_fusion
  9.8 0.0 copy-start.6
  9.8 0.5 %copy-done.4 = f32[33,64]{1,0:T(8,128)S(1)} copy-done((f32[33,64]{1,0:T(8,128)S(1)}, f32[33,64]{1,0:T(8,128)}, u32[]{:S(2)}) %copy-start.4) | copy-done | bytes 8472
  10.3 0.1 copy-done.6
  10.4 0.7 %fusion.1 = f32[512,64]{0,1:T(8,128)S(1)} fusion(f32[33,64]{1,0:T(8,128)S(1)} %copy-done.4, f32[512,16]{0,1:T(8,128)S(1)} %get-tuple-element.14, f32[512,16]{0,1:T(8,128)S(1)} %get-tuple-element.13, f32[512,1]{0,1:T(1,128)S(1)} %convert_multiply_fusion, f32[64]{0:T(128)S(1)} %copy-done.6), kind=kOutput, calls=%fused_computation.3 | convolution fusion | flops 13075456 | bytes 207360 | tf_op jit(solution)/shard_map/dot_general | solution.py:21
  11.2 0.0 copy-done
  11.2 0.3 fusion.3
  11.6 0.6 %pad_convert_fusion.filt_ref = f32[5,32,128]{2,1,0:T(8,128)} fusion(bf16[4,32,128]{2,1,0:T(8,128)(2,1)S(1)} %bitcast.46), kind=kLoop, calls=%fused_computation.28 | loop fusion | flops 20480 | bytes 114688 | tf_op jit(solution)/shard_map/concatenate | solution.py:112
  12.2 0.0 collective-permute-done
  12.2 3.8 %collective-permute-done.1 = bf16[512,128]{1,0:T(8,128)(2,1)S(1)} collective-permute-done((bf16[512,128]{1,0:T(8,128)(2,1)S(1)}, bf16[512,128]{1,0:T(8,128)(2,1)S(1)}, u32[]{:S(2)}, u32[]{:S(2)}) %collective-permute-start.1) | collective-permute-done | bytes 131104 | tf_op jit(solution)/shard_map/ppermute | solution.py:89
  16.0 0.0 collective-permute-done.2
  16.0 0.9 %pad_maximum_fusion.z_ref = bf16[4,512,128]{2,1,0:T(8,128)(2,1)} fusion(bf16[1,512,128]{2,1,0:T(8,128)(2,1)S(1)} %bitcast.49, bf16[1,512,128]{2,1,0:T(8,128)(2,1)S(1)} %bitcast.48, bf16[1,512,128]{2,1,0:T(8,128)(2,1)S(1)} %bitcast.47, bf16[1,512,128]{2,1,0:T(8,128)(2,1)S(1)} %get-tuple-element.9), kind=kLoop, calls=%fused_computation.13 | loop fusion | flops 786432 | bytes 1048576 | tf_op jit(solution)/shard_map/stack | solution.py:90
  16.9 3.3 %shard_map.82 = bf16[4,512,128]{2,1,0:T(8,128)(2,1)} custom-call(s32[1]{0:T(128)} %bitcast.s_ref, f32[5,32,128]{2,1,0:T(8,128)} %pad_convert_fusion.filt_ref, bf16[4,512,128]{2,1,0:T(8,128)(2,1)} %pad_maximum_fusion.z_ref), custom_call_target="tpu_custom_call" | custom-call | tf_op jit(solution)/shard_map/pallas_call | solution.py:60
  20.2 1.1 %fusion.19 = (bf16[1,512,128]{2,1,0:T(8,128)(2,1)S(1)}, bf16[512,128]{1,0:T(8,128)(2,1)S(1)}, bf16[512,128]{1,0:T(8,128)(2,1)S(1)}, bf16[512,128]{1,0:T(8,128)(2,1)S(1)}) fusion(bf16[4,512,128]{2,1,0:T(8,128)(2,1)} %shard_map.82), kind=kLoop, calls=%fused_computation.53 | loop fusion | bytes 1048576 | tf_op jit(solution)/shard_map/slice | solution.py:83
  21.3 3.3 %collective-permute-start.3 = (bf16[512,128]{1,0:T(8,128)(2,1)S(1)}, bf16[512,128]{1,0:T(8,128)(2,1)S(1)}, u32[]{:S(2)}, u32[]{:S(2)}) collective-permute-start(bf16[512,128]{1,0:T(8,128)(2,1)S(1)} %get-tuple-element.8), channel_id=1, source_target_pairs={{0,4},{4,8},{8,12},{12,0},{1,5},{5,9},{9,13},{13,1},{2,6},{6,10},{... | collective-permute-start | bytes 393224 | tf_op jit(solution)/shard_map/ppermute | solution.py:89
  24.6 1.6 %collective-permute-start.4 = (bf16[512,128]{1,0:T(8,128)(2,1)S(1)}, bf16[512,128]{1,0:T(8,128)(2,1)S(1)}, u32[]{:S(2)}, u32[]{:S(2)}) collective-permute-start(bf16[512,128]{1,0:T(8,128)(2,1)S(1)} %get-tuple-element.7), channel_id=1, source_target_pairs={{0,8},{4,12},{8,0},{12,4},{1,9},{5,13},{9,1},{13,5},{2,10},{6,14},... | collective-permute-start | bytes 393224 | tf_op jit(solution)/shard_map/ppermute | solution.py:89
  26.3 0.8 %collective-permute-start.5 = (bf16[512,128]{1,0:T(8,128)(2,1)S(1)}, bf16[512,128]{1,0:T(8,128)(2,1)S(1)}, u32[]{:S(2)}, u32[]{:S(2)}) collective-permute-start(bf16[512,128]{1,0:T(8,128)(2,1)S(1)} %get-tuple-element.6), channel_id=1, source_target_pairs={{0,12},{4,0},{8,4},{12,8},{1,13},{5,1},{9,5},{13,9},{2,14},{6,2},{... | collective-permute-start | bytes 393224 | tf_op jit(solution)/shard_map/ppermute | solution.py:89
  27.1 2.6 %collective-permute-done.3 = bf16[512,128]{1,0:T(8,128)(2,1)S(1)} collective-permute-done((bf16[512,128]{1,0:T(8,128)(2,1)S(1)}, bf16[512,128]{1,0:T(8,128)(2,1)S(1)}, u32[]{:S(2)}, u32[]{:S(2)}) %collective-permute-start.3) | collective-permute-done | bytes 131104 | tf_op jit(solution)/shard_map/ppermute | solution.py:89
  29.7 4.6 %collective-permute-done.4 = bf16[512,128]{1,0:T(8,128)(2,1)S(1)} collective-permute-done((bf16[512,128]{1,0:T(8,128)(2,1)S(1)}, bf16[512,128]{1,0:T(8,128)(2,1)S(1)}, u32[]{:S(2)}, u32[]{:S(2)}) %collective-permute-start.4) | collective-permute-done | bytes 131104 | tf_op jit(solution)/shard_map/ppermute | solution.py:89
  34.4 0.0 collective-permute-done.5
  34.4 0.1 pad_maximum_fusion.1
  34.4 0.0 copy-start.3
  34.4 0.0 copy-start.5
  34.5 0.6 %gather_fusion = bf16[4,512,128]{2,1,0:T(8,128)(2,1)S(1)} fusion(bf16[4,512,128]{2,1,0:T(8,128)(2,1)S(1)} %pad_maximum_fusion.1, s32[1024]{0:T(1024)S(1)} %pad_clamp_fusion), kind=kCustom, calls=%fused_computation | custom fusion | bytes 1048592 | tf_op jit(solution)/shard_map/jit(_take)/gather | solution.py:117
  35.1 0.0 copy-start.1
  35.1 0.0 copy-start.2
  35.1 0.2 copy.16
  35.4 0.1 copy-done.3
  35.5 0.0 copy-done.5
  35.5 0.7 %copy-done.1 = bf16[128,2048]{1,0:T(8,128)(2,1)S(1)} copy-done((bf16[128,2048]{1,0:T(8,128)(2,1)S(1)}, bf16[128,2048]{1,0:T(8,128)(2,1)}, u32[]{:S(2)}) %copy-start.1) | copy-done | bytes 524312
  36.2 0.2 copy-done.2
  36.4 1.2 %fusion.5 = bf16[128,2048]{1,0:T(8,128)(2,1)} fusion(bf16[128,2048]{1,0:T(8,128)(2,1)S(1)} %copy-done.3, bf16[128,2048]{1,0:T(8,128)(2,1)S(1)} %copy-done.1, bf16[128,2048]{1,0:T(8,128)(2,1)S(1)} %copy-done.2, f32[2048]{0:T(1024)S(1)} %copy-done.5, bf16[2048,128]{0,1:T(8,128)(2,1)S(1)} %copy.16, pred[2048]{0:T(1024)(128)(4,1)S(1)} %bitcast.53), kind=kLoop, calls=%fused_computation.9 | loop fusion | flops 2883584 | bytes 2631680 | tf_op jit(solution)/shard_map/convert_element_type | solution.py:120
  (9 shorter events, 0.1 us)
Async XLA Ops:
  0.0 11.2 %copy-start = (f32[64,128]{1,0:T(8,128)S(1)}, f32[64,128]{1,0:T(8,128)}, u32[]{:S(2)}) copy-start(f32[64,128]{1,0:T(8,128)} %param.13) | copy-start | bytes 98308
  1.7 10.5 %collective-permute-start = (bf16[512,128]{1,0:T(8,128)(2,1)S(1)}, bf16[512,128]{1,0:T(8,128)(2,1)S(1)}, u32[]{:S(2)}, u32[]{:S(2)}) collective-permute-start(bf16[512,128]{1,0:T(8,128)(2,1)S(1)} %get-tuple-element.12), channel_id=1, source_target_pairs={{0,4},{4,8},{8,12},{12,0},{1,5},{5,9},{9,13},{13,1},{2,6},{6,10},{... | collective-permute-start | bytes 393224 | tf_op jit(solution)/shard_map/ppermute | solution.py:89
  4.8 11.2 %collective-permute-start.1 = (bf16[512,128]{1,0:T(8,128)(2,1)S(1)}, bf16[512,128]{1,0:T(8,128)(2,1)S(1)}, u32[]{:S(2)}, u32[]{:S(2)}) collective-permute-start(bf16[512,128]{1,0:T(8,128)(2,1)S(1)} %get-tuple-element.11), channel_id=1, source_target_pairs={{0,8},{4,12},{8,0},{12,4},{1,9},{5,13},{9,1},{13,5},{2,10},{6,14},... | collective-permute-start | bytes 393224 | tf_op jit(solution)/shard_map/ppermute | solution.py:89
  7.4 8.6 %collective-permute-start.2 = (bf16[512,128]{1,0:T(8,128)(2,1)S(1)}, bf16[512,128]{1,0:T(8,128)(2,1)S(1)}, u32[]{:S(2)}, u32[]{:S(2)}) collective-permute-start(bf16[512,128]{1,0:T(8,128)(2,1)S(1)} %get-tuple-element.10), channel_id=1, source_target_pairs={{0,12},{4,0},{8,4},{12,8},{1,13},{5,1},{9,5},{13,9},{2,14},{6,2},{... | collective-permute-start | bytes 393224 | tf_op jit(solution)/shard_map/ppermute | solution.py:89
  8.8 0.7 %copy-start.7 = (f32[128]{0:T(128)S(1)}, f32[128]{0:T(128)}, u32[]{:S(2)}) copy-start(f32[128]{0:T(128)} %param.14) | copy-start | bytes 1540
  9.6 0.7 %copy-start.4 = (f32[33,64]{1,0:T(8,128)S(1)}, f32[33,64]{1,0:T(8,128)}, u32[]{:S(2)}) copy-start(f32[33,64]{1,0:T(8,128)} %param.11) | copy-start | bytes 25348
  9.8 0.7 %copy-start.6 = (f32[64]{0:T(128)S(1)}, f32[64]{0:T(128)}, u32[]{:S(2)}) copy-start(f32[64]{0:T(128)} %param.12) | copy-start | bytes 772
  21.3 8.4 %collective-permute-start.3 = (bf16[512,128]{1,0:T(8,128)(2,1)S(1)}, bf16[512,128]{1,0:T(8,128)(2,1)S(1)}, u32[]{:S(2)}, u32[]{:S(2)}) collective-permute-start(bf16[512,128]{1,0:T(8,128)(2,1)S(1)} %get-tuple-element.8), channel_id=1, source_target_pairs={{0,4},{4,8},{8,12},{12,0},{1,5},{5,9},{9,13},{13,1},{2,6},{6,10},{... | collective-permute-start | bytes 393224 | tf_op jit(solution)/shard_map/ppermute | solution.py:89
  24.6 9.7 %collective-permute-start.4 = (bf16[512,128]{1,0:T(8,128)(2,1)S(1)}, bf16[512,128]{1,0:T(8,128)(2,1)S(1)}, u32[]{:S(2)}, u32[]{:S(2)}) collective-permute-start(bf16[512,128]{1,0:T(8,128)(2,1)S(1)} %get-tuple-element.7), channel_id=1, source_target_pairs={{0,8},{4,12},{8,0},{12,4},{1,9},{5,13},{9,1},{13,5},{2,10},{6,14},... | collective-permute-start | bytes 393224 | tf_op jit(solution)/shard_map/ppermute | solution.py:89
  26.3 8.1 %collective-permute-start.5 = (bf16[512,128]{1,0:T(8,128)(2,1)S(1)}, bf16[512,128]{1,0:T(8,128)(2,1)S(1)}, u32[]{:S(2)}, u32[]{:S(2)}) collective-permute-start(bf16[512,128]{1,0:T(8,128)(2,1)S(1)} %get-tuple-element.6), channel_id=1, source_target_pairs={{0,12},{4,0},{8,4},{12,8},{1,13},{5,1},{9,5},{13,9},{2,14},{6,2},{... | collective-permute-start | bytes 393224 | tf_op jit(solution)/shard_map/ppermute | solution.py:89
  34.4 1.0 %copy-start.3 = (bf16[128,2048]{1,0:T(8,128)(2,1)S(1)}, bf16[128,2048]{1,0:T(8,128)(2,1)}, u32[]{:S(2)}) copy-start(bf16[128,2048]{1,0:T(8,128)(2,1)} %param.8) | copy-start | bytes 1572868
  34.4 1.0 %copy-start.5 = (f32[2048]{0:T(1024)S(1)}, f32[2048]{0:T(1024)}, u32[]{:S(2)}) copy-start(f32[2048]{0:T(1024)} %param.15) | copy-start | bytes 24580
  35.1 1.1 %copy-start.1 = (bf16[128,2048]{1,0:T(8,128)(2,1)S(1)}, bf16[128,2048]{1,0:T(8,128)(2,1)}, u32[]{:S(2)}) copy-start(bf16[128,2048]{1,0:T(8,128)(2,1)} %param.10) | copy-start | bytes 1572868
  35.1 1.2 %copy-start.2 = (bf16[128,2048]{1,0:T(8,128)(2,1)S(1)}, bf16[128,2048]{1,0:T(8,128)(2,1)}, u32[]{:S(2)}) copy-start(bf16[128,2048]{1,0:T(8,128)(2,1)} %param.9) | copy-start | bytes 1572868

commit v16 on v10

--- a/solution.py
+++ b/solution.py
@@ -26,18 +26,20 @@
     return (raw * envelope).astype(jnp.bfloat16)
 
 
-def toeplitz_kernel(s_ref, filt_ref, z_ref, o_ref, x_ref, acc_ref):
-    nb = z_ref.shape[0]
+def toeplitz_kernel(s_ref, filt_ref, *refs):
+    nb = filt_ref.shape[0] - 1
+    z_refs = refs[:nb]
+    o_ref, x_ref, acc_ref = refs[nb:]
     fb = filt_ref.shape[1]
-    block = z_ref.shape[2]
+    block = filt_ref.shape[2]
     s = s_ref[0]
     upper = (lax.broadcasted_iota(jnp.int32, (block, block), 1)
              >= lax.broadcasted_iota(jnp.int32, (block, block), 0))
     for g in range(fb):
         ch = slice(g * GROUP, (g + 1) * GROUP)
-        for j in range(nb):
-            x_ref[j * GROUP:(j + 1) * GROUP, :] = z_ref[(s - j + nb) % nb, ch, :]
-        acc_ref[...] = jnp.zeros(acc_ref.shape, jnp.float32)
+        for k in range(nb):
+            j = (s - k + nb) % nb
+            x_ref[pl.ds(pl.multiple_of(j * GROUP, GROUP), GROUP), :] = z_refs[k][ch, :]
         prev = None
         for d in range(nb):
             w = filt_ref[d + 1, pl.ds(g, block, stride=0), :]
@@ -45,17 +47,20 @@
             low = 0.0 if prev is None else prev
             t = jnp.where(upper, cur, low).astype(jnp.bfloat16)
             rows = (nb - d) * GROUP
-            acc_ref[d * GROUP:, :] += jnp.dot(
-                x_ref[:rows, :], t, preferred_element_type=jnp.float32
-            )
+            part = jnp.dot(x_ref[:rows, :], t, preferred_element_type=jnp.float32)
+            if d == 0:
+                acc_ref[...] = part
+            else:
+                acc_ref[d * GROUP:, :] += part
             prev = cur
         for i in range(nb):
             o_ref[(i - s + nb) % nb, ch, :] = (
                 acc_ref[i * GROUP:(i + 1) * GROUP, :].astype(jnp.bfloat16))
 
 
-def toeplitz_conv(s, filt, z):
-    nb, chans, block = z.shape
+def toeplitz_conv(s, filt, pieces):
+    nb = len(pieces)
+    chans, block = pieces[0].shape
     count = chans // GROUP
     fb = min(FILTERS_PER_STEP, count)
     return pl.pallas_call(
@@ -64,15 +69,13 @@
         grid_spec=pltpu.PrefetchScalarGridSpec(
             num_scalar_prefetch=1,
             grid=(count // fb,),
-            in_specs=[
-                pl.BlockSpec((nb + 1, fb, block), lambda i, s_: (0, i, 0)),
-                pl.BlockSpec((nb, fb * GROUP, block), lambda i, s_: (0, i, 0)),
-            ],
+            in_specs=[pl.BlockSpec((nb + 1, fb, block), lambda i, s_: (0, i, 0))]
+            + [pl.BlockSpec((fb * GROUP, block), lambda i, s_: (i, 0))] * nb,
             out_specs=pl.BlockSpec((nb, fb * GROUP, block), lambda i, s_: (0, i, 0)),
             scratch_shapes=[pltpu.VMEM((nb * GROUP, block), jnp.bfloat16),
                             pltpu.VMEM((nb * GROUP, block), jnp.float32)],
         ),
-    )(s, filt, z)
+    )(s, filt, *pieces)
 
 
 def exchange(x, nb, s, ordered):
@@ -83,7 +86,7 @@
         else:
             piece = lax.dynamic_index_in_dim(x, (s + k) % nb, 0, keepdims=False)
         got.append(lax.ppermute(piece, "seq", [(i, (i + k) % nb) for i in range(nb)]))
-    return jnp.stack(got)
+    return got
 
 
 def per_device(
@@ -108,7 +111,7 @@
     filt = jnp.concatenate([jnp.zeros((1, sub, own_rows), jnp.float32), lagged], axis=0)
     s_arr = jnp.reshape(s, (1,)).astype(jnp.int32)
     conv_parts = toeplitz_conv(s_arr, filt, got)
-    back = exchange(conv_parts, nb, s, True)
+    back = jnp.stack(exchange(conv_parts, nb, s, True))
     order = (s - jnp.arange(nb, dtype=jnp.int32) + nb) % nb
     back = jnp.take(back, order, axis=0)
     conv = back.reshape(width, own_rows).T.astype(jnp.float32)

time: 38.2 us -> 39.9 us (1.045)
  waiting for transfers between devices: 11.1 us -> 12.8 us
  local copies, waits for them, and re-layouts: 4.72 us -> 6.05 us
  other arithmetic: 4.42 us -> 3.55 us
    ppermute x6, waiting for transfers between devices: 11.1 us -> 12.8 us  [exchange(): lax.ppermute(piece, 'seq', [(i, (i + k) % nb) for i in range(nb)])]
    another operation x2 -> x1, other arithmetic: 0.93 us -> 0.07 us  [per_device(): back = jnp.stack(exchange(conv_parts, nb, s, True))]
    squeeze x0 -> x1, local copies, waits for them, and re-layouts: none -> 0.69 us  [exchange(): piece = lax.dynamic_index_in_dim(x, (s + k) % nb, 0, keepdims=False)]
    unnamed x18 -> x24, local copies, waits for them, and re-layouts: 2.41 us -> 3.09 us
  transfers between devices with their start and end apart: 6 -> 6, of which waited for: 3 -> 4; matrix products, arithmetic and copies ran while one was open for 6% -> 5% of each run, Pallas kernels for 0% -> 0%
where the time goes in v16:
time: 39.9 us; the launch traced here: 39.6 us
  waiting for transfers between devices  12.8 us (32%)
  starting transfers between devices  12.7 us (32%)
  local copies, waits for them, and re-layouts  6.05 us (15%)
  other arithmetic  3.55 us (9%)
  Pallas kernels  3.25 us (8%)
  matrix products  1.07 us (3%)
    ppermute x6, waiting for transfers between devices, exchange(): lax.ppermute(piece, 'seq', [(i, (i + k) % nb) for i in range(nb)])  12.8 us
    ppermute x6, starting transfers between devices, exchange(): lax.ppermute(piece, 'seq', [(i, (i + k) % nb) for i in range(nb)])  12.7 us
    pallas_call x1, Pallas kernels, toeplitz_conv(): pl.pallas_call(toeplitz_kernel, out_shape=jax.ShapeDtypeStruct((nb, chans...  3.25 us
    unnamed x24, local copies, waits for them, and re-layouts  3.09 us
    transpose x1, other arithmetic, per_device(): gated_t = gated.T.reshape(nb, sub * GROUP, own_rows)  1.33 us
    convert_element_type x1, other arithmetic, per_device(): return mixed.astype(jnp.bfloat16)  1.18 us
    slice x1, local copies, waits for them, and re-layouts, exchange(): x[0]  1.13 us
    gather x2, local copies, waits for them, and re-layouts, per_device(): back = jnp.take(back, order, axis=0)  0.86 us
  transfers between devices with their start and end apart: 6, of which 4 were waited for; matrix products, arithmetic and copies ran while one was open for 5% of the time, Pallas kernels for 0%

profile of v16, /device:TPU:0, one launch (start us, length us, event | category | flops | bytes accessed | tf_op | source)
XLA Modules:
  0.0 39.6 jit_solution(7271252185985711724)
XLA Ops:
  0.0 0.0 copy-start
  0.0 1.3 %fusion.7 = bf16[2048,128]{0,1:T(8,128)(2,1)S(1)} fusion(bf16[128,2048]{1,0:T(8,128)(2,1)} %param.10, bf16[128,2048]{1,0:T(8,128)(2,1)} %param.9), kind=kLoop, calls=%fused_computation.12 | loop fusion | flops 1310720 | bytes 1572864 | tf_op jit(solution)/shard_map/transpose | solution.py:104
  1.3 0.3 copy.26
  1.6 0.7 %dynamic-slice_bitcast_fusion = (bf16[512,128]{1,0:T(8,128)(2,1)S(1)}, bf16[512,128]{1,0:T(8,128)(2,1)S(1)}, bf16[512,128]{1,0:T(8,128)(2,1)S(1)}, bf16[512,128]{1,0:T(8,128)(2,1)}) fusion(bf16[4,512,128]{2,1,0:T(8,128)(2,1)S(1)} %bitcast.43, s32[]{:T(128)S(6)} %select_n.79, s32[]{:T(128)S(6)} %select_n.77, s32[]{:T(128)S(6)} %select_n.75, s32[]{:T(128)S(6)} %select_n.73), kind=kLoop, calls=%fused_computation.17 | loop fusion | bytes 1048592 | tf_op jit(solution)/shard_map/jit(dynamic_index_in_dim)/squeeze | solution.py:87
  2.3 3.1 %collective-permute-start = (bf16[512,128]{1,0:T(8,128)(2,1)S(1)}, bf16[512,128]{1,0:T(8,128)(2,1)S(1)}, u32[]{:S(2)}, u32[]{:S(2)}) collective-permute-start(bf16[512,128]{1,0:T(8,128)(2,1)S(1)} %get-tuple-element.11), channel_id=1, source_target_pairs={{0,4},{4,8},{8,12},{12,0},{1,5},{5,9},{9,13},{13,1},{2,6},{6,10},{... | collective-permute-start | bytes 393224 | tf_op jit(solution)/shard_map/ppermute | solution.py:88
  5.4 2.6 %collective-permute-start.1 = (bf16[512,128]{1,0:T(8,128)(2,1)S(1)}, bf16[512,128]{1,0:T(8,128)(2,1)S(1)}, u32[]{:S(2)}, u32[]{:S(2)}) collective-permute-start(bf16[512,128]{1,0:T(8,128)(2,1)S(1)} %get-tuple-element.10), channel_id=1, source_target_pairs={{0,8},{4,12},{8,0},{12,4},{1,9},{5,13},{9,1},{13,5},{2,10},{6,14},... | collective-permute-start | bytes 393224 | tf_op jit(solution)/shard_map/ppermute | solution.py:88
  8.0 1.3 %collective-permute-start.2 = (bf16[512,128]{1,0:T(8,128)(2,1)S(1)}, bf16[512,128]{1,0:T(8,128)(2,1)S(1)}, u32[]{:S(2)}, u32[]{:S(2)}) collective-permute-start(bf16[512,128]{1,0:T(8,128)(2,1)S(1)} %get-tuple-element.9), channel_id=1, source_target_pairs={{0,12},{4,0},{8,4},{12,8},{1,13},{5,1},{9,5},{13,9},{2,14},{6,2},{... | collective-permute-start | bytes 393224 | tf_op jit(solution)/shard_map/ppermute | solution.py:88
  9.4 0.1 broadcast_bitcast_fusion
  9.4 0.0 copy-start.10
  9.4 0.7 %copy-done.10 = f32[128]{0:T(128)S(1)} copy-done((f32[128]{0:T(128)S(1)}, f32[128]{0:T(128)}, u32[]{:S(2)}) %copy-start.10) | copy-done | bytes 536
  10.1 0.1 multiply_sqrt_fusion
  10.2 0.0 copy-start.7
  10.2 0.2 multiply_cosine_fusion
  10.4 0.0 copy-start.9
  10.4 0.5 %copy-done.7 = f32[33,64]{1,0:T(8,128)S(1)} copy-done((f32[33,64]{1,0:T(8,128)S(1)}, f32[33,64]{1,0:T(8,128)}, u32[]{:S(2)}) %copy-start.7) | copy-done | bytes 8472
  10.9 0.1 copy-done.9
  11.0 0.7 %fusion.1 = f32[512,64]{0,1:T(8,128)S(1)} fusion(f32[33,64]{1,0:T(8,128)S(1)} %copy-done.7, f32[512,16]{0,1:T(8,128)S(1)} %get-tuple-element.14, f32[512,16]{0,1:T(8,128)S(1)} %get-tuple-element.13, f32[512,1]{0,1:T(1,128)S(1)} %convert_multiply_fusion, f32[64]{0:T(128)S(1)} %copy-done.9), kind=kOutput, calls=%fused_computation.3 | convolution fusion | flops 13075456 | bytes 207360 | tf_op jit(solution)/shard_map/dot_general | solution.py:22
  11.8 0.0 copy-done
  11.8 0.3 fusion.3
  12.1 0.6 %pad_convert_fusion.filt_ref = f32[5,32,128]{2,1,0:T(8,128)} fusion(bf16[4,32,128]{2,1,0:T(8,128)(2,1)S(1)} %bitcast.45), kind=kLoop, calls=%fused_computation.28 | loop fusion | flops 20480 | bytes 114688 | tf_op jit(solution)/shard_map/concatenate | solution.py:111
  12.8 0.0 collective-permute-done.refs_1_
  12.8 0.0 copy-start.4
  12.8 3.8 %collective-permute-done.1.refs_2_ = bf16[512,128]{1,0:T(8,128)(2,1)S(1)} collective-permute-done((bf16[512,128]{1,0:T(8,128)(2,1)S(1)}, bf16[512,128]{1,0:T(8,128)(2,1)S(1)}, u32[]{:S(2)}, u32[]{:S(2)}) %collective-permute-start.1) | collective-permute-done | bytes 131104 | tf_op jit(solution)/shard_map/ppermute | solution.py:88
  16.6 0.0 copy-start.5
  16.6 0.0 collective-permute-done.2.refs_3_
  16.6 0.0 copy-start.6
  16.6 0.0 copy-done.4
  16.6 0.6 %copy-done.5 = bf16[512,128]{1,0:T(8,128)(2,1)} copy-done((bf16[512,128]{1,0:T(8,128)(2,1)}, bf16[512,128]{1,0:T(8,128)(2,1)S(1)}, u32[]{:S(2)}) %copy-start.5) | copy-done | bytes 131096
  17.3 0.0 copy-done.6
  17.3 3.2 %shard_map.82 = bf16[4,512,128]{2,1,0:T(8,128)(2,1)} custom-call(s32[1]{0:T(128)} %bitcast.s_ref, f32[5,32,128]{2,1,0:T(8,128)} %pad_convert_fusion.filt_ref, bf16[512,128]{1,0:T(8,128)(2,1)} %get-tuple-element.12.refs_0_, bf16[512,128]{1,0:T(8,128)(2,1)} %copy-done.4, bf16[512,128]{1,0:T(8,128)(2,1)} %copy-done.5, bf16[512,128]{1,0:T(8,128)(2,1)} %copy-done.6), custom_call_target="tpu_custom_call" | custom-call | tf_op jit(solution)/shard_map/pallas_call | solution.py:66
  20.5 1.1 %fusion.19 = (bf16[1,512,128]{2,1,0:T(8,128)(2,1)S(1)}, bf16[512,128]{1,0:T(8,128)(2,1)S(1)}, bf16[512,128]{1,0:T(8,128)(2,1)S(1)}, bf16[512,128]{1,0:T(8,128)(2,1)S(1)}) fusion(bf16[4,512,128]{2,1,0:T(8,128)(2,1)} %shard_map.82), kind=kLoop, calls=%fused_computation.52 | loop fusion | bytes 1048576 | tf_op jit(solution)/shard_map/slice | solution.py:82
  21.7 2.3 %collective-permute-start.4 = (bf16[512,128]{1,0:T(8,128)(2,1)S(1)}, bf16[512,128]{1,0:T(8,128)(2,1)S(1)}, u32[]{:S(2)}, u32[]{:S(2)}) collective-permute-start(bf16[512,128]{1,0:T(8,128)(2,1)S(1)} %get-tuple-element.7), channel_id=1, source_target_pairs={{0,8},{4,12},{8,0},{12,4},{1,9},{5,13},{9,1},{13,5},{2,10},{6,14},... | collective-permute-start | bytes 393224 | tf_op jit(solution)/shard_map/ppermute | solution.py:88
  24.0 3.4 %collective-permute-start.5 = (bf16[512,128]{1,0:T(8,128)(2,1)S(1)}, bf16[512,128]{1,0:T(8,128)(2,1)S(1)}, u32[]{:S(2)}, u32[]{:S(2)}) collective-permute-start(bf16[512,128]{1,0:T(8,128)(2,1)S(1)} %get-tuple-element.6), channel_id=1, source_target_pairs={{0,12},{4,0},{8,4},{12,8},{1,13},{5,1},{9,5},{13,9},{2,14},{6,2},{... | collective-permute-start | bytes 393224 | tf_op jit(solution)/shard_map/ppermute | solution.py:88
  27.4 0.0 collective-permute-start.3
  27.4 3.6 %collective-permute-done.4 = bf16[512,128]{1,0:T(8,128)(2,1)S(1)} collective-permute-done((bf16[512,128]{1,0:T(8,128)(2,1)S(1)}, bf16[512,128]{1,0:T(8,128)(2,1)S(1)}, u32[]{:S(2)}, u32[]{:S(2)}) %collective-permute-start.4) | collective-permute-done | bytes 131104 | tf_op jit(solution)/shard_map/ppermute | solution.py:88
  31.0 0.3 collective-permute-done.5
  31.2 5.2 %collective-permute-done.3 = bf16[512,128]{1,0:T(8,128)(2,1)S(1)} collective-permute-done((bf16[512,128]{1,0:T(8,128)(2,1)S(1)}, bf16[512,128]{1,0:T(8,128)(2,1)S(1)}, u32[]{:S(2)}, u32[]{:S(2)}) %collective-permute-start.3) | collective-permute-done | bytes 131104 | tf_op jit(solution)/shard_map/ppermute | solution.py:88
  36.4 0.1 pad_maximum_fusion
  36.5 0.0 copy-start.3
  36.5 0.0 copy-start.8
  36.5 0.6 %gather_fusion = bf16[4,512,128]{2,1,0:T(8,128)(2,1)S(1)} fusion(bf16[4,512,128]{2,1,0:T(8,128)(2,1)S(1)} %pad_maximum_fusion, s32[1024]{0:T(1024)S(1)} %pad_clamp_fusion), kind=kCustom, calls=%fused_computation | custom fusion | bytes 1048592 | tf_op jit(solution)/shard_map/jit(_take)/gather | solution.py:116
  37.2 0.0 copy-start.1
  37.2 0.0 copy-start.2
  37.2 0.2 copy.25
  37.4 0.1 copy-done.3
  37.5 0.0 copy-done.8
  37.5 0.7 %copy-done.1 = bf16[128,2048]{1,0:T(8,128)(2,1)S(1)} copy-done((bf16[128,2048]{1,0:T(8,128)(2,1)S(1)}, bf16[128,2048]{1,0:T(8,128)(2,1)}, u32[]{:S(2)}) %copy-start.1) | copy-done | bytes 524312
  38.2 0.2 copy-done.2
  38.4 1.2 %fusion.5 = bf16[128,2048]{1,0:T(8,128)(2,1)} fusion(bf16[128,2048]{1,0:T(8,128)(2,1)S(1)} %copy-done.3, bf16[128,2048]{1,0:T(8,128)(2,1)S(1)} %copy-done.1, bf16[128,2048]{1,0:T(8,128)(2,1)S(1)} %copy-done.2, f32[2048]{0:T(1024)S(1)} %copy-done.8, bf16[2048,128]{0,1:T(8,128)(2,1)S(1)} %copy.25, pred[2048]{0:T(1024)(128)(4,1)S(1)} %bitcast.49), kind=kLoop, calls=%fused_computation.9 | loop fusion | flops 2883584 | bytes 2631680 | tf_op jit(solution)/shard_map/convert_element_type | solution.py:119
  (8 shorter events, 0.1 us)
Async XLA Ops:
  0.0 11.8 %copy-start = (f32[64,128]{1,0:T(8,128)S(1)}, f32[64,128]{1,0:T(8,128)}, u32[]{:S(2)}) copy-start(f32[64,128]{1,0:T(8,128)} %param.13) | copy-start | bytes 98308
  2.3 10.5 %collective-permute-start = (bf16[512,128]{1,0:T(8,128)(2,1)S(1)}, bf16[512,128]{1,0:T(8,128)(2,1)S(1)}, u32[]{:S(2)}, u32[]{:S(2)}) collective-permute-start(bf16[512,128]{1,0:T(8,128)(2,1)S(1)} %get-tuple-element.11), channel_id=1, source_target_pairs={{0,4},{4,8},{8,12},{12,0},{1,5},{5,9},{9,13},{13,1},{2,6},{6,10},{... | collective-permute-start | bytes 393224 | tf_op jit(solution)/shard_map/ppermute | solution.py:88
  5.4 11.2 %collective-permute-start.1 = (bf16[512,128]{1,0:T(8,128)(2,1)S(1)}, bf16[512,128]{1,0:T(8,128)(2,1)S(1)}, u32[]{:S(2)}, u32[]{:S(2)}) collective-permute-start(bf16[512,128]{1,0:T(8,128)(2,1)S(1)} %get-tuple-element.10), channel_id=1, source_target_pairs={{0,8},{4,12},{8,0},{12,4},{1,9},{5,13},{9,1},{13,5},{2,10},{6,14},... | collective-permute-start | bytes 393224 | tf_op jit(solution)/shard_map/ppermute | solution.py:88
  8.0 8.6 %collective-permute-start.2 = (bf16[512,128]{1,0:T(8,128)(2,1)S(1)}, bf16[512,128]{1,0:T(8,128)(2,1)S(1)}, u32[]{:S(2)}, u32[]{:S(2)}) collective-permute-start(bf16[512,128]{1,0:T(8,128)(2,1)S(1)} %get-tuple-element.9), channel_id=1, source_target_pairs={{0,12},{4,0},{8,4},{12,8},{1,13},{5,1},{9,5},{13,9},{2,14},{6,2},{... | collective-permute-start | bytes 393224 | tf_op jit(solution)/shard_map/ppermute | solution.py:88
  9.4 0.7 %copy-start.10 = (f32[128]{0:T(128)S(1)}, f32[128]{0:T(128)}, u32[]{:S(2)}) copy-start(f32[128]{0:T(128)} %param.14) | copy-start | bytes 1540
  10.2 0.7 %copy-start.7 = (f32[33,64]{1,0:T(8,128)S(1)}, f32[33,64]{1,0:T(8,128)}, u32[]{:S(2)}) copy-start(f32[33,64]{1,0:T(8,128)} %param.11) | copy-start | bytes 25348
  10.4 0.7 %copy-start.9 = (f32[64]{0:T(128)S(1)}, f32[64]{0:T(128)}, u32[]{:S(2)}) copy-start(f32[64]{0:T(128)} %param.12) | copy-start | bytes 772
  12.8 3.8 %copy-start.4 = (bf16[512,128]{1,0:T(8,128)(2,1)}, bf16[512,128]{1,0:T(8,128)(2,1)S(1)}, u32[]{:S(2)}) copy-start(bf16[512,128]{1,0:T(8,128)(2,1)S(1)} %collective-permute-done.refs_1_) | copy-start | bytes 393220
  16.6 0.6 %copy-start.5 = (bf16[512,128]{1,0:T(8,128)(2,1)}, bf16[512,128]{1,0:T(8,128)(2,1)S(1)}, u32[]{:S(2)}) copy-start(bf16[512,128]{1,0:T(8,128)(2,1)S(1)} %collective-permute-done.1.refs_2_) | copy-start | bytes 393220
  16.6 0.7 %copy-start.6 = (bf16[512,128]{1,0:T(8,128)(2,1)}, bf16[512,128]{1,0:T(8,128)(2,1)S(1)}, u32[]{:S(2)}) copy-start(bf16[512,128]{1,0:T(8,128)(2,1)S(1)} %collective-permute-done.2.refs_3_) | copy-start | bytes 393220
  21.7 9.3 %collective-permute-start.4 = (bf16[512,128]{1,0:T(8,128)(2,1)S(1)}, bf16[512,128]{1,0:T(8,128)(2,1)S(1)}, u32[]{:S(2)}, u32[]{:S(2)}) collective-permute-start(bf16[512,128]{1,0:T(8,128)(2,1)S(1)} %get-tuple-element.7), channel_id=1, source_target_pairs={{0,8},{4,12},{8,0},{12,4},{1,9},{5,13},{9,1},{13,5},{2,10},{6,14},... | collective-permute-start | bytes 393224 | tf_op jit(solution)/shard_map/ppermute | solution.py:88
  24.0 7.3 %collective-permute-start.5 = (bf16[512,128]{1,0:T(8,128)(2,1)S(1)}, bf16[512,128]{1,0:T(8,128)(2,1)S(1)}, u32[]{:S(2)}, u32[]{:S(2)}) collective-permute-start(bf16[512,128]{1,0:T(8,128)(2,1)S(1)} %get-tuple-element.6), channel_id=1, source_target_pairs={{0,12},{4,0},{8,4},{12,8},{1,13},{5,1},{9,5},{13,9},{2,14},{6,2},{... | collective-permute-start | bytes 393224 | tf_op jit(solution)/shard_map/ppermute | solution.py:88
  27.4 9.1 %collective-permute-start.3 = (bf16[512,128]{1,0:T(8,128)(2,1)S(1)}, bf16[512,128]{1,0:T(8,128)(2,1)S(1)}, u32[]{:S(2)}, u32[]{:S(2)}) collective-permute-start(bf16[512,128]{1,0:T(8,128)(2,1)S(1)} %get-tuple-element.8), channel_id=1, source_target_pairs={{0,4},{4,8},{8,12},{12,0},{1,5},{5,9},{9,13},{13,1},{2,6},{6,10},{... | collective-permute-start | bytes 393224 | tf_op jit(solution)/shard_map/ppermute | solution.py:88
  36.5 1.0 %copy-start.3 = (bf16[128,2048]{1,0:T(8,128)(2,1)S(1)}, bf16[128,2048]{1,0:T(8,128)(2,1)}, u32[]{:S(2)}) copy-start(bf16[128,2048]{1,0:T(8,128)(2,1)} %param.8) | copy-start | bytes 1572868
  36.5 1.0 %copy-start.8 = (f32[2048]{0:T(1024)S(1)}, f32[2048]{0:T(1024)}, u32[]{:S(2)}) copy-start(f32[2048]{0:T(1024)} %param.15) | copy-start | bytes 24580
  37.2 1.1 %copy-start.1 = (bf16[128,2048]{1,0:T(8,128)(2,1)S(1)}, bf16[128,2048]{1,0:T(8,128)(2,1)}, u32[]{:S(2)}) copy-start(bf16[128,2048]{1,0:T(8,128)(2,1)} %param.10) | copy-start | bytes 1572868
  37.2 1.2 %copy-start.2 = (bf16[128,2048]{1,0:T(8,128)(2,1)S(1)}, bf16[128,2048]{1,0:T(8,128)(2,1)}, u32[]{:S(2)}) copy-start(bf16[128,2048]{1,0:T(8,128)(2,1)} %param.9) | copy-start | bytes 1572868

commit v17 on v10

--- a/solution.py
+++ b/solution.py
@@ -26,8 +26,10 @@
     return (raw * envelope).astype(jnp.bfloat16)
 
 
-def toeplitz_kernel(s_ref, filt_ref, z_ref, o_ref, x_ref, acc_ref):
+def toeplitz_kernel(s_ref, filt_ref, z_ref, *refs):
     nb = z_ref.shape[0]
+    o_refs = refs[:nb]
+    x_ref, acc_ref = refs[nb:]
     fb = filt_ref.shape[1]
     block = z_ref.shape[2]
     s = s_ref[0]
@@ -49,9 +51,10 @@
                 x_ref[:rows, :], t, preferred_element_type=jnp.float32
             )
             prev = cur
-        for i in range(nb):
-            o_ref[(i - s + nb) % nb, ch, :] = (
-                acc_ref[i * GROUP:(i + 1) * GROUP, :].astype(jnp.bfloat16))
+        for k in range(nb):
+            i = (s + k) % nb
+            o_refs[k][ch, :] = acc_ref[pl.ds(pl.multiple_of(i * GROUP, GROUP), GROUP), :].astype(
+                jnp.bfloat16)
 
 
 def toeplitz_conv(s, filt, z):
@@ -60,7 +63,7 @@
     fb = min(FILTERS_PER_STEP, count)
     return pl.pallas_call(
         toeplitz_kernel,
-        out_shape=jax.ShapeDtypeStruct((nb, chans, block), jnp.bfloat16),
+        out_shape=[jax.ShapeDtypeStruct((chans, block), jnp.bfloat16) for _ in range(nb)],
         grid_spec=pltpu.PrefetchScalarGridSpec(
             num_scalar_prefetch=1,
             grid=(count // fb,),
@@ -68,7 +71,7 @@
                 pl.BlockSpec((nb + 1, fb, block), lambda i, s_: (0, i, 0)),
                 pl.BlockSpec((nb, fb * GROUP, block), lambda i, s_: (0, i, 0)),
             ],
-            out_specs=pl.BlockSpec((nb, fb * GROUP, block), lambda i, s_: (0, i, 0)),
+            out_specs=[pl.BlockSpec((fb * GROUP, block), lambda i, s_: (i, 0))] * nb,
             scratch_shapes=[pltpu.VMEM((nb * GROUP, block), jnp.bfloat16),
                             pltpu.VMEM((nb * GROUP, block), jnp.float32)],
         ),

time: 38.2 us -> 38.1 us (level)
  local copies, waits for them, and re-layouts: 4.72 us -> 3.59 us
  other arithmetic: 4.42 us -> 5.32 us
    slice x1 -> x0, local copies, waits for them, and re-layouts: 1.13 us -> none  [exchange(): x[0]]
    another operation x2, other arithmetic: 0.93 us -> 1.83 us  [exchange(): return jnp.stack(got)]
where the time goes in v17:
time: 38.1 us; the launch traced here: 37.5 us
  starting transfers between devices  12.8 us (34%)
  waiting for transfers between devices  11.3 us (30%)
  other arithmetic  5.32 us (14%)
  local copies, waits for them, and re-layouts  3.59 us (9%)
  Pallas kernels  3.26 us (9%)
  matrix products  1.07 us (3%)
    ppermute x6, starting transfers between devices, exchange(): lax.ppermute(piece, 'seq', [(i, (i + k) % nb) for i in range(nb)])  12.8 us
    ppermute x6, waiting for transfers between devices, exchange(): lax.ppermute(piece, 'seq', [(i, (i + k) % nb) for i in range(nb)])  11.3 us
    pallas_call x1, Pallas kernels, toeplitz_conv(): pl.pallas_call(toeplitz_kernel, out_shape=[jax.ShapeDtypeStruct((chans, b...  3.26 us
    unnamed x18, local copies, waits for them, and re-layouts  2.41 us
    another operation x2, other arithmetic, exchange(): return jnp.stack(got)  1.83 us
    transpose x1, other arithmetic, per_device(): gated_t = gated.T.reshape(nb, sub * GROUP, own_rows)  1.33 us
    convert_element_type x1, other arithmetic, per_device(): return mixed.astype(jnp.bfloat16)  1.18 us
    gather x2, local copies, waits for them, and re-layouts, per_device(): back = jnp.take(back, order, axis=0)  0.86 us
  transfers between devices with their start and end apart: 6, of which 3 were waited for; matrix products, arithmetic and copies ran while one was open for 6% of the time, Pallas kernels for 0%

profile of v17, /device:TPU:0, one launch (start us, length us, event | category | flops | bytes accessed | tf_op | source)
XLA Modules:
  0.0 37.5 jit_solution(15061051932177641397)
XLA Ops:
  0.0 0.0 copy-start
  0.0 1.3 %fusion.7 = bf16[2048,128]{0,1:T(8,128)(2,1)S(1)} fusion(bf16[128,2048]{1,0:T(8,128)(2,1)} %param.10, bf16[128,2048]{1,0:T(8,128)(2,1)} %param.9), kind=kLoop, calls=%fused_computation.12 | loop fusion | flops 1310720 | bytes 1572864 | tf_op jit(solution)/shard_map/transpose | solution.py:104
  1.3 0.3 copy.15
  1.7 3.1 %collective-permute-start = (bf16[512,128]{1,0:T(8,128)(2,1)S(1)}, bf16[512,128]{1,0:T(8,128)(2,1)S(1)}, u32[]{:S(2)}, u32[]{:S(2)}) collective-permute-start(bf16[512,128]{1,0:T(8,128)(2,1)S(1)} %get-tuple-element.16), channel_id=1, source_target_pairs={{0,4},{4,8},{8,12},{12,0},{1,5},{5,9},{9,13},{13,1},{2,6},{6,10},{... | collective-permute-start | bytes 393224 | tf_op jit(solution)/shard_map/ppermute | solution.py:88
  4.8 2.6 %collective-permute-start.1 = (bf16[512,128]{1,0:T(8,128)(2,1)S(1)}, bf16[512,128]{1,0:T(8,128)(2,1)S(1)}, u32[]{:S(2)}, u32[]{:S(2)}) collective-permute-start(bf16[512,128]{1,0:T(8,128)(2,1)S(1)} %get-tuple-element.15), channel_id=1, source_target_pairs={{0,8},{4,12},{8,0},{12,4},{1,9},{5,13},{9,1},{13,5},{2,10},{6,14},... | collective-permute-start | bytes 393224 | tf_op jit(solution)/shard_map/ppermute | solution.py:88
  7.4 1.3 %collective-permute-start.2 = (bf16[512,128]{1,0:T(8,128)(2,1)S(1)}, bf16[512,128]{1,0:T(8,128)(2,1)S(1)}, u32[]{:S(2)}, u32[]{:S(2)}) collective-permute-start(bf16[512,128]{1,0:T(8,128)(2,1)S(1)} %get-tuple-element.14), channel_id=1, source_target_pairs={{0,12},{4,0},{8,4},{12,8},{1,13},{5,1},{9,5},{13,9},{2,14},{6,2},{... | collective-permute-start | bytes 393224 | tf_op jit(solution)/shard_map/ppermute | solution.py:88
  8.8 0.1 broadcast_bitcast_fusion
  8.8 0.0 copy-start.7
  8.9 0.7 %copy-done.7 = f32[128]{0:T(128)S(1)} copy-done((f32[128]{0:T(128)S(1)}, f32[128]{0:T(128)}, u32[]{:S(2)}) %copy-start.7) | copy-done | bytes 536
  9.5 0.1 multiply_sqrt_fusion
  9.6 0.0 copy-start.4
  9.6 0.2 multiply_cosine_fusion
  9.8 0.0 copy-start.6
  9.8 0.5 %copy-done.4 = f32[33,64]{1,0:T(8,128)S(1)} copy-done((f32[33,64]{1,0:T(8,128)S(1)}, f32[33,64]{1,0:T(8,128)}, u32[]{:S(2)}) %copy-start.4) | copy-done | bytes 8472
  10.3 0.1 copy-done.6
  10.4 0.7 %fusion.1 = f32[512,64]{0,1:T(8,128)S(1)} fusion(f32[33,64]{1,0:T(8,128)S(1)} %copy-done.4, f32[512,16]{0,1:T(8,128)S(1)} %get-tuple-element.18, f32[512,16]{0,1:T(8,128)S(1)} %get-tuple-element.17, f32[512,1]{0,1:T(1,128)S(1)} %convert_multiply_fusion, f32[64]{0:T(128)S(1)} %copy-done.6), kind=kOutput, calls=%fused_computation.3 | convolution fusion | flops 13075456 | bytes 207360 | tf_op jit(solution)/shard_map/dot_general | solution.py:22
  11.2 0.0 copy-done
  11.2 0.3 fusion.3
  11.6 0.6 %pad_convert_fusion.filt_ref = f32[5,32,128]{2,1,0:T(8,128)} fusion(bf16[4,32,128]{2,1,0:T(8,128)(2,1)S(1)} %bitcast.41), kind=kLoop, calls=%fused_computation.25 | loop fusion | flops 20480 | bytes 114688 | tf_op jit(solution)/shard_map/concatenate | solution.py:111
  12.2 0.0 collective-permute-done
  12.2 3.8 %collective-permute-done.1 = bf16[512,128]{1,0:T(8,128)(2,1)S(1)} collective-permute-done((bf16[512,128]{1,0:T(8,128)(2,1)S(1)}, bf16[512,128]{1,0:T(8,128)(2,1)S(1)}, u32[]{:S(2)}, u32[]{:S(2)}) %collective-permute-start.1) | collective-permute-done | bytes 131104 | tf_op jit(solution)/shard_map/ppermute | solution.py:88
  16.0 0.0 collective-permute-done.2
  16.0 0.9 %pad_maximum_fusion.z_ref = bf16[4,512,128]{2,1,0:T(8,128)(2,1)} fusion(bf16[1,512,128]{2,1,0:T(8,128)(2,1)S(1)} %bitcast.44, bf16[1,512,128]{2,1,0:T(8,128)(2,1)S(1)} %bitcast.43, bf16[1,512,128]{2,1,0:T(8,128)(2,1)S(1)} %bitcast.42, bf16[1,512,128]{2,1,0:T(8,128)(2,1)S(1)} %get-tuple-element.13), kind=kLoop, calls=%fused_computation.13 | loop fusion | flops 786432 | bytes 1048576 | tf_op jit(solution)/shard_map/stack | solution.py:89
  16.9 3.3 %shard_map.82 = (bf16[512,128]{1,0:T(8,128)(2,1)}, bf16[512,128]{1,0:T(8,128)(2,1)}, bf16[512,128]{1,0:T(8,128)(2,1)}, bf16[512,128]{1,0:T(8,128)(2,1)}) custom-call(s32[1]{0:T(128)} %bitcast.s_ref, f32[5,32,128]{2,1,0:T(8,128)} %pad_convert_fusion.filt_ref, bf16[4,512,128]{2,1,0:T(8,128)(2,1)} %pad_maximum_fusion.z_ref), custom_call_target="tpu_custom_call" | custom-call | tf_op jit(solution)/shard_map/pallas_call | solution.py:64
  20.1 3.3 %collective-permute-start.3 = (bf16[512,128]{1,0:T(8,128)(2,1)}, bf16[512,128]{1,0:T(8,128)(2,1)S(1)}, u32[]{:S(2)}, u32[]{:S(2)}) collective-permute-start(bf16[512,128]{1,0:T(8,128)(2,1)} %get-tuple-element.10), channel_id=1, source_target_pairs={{0,4},{4,8},{8,12},{12,0},{1,5},{5,9},{9,13},{13,1},{2,6},{6,10},{... | collective-permute-start | bytes 393224 | tf_op jit(solution)/shard_map/ppermute | solution.py:88
  23.5 1.6 %collective-permute-start.4 = (bf16[512,128]{1,0:T(8,128)(2,1)}, bf16[512,128]{1,0:T(8,128)(2,1)S(1)}, u32[]{:S(2)}, u32[]{:S(2)}) collective-permute-start(bf16[512,128]{1,0:T(8,128)(2,1)} %get-tuple-element.11), channel_id=1, source_target_pairs={{0,8},{4,12},{8,0},{12,4},{1,9},{5,13},{9,1},{13,5},{2,10},{6,14},... | collective-permute-start | bytes 393224 | tf_op jit(solution)/shard_map/ppermute | solution.py:88
  25.1 0.8 %collective-permute-start.5 = (bf16[512,128]{1,0:T(8,128)(2,1)}, bf16[512,128]{1,0:T(8,128)(2,1)S(1)}, u32[]{:S(2)}, u32[]{:S(2)}) collective-permute-start(bf16[512,128]{1,0:T(8,128)(2,1)} %get-tuple-element.12), channel_id=1, source_target_pairs={{0,12},{4,0},{8,4},{12,8},{1,13},{5,1},{9,5},{13,9},{2,14},{6,2},{... | collective-permute-start | bytes 393224 | tf_op jit(solution)/shard_map/ppermute | solution.py:88
  25.9 2.8 %collective-permute-done.3 = bf16[512,128]{1,0:T(8,128)(2,1)S(1)} collective-permute-done((bf16[512,128]{1,0:T(8,128)(2,1)}, bf16[512,128]{1,0:T(8,128)(2,1)S(1)}, u32[]{:S(2)}, u32[]{:S(2)}) %collective-permute-start.3) | collective-permute-done | bytes 131104 | tf_op jit(solution)/shard_map/ppermute | solution.py:88
  28.7 4.7 %collective-permute-done.4 = bf16[512,128]{1,0:T(8,128)(2,1)S(1)} collective-permute-done((bf16[512,128]{1,0:T(8,128)(2,1)}, bf16[512,128]{1,0:T(8,128)(2,1)S(1)}, u32[]{:S(2)}, u32[]{:S(2)}) %collective-permute-start.4) | collective-permute-done | bytes 131104 | tf_op jit(solution)/shard_map/ppermute | solution.py:88
  33.4 0.0 collective-permute-done.5
  33.4 1.0 %pad_maximum_fusion.1 = bf16[4,512,128]{2,1,0:T(8,128)(2,1)S(1)} fusion(bf16[1,512,128]{2,1,0:T(8,128)(2,1)S(1)} %bitcast.48, bf16[1,512,128]{2,1,0:T(8,128)(2,1)S(1)} %bitcast.47, bf16[1,512,128]{2,1,0:T(8,128)(2,1)S(1)} %bitcast.46, bf16[1,512,128]{2,1,0:T(8,128)(2,1)} %bitcast.45), kind=kLoop, calls=%fused_computation.14 | loop fusion | flops 786432 | bytes 1048576 | tf_op jit(solution)/shard_map/stack | solution.py:89
  34.4 0.0 copy-start.3
  34.4 0.0 copy-start.5
  34.4 0.6 %gather_fusion = bf16[4,512,128]{2,1,0:T(8,128)(2,1)S(1)} fusion(bf16[4,512,128]{2,1,0:T(8,128)(2,1)S(1)} %pad_maximum_fusion.1, s32[1024]{0:T(1024)S(1)} %pad_clamp_fusion), kind=kCustom, calls=%fused_computation | custom fusion | bytes 1048592 | tf_op jit(solution)/shard_map/jit(_take)/gather | solution.py:116
  35.0 0.0 copy-start.1
  35.0 0.0 copy-start.2
  35.1 0.2 copy.16
  35.3 0.1 copy-done.3
  35.4 0.0 copy-done.5
  35.4 0.7 %copy-done.1 = bf16[128,2048]{1,0:T(8,128)(2,1)S(1)} copy-done((bf16[128,2048]{1,0:T(8,128)(2,1)S(1)}, bf16[128,2048]{1,0:T(8,128)(2,1)}, u32[]{:S(2)}) %copy-start.1) | copy-done | bytes 524312
  36.1 0.2 copy-done.2
  36.3 1.2 %fusion.5 = bf16[128,2048]{1,0:T(8,128)(2,1)} fusion(bf16[128,2048]{1,0:T(8,128)(2,1)S(1)} %copy-done.3, bf16[128,2048]{1,0:T(8,128)(2,1)S(1)} %copy-done.1, bf16[128,2048]{1,0:T(8,128)(2,1)S(1)} %copy-done.2, f32[2048]{0:T(1024)S(1)} %copy-done.5, bf16[2048,128]{0,1:T(8,128)(2,1)S(1)} %copy.16, pred[2048]{0:T(1024)(128)(4,1)S(1)} %bitcast.49), kind=kLoop, calls=%fused_computation.9 | loop fusion | flops 2883584 | bytes 2631680 | tf_op jit(solution)/shard_map/convert_element_type | solution.py:119
  (9 shorter events, 0.1 us)
Async XLA Ops:
  0.0 11.2 %copy-start = (f32[64,128]{1,0:T(8,128)S(1)}, f32[64,128]{1,0:T(8,128)}, u32[]{:S(2)}) copy-start(f32[64,128]{1,0:T(8,128)} %param.13) | copy-start | bytes 98308
  1.7 10.5 %collective-permute-start = (bf16[512,128]{1,0:T(8,128)(2,1)S(1)}, bf16[512,128]{1,0:T(8,128)(2,1)S(1)}, u32[]{:S(2)}, u32[]{:S(2)}) collective-permute-start(bf16[512,128]{1,0:T(8,128)(2,1)S(1)} %get-tuple-element.16), channel_id=1, source_target_pairs={{0,4},{4,8},{8,12},{12,0},{1,5},{5,9},{9,13},{13,1},{2,6},{6,10},{... | collective-permute-start | bytes 393224 | tf_op jit(solution)/shard_map/ppermute | solution.py:88
  4.8 11.2 %collective-permute-start.1 = (bf16[512,128]{1,0:T(8,128)(2,1)S(1)}, bf16[512,128]{1,0:T(8,128)(2,1)S(1)}, u32[]{:S(2)}, u32[]{:S(2)}) collective-permute-start(bf16[512,128]{1,0:T(8,128)(2,1)S(1)} %get-tuple-element.15), channel_id=1, source_target_pairs={{0,8},{4,12},{8,0},{12,4},{1,9},{5,13},{9,1},{13,5},{2,10},{6,14},... | collective-permute-start | bytes 393224 | tf_op jit(solution)/shard_map/ppermute | solution.py:88
  7.4 8.6 %collective-permute-start.2 = (bf16[512,128]{1,0:T(8,128)(2,1)S(1)}, bf16[512,128]{1,0:T(8,128)(2,1)S(1)}, u32[]{:S(2)}, u32[]{:S(2)}) collective-permute-start(bf16[512,128]{1,0:T(8,128)(2,1)S(1)} %get-tuple-element.14), channel_id=1, source_target_pairs={{0,12},{4,0},{8,4},{12,8},{1,13},{5,1},{9,5},{13,9},{2,14},{6,2},{... | collective-permute-start | bytes 393224 | tf_op jit(solution)/shard_map/ppermute | solution.py:88
  8.8 0.7 %copy-start.7 = (f32[128]{0:T(128)S(1)}, f32[128]{0:T(128)}, u32[]{:S(2)}) copy-start(f32[128]{0:T(128)} %param.14) | copy-start | bytes 1540
  9.6 0.7 %copy-start.4 = (f32[33,64]{1,0:T(8,128)S(1)}, f32[33,64]{1,0:T(8,128)}, u32[]{:S(2)}) copy-start(f32[33,64]{1,0:T(8,128)} %param.11) | copy-start | bytes 25348
  9.8 0.7 %copy-start.6 = (f32[64]{0:T(128)S(1)}, f32[64]{0:T(128)}, u32[]{:S(2)}) copy-start(f32[64]{0:T(128)} %param.12) | copy-start | bytes 772
  20.1 8.6 %collective-permute-start.3 = (bf16[512,128]{1,0:T(8,128)(2,1)}, bf16[512,128]{1,0:T(8,128)(2,1)S(1)}, u32[]{:S(2)}, u32[]{:S(2)}) collective-permute-start(bf16[512,128]{1,0:T(8,128)(2,1)} %get-tuple-element.10), channel_id=1, source_target_pairs={{0,4},{4,8},{8,12},{12,0},{1,5},{5,9},{9,13},{13,1},{2,6},{6,10},{... | collective-permute-start | bytes 393224 | tf_op jit(solution)/shard_map/ppermute | solution.py:88
  23.5 9.9 %collective-permute-start.4 = (bf16[512,128]{1,0:T(8,128)(2,1)}, bf16[512,128]{1,0:T(8,128)(2,1)S(1)}, u32[]{:S(2)}, u32[]{:S(2)}) collective-permute-start(bf16[512,128]{1,0:T(8,128)(2,1)} %get-tuple-element.11), channel_id=1, source_target_pairs={{0,8},{4,12},{8,0},{12,4},{1,9},{5,13},{9,1},{13,5},{2,10},{6,14},... | collective-permute-start | bytes 393224 | tf_op jit(solution)/shard_map/ppermute | solution.py:88
  25.1 8.3 %collective-permute-start.5 = (bf16[512,128]{1,0:T(8,128)(2,1)}, bf16[512,128]{1,0:T(8,128)(2,1)S(1)}, u32[]{:S(2)}, u32[]{:S(2)}) collective-permute-start(bf16[512,128]{1,0:T(8,128)(2,1)} %get-tuple-element.12), channel_id=1, source_target_pairs={{0,12},{4,0},{8,4},{12,8},{1,13},{5,1},{9,5},{13,9},{2,14},{6,2},{... | collective-permute-start | bytes 393224 | tf_op jit(solution)/shard_map/ppermute | solution.py:88
  34.4 1.0 %copy-start.3 = (bf16[128,2048]{1,0:T(8,128)(2,1)S(1)}, bf16[128,2048]{1,0:T(8,128)(2,1)}, u32[]{:S(2)}) copy-start(bf16[128,2048]{1,0:T(8,128)(2,1)} %param.8) | copy-start | bytes 1572868
  34.4 1.0 %copy-start.5 = (f32[2048]{0:T(1024)S(1)}, f32[2048]{0:T(1024)}, u32[]{:S(2)}) copy-start(f32[2048]{0:T(1024)} %param.15) | copy-start | bytes 24580
  35.0 1.1 %copy-start.1 = (bf16[128,2048]{1,0:T(8,128)(2,1)S(1)}, bf16[128,2048]{1,0:T(8,128)(2,1)}, u32[]{:S(2)}) copy-start(bf16[128,2048]{1,0:T(8,128)(2,1)} %param.10) | copy-start | bytes 1572868
  35.0 1.2 %copy-start.2 = (bf16[128,2048]{1,0:T(8,128)(2,1)S(1)}, bf16[128,2048]{1,0:T(8,128)(2,1)}, u32[]{:S(2)}) copy-start(bf16[128,2048]{1,0:T(8,128)(2,1)} %param.9) | copy-start | bytes 1572868

commit v18 on v17

--- a/solution.py
+++ b/solution.py
@@ -86,7 +86,7 @@
         else:
             piece = lax.dynamic_index_in_dim(x, (s + k) % nb, 0, keepdims=False)
         got.append(lax.ppermute(piece, "seq", [(i, (i + k) % nb) for i in range(nb)]))
-    return jnp.stack(got)
+    return got
 
 
 def per_device(
@@ -110,10 +110,16 @@
     lagged = filters.astype(jnp.float32).reshape(nb, own_rows, sub).transpose(0, 2, 1)
     filt = jnp.concatenate([jnp.zeros((1, sub, own_rows), jnp.float32), lagged], axis=0)
     s_arr = jnp.reshape(s, (1,)).astype(jnp.int32)
-    conv_parts = toeplitz_conv(s_arr, filt, got)
+    conv_parts = toeplitz_conv(s_arr, filt, jnp.stack(got))
     back = exchange(conv_parts, nb, s, True)
-    order = (s - jnp.arange(nb, dtype=jnp.int32) + nb) % nb
-    back = jnp.take(back, order, axis=0)
+    chunks = []
+    for c in range(nb):
+        src_k = (s - c + nb) % nb
+        piece = back[0]
+        for k in range(1, nb):
+            piece = jnp.where(src_k == k, back[k], piece)
+        chunks.append(piece)
+    back = jnp.concatenate(chunks, axis=0)
     conv = back.reshape(width, own_rows).T.astype(jnp.float32)
     mixed = outer_gate.astype(jnp.float32) * (conv + skip_gain[None, :] * gated_f)
     return mixed.astype(jnp.bfloat16)

time: 38.1 us -> 38.2 us (level)
  waiting for transfers between devices: 11.3 us -> 17 us
  starting transfers between devices: 12.8 us -> 9.04 us
  other arithmetic: 5.32 us -> 2.46 us
  local copies, waits for them, and re-layouts: 3.59 us -> 4.9 us
    ppermute x6, waiting for transfers between devices: 11.3 us -> 17 us  [exchange(): lax.ppermute(piece, 'seq', [(i, (i + k) % nb) for i in range(nb)])]
    ppermute x6, starting transfers between devices: 12.8 us -> 9.04 us  [exchange(): lax.ppermute(piece, 'seq', [(i, (i + k) % nb) for i in range(nb)])]
    unnamed x18 -> x19, local copies, waits for them, and re-layouts: 2.41 us -> 3.84 us
    transpose x1 -> x0, other arithmetic: 1.33 us -> none  [per_device(): gated_t = gated.T.reshape(nb, sub * GROUP, own_rows)]
    convert_element_type x0 -> x1, local copies, waits for them, and re-layouts: none -> 1.01 us  [per_device(): return mixed.astype(jnp.bfloat16)]
    another operation x2 -> x1, other arithmetic: 1.83 us -> 0.86 us  [per_device(): conv_parts = toeplitz_conv(s_arr, filt, jnp.stack(got))]
    gather x2 -> x0, local copies, waits for them, and re-layouts: 0.86 us -> none  [per_device(): back = jnp.take(back, order, axis=0)]
    convert_element_type x1, other arithmetic: 1.18 us -> 0.45 us  [per_device(): return mixed.astype(jnp.bfloat16)]
  transfers between devices with their start and end apart: 6 -> 6, of which waited for: 3 -> 4; matrix products, arithmetic and copies ran while one was open for 6% -> 6% of each run, Pallas kernels for 0% -> 0%
where the time goes in v18:
time: 38.2 us; the launch traced here: 37.9 us
  waiting for transfers between devices  17 us (45%)
  starting transfers between devices  9.04 us (24%)
  local copies, waits for them, and re-layouts  4.9 us (13%)
  Pallas kernels  3.33 us (9%)
  other arithmetic  2.46 us (6%)
  matrix products  1.07 us (3%)
    ppermute x6, waiting for transfers between devices, exchange(): lax.ppermute(piece, 'seq', [(i, (i + k) % nb) for i in range(nb)])  17 us
    ppermute x6, starting transfers between devices, exchange(): lax.ppermute(piece, 'seq', [(i, (i + k) % nb) for i in range(nb)])  9.04 us
    unnamed x19, local copies, waits for them, and re-layouts  3.84 us
    pallas_call x1, Pallas kernels, toeplitz_conv(): pl.pallas_call(toeplitz_kernel, out_shape=[jax.ShapeDtypeStruct((chans, b...  3.33 us
    convert_element_type x1, local copies, waits for them, and re-layouts, per_device(): return mixed.astype(jnp.bfloat16)  1.01 us
    another operation x1, other arithmetic, per_device(): conv_parts = toeplitz_conv(s_arr, filt, jnp.stack(got))  0.86 us
  transfers between devices with their start and end apart: 6, of which 4 were waited for; matrix products, arithmetic and copies ran while one was open for 6% of the time, Pallas kernels for 0%

profile of v18, /device:TPU:0, one launch (start us, length us, event | category | flops | bytes accessed | tf_op | source)
XLA Modules:
  0.0 37.9 jit_solution(2903674203346327762)
XLA Ops:
  0.0 0.0 copy-start
  0.0 0.0 copy-start.1
  0.0 1.4 %copy.20 = bf16[128,2048]{0,1:T(8,128)(2,1)S(1)} copy(bf16[128,2048]{1,0:T(8,128)(2,1)} %param.9) | data formatting | bytes 1048576 | tf_op args[1]
  1.4 0.0 copy-done.1
  1.4 0.3 copy.21
  1.7 0.1 fusion.6
  1.9 5.1 %collective-permute-start.2 = (bf16[512,128]{1,0:T(8,128)(2,1)S(1)}, bf16[512,128]{1,0:T(8,128)(2,1)S(1)}, u32[]{:S(2)}, u32[]{:S(2)}) collective-permute-start(bf16[512,128]{1,0:T(8,128)(2,1)S(1)} %get-tuple-element.18), channel_id=1, source_target_pairs={{0,12},{4,0},{8,4},{12,8},{1,13},{5,1},{9,5},{13,9},{2,14},{6,2},{... | collective-permute-start | bytes 393224 | tf_op jit(solution)/shard_map/ppermute | solution.py:88
  7.0 0.0 collective-permute-start
  7.0 1.0 %collective-permute-start.1 = (bf16[512,128]{1,0:T(8,128)(2,1)S(1)}, bf16[512,128]{1,0:T(8,128)(2,1)S(1)}, u32[]{:S(2)}, u32[]{:S(2)}) collective-permute-start(bf16[512,128]{1,0:T(8,128)(2,1)S(1)} %get-tuple-element.19), channel_id=1, source_target_pairs={{0,8},{4,12},{8,0},{12,4},{1,9},{5,13},{9,1},{13,5},{2,10},{6,14},... | collective-permute-start | bytes 393224 | tf_op jit(solution)/shard_map/ppermute | solution.py:88
  8.1 0.0 copy-start.7
  8.1 0.6 %copy-done.7 = f32[128]{0:T(128)S(1)} copy-done((f32[128]{0:T(128)S(1)}, f32[128]{0:T(128)}, u32[]{:S(2)}) %copy-start.7) | copy-done | bytes 536
  8.7 0.1 multiply_sqrt_fusion
  8.8 0.0 copy-start.4
  8.8 0.2 multiply_cosine_fusion
  9.0 0.0 copy-start.6
  9.0 0.5 %copy-done.4 = f32[33,64]{1,0:T(8,128)S(1)} copy-done((f32[33,64]{1,0:T(8,128)S(1)}, f32[33,64]{1,0:T(8,128)}, u32[]{:S(2)}) %copy-start.4) | copy-done | bytes 8472
  9.5 0.1 copy-done.6
  9.7 0.7 %fusion.1 = f32[512,64]{0,1:T(8,128)S(1)} fusion(f32[33,64]{1,0:T(8,128)S(1)} %copy-done.4, f32[512,16]{0,1:T(8,128)S(1)} %get-tuple-element.22, f32[512,16]{0,1:T(8,128)S(1)} %get-tuple-element.21, f32[512,1]{0,1:T(1,128)S(1)} %convert_multiply_fusion, f32[64]{0:T(128)S(1)} %copy-done.6), kind=kOutput, calls=%fused_computation.2 | convolution fusion | flops 13075456 | bytes 207360 | tf_op jit(solution)/shard_map/dot_general | solution.py:22
  10.4 0.0 copy-done
  10.4 0.3 fusion.3
  10.8 0.6 %pad_convert_fusion.filt_ref = f32[5,32,128]{2,1,0:T(8,128)} fusion(bf16[4,32,128]{2,1,0:T(8,128)(2,1)S(1)} %bitcast.30), kind=kLoop, calls=%fused_computation.26 | loop fusion | flops 20480 | bytes 114688 | tf_op jit(solution)/shard_map/concatenate | solution.py:111
  11.4 0.0 collective-permute-done.2
  11.4 3.8 %collective-permute-done = bf16[512,128]{1,0:T(8,128)(2,1)S(1)} collective-permute-done((bf16[512,128]{1,0:T(8,128)(2,1)S(1)}, bf16[512,128]{1,0:T(8,128)(2,1)S(1)}, u32[]{:S(2)}, u32[]{:S(2)}) %collective-permute-start) | collective-permute-done | bytes 131104 | tf_op jit(solution)/shard_map/ppermute | solution.py:88
  15.2 3.3 %collective-permute-done.1 = bf16[512,128]{1,0:T(8,128)(2,1)S(1)} collective-permute-done((bf16[512,128]{1,0:T(8,128)(2,1)S(1)}, bf16[512,128]{1,0:T(8,128)(2,1)S(1)}, u32[]{:S(2)}, u32[]{:S(2)}) %collective-permute-start.1) | collective-permute-done | bytes 131104 | tf_op jit(solution)/shard_map/ppermute | solution.py:88
  18.5 0.9 %pad_maximum_fusion.z_ref = bf16[4,512,128]{2,1,0:T(8,128)(2,1)} fusion(bf16[1,512,128]{2,1,0:T(8,128)(2,1)S(1)} %bitcast.31, bf16[1,512,128]{2,1,0:T(8,128)(2,1)S(1)} %bitcast.33, bf16[1,512,128]{2,1,0:T(8,128)(2,1)S(1)} %bitcast.32, bf16[1,512,128]{2,1,0:T(8,128)(2,1)S(1)} %get-tuple-element.17), kind=kLoop, calls=%fused_computation.11 | loop fusion | flops 786432 | bytes 1048576 | tf_op jit(solution)/shard_map/stack | solution.py:113
  19.4 0.0 copy-start.2
  19.4 3.3 %shard_map.82 = (bf16[512,128]{1,0:T(8,128)(2,1)}, bf16[512,128]{1,0:T(8,128)(2,1)}, bf16[512,128]{1,0:T(8,128)(2,1)}, bf16[512,128]{1,0:T(8,128)(2,1)}) custom-call(s32[1]{0:T(128)} %bitcast.s_ref, f32[5,32,128]{2,1,0:T(8,128)} %pad_convert_fusion.filt_ref, bf16[4,512,128]{2,1,0:T(8,128)(2,1)} %pad_maximum_fusion.z_ref), custom_call_target="tpu_custom_call" | custom-call | tf_op jit(solution)/shard_map/pallas_call | solution.py:64
  22.7 2.3 %collective-permute-start.3 = (bf16[512,128]{1,0:T(8,128)(2,1)}, bf16[512,128]{1,0:T(8,128)(2,1)S(1)}, u32[]{:S(2)}, u32[]{:S(2)}) collective-permute-start(bf16[512,128]{1,0:T(8,128)(2,1)} %get-tuple-element.9), channel_id=1, source_target_pairs={{0,12},{4,0},{8,4},{12,8},{1,13},{5,1},{9,5},{13,9},{2,14},{6,2},{... | collective-permute-start | bytes 393224 | tf_op jit(solution)/shard_map/ppermute | solution.py:88
  24.9 0.0 collective-permute-start.4
  25.0 0.6 %collective-permute-start.5 = (bf16[512,128]{1,0:T(8,128)(2,1)}, bf16[512,128]{1,0:T(8,128)(2,1)S(1)}, u32[]{:S(2)}, u32[]{:S(2)}) collective-permute-start(bf16[512,128]{1,0:T(8,128)(2,1)} %get-tuple-element.11), channel_id=1, source_target_pairs={{0,4},{4,8},{8,12},{12,0},{1,5},{5,9},{9,13},{13,1},{2,6},{6,10},{... | collective-permute-start | bytes 393224 | tf_op jit(solution)/shard_map/ppermute | solution.py:88
  25.6 0.0 copy-done.2
  25.6 0.0 copy-start.3
  25.6 0.3 copy.18
  25.9 3.3 %collective-permute-done.3 = bf16[512,128]{1,0:T(8,128)(2,1)S(1)} collective-permute-done((bf16[512,128]{1,0:T(8,128)(2,1)}, bf16[512,128]{1,0:T(8,128)(2,1)S(1)}, u32[]{:S(2)}, u32[]{:S(2)}) %collective-permute-start.3) | collective-permute-done | bytes 131104 | tf_op jit(solution)/shard_map/ppermute | solution.py:88
  29.2 6.6 %collective-permute-done.4 = bf16[512,128]{1,0:T(8,128)(2,1)S(1)} collective-permute-done((bf16[512,128]{1,0:T(8,128)(2,1)}, bf16[512,128]{1,0:T(8,128)(2,1)S(1)}, u32[]{:S(2)}, u32[]{:S(2)}) %collective-permute-start.4) | collective-permute-done | bytes 131104 | tf_op jit(solution)/shard_map/ppermute | solution.py:88
  35.8 0.0 collective-permute-done.5
  35.8 0.0 copy-done.3
  35.8 0.0 copy-start.5
  35.8 0.1 select_select_fusion.3
  35.9 0.6 %copy-done.5 = f32[2048]{0:T(1024)S(1)} copy-done((f32[2048]{0:T(1024)S(1)}, f32[2048]{0:T(1024)}, u32[]{:S(2)}) %copy-start.5) | copy-done | bytes 8216
  36.5 0.4 %fusion.5 = bf16[128,2048]{0,1:T(8,128)(2,1)S(1)} fusion(bf16[128,2048]{0,1:T(8,128)(2,1)S(1)} %copy.18, bf16[128,2048]{0,1:T(8,128)(2,1)S(1)} %copy.21, bf16[128,2048]{0,1:T(8,128)(2,1)S(1)} %copy.20, bf16[512,128]{1,0:T(8,128)(2,1)S(1)} %get-tuple-element.14, bf16[512,128]{1,0:T(8,128)(2,1)S(1)} %get-tuple-element.15, ...), kind=kLoop, calls=%fused_computation.8 | loop fusion | flops 4456448 | bytes 2629632 | tf_op jit(solution)/shard_map/convert_element_type | solution.py:125
  36.9 1.0 %copy.22 = bf16[128,2048]{1,0:T(8,128)(2,1)} copy(bf16[128,2048]{0,1:T(8,128)(2,1)S(1)} %fusion.5) | data formatting | bytes 1048576 | tf_op jit(solution)/shard_map/convert_element_type | solution.py:125
  (5 shorter events, 0.1 us)
Async XLA Ops:
  0.0 10.4 %copy-start = (f32[64,128]{1,0:T(8,128)S(1)}, f32[64,128]{1,0:T(8,128)}, u32[]{:S(2)}) copy-start(f32[64,128]{1,0:T(8,128)} %param.13) | copy-start | bytes 98308
  0.0 1.4 %copy-start.1 = (bf16[128,2048]{1,0:T(8,128)(2,1)S(1)}, bf16[128,2048]{1,0:T(8,128)(2,1)}, u32[]{:S(2)}) copy-start(bf16[128,2048]{1,0:T(8,128)(2,1)} %param.10) | copy-start | bytes 1572868
  1.9 9.5 %collective-permute-start.2 = (bf16[512,128]{1,0:T(8,128)(2,1)S(1)}, bf16[512,128]{1,0:T(8,128)(2,1)S(1)}, u32[]{:S(2)}, u32[]{:S(2)}) collective-permute-start(bf16[512,128]{1,0:T(8,128)(2,1)S(1)} %get-tuple-element.18), channel_id=1, source_target_pairs={{0,12},{4,0},{8,4},{12,8},{1,13},{5,1},{9,5},{13,9},{2,14},{6,2},{... | collective-permute-start | bytes 393224 | tf_op jit(solution)/shard_map/ppermute | solution.py:88
  7.0 8.2 %collective-permute-start = (bf16[512,128]{1,0:T(8,128)(2,1)S(1)}, bf16[512,128]{1,0:T(8,128)(2,1)S(1)}, u32[]{:S(2)}, u32[]{:S(2)}) collective-permute-start(bf16[512,128]{1,0:T(8,128)(2,1)S(1)} %get-tuple-element.20), channel_id=1, source_target_pairs={{0,4},{4,8},{8,12},{12,0},{1,5},{5,9},{9,13},{13,1},{2,6},{6,10},{... | collective-permute-start | bytes 393224 | tf_op jit(solution)/shard_map/ppermute | solution.py:88
  7.0 11.5 %collective-permute-start.1 = (bf16[512,128]{1,0:T(8,128)(2,1)S(1)}, bf16[512,128]{1,0:T(8,128)(2,1)S(1)}, u32[]{:S(2)}, u32[]{:S(2)}) collective-permute-start(bf16[512,128]{1,0:T(8,128)(2,1)S(1)} %get-tuple-element.19), channel_id=1, source_target_pairs={{0,8},{4,12},{8,0},{12,4},{1,9},{5,13},{9,1},{13,5},{2,10},{6,14},... | collective-permute-start | bytes 393224 | tf_op jit(solution)/shard_map/ppermute | solution.py:88
  8.1 0.7 %copy-start.7 = (f32[128]{0:T(128)S(1)}, f32[128]{0:T(128)}, u32[]{:S(2)}) copy-start(f32[128]{0:T(128)} %param.14) | copy-start | bytes 1540
  8.8 0.7 %copy-start.4 = (f32[33,64]{1,0:T(8,128)S(1)}, f32[33,64]{1,0:T(8,128)}, u32[]{:S(2)}) copy-start(f32[33,64]{1,0:T(8,128)} %param.11) | copy-start | bytes 25348
  9.0 0.7 %copy-start.6 = (f32[64]{0:T(128)S(1)}, f32[64]{0:T(128)}, u32[]{:S(2)}) copy-start(f32[64]{0:T(128)} %param.12) | copy-start | bytes 772
  19.4 6.2 %copy-start.2 = (bf16[128,2048]{1,0:T(8,128)(2,1)S(1)}, bf16[128,2048]{1,0:T(8,128)(2,1)}, u32[]{:S(2)}) copy-start(bf16[128,2048]{1,0:T(8,128)(2,1)} %param.8) | copy-start | bytes 1572868
  22.7 6.5 %collective-permute-start.3 = (bf16[512,128]{1,0:T(8,128)(2,1)}, bf16[512,128]{1,0:T(8,128)(2,1)S(1)}, u32[]{:S(2)}, u32[]{:S(2)}) collective-permute-start(bf16[512,128]{1,0:T(8,128)(2,1)} %get-tuple-element.9), channel_id=1, source_target_pairs={{0,12},{4,0},{8,4},{12,8},{1,13},{5,1},{9,5},{13,9},{2,14},{6,2},{... | collective-permute-start | bytes 393224 | tf_op jit(solution)/shard_map/ppermute | solution.py:88
  24.9 10.8 %collective-permute-start.4 = (bf16[512,128]{1,0:T(8,128)(2,1)}, bf16[512,128]{1,0:T(8,128)(2,1)S(1)}, u32[]{:S(2)}, u32[]{:S(2)}) collective-permute-start(bf16[512,128]{1,0:T(8,128)(2,1)} %get-tuple-element.10), channel_id=1, source_target_pairs={{0,8},{4,12},{8,0},{12,4},{1,9},{5,13},{9,1},{13,5},{2,10},{6,14},... | collective-permute-start | bytes 393224 | tf_op jit(solution)/shard_map/ppermute | solution.py:88
  25.0 10.8 %collective-permute-start.5 = (bf16[512,128]{1,0:T(8,128)(2,1)}, bf16[512,128]{1,0:T(8,128)(2,1)S(1)}, u32[]{:S(2)}, u32[]{:S(2)}) collective-permute-start(bf16[512,128]{1,0:T(8,128)(2,1)} %get-tuple-element.11), channel_id=1, source_target_pairs={{0,4},{4,8},{8,12},{12,0},{1,5},{5,9},{9,13},{13,1},{2,6},{6,10},{... | collective-permute-start | bytes 393224 | tf_op jit(solution)/shard_map/ppermute | solution.py:88
  25.6 10.2 %copy-start.3 = (bf16[512,128]{1,0:T(8,128)(2,1)S(1)}, bf16[512,128]{1,0:T(8,128)(2,1)}, u32[]{:S(2)}) copy-start(bf16[512,128]{1,0:T(8,128)(2,1)} %get-tuple-element.12) | copy-start | bytes 393220
  35.8 0.7 %copy-start.5 = (f32[2048]{0:T(1024)S(1)}, f32[2048]{0:T(1024)}, u32[]{:S(2)}) copy-start(f32[2048]{0:T(1024)} %param.15) | copy-start | bytes 24580

commit v19 on v10

--- a/solution.py
+++ b/solution.py
@@ -111,7 +111,7 @@
     back = exchange(conv_parts, nb, s, True)
     order = (s - jnp.arange(nb, dtype=jnp.int32) + nb) % nb
     back = jnp.take(back, order, axis=0)
-    conv = back.reshape(width, own_rows).T.astype(jnp.float32)
+    conv = lax.optimization_barrier(back.reshape(width, own_rows).T).astype(jnp.float32)
     mixed = outer_gate.astype(jnp.float32) * (conv + skip_gain[None, :] * gated_f)
     return mixed.astype(jnp.bfloat16)
 

time: 38.2 us -> 38.4 us (level)
  no operation moved by 1% of the time
where the time goes in v19:
time: 38.4 us; the launch traced here: 37.7 us
  starting transfers between devices  12.8 us (33%)
  waiting for transfers between devices  11.1 us (29%)
  local copies, waits for them, and re-layouts  4.88 us (13%)
  other arithmetic  4.45 us (12%)
  Pallas kernels  3.27 us (9%)
  matrix products  1.07 us (3%)
    ppermute x6, starting transfers between devices, exchange(): lax.ppermute(piece, 'seq', [(i, (i + k) % nb) for i in range(nb)])  12.8 us
    ppermute x6, waiting for transfers between devices, exchange(): lax.ppermute(piece, 'seq', [(i, (i + k) % nb) for i in range(nb)])  11.1 us
    pallas_call x1, Pallas kernels, toeplitz_conv(): pl.pallas_call(toeplitz_kernel, out_shape=jax.ShapeDtypeStruct((nb, chans...  3.27 us
    unnamed x18, local copies, waits for them, and re-layouts  2.56 us
    transpose x1, other arithmetic, per_device(): gated_t = gated.T.reshape(nb, sub * GROUP, own_rows)  1.33 us
    convert_element_type x1, other arithmetic, per_device(): return mixed.astype(jnp.bfloat16)  1.16 us
    slice x1, local copies, waits for them, and re-layouts, exchange(): x[0]  1.13 us
    another operation x2, other arithmetic, exchange(): return jnp.stack(got)  0.93 us
  transfers between devices with their start and end apart: 6, of which 3 were waited for; matrix products, arithmetic and copies ran while one was open for 6% of the time, Pallas kernels for 0%

profile of v19, /device:TPU:0, one launch (start us, length us, event | category | flops | bytes accessed | tf_op | source)
XLA Modules:
  0.0 37.7 jit_solution(9773387351334693190)
XLA Ops:
  0.0 0.0 copy-start
  0.0 1.3 %fusion.5 = bf16[2048,128]{0,1:T(8,128)(2,1)S(1)} fusion(bf16[128,2048]{1,0:T(8,128)(2,1)} %param.10, bf16[128,2048]{1,0:T(8,128)(2,1)} %param.9), kind=kLoop, calls=%fused_computation.10 | loop fusion | flops 1310720 | bytes 1572864 | tf_op jit(solution)/shard_map/transpose | solution.py:101
  1.3 0.3 copy.15
  1.7 3.1 %collective-permute-start = (bf16[512,128]{1,0:T(8,128)(2,1)S(1)}, bf16[512,128]{1,0:T(8,128)(2,1)S(1)}, u32[]{:S(2)}, u32[]{:S(2)}) collective-permute-start(bf16[512,128]{1,0:T(8,128)(2,1)S(1)} %get-tuple-element.12), channel_id=1, source_target_pairs={{0,4},{4,8},{8,12},{12,0},{1,5},{5,9},{9,13},{13,1},{2,6},{6,10},{... | collective-permute-start | bytes 393224 | tf_op jit(solution)/shard_map/ppermute | solution.py:85
  4.8 2.6 %collective-permute-start.1 = (bf16[512,128]{1,0:T(8,128)(2,1)S(1)}, bf16[512,128]{1,0:T(8,128)(2,1)S(1)}, u32[]{:S(2)}, u32[]{:S(2)}) collective-permute-start(bf16[512,128]{1,0:T(8,128)(2,1)S(1)} %get-tuple-element.11), channel_id=1, source_target_pairs={{0,8},{4,12},{8,0},{12,4},{1,9},{5,13},{9,1},{13,5},{2,10},{6,14},... | collective-permute-start | bytes 393224 | tf_op jit(solution)/shard_map/ppermute | solution.py:85
  7.4 1.3 %collective-permute-start.2 = (bf16[512,128]{1,0:T(8,128)(2,1)S(1)}, bf16[512,128]{1,0:T(8,128)(2,1)S(1)}, u32[]{:S(2)}, u32[]{:S(2)}) collective-permute-start(bf16[512,128]{1,0:T(8,128)(2,1)S(1)} %get-tuple-element.10), channel_id=1, source_target_pairs={{0,12},{4,0},{8,4},{12,8},{1,13},{5,1},{9,5},{13,9},{2,14},{6,2},{... | collective-permute-start | bytes 393224 | tf_op jit(solution)/shard_map/ppermute | solution.py:85
  8.8 0.1 broadcast_bitcast_fusion
  8.8 0.0 copy-start.7
  8.9 0.7 %copy-done.7 = f32[128]{0:T(128)S(1)} copy-done((f32[128]{0:T(128)S(1)}, f32[128]{0:T(128)}, u32[]{:S(2)}) %copy-start.7) | copy-done | bytes 536
  9.5 0.1 multiply_sqrt_fusion
  9.6 0.0 copy-start.4
  9.6 0.2 multiply_cosine_fusion
  9.8 0.0 copy-start.6
  9.8 0.5 %copy-done.4 = f32[33,64]{1,0:T(8,128)S(1)} copy-done((f32[33,64]{1,0:T(8,128)S(1)}, f32[33,64]{1,0:T(8,128)}, u32[]{:S(2)}) %copy-start.4) | copy-done | bytes 8472
  10.3 0.1 copy-done.6
  10.4 0.7 %fusion.1 = f32[512,64]{0,1:T(8,128)S(1)} fusion(f32[33,64]{1,0:T(8,128)S(1)} %copy-done.4, f32[512,16]{0,1:T(8,128)S(1)} %get-tuple-element.14, f32[512,16]{0,1:T(8,128)S(1)} %get-tuple-element.13, f32[512,1]{0,1:T(1,128)S(1)} %convert_multiply_fusion, f32[64]{0:T(128)S(1)} %copy-done.6), kind=kOutput, calls=%fused_computation.3 | convolution fusion | flops 13075456 | bytes 207360 | tf_op jit(solution)/shard_map/dot_general | solution.py:22
  11.2 0.0 copy-done
  11.2 0.3 fusion.3
  11.6 0.6 %pad_convert_fusion.filt_ref = f32[5,32,128]{2,1,0:T(8,128)} fusion(bf16[4,32,128]{2,1,0:T(8,128)(2,1)S(1)} %bitcast.42), kind=kLoop, calls=%fused_computation.27 | loop fusion | flops 20480 | bytes 114688 | tf_op jit(solution)/shard_map/concatenate | solution.py:108
  12.2 0.0 collective-permute-done
  12.2 3.8 %collective-permute-done.1 = bf16[512,128]{1,0:T(8,128)(2,1)S(1)} collective-permute-done((bf16[512,128]{1,0:T(8,128)(2,1)S(1)}, bf16[512,128]{1,0:T(8,128)(2,1)S(1)}, u32[]{:S(2)}, u32[]{:S(2)}) %collective-permute-start.1) | collective-permute-done | bytes 131104 | tf_op jit(solution)/shard_map/ppermute | solution.py:85
  16.0 0.0 collective-permute-done.2
  16.0 0.9 %pad_maximum_fusion.z_ref = bf16[4,512,128]{2,1,0:T(8,128)(2,1)} fusion(bf16[1,512,128]{2,1,0:T(8,128)(2,1)S(1)} %bitcast.45, bf16[1,512,128]{2,1,0:T(8,128)(2,1)S(1)} %bitcast.44, bf16[1,512,128]{2,1,0:T(8,128)(2,1)S(1)} %bitcast.43, bf16[1,512,128]{2,1,0:T(8,128)(2,1)S(1)} %get-tuple-element.9), kind=kLoop, calls=%fused_computation.11 | loop fusion | flops 786432 | bytes 1048576 | tf_op jit(solution)/shard_map/stack | solution.py:86
  16.9 3.3 %shard_map.82 = bf16[4,512,128]{2,1,0:T(8,128)(2,1)} custom-call(s32[1]{0:T(128)} %bitcast.s_ref, f32[5,32,128]{2,1,0:T(8,128)} %pad_convert_fusion.filt_ref, bf16[4,512,128]{2,1,0:T(8,128)(2,1)} %pad_maximum_fusion.z_ref), custom_call_target="tpu_custom_call" | custom-call | tf_op jit(solution)/shard_map/pallas_call | solution.py:61
  20.2 1.1 %fusion.17 = (bf16[1,512,128]{2,1,0:T(8,128)(2,1)S(1)}, bf16[512,128]{1,0:T(8,128)(2,1)S(1)}, bf16[512,128]{1,0:T(8,128)(2,1)S(1)}, bf16[512,128]{1,0:T(8,128)(2,1)S(1)}) fusion(bf16[4,512,128]{2,1,0:T(8,128)(2,1)} %shard_map.82), kind=kLoop, calls=%fused_computation.52 | loop fusion | bytes 1048576 | tf_op jit(solution)/shard_map/slice | solution.py:79
  21.3 3.3 %collective-permute-start.3 = (bf16[512,128]{1,0:T(8,128)(2,1)S(1)}, bf16[512,128]{1,0:T(8,128)(2,1)S(1)}, u32[]{:S(2)}, u32[]{:S(2)}) collective-permute-start(bf16[512,128]{1,0:T(8,128)(2,1)S(1)} %get-tuple-element.8), channel_id=1, source_target_pairs={{0,4},{4,8},{8,12},{12,0},{1,5},{5,9},{9,13},{13,1},{2,6},{6,10},{... | collective-permute-start | bytes 393224 | tf_op jit(solution)/shard_map/ppermute | solution.py:85
  24.6 1.6 %collective-permute-start.4 = (bf16[512,128]{1,0:T(8,128)(2,1)S(1)}, bf16[512,128]{1,0:T(8,128)(2,1)S(1)}, u32[]{:S(2)}, u32[]{:S(2)}) collective-permute-start(bf16[512,128]{1,0:T(8,128)(2,1)S(1)} %get-tuple-element.7), channel_id=1, source_target_pairs={{0,8},{4,12},{8,0},{12,4},{1,9},{5,13},{9,1},{13,5},{2,10},{6,14},... | collective-permute-start | bytes 393224 | tf_op jit(solution)/shard_map/ppermute | solution.py:85
  26.3 0.8 %collective-permute-start.5 = (bf16[512,128]{1,0:T(8,128)(2,1)S(1)}, bf16[512,128]{1,0:T(8,128)(2,1)S(1)}, u32[]{:S(2)}, u32[]{:S(2)}) collective-permute-start(bf16[512,128]{1,0:T(8,128)(2,1)S(1)} %get-tuple-element.6), channel_id=1, source_target_pairs={{0,12},{4,0},{8,4},{12,8},{1,13},{5,1},{9,5},{13,9},{2,14},{6,2},{... | collective-permute-start | bytes 393224 | tf_op jit(solution)/shard_map/ppermute | solution.py:85
  27.1 2.6 %collective-permute-done.3 = bf16[512,128]{1,0:T(8,128)(2,1)S(1)} collective-permute-done((bf16[512,128]{1,0:T(8,128)(2,1)S(1)}, bf16[512,128]{1,0:T(8,128)(2,1)S(1)}, u32[]{:S(2)}, u32[]{:S(2)}) %collective-permute-start.3) | collective-permute-done | bytes 131104 | tf_op jit(solution)/shard_map/ppermute | solution.py:85
  29.7 4.6 %collective-permute-done.4 = bf16[512,128]{1,0:T(8,128)(2,1)S(1)} collective-permute-done((bf16[512,128]{1,0:T(8,128)(2,1)S(1)}, bf16[512,128]{1,0:T(8,128)(2,1)S(1)}, u32[]{:S(2)}, u32[]{:S(2)}) %collective-permute-start.4) | collective-permute-done | bytes 131104 | tf_op jit(solution)/shard_map/ppermute | solution.py:85
  34.4 0.0 collective-permute-done.5
  34.4 0.1 pad_maximum_fusion.1
  34.4 0.6 %gather_fusion = bf16[4,512,128]{2,1,0:T(8,128)(2,1)S(1)} fusion(bf16[4,512,128]{2,1,0:T(8,128)(2,1)S(1)} %pad_maximum_fusion.1, s32[1024]{0:T(1024)S(1)} %pad_clamp_fusion), kind=kCustom, calls=%fused_computation | custom fusion | bytes 1048592 | tf_op jit(solution)/shard_map/jit(_take)/gather | solution.py:113
  35.1 0.0 copy-start.3
  35.1 0.0 copy-start.5
  35.1 0.2 copy.16
  35.3 0.0 copy-start.1
  35.3 0.0 copy-start.2
  35.4 0.1 select_bitcast_fusion
  35.4 0.7 %copy-done.3 = bf16[128,2048]{1,0:T(8,128)(2,1)S(1)} copy-done((bf16[128,2048]{1,0:T(8,128)(2,1)S(1)}, bf16[128,2048]{1,0:T(8,128)(2,1)}, u32[]{:S(2)}) %copy-start.3) | copy-done | bytes 524312
  36.1 0.0 copy-done.5
  36.1 0.3 copy-done.1
  36.4 0.2 copy-done.2
  36.6 1.2 %multiply_convert_fusion = bf16[128,2048]{1,0:T(8,128)(2,1)} fusion(bf16[128,2048]{1,0:T(8,128)(2,1)S(1)} %select_bitcast_fusion, bf16[128,2048]{1,0:T(8,128)(2,1)S(1)} %copy-done.3, bf16[128,2048]{1,0:T(8,128)(2,1)S(1)} %copy-done.1, bf16[128,2048]{1,0:T(8,128)(2,1)S(1)} %copy-done.2, f32[2048]{0:T(1024)S(1)} %copy-done.5), kind=kLoop, calls=%fused_computation.7 | loop fusion | flops 2621440 | bytes 2629632 | tf_op jit(solution)/shard_map/convert_element_type | solution.py:116
  (9 shorter events, 0.1 us)
Async XLA Ops:
  0.0 11.2 %copy-start = (f32[64,128]{1,0:T(8,128)S(1)}, f32[64,128]{1,0:T(8,128)}, u32[]{:S(2)}) copy-start(f32[64,128]{1,0:T(8,128)} %param.13) | copy-start | bytes 98308
  1.7 10.5 %collective-permute-start = (bf16[512,128]{1,0:T(8,128)(2,1)S(1)}, bf16[512,128]{1,0:T(8,128)(2,1)S(1)}, u32[]{:S(2)}, u32[]{:S(2)}) collective-permute-start(bf16[512,128]{1,0:T(8,128)(2,1)S(1)} %get-tuple-element.12), channel_id=1, source_target_pairs={{0,4},{4,8},{8,12},{12,0},{1,5},{5,9},{9,13},{13,1},{2,6},{6,10},{... | collective-permute-start | bytes 393224 | tf_op jit(solution)/shard_map/ppermute | solution.py:85
  4.8 11.2 %collective-permute-start.1 = (bf16[512,128]{1,0:T(8,128)(2,1)S(1)}, bf16[512,128]{1,0:T(8,128)(2,1)S(1)}, u32[]{:S(2)}, u32[]{:S(2)}) collective-permute-start(bf16[512,128]{1,0:T(8,128)(2,1)S(1)} %get-tuple-element.11), channel_id=1, source_target_pairs={{0,8},{4,12},{8,0},{12,4},{1,9},{5,13},{9,1},{13,5},{2,10},{6,14},... | collective-permute-start | bytes 393224 | tf_op jit(solution)/shard_map/ppermute | solution.py:85
  7.4 8.6 %collective-permute-start.2 = (bf16[512,128]{1,0:T(8,128)(2,1)S(1)}, bf16[512,128]{1,0:T(8,128)(2,1)S(1)}, u32[]{:S(2)}, u32[]{:S(2)}) collective-permute-start(bf16[512,128]{1,0:T(8,128)(2,1)S(1)} %get-tuple-element.10), channel_id=1, source_target_pairs={{0,12},{4,0},{8,4},{12,8},{1,13},{5,1},{9,5},{13,9},{2,14},{6,2},{... | collective-permute-start | bytes 393224 | tf_op jit(solution)/shard_map/ppermute | solution.py:85
  8.8 0.7 %copy-start.7 = (f32[128]{0:T(128)S(1)}, f32[128]{0:T(128)}, u32[]{:S(2)}) copy-start(f32[128]{0:T(128)} %param.14) | copy-start | bytes 1540
  9.6 0.7 %copy-start.4 = (f32[33,64]{1,0:T(8,128)S(1)}, f32[33,64]{1,0:T(8,128)}, u32[]{:S(2)}) copy-start(f32[33,64]{1,0:T(8,128)} %param.11) | copy-start | bytes 25348
  9.8 0.7 %copy-start.6 = (f32[64]{0:T(128)S(1)}, f32[64]{0:T(128)}, u32[]{:S(2)}) copy-start(f32[64]{0:T(128)} %param.12) | copy-start | bytes 772
  21.3 8.4 %collective-permute-start.3 = (bf16[512,128]{1,0:T(8,128)(2,1)S(1)}, bf16[512,128]{1,0:T(8,128)(2,1)S(1)}, u32[]{:S(2)}, u32[]{:S(2)}) collective-permute-start(bf16[512,128]{1,0:T(8,128)(2,1)S(1)} %get-tuple-element.8), channel_id=1, source_target_pairs={{0,4},{4,8},{8,12},{12,0},{1,5},{5,9},{9,13},{13,1},{2,6},{6,10},{... | collective-permute-start | bytes 393224 | tf_op jit(solution)/shard_map/ppermute | solution.py:85
  24.6 9.7 %collective-permute-start.4 = (bf16[512,128]{1,0:T(8,128)(2,1)S(1)}, bf16[512,128]{1,0:T(8,128)(2,1)S(1)}, u32[]{:S(2)}, u32[]{:S(2)}) collective-permute-start(bf16[512,128]{1,0:T(8,128)(2,1)S(1)} %get-tuple-element.7), channel_id=1, source_target_pairs={{0,8},{4,12},{8,0},{12,4},{1,9},{5,13},{9,1},{13,5},{2,10},{6,14},... | collective-permute-start | bytes 393224 | tf_op jit(solution)/shard_map/ppermute | solution.py:85
  26.3 8.1 %collective-permute-start.5 = (bf16[512,128]{1,0:T(8,128)(2,1)S(1)}, bf16[512,128]{1,0:T(8,128)(2,1)S(1)}, u32[]{:S(2)}, u32[]{:S(2)}) collective-permute-start(bf16[512,128]{1,0:T(8,128)(2,1)S(1)} %get-tuple-element.6), channel_id=1, source_target_pairs={{0,12},{4,0},{8,4},{12,8},{1,13},{5,1},{9,5},{13,9},{2,14},{6,2},{... | collective-permute-start | bytes 393224 | tf_op jit(solution)/shard_map/ppermute | solution.py:85
  35.1 1.0 %copy-start.3 = (bf16[128,2048]{1,0:T(8,128)(2,1)S(1)}, bf16[128,2048]{1,0:T(8,128)(2,1)}, u32[]{:S(2)}) copy-start(bf16[128,2048]{1,0:T(8,128)(2,1)} %param.8) | copy-start | bytes 1572868
  35.1 1.0 %copy-start.5 = (f32[2048]{0:T(1024)S(1)}, f32[2048]{0:T(1024)}, u32[]{:S(2)}) copy-start(f32[2048]{0:T(1024)} %param.15) | copy-start | bytes 24580
  35.3 1.1 %copy-start.1 = (bf16[128,2048]{1,0:T(8,128)(2,1)S(1)}, bf16[128,2048]{1,0:T(8,128)(2,1)}, u32[]{:S(2)}) copy-start(bf16[128,2048]{1,0:T(8,128)(2,1)} %param.10) | copy-start | bytes 1572868
  35.3 1.2 %copy-start.2 = (bf16[128,2048]{1,0:T(8,128)(2,1)S(1)}, bf16[128,2048]{1,0:T(8,128)(2,1)}, u32[]{:S(2)}) copy-start(bf16[128,2048]{1,0:T(8,128)(2,1)} %param.9) | copy-start | bytes 1572868

commit v20 on v10

--- a/solution.py
+++ b/solution.py
@@ -98,8 +98,16 @@
     gated_f = lax.reduce_precision(
         inner_gate.astype(jnp.float32) * signal.astype(jnp.float32), exponent_bits=8, mantissa_bits=7)
     gated = gated_f.astype(jnp.bfloat16)
-    gated_t = gated.T.reshape(nb, sub * GROUP, own_rows)
-    got = exchange(gated_t, nb, s, False)
+    chunk = sub * GROUP
+    pieces = []
+    for k in range(nb):
+        start = ((s + k) % nb) * chunk
+        part = lax.reduce_precision(
+            lax.dynamic_slice_in_dim(inner_gate, start, chunk, 1).astype(jnp.float32)
+            * lax.dynamic_slice_in_dim(signal, start, chunk, 1).astype(jnp.float32),
+            exponent_bits=8, mantissa_bits=7)
+        pieces.append(part.astype(jnp.bfloat16).T)
+    got = exchange(pieces, nb, s, True)
     positions = jnp.arange(total_rows, dtype=jnp.int32).astype(jnp.float32)
     my_out = lax.dynamic_slice_in_dim(filter_out, s * sub, sub, 1)
     my_decay = lax.dynamic_slice_in_dim(decay, s * sub, sub, 0)

time: 38.2 us -> 38.2 us (level)
  local copies, waits for them, and re-layouts: 4.72 us -> 6.75 us
  other arithmetic: 4.42 us -> 3.24 us
  waiting for transfers between devices: 11.1 us -> 10.1 us
    dynamic_slice x1, local copies, waits for them, and re-layouts: 0.05 us -> 1.4 us  [per_device(): lax.dynamic_slice_in_dim(signal, start, chunk, 1).astype(jnp.float32)]
    transpose x1 -> x3, other arithmetic: 1.33 us -> 0.12 us  [per_device(): pieces.append(part.astype(jnp.bfloat16).T)]
    ppermute x6, waiting for transfers between devices: 11.1 us -> 10.1 us  [exchange(): lax.ppermute(piece, 'seq', [(i, (i + k) % nb) for i in range(nb)])]
    unnamed x18 -> x26, local copies, waits for them, and re-layouts: 2.41 us -> 3.36 us
    another operation x2 -> x3, other arithmetic: 0.93 us -> 0.97 us  [exchange(): return jnp.stack(got)]
  transfers between devices with their start and end apart: 6 -> 6, of which waited for: 3 -> 4; matrix products, arithmetic and copies ran while one was open for 6% -> 8% of each run, Pallas kernels for 0% -> 0%
where the time goes in v20:
time: 38.2 us; the launch traced here: 37.6 us
  starting transfers between devices  12.9 us (34%)
  waiting for transfers between devices  10.1 us (26%)
  local copies, waits for them, and re-layouts  6.75 us (18%)
  Pallas kernels  3.27 us (9%)
  other arithmetic  3.24 us (8%)
  matrix products  1.07 us (3%)
    ppermute x6, starting transfers between devices, exchange(): lax.ppermute(piece, 'seq', [(i, (i + k) % nb) for i in range(nb)])  12.9 us
    ppermute x6, waiting for transfers between devices, exchange(): lax.ppermute(piece, 'seq', [(i, (i + k) % nb) for i in range(nb)])  10.1 us
    unnamed x26, local copies, waits for them, and re-layouts  3.36 us
    pallas_call x1, Pallas kernels, toeplitz_conv(): pl.pallas_call(toeplitz_kernel, out_shape=jax.ShapeDtypeStruct((nb, chans...  3.27 us
    dynamic_slice x1, local copies, waits for them, and re-layouts, per_device(): lax.dynamic_slice_in_dim(signal, start, chunk, 1).astype(jnp.float32)  1.4 us
    convert_element_type x1, other arithmetic, per_device(): return mixed.astype(jnp.bfloat16)  1.18 us
    slice x1, local copies, waits for them, and re-layouts, exchange(): x[0]  1.13 us
    another operation x3, other arithmetic, exchange(): return jnp.stack(got)  0.97 us
  transfers between devices with their start and end apart: 6, of which 4 were waited for; matrix products, arithmetic and copies ran while one was open for 8% of the time, Pallas kernels for 0%

profile of v20, /device:TPU:0, one launch (start us, length us, event | category | flops | bytes accessed | tf_op | source)
XLA Modules:
  0.0 37.6 jit_solution(14667892743026095025)
XLA Ops:
  0.0 0.0 copy-start
  0.0 1.4 %constant_dynamic-slice_fusion.6 = (bf16[128,512]{1,0:T(8,128)(2,1)S(1)}, bf16[128,512]{1,0:T(8,128)(2,1)S(1)}, bf16[128,512]{1,0:T(8,128)(2,1)S(1)}, bf16[128,5...) fusion(bf16[128,2048]{1,0:T(8,128)(2,1)} %param.10, ...), kind=kLoop, calls=%fused_computation.43 | loop fusion | bytes 2097168 | tf_op jit(solution)/shard_map/dynamic_slice | solution.py:107
  1.4 0.1 copy.40
  1.5 0.1 copy.41
  1.7 3.1 %collective-permute-start = (bf16[512,128]{1,0:T(8,128)(2,1)S(1)}, bf16[512,128]{1,0:T(8,128)(2,1)S(1)}, u32[]{:S(2)}, u32[]{:S(2)}) collective-permute-start(bf16[512,128]{1,0:T(8,128)(2,1)S(1)} %fusion.7), channel_id=1, source_target_pairs={{0,4},{4,8},{8,12},{12,0},{1,5},{5,9},{9,13},{13,1},{2,6},{6,10},{... | collective-permute-start | bytes 393224 | tf_op jit(solution)/shard_map/ppermute | solution.py:85
  4.8 0.1 copy.42
  4.9 0.1 copy.43
  5.1 2.7 %collective-permute-start.1 = (bf16[512,128]{1,0:T(8,128)(2,1)S(1)}, bf16[512,128]{1,0:T(8,128)(2,1)S(1)}, u32[]{:S(2)}, u32[]{:S(2)}) collective-permute-start(bf16[512,128]{1,0:T(8,128)(2,1)S(1)} %fusion.8), channel_id=1, source_target_pairs={{0,8},{4,12},{8,0},{12,4},{1,9},{5,13},{9,1},{13,5},{2,10},{6,14},... | collective-permute-start | bytes 393224 | tf_op jit(solution)/shard_map/ppermute | solution.py:85
  7.8 0.1 copy.44
  7.9 0.1 copy.45
  8.1 1.4 %collective-permute-start.2 = (bf16[512,128]{1,0:T(8,128)(2,1)S(1)}, bf16[512,128]{1,0:T(8,128)(2,1)S(1)}, u32[]{:S(2)}, u32[]{:S(2)}) collective-permute-start(bf16[512,128]{1,0:T(8,128)(2,1)S(1)} %fusion.9), channel_id=1, source_target_pairs={{0,12},{4,0},{8,4},{12,8},{1,13},{5,1},{9,5},{13,9},{2,14},{6,2},{... | collective-permute-start | bytes 393224 | tf_op jit(solution)/shard_map/ppermute | solution.py:85
  9.5 0.1 copy.38
  9.6 0.1 copy.39
  9.8 0.1 broadcast_bitcast_fusion
  9.9 0.0 copy-start.7
  9.9 0.6 %copy-done.7 = f32[128]{0:T(128)S(1)} copy-done((f32[128]{0:T(128)S(1)}, f32[128]{0:T(128)}, u32[]{:S(2)}) %copy-start.7) | copy-done | bytes 536
  10.5 0.1 multiply_sqrt_fusion
  10.6 0.0 copy-start.4
  10.6 0.2 multiply_cosine_fusion
  10.8 0.0 copy-start.6
  10.8 0.5 %copy-done.4 = f32[33,64]{1,0:T(8,128)S(1)} copy-done((f32[33,64]{1,0:T(8,128)S(1)}, f32[33,64]{1,0:T(8,128)}, u32[]{:S(2)}) %copy-start.4) | copy-done | bytes 8472
  11.4 0.1 copy-done.6
  11.5 0.7 %fusion.1 = f32[512,64]{0,1:T(8,128)S(1)} fusion(f32[33,64]{1,0:T(8,128)S(1)} %copy-done.4, f32[512,16]{0,1:T(8,128)S(1)} %get-tuple-element.18, f32[512,16]{0,1:T(8,128)S(1)} %get-tuple-element.17, f32[512,1]{0,1:T(1,128)S(1)} %convert_multiply_fusion, f32[64]{0:T(128)S(1)} %copy-done.6), kind=kOutput, calls=%fused_computation.3 | convolution fusion | flops 13075456 | bytes 207360 | tf_op jit(solution)/shard_map/dot_general | solution.py:22
  12.2 0.0 copy-done
  12.2 0.3 fusion.3
  12.6 0.6 %pad_convert_fusion.filt_ref = f32[5,32,128]{2,1,0:T(8,128)} fusion(bf16[4,32,128]{2,1,0:T(8,128)(2,1)S(1)} %bitcast.46), kind=kLoop, calls=%fused_computation.30 | loop fusion | flops 20480 | bytes 114688 | tf_op jit(solution)/shard_map/concatenate | solution.py:116
  13.2 0.0 collective-permute-done
  13.2 2.8 %collective-permute-done.1 = bf16[512,128]{1,0:T(8,128)(2,1)S(1)} collective-permute-done((bf16[512,128]{1,0:T(8,128)(2,1)S(1)}, bf16[512,128]{1,0:T(8,128)(2,1)S(1)}, u32[]{:S(2)}, u32[]{:S(2)}) %collective-permute-start.1) | collective-permute-done | bytes 131104 | tf_op jit(solution)/shard_map/ppermute | solution.py:85
  16.1 0.1 collective-permute-done.2
  16.2 0.9 %pad_maximum_fusion.z_ref = bf16[4,512,128]{2,1,0:T(8,128)(2,1)} fusion(bf16[1,512,128]{2,1,0:T(8,128)(2,1)S(1)} %bitcast.49, bf16[1,512,128]{2,1,0:T(8,128)(2,1)S(1)} %bitcast.48, bf16[1,512,128]{2,1,0:T(8,128)(2,1)S(1)} %bitcast.47, bf16[1,512,128]{2,1,0:T(8,128)(2,1)S(1)} %fusion.6), kind=kLoop, calls=%fused_computation.10 | loop fusion | flops 786432 | bytes 1048576 | tf_op jit(solution)/shard_map/stack | solution.py:86
  17.0 3.3 %shard_map.82 = bf16[4,512,128]{2,1,0:T(8,128)(2,1)} custom-call(s32[1]{0:T(128)} %bitcast.s_ref, f32[5,32,128]{2,1,0:T(8,128)} %pad_convert_fusion.filt_ref, bf16[4,512,128]{2,1,0:T(8,128)(2,1)} %pad_maximum_fusion.z_ref), custom_call_target="tpu_custom_call" | custom-call | tf_op jit(solution)/shard_map/pallas_call | solution.py:61
  20.3 1.1 %fusion.21 = (bf16[1,512,128]{2,1,0:T(8,128)(2,1)S(1)}, bf16[512,128]{1,0:T(8,128)(2,1)S(1)}, bf16[512,128]{1,0:T(8,128)(2,1)S(1)}, bf16[512,128]{1,0:T(8,128)(2,1)S(1)}) fusion(bf16[4,512,128]{2,1,0:T(8,128)(2,1)} %shard_map.82), kind=kLoop, calls=%fused_computation.62 | loop fusion | bytes 1048576 | tf_op jit(solution)/shard_map/slice | solution.py:79
  21.4 3.3 %collective-permute-start.3 = (bf16[512,128]{1,0:T(8,128)(2,1)S(1)}, bf16[512,128]{1,0:T(8,128)(2,1)S(1)}, u32[]{:S(2)}, u32[]{:S(2)}) collective-permute-start(bf16[512,128]{1,0:T(8,128)(2,1)S(1)} %get-tuple-element.8), channel_id=1, source_target_pairs={{0,4},{4,8},{8,12},{12,0},{1,5},{5,9},{9,13},{13,1},{2,6},{6,10},{... | collective-permute-start | bytes 393224 | tf_op jit(solution)/shard_map/ppermute | solution.py:85
  24.7 1.6 %collective-permute-start.4 = (bf16[512,128]{1,0:T(8,128)(2,1)S(1)}, bf16[512,128]{1,0:T(8,128)(2,1)S(1)}, u32[]{:S(2)}, u32[]{:S(2)}) collective-permute-start(bf16[512,128]{1,0:T(8,128)(2,1)S(1)} %get-tuple-element.7), channel_id=1, source_target_pairs={{0,8},{4,12},{8,0},{12,4},{1,9},{5,13},{9,1},{13,5},{2,10},{6,14},... | collective-permute-start | bytes 393224 | tf_op jit(solution)/shard_map/ppermute | solution.py:85
  26.3 0.9 %collective-permute-start.5 = (bf16[512,128]{1,0:T(8,128)(2,1)S(1)}, bf16[512,128]{1,0:T(8,128)(2,1)S(1)}, u32[]{:S(2)}, u32[]{:S(2)}) collective-permute-start(bf16[512,128]{1,0:T(8,128)(2,1)S(1)} %get-tuple-element.6), channel_id=1, source_target_pairs={{0,12},{4,0},{8,4},{12,8},{1,13},{5,1},{9,5},{13,9},{2,14},{6,2},{... | collective-permute-start | bytes 393224 | tf_op jit(solution)/shard_map/ppermute | solution.py:85
  27.2 2.5 %collective-permute-done.3 = bf16[512,128]{1,0:T(8,128)(2,1)S(1)} collective-permute-done((bf16[512,128]{1,0:T(8,128)(2,1)S(1)}, bf16[512,128]{1,0:T(8,128)(2,1)S(1)}, u32[]{:S(2)}, u32[]{:S(2)}) %collective-permute-start.3) | collective-permute-done | bytes 131104 | tf_op jit(solution)/shard_map/ppermute | solution.py:85
  29.7 4.7 %collective-permute-done.4 = bf16[512,128]{1,0:T(8,128)(2,1)S(1)} collective-permute-done((bf16[512,128]{1,0:T(8,128)(2,1)S(1)}, bf16[512,128]{1,0:T(8,128)(2,1)S(1)}, u32[]{:S(2)}, u32[]{:S(2)}) %collective-permute-start.4) | collective-permute-done | bytes 131104 | tf_op jit(solution)/shard_map/ppermute | solution.py:85
  34.4 0.0 collective-permute-done.5
  34.4 0.1 pad_maximum_fusion.1
  34.4 0.0 copy-start.3
  34.5 0.0 copy-start.5
  34.5 0.6 %gather_fusion = bf16[4,512,128]{2,1,0:T(8,128)(2,1)S(1)} fusion(bf16[4,512,128]{2,1,0:T(8,128)(2,1)S(1)} %pad_maximum_fusion.1, s32[1024]{0:T(1024)S(1)} %pad_clamp_fusion), kind=kCustom, calls=%fused_computation | custom fusion | bytes 1048592 | tf_op jit(solution)/shard_map/jit(_take)/gather | solution.py:121
  35.1 0.0 copy-start.1
  35.1 0.0 copy-start.2
  35.2 0.2 copy.37
  35.4 0.1 copy-done.3
  35.5 0.0 copy-done.5
  35.5 0.7 %copy-done.1 = bf16[128,2048]{1,0:T(8,128)(2,1)S(1)} copy-done((bf16[128,2048]{1,0:T(8,128)(2,1)S(1)}, bf16[128,2048]{1,0:T(8,128)(2,1)}, u32[]{:S(2)}) %copy-start.1) | copy-done | bytes 524312
  36.2 0.2 copy-done.2
  36.4 1.2 %fusion.5 = bf16[128,2048]{1,0:T(8,128)(2,1)} fusion(bf16[128,2048]{1,0:T(8,128)(2,1)S(1)} %copy-done.1, bf16[128,2048]{1,0:T(8,128)(2,1)S(1)} %copy-done.2, bf16[128,2048]{1,0:T(8,128)(2,1)S(1)} %copy-done.3, f32[2048]{0:T(1024)S(1)} %copy-done.5, bf16[2048,128]{0,1:T(8,128)(2,1)S(1)} %copy.37, pred[2048]{0:T(1024)(128)(4,1)S(1)} %bitcast.53), kind=kLoop, calls=%fused_computation.9 | loop fusion | flops 2883584 | bytes 2631680 | tf_op jit(solution)/shard_map/convert_element_type | solution.py:124
  (12 shorter events, 0.2 us)
Async XLA Ops:
  0.0 12.2 %copy-start = (f32[64,128]{1,0:T(8,128)S(1)}, f32[64,128]{1,0:T(8,128)}, u32[]{:S(2)}) copy-start(f32[64,128]{1,0:T(8,128)} %param.13) | copy-start | bytes 98308
  1.7 11.5 %collective-permute-start = (bf16[512,128]{1,0:T(8,128)(2,1)S(1)}, bf16[512,128]{1,0:T(8,128)(2,1)S(1)}, u32[]{:S(2)}, u32[]{:S(2)}) collective-permute-start(bf16[512,128]{1,0:T(8,128)(2,1)S(1)} %fusion.7), channel_id=1, source_target_pairs={{0,4},{4,8},{8,12},{12,0},{1,5},{5,9},{9,13},{13,1},{2,6},{6,10},{... | collective-permute-start | bytes 393224 | tf_op jit(solution)/shard_map/ppermute | solution.py:85
  5.1 11.0 %collective-permute-start.1 = (bf16[512,128]{1,0:T(8,128)(2,1)S(1)}, bf16[512,128]{1,0:T(8,128)(2,1)S(1)}, u32[]{:S(2)}, u32[]{:S(2)}) collective-permute-start(bf16[512,128]{1,0:T(8,128)(2,1)S(1)} %fusion.8), channel_id=1, source_target_pairs={{0,8},{4,12},{8,0},{12,4},{1,9},{5,13},{9,1},{13,5},{2,10},{6,14},... | collective-permute-start | bytes 393224 | tf_op jit(solution)/shard_map/ppermute | solution.py:85
  8.1 8.1 %collective-permute-start.2 = (bf16[512,128]{1,0:T(8,128)(2,1)S(1)}, bf16[512,128]{1,0:T(8,128)(2,1)S(1)}, u32[]{:S(2)}, u32[]{:S(2)}) collective-permute-start(bf16[512,128]{1,0:T(8,128)(2,1)S(1)} %fusion.9), channel_id=1, source_target_pairs={{0,12},{4,0},{8,4},{12,8},{1,13},{5,1},{9,5},{13,9},{2,14},{6,2},{... | collective-permute-start | bytes 393224 | tf_op jit(solution)/shard_map/ppermute | solution.py:85
  9.9 0.7 %copy-start.7 = (f32[128]{0:T(128)S(1)}, f32[128]{0:T(128)}, u32[]{:S(2)}) copy-start(f32[128]{0:T(128)} %param.14) | copy-start | bytes 1540
  10.6 0.7 %copy-start.4 = (f32[33,64]{1,0:T(8,128)S(1)}, f32[33,64]{1,0:T(8,128)}, u32[]{:S(2)}) copy-start(f32[33,64]{1,0:T(8,128)} %param.11) | copy-start | bytes 25348
  10.8 0.7 %copy-start.6 = (f32[64]{0:T(128)S(1)}, f32[64]{0:T(128)}, u32[]{:S(2)}) copy-start(f32[64]{0:T(128)} %param.12) | copy-start | bytes 772
  21.4 8.3 %collective-permute-start.3 = (bf16[512,128]{1,0:T(8,128)(2,1)S(1)}, bf16[512,128]{1,0:T(8,128)(2,1)S(1)}, u32[]{:S(2)}, u32[]{:S(2)}) collective-permute-start(bf16[512,128]{1,0:T(8,128)(2,1)S(1)} %get-tuple-element.8), channel_id=1, source_target_pairs={{0,4},{4,8},{8,12},{12,0},{1,5},{5,9},{9,13},{13,1},{2,6},{6,10},{... | collective-permute-start | bytes 393224 | tf_op jit(solution)/shard_map/ppermute | solution.py:85
  24.7 9.7 %collective-permute-start.4 = (bf16[512,128]{1,0:T(8,128)(2,1)S(1)}, bf16[512,128]{1,0:T(8,128)(2,1)S(1)}, u32[]{:S(2)}, u32[]{:S(2)}) collective-permute-start(bf16[512,128]{1,0:T(8,128)(2,1)S(1)} %get-tuple-element.7), channel_id=1, source_target_pairs={{0,8},{4,12},{8,0},{12,4},{1,9},{5,13},{9,1},{13,5},{2,10},{6,14},... | collective-permute-start | bytes 393224 | tf_op jit(solution)/shard_map/ppermute | solution.py:85
  26.3 8.1 %collective-permute-start.5 = (bf16[512,128]{1,0:T(8,128)(2,1)S(1)}, bf16[512,128]{1,0:T(8,128)(2,1)S(1)}, u32[]{:S(2)}, u32[]{:S(2)}) collective-permute-start(bf16[512,128]{1,0:T(8,128)(2,1)S(1)} %get-tuple-element.6), channel_id=1, source_target_pairs={{0,12},{4,0},{8,4},{12,8},{1,13},{5,1},{9,5},{13,9},{2,14},{6,2},{... | collective-permute-start | bytes 393224 | tf_op jit(solution)/shard_map/ppermute | solution.py:85
  34.4 1.0 %copy-start.3 = (bf16[128,2048]{1,0:T(8,128)(2,1)S(1)}, bf16[128,2048]{1,0:T(8,128)(2,1)}, u32[]{:S(2)}) copy-start(bf16[128,2048]{1,0:T(8,128)(2,1)} %param.8) | copy-start | bytes 1572868
  34.5 1.0 %copy-start.5 = (f32[2048]{0:T(1024)S(1)}, f32[2048]{0:T(1024)}, u32[]{:S(2)}) copy-start(f32[2048]{0:T(1024)} %param.15) | copy-start | bytes 24580
  35.1 1.1 %copy-start.1 = (bf16[128,2048]{1,0:T(8,128)(2,1)S(1)}, bf16[128,2048]{1,0:T(8,128)(2,1)}, u32[]{:S(2)}) copy-start(bf16[128,2048]{1,0:T(8,128)(2,1)} %param.10) | copy-start | bytes 1572868
  35.1 1.2 %copy-start.2 = (bf16[128,2048]{1,0:T(8,128)(2,1)S(1)}, bf16[128,2048]{1,0:T(8,128)(2,1)}, u32[]{:S(2)}) copy-start(bf16[128,2048]{1,0:T(8,128)(2,1)} %param.9) | copy-start | bytes 1572868

commit v21 on v18

--- a/solution.py
+++ b/solution.py
@@ -101,8 +101,16 @@
     gated_f = lax.reduce_precision(
         inner_gate.astype(jnp.float32) * signal.astype(jnp.float32), exponent_bits=8, mantissa_bits=7)
     gated = gated_f.astype(jnp.bfloat16)
-    gated_t = gated.T.reshape(nb, sub * GROUP, own_rows)
-    got = exchange(gated_t, nb, s, False)
+    chunk = sub * GROUP
+    pieces = []
+    for k in range(nb):
+        start = ((s + k) % nb) * chunk
+        part = lax.reduce_precision(
+            lax.dynamic_slice_in_dim(inner_gate, start, chunk, 1).astype(jnp.float32)
+            * lax.dynamic_slice_in_dim(signal, start, chunk, 1).astype(jnp.float32),
+            exponent_bits=8, mantissa_bits=7)
+        pieces.append(part.astype(jnp.bfloat16).T)
+    got = exchange(pieces, nb, s, True)
     positions = jnp.arange(total_rows, dtype=jnp.int32).astype(jnp.float32)
     my_out = lax.dynamic_slice_in_dim(filter_out, s * sub, sub, 1)
     my_decay = lax.dynamic_slice_in_dim(decay, s * sub, sub, 0)

time: 38.2 us -> 39.6 us (1.037)
  starting transfers between devices: 9.04 us -> 12 us
  waiting for transfers between devices: 17 us -> 15.4 us
    ppermute x6, starting transfers between devices: 9.04 us -> 12 us  [exchange(): lax.ppermute(piece, 'seq', [(i, (i + k) % nb) for i in range(nb)])]
    ppermute x6, waiting for transfers between devices: 17 us -> 15.4 us  [exchange(): lax.ppermute(piece, 'seq', [(i, (i + k) % nb) for i in range(nb)])]
    another operation x1 -> x2, other arithmetic: 0.86 us -> 1.01 us  [per_device(): conv_parts = toeplitz_conv(s_arr, filt, jnp.stack(got))]
  transfers between devices with their start and end apart: 6 -> 6, of which waited for: 4 -> 3; matrix products, arithmetic and copies ran while one was open for 6% -> 6% of each run, Pallas kernels for 0% -> 0%
where the time goes in v21:
time: 39.6 us; the launch traced here: 39.4 us
  waiting for transfers between devices  15.4 us (39%)
  starting transfers between devices  12 us (30%)
  local copies, waits for them, and re-layouts  4.86 us (12%)
  Pallas kernels  3.33 us (8%)
  other arithmetic  2.47 us (6%)
  matrix products  1.07 us (3%)
    ppermute x6, waiting for transfers between devices, exchange(): lax.ppermute(piece, 'seq', [(i, (i + k) % nb) for i in range(nb)])  15.4 us
    ppermute x6, starting transfers between devices, exchange(): lax.ppermute(piece, 'seq', [(i, (i + k) % nb) for i in range(nb)])  12 us
    unnamed x19, local copies, waits for them, and re-layouts  3.84 us
    pallas_call x1, Pallas kernels, toeplitz_conv(): pl.pallas_call(toeplitz_kernel, out_shape=[jax.ShapeDtypeStruct((chans, b...  3.33 us
    another operation x2, other arithmetic, per_device(): conv_parts = toeplitz_conv(s_arr, filt, jnp.stack(got))  1.01 us
    convert_element_type x1, local copies, waits for them, and re-layouts, per_device(): return mixed.astype(jnp.bfloat16)  1.01 us
  transfers between devices with their start and end apart: 6, of which 3 were waited for; matrix products, arithmetic and copies ran while one was open for 6% of the time, Pallas kernels for 0%

profile of v21, /device:TPU:0, one launch (start us, length us, event | category | flops | bytes accessed | tf_op | source)
XLA Modules:
  0.0 39.4 jit_solution(1312303385720037395)
XLA Ops:
  0.0 0.0 copy-start
  0.0 0.0 copy-start.1
  0.0 1.4 %copy.36 = bf16[128,2048]{0,1:T(8,128)(2,1)S(1)} copy(bf16[128,2048]{1,0:T(8,128)(2,1)} %param.9) | data formatting | bytes 1048576 | tf_op args[1]
  1.4 0.0 copy-done.1
  1.4 0.3 copy.37
  1.7 0.1 fusion.6
  1.8 3.1 %collective-permute-start = (bf16[512,128]{1,0:T(8,128)(2,1)S(1)}, bf16[512,128]{1,0:T(8,128)(2,1)S(1)}, u32[]{:S(2)}, u32[]{:S(2)}) collective-permute-start(bf16[512,128]{1,0:T(8,128)(2,1)S(1)} %get-tuple-element.16), channel_id=1, source_target_pairs={{0,4},{4,8},{8,12},{12,0},{1,5},{5,9},{9,13},{13,1},{2,6},{6,10},{... | collective-permute-start | bytes 393224 | tf_op jit(solution)/shard_map/ppermute | solution.py:88
  4.9 2.6 %collective-permute-start.1 = (bf16[512,128]{1,0:T(8,128)(2,1)S(1)}, bf16[512,128]{1,0:T(8,128)(2,1)S(1)}, u32[]{:S(2)}, u32[]{:S(2)}) collective-permute-start(bf16[512,128]{1,0:T(8,128)(2,1)S(1)} %get-tuple-element.15), channel_id=1, source_target_pairs={{0,8},{4,12},{8,0},{12,4},{1,9},{5,13},{9,1},{13,5},{2,10},{6,14},... | collective-permute-start | bytes 393224 | tf_op jit(solution)/shard_map/ppermute | solution.py:88
  7.5 1.3 %collective-permute-start.2 = (bf16[512,128]{1,0:T(8,128)(2,1)S(1)}, bf16[512,128]{1,0:T(8,128)(2,1)S(1)}, u32[]{:S(2)}, u32[]{:S(2)}) collective-permute-start(bf16[512,128]{1,0:T(8,128)(2,1)S(1)} %get-tuple-element.14), channel_id=1, source_target_pairs={{0,12},{4,0},{8,4},{12,8},{1,13},{5,1},{9,5},{13,9},{2,14},{6,2},{... | collective-permute-start | bytes 393224 | tf_op jit(solution)/shard_map/ppermute | solution.py:88
  8.9 0.0 copy-start.7
  8.9 0.6 %copy-done.7 = f32[128]{0:T(128)S(1)} copy-done((f32[128]{0:T(128)S(1)}, f32[128]{0:T(128)}, u32[]{:S(2)}) %copy-start.7) | copy-done | bytes 536
  9.6 0.1 multiply_sqrt_fusion
  9.6 0.0 copy-start.4
  9.7 0.2 multiply_cosine_fusion
  9.9 0.0 copy-start.6
  9.9 0.5 %copy-done.4 = f32[33,64]{1,0:T(8,128)S(1)} copy-done((f32[33,64]{1,0:T(8,128)S(1)}, f32[33,64]{1,0:T(8,128)}, u32[]{:S(2)}) %copy-start.4) | copy-done | bytes 8472
  10.4 0.1 copy-done.6
  10.5 0.7 %fusion.1 = f32[512,64]{0,1:T(8,128)S(1)} fusion(f32[33,64]{1,0:T(8,128)S(1)} %copy-done.4, f32[512,16]{0,1:T(8,128)S(1)} %get-tuple-element.22, f32[512,16]{0,1:T(8,128)S(1)} %get-tuple-element.21, f32[512,1]{0,1:T(1,128)S(1)} %convert_multiply_fusion, f32[64]{0:T(128)S(1)} %copy-done.6), kind=kOutput, calls=%fused_computation.2 | convolution fusion | flops 13075456 | bytes 207360 | tf_op jit(solution)/shard_map/dot_general | solution.py:22
  11.3 0.0 copy-done
  11.3 0.3 fusion.3
  11.6 0.6 %pad_convert_fusion.filt_ref = f32[5,32,128]{2,1,0:T(8,128)} fusion(bf16[4,32,128]{2,1,0:T(8,128)(2,1)S(1)} %bitcast.30), kind=kLoop, calls=%fused_computation.29 | loop fusion | flops 20480 | bytes 114688 | tf_op jit(solution)/shard_map/concatenate | solution.py:119
  12.3 0.0 collective-permute-done
  12.3 3.9 %collective-permute-done.1 = bf16[512,128]{1,0:T(8,128)(2,1)S(1)} collective-permute-done((bf16[512,128]{1,0:T(8,128)(2,1)S(1)}, bf16[512,128]{1,0:T(8,128)(2,1)S(1)}, u32[]{:S(2)}, u32[]{:S(2)}) %collective-permute-start.1) | collective-permute-done | bytes 131104 | tf_op jit(solution)/shard_map/ppermute | solution.py:88
  16.2 0.0 collective-permute-done.2
  16.2 0.9 %pad_maximum_fusion.z_ref = bf16[4,512,128]{2,1,0:T(8,128)(2,1)} fusion(bf16[1,512,128]{2,1,0:T(8,128)(2,1)S(1)} %bitcast.33, bf16[1,512,128]{2,1,0:T(8,128)(2,1)S(1)} %bitcast.32, bf16[1,512,128]{2,1,0:T(8,128)(2,1)S(1)} %bitcast.31, bf16[1,512,128]{2,1,0:T(8,128)(2,1)S(1)} %get-tuple-element.13), kind=kLoop, calls=%fused_computation.9 | loop fusion | flops 786432 | bytes 1048576 | tf_op jit(solution)/shard_map/stack | solution.py:121
  17.0 0.0 copy-start.2
  17.0 3.3 %shard_map.82 = (bf16[512,128]{1,0:T(8,128)(2,1)}, bf16[512,128]{1,0:T(8,128)(2,1)}, bf16[512,128]{1,0:T(8,128)(2,1)}, bf16[512,128]{1,0:T(8,128)(2,1)}) custom-call(s32[1]{0:T(128)} %bitcast.s_ref, f32[5,32,128]{2,1,0:T(8,128)} %pad_convert_fusion.filt_ref, bf16[4,512,128]{2,1,0:T(8,128)(2,1)} %pad_maximum_fusion.z_ref), custom_call_target="tpu_custom_call" | custom-call | tf_op jit(solution)/shard_map/pallas_call | solution.py:64
  20.4 4.4 %collective-permute-start.3 = (bf16[512,128]{1,0:T(8,128)(2,1)}, bf16[512,128]{1,0:T(8,128)(2,1)S(1)}, u32[]{:S(2)}, u32[]{:S(2)}) collective-permute-start(bf16[512,128]{1,0:T(8,128)(2,1)} %get-tuple-element.9), channel_id=1, source_target_pairs={{0,12},{4,0},{8,4},{12,8},{1,13},{5,1},{9,5},{13,9},{2,14},{6,2},{... | collective-permute-start | bytes 393224 | tf_op jit(solution)/shard_map/ppermute | solution.py:88
  24.7 0.4 %collective-permute-start.4 = (bf16[512,128]{1,0:T(8,128)(2,1)}, bf16[512,128]{1,0:T(8,128)(2,1)S(1)}, u32[]{:S(2)}, u32[]{:S(2)}) collective-permute-start(bf16[512,128]{1,0:T(8,128)(2,1)} %get-tuple-element.10), channel_id=1, source_target_pairs={{0,8},{4,12},{8,0},{12,4},{1,9},{5,13},{9,1},{13,5},{2,10},{6,14},... | collective-permute-start | bytes 393224 | tf_op jit(solution)/shard_map/ppermute | solution.py:88
  25.2 0.2 collective-permute-start.5
  25.4 0.0 copy-done.2
  25.4 0.0 copy-start.3
  25.4 0.3 copy.34
  25.7 3.3 %collective-permute-done.3 = bf16[512,128]{1,0:T(8,128)(2,1)S(1)} collective-permute-done((bf16[512,128]{1,0:T(8,128)(2,1)}, bf16[512,128]{1,0:T(8,128)(2,1)S(1)}, u32[]{:S(2)}, u32[]{:S(2)}) %collective-permute-start.3) | collective-permute-done | bytes 131104 | tf_op jit(solution)/shard_map/ppermute | solution.py:88
  28.9 8.2 %collective-permute-done.4 = bf16[512,128]{1,0:T(8,128)(2,1)S(1)} collective-permute-done((bf16[512,128]{1,0:T(8,128)(2,1)}, bf16[512,128]{1,0:T(8,128)(2,1)S(1)}, u32[]{:S(2)}, u32[]{:S(2)}) %collective-permute-start.4) | collective-permute-done | bytes 131104 | tf_op jit(solution)/shard_map/ppermute | solution.py:88
  37.2 0.0 collective-permute-done.5
  37.2 0.0 copy-done.3
  37.2 0.0 copy-start.5
  37.2 0.1 select_select_fusion.3
  37.3 0.6 %copy-done.5 = f32[2048]{0:T(1024)S(1)} copy-done((f32[2048]{0:T(1024)S(1)}, f32[2048]{0:T(1024)}, u32[]{:S(2)}) %copy-start.5) | copy-done | bytes 8216
  37.9 0.4 %fusion.5 = bf16[128,2048]{0,1:T(8,128)(2,1)S(1)} fusion(bf16[128,2048]{0,1:T(8,128)(2,1)S(1)} %copy.37, bf16[128,2048]{0,1:T(8,128)(2,1)S(1)} %copy.36, bf16[128,2048]{0,1:T(8,128)(2,1)S(1)} %copy.34, bf16[512,128]{1,0:T(8,128)(2,1)S(1)} %get-tuple-element.18, bf16[512,128]{1,0:T(8,128)(2,1)S(1)} %get-tuple-element.19, ...), kind=kLoop, calls=%fused_computation.8 | loop fusion | flops 4456448 | bytes 2629632 | tf_op jit(solution)/shard_map/convert_element_type | solution.py:133
  38.4 1.0 %copy.46 = bf16[128,2048]{1,0:T(8,128)(2,1)} copy(bf16[128,2048]{0,1:T(8,128)(2,1)S(1)} %fusion.5) | data formatting | bytes 1048576 | tf_op jit(solution)/shard_map/convert_element_type | solution.py:133
  (4 shorter events, 0.0 us)
Async XLA Ops:
  0.0 11.3 %copy-start = (f32[64,128]{1,0:T(8,128)S(1)}, f32[64,128]{1,0:T(8,128)}, u32[]{:S(2)}) copy-start(f32[64,128]{1,0:T(8,128)} %param.13) | copy-start | bytes 98308
  0.0 1.4 %copy-start.1 = (bf16[128,2048]{1,0:T(8,128)(2,1)S(1)}, bf16[128,2048]{1,0:T(8,128)(2,1)}, u32[]{:S(2)}) copy-start(bf16[128,2048]{1,0:T(8,128)(2,1)} %param.10) | copy-start | bytes 1572868
  1.8 10.4 %collective-permute-start = (bf16[512,128]{1,0:T(8,128)(2,1)S(1)}, bf16[512,128]{1,0:T(8,128)(2,1)S(1)}, u32[]{:S(2)}, u32[]{:S(2)}) collective-permute-start(bf16[512,128]{1,0:T(8,128)(2,1)S(1)} %get-tuple-element.16), channel_id=1, source_target_pairs={{0,4},{4,8},{8,12},{12,0},{1,5},{5,9},{9,13},{13,1},{2,6},{6,10},{... | collective-permute-start | bytes 393224 | tf_op jit(solution)/shard_map/ppermute | solution.py:88
  4.9 11.2 %collective-permute-start.1 = (bf16[512,128]{1,0:T(8,128)(2,1)S(1)}, bf16[512,128]{1,0:T(8,128)(2,1)S(1)}, u32[]{:S(2)}, u32[]{:S(2)}) collective-permute-start(bf16[512,128]{1,0:T(8,128)(2,1)S(1)} %get-tuple-element.15), channel_id=1, source_target_pairs={{0,8},{4,12},{8,0},{12,4},{1,9},{5,13},{9,1},{13,5},{2,10},{6,14},... | collective-permute-start | bytes 393224 | tf_op jit(solution)/shard_map/ppermute | solution.py:88
  7.5 8.6 %collective-permute-start.2 = (bf16[512,128]{1,0:T(8,128)(2,1)S(1)}, bf16[512,128]{1,0:T(8,128)(2,1)S(1)}, u32[]{:S(2)}, u32[]{:S(2)}) collective-permute-start(bf16[512,128]{1,0:T(8,128)(2,1)S(1)} %get-tuple-element.14), channel_id=1, source_target_pairs={{0,12},{4,0},{8,4},{12,8},{1,13},{5,1},{9,5},{13,9},{2,14},{6,2},{... | collective-permute-start | bytes 393224 | tf_op jit(solution)/shard_map/ppermute | solution.py:88
  8.9 0.7 %copy-start.7 = (f32[128]{0:T(128)S(1)}, f32[128]{0:T(128)}, u32[]{:S(2)}) copy-start(f32[128]{0:T(128)} %param.14) | copy-start | bytes 1540
  9.6 0.7 %copy-start.4 = (f32[33,64]{1,0:T(8,128)S(1)}, f32[33,64]{1,0:T(8,128)}, u32[]{:S(2)}) copy-start(f32[33,64]{1,0:T(8,128)} %param.11) | copy-start | bytes 25348
  9.9 0.7 %copy-start.6 = (f32[64]{0:T(128)S(1)}, f32[64]{0:T(128)}, u32[]{:S(2)}) copy-start(f32[64]{0:T(128)} %param.12) | copy-start | bytes 772
  17.0 8.3 %copy-start.2 = (bf16[128,2048]{1,0:T(8,128)(2,1)S(1)}, bf16[128,2048]{1,0:T(8,128)(2,1)}, u32[]{:S(2)}) copy-start(bf16[128,2048]{1,0:T(8,128)(2,1)} %param.8) | copy-start | bytes 1572868
  20.4 8.6 %collective-permute-start.3 = (bf16[512,128]{1,0:T(8,128)(2,1)}, bf16[512,128]{1,0:T(8,128)(2,1)S(1)}, u32[]{:S(2)}, u32[]{:S(2)}) collective-permute-start(bf16[512,128]{1,0:T(8,128)(2,1)} %get-tuple-element.9), channel_id=1, source_target_pairs={{0,12},{4,0},{8,4},{12,8},{1,13},{5,1},{9,5},{13,9},{2,14},{6,2},{... | collective-permute-start | bytes 393224 | tf_op jit(solution)/shard_map/ppermute | solution.py:88
  24.7 12.4 %collective-permute-start.4 = (bf16[512,128]{1,0:T(8,128)(2,1)}, bf16[512,128]{1,0:T(8,128)(2,1)S(1)}, u32[]{:S(2)}, u32[]{:S(2)}) collective-permute-start(bf16[512,128]{1,0:T(8,128)(2,1)} %get-tuple-element.10), channel_id=1, source_target_pairs={{0,8},{4,12},{8,0},{12,4},{1,9},{5,13},{9,1},{13,5},{2,10},{6,14},... | collective-permute-start | bytes 393224 | tf_op jit(solution)/shard_map/ppermute | solution.py:88
  25.2 12.0 %collective-permute-start.5 = (bf16[512,128]{1,0:T(8,128)(2,1)}, bf16[512,128]{1,0:T(8,128)(2,1)S(1)}, u32[]{:S(2)}, u32[]{:S(2)}) collective-permute-start(bf16[512,128]{1,0:T(8,128)(2,1)} %get-tuple-element.11), channel_id=1, source_target_pairs={{0,4},{4,8},{8,12},{12,0},{1,5},{5,9},{9,13},{13,1},{2,6},{6,10},{... | collective-permute-start | bytes 393224 | tf_op jit(solution)/shard_map/ppermute | solution.py:88
  25.4 11.8 %copy-start.3 = (bf16[512,128]{1,0:T(8,128)(2,1)S(1)}, bf16[512,128]{1,0:T(8,128)(2,1)}, u32[]{:S(2)}) copy-start(bf16[512,128]{1,0:T(8,128)(2,1)} %get-tuple-element.12) | copy-start | bytes 393220
  37.2 0.7 %copy-start.5 = (f32[2048]{0:T(1024)S(1)}, f32[2048]{0:T(1024)}, u32[]{:S(2)}) copy-start(f32[2048]{0:T(1024)} %param.15) | copy-start | bytes 24580
